TPU v7x, 256 devices: a whole 4x4x8 slice. The times are simulated.
256 devices in a mesh: section: 2 (over y_hi), grp: 4 (over x), tok: 32 (over y_lo, z, core).
Axes of the slice: x: 4, y: 4 (y_hi: 2, y_lo: 2; y = y_hi * 2 + y_lo), z: 8, core: 2. Of those that a mesh axis runs over, the one named last changes fastest.
Arguments:
- image_in: bfloat16 [2, 4, 128, 3072], P('section', 'grp', 'tok'), may hold values from -1.5 to 1.5
- text_in: bfloat16 [2, 4, 512, 3072], P('section', 'grp', 'tok'), may hold values from -1.5 to 1.5
- text_length: int32 [4], P('grp'), may hold values from 256 to 512, as said below
- entry_order: int32 [4, 4], P('grp'), may hold values from 0 to 3, as said below
- step_index: int32 [4, 4], P('grp'), may hold values from 0 to 3
- image_modulation: bfloat16 [2, 4, 18432], P('section'), may hold values from -3 to 3
- text_modulation: bfloat16 [2, 4, 9216], P('section'), may hold values from -3 to 3
- image_to_heads: bfloat16 [2, 3072, 9216], P('section', None, 'tok'), may hold values from -0.109375 to 0.109375
- text_to_heads: bfloat16 [2, 3072, 9216], P('section', None, 'tok'), may hold values from -0.109375 to 0.109375
- head_gain: float32 [2, 4, 128], P('section'), may hold values from 0.5 to 2
- image_from_heads: bfloat16 [2, 3072, 3072], P('section', None, 'tok'), may hold values from -0.109375 to 0.109375
- text_from_heads: bfloat16 [2, 3072, 3072], P('section', None, 'tok'), may hold values from -0.109375 to 0.109375
- image_up: bfloat16 [2, 3072, 12288], P('section', None, 'tok'), may hold values from -0.109375 to 0.109375
- image_down: bfloat16 [2, 12288, 3072], P('section', 'tok'), may hold values from -0.0546875 to 0.0546875
- stale_cache: bfloat16 [2, 4, 512, 6144], P('section', 'grp', 'tok'), may hold values from -400 to 400
- final_modulation: bfloat16 [4, 6144], replicated, may hold values from -3 to 3
- final_weight: bfloat16 [3072, 64], P(None, 'section'), may hold values from -0.109375 to 0.109375
- latents: float32 [4, 128, 64], P('grp', 'tok', 'section'), may hold values from -6 to 6
Outputs:
- image_handoff: bfloat16 [2, 4, 128, 3072], P('section', 'grp', 'tok')
- text_handoff: bfloat16 [2, 4, 512, 3072], P('section', 'grp', 'tok')
- fresh_cache: bfloat16 [2, 4, 512, 6144], P('section', 'grp', 'tok')
- latents_next: float32 [4, 128, 64], P('grp', 'tok', 'section')
Inputs may be any that keep to these rules, and one draw needn't show every extreme that they name: `text_length`: valid text tokens of each request; some request has exactly 512. `entry_order`: each row is a permutation of the 4 patch numbers.
All inputs are finite; a program needn't handle non-finite values.
Results may differ from a plain program's by a relative error of at most 0.023.
The roundings to bfloat16 on the way count: a program that leaves them out, or rounds other values in their place, can miss the bound.
Values may be sent and summed in bfloat16 or wider, within the bound.
No kernel may reach another device: no remote copies, remote signals or barrier semaphores. Data moves between devices by JAX's collectives and lax.ppermute only.
A program may use at most 128 MiB of HBM per device.

v0:
```python
import jax
import jax.numpy as jnp
from jax import lax
from jax.sharding import PartitionSpec as P

HDIM = 128
TSTEPS = 4


eps = 1e-06
masked_score = -1e30


def from_behind(block, axis, distance):
    devices = range(lax.axis_size(axis))
    route = [((i - distance) % len(devices), i) for i in devices]
    return lax.ppermute(block, axis, route)


def layer_norm(field):
    mean = jnp.mean(field, axis=-1, keepdims=True)
    centred = field - mean
    spread = jnp.mean(centred * centred, axis=-1, keepdims=True)
    return centred * lax.rsqrt(spread + eps)


def modulate(field, shift, scale):
    return layer_norm(field) * (1.0 + scale) + shift


def head_norm(field, gain):
    height, width = field.shape
    shaped = field.reshape(height, width // HDIM, HDIM)
    power = jnp.mean(shaped * shaped, axis=-1, keepdims=True)
    return (shaped * lax.rsqrt(power + eps) * gain).reshape(height, width)


def attend(carry, queries, piece, valid):
    highest, total, mixed = carry
    height, width = queries.shape
    heads = width // HDIM
    keys = piece[:, :width].reshape(-1, heads, HDIM)
    values = piece[:, width:].reshape(-1, heads, HDIM)
    scores = jnp.einsum(
        "qhd,khd->qhk",
        queries.reshape(height, heads, HDIM),
        keys,
        preferred_element_type=jnp.float32,
    ) * HDIM ** (-0.5)
    scores = jnp.where(valid[None, None, :], scores, masked_score)
    new_high = jnp.maximum(highest, jnp.max(scores, axis=-1))
    expo = jnp.where(valid[None, None, :], jnp.exp(scores - new_high[..., None]), 0.0)
    keep = jnp.exp(highest - new_high)
    total = total * keep + jnp.sum(expo, axis=-1)
    mixed = mixed * keep[..., None] + jnp.einsum(
        "qhk,khd->qhd", expo.astype(jnp.bfloat16), values, preferred_element_type=jnp.float32
    )
    return (new_high, total, mixed)


def empty_carry(height, heads):
    return (
        jnp.full((height, heads), masked_score, jnp.float32),
        jnp.zeros((height, heads), jnp.float32),
        jnp.zeros((height, heads, HDIM), jnp.float32),
    )


def shards(
    image_in,
    text_in,
    text_length,
    entry_order,
    step_index,
    image_modulation,
    text_modulation,
    image_to_heads,
    text_to_heads,
    head_gain,
    image_from_heads,
    text_from_heads,
    image_up,
    image_down,
    stale_cache,
    final_modulation,
    final_weight,
    latents,
):
    section = lax.axis_index("section")
    last_section = lax.axis_size("section") - 1
    position = lax.axis_index("tok")
    image_x = image_in[0, 0].astype(jnp.float32)
    text_x = text_in[0, 0].astype(jnp.float32)
    image_rows = image_x.shape[0]
    width = image_x.shape[1]
    heads = width // HDIM
    patch = lax.dynamic_index_in_dim(entry_order[0], section, 0, False)
    step_now = lax.dynamic_index_in_dim(step_index[0], patch, 0, False)
    modul = (
        lax.dynamic_index_in_dim(image_modulation[0], step_now, 0, False)
        .astype(jnp.float32)
        .reshape(6, width)
    )
    text_mod = (
        lax.dynamic_index_in_dim(text_modulation[0], step_now, 0, False)
        .astype(jnp.float32)
        .reshape(3, width)
    )
    image_normed = modulate(image_x, modul[0], modul[1]).astype(jnp.bfloat16)
    text_normed = modulate(text_x, text_mod[0], text_mod[1]).astype(jnp.bfloat16)
    every_image, every_text = (
        lax.all_gather(image_normed, "tok", axis=0, tiled=True),
        lax.all_gather(text_normed, "tok", axis=0, tiled=True),
    )
    image_cols = jnp.dot(every_image, image_to_heads[0], preferred_element_type=jnp.float32).astype(
        jnp.bfloat16
    )
    text_cols = jnp.dot(every_text, text_to_heads[0], preferred_element_type=jnp.float32).astype(
        jnp.bfloat16
    )
    image_proj, text_proj = (
        lax.all_to_all(image_cols, "tok", split_axis=0, concat_axis=1, tiled=True),
        lax.all_to_all(text_cols, "tok", split_axis=0, concat_axis=1, tiled=True),
    )
    gains = head_gain[0]
    image_query = head_norm(image_proj[:, :width].astype(jnp.float32), gains[0]).astype(
        jnp.bfloat16
    )
    image_key = head_norm(image_proj[:, width : 2 * width].astype(jnp.float32), gains[1]).astype(
        jnp.bfloat16
    )
    text_query = head_norm(text_proj[:, :width].astype(jnp.float32), gains[2]).astype(jnp.bfloat16)
    text_key = head_norm(text_proj[:, width : 2 * width].astype(jnp.float32), gains[3]).astype(
        jnp.bfloat16
    )
    fresh_image = jnp.concatenate([image_key, image_proj[:, 2 * width :]], axis=1)
    fresh_text = jnp.concatenate([text_key, text_proj[:, 2 * width :]], axis=1)
    queries = jnp.concatenate([image_query, text_query], axis=0)
    query_rows = queries.shape[0]
    patch_rows = lax.all_gather(fresh_image, "tok", axis=0, tiled=True)
    stale = stale_cache[0, 0]
    cache_rows = stale.shape[0]
    patch_len = patch_rows.shape[0]
    first_row = position * cache_rows
    begin = patch * patch_len
    offset = jnp.clip(first_row - begin, 0, patch_len - cache_rows)
    window = lax.dynamic_slice_in_dim(patch_rows, offset, cache_rows, 0)
    inside = jnp.logical_and(first_row >= begin, first_row < begin + patch_len)
    current = jnp.where(inside, window, stale)
    text_count = text_length[0]
    piece = lax.all_gather(current, "tok", axis=0, tiled=True)
    carry = attend(
        empty_carry(query_rows, heads), queries, piece, jnp.ones((piece.shape[0],), bool)
    )
    piece = lax.all_gather(fresh_text, "tok", axis=0, tiled=True)
    where_text = jnp.arange(piece.shape[0], dtype=jnp.int32)
    highest, total, mixed = attend(carry, queries, piece, where_text < text_count)
    attended = (mixed / total[..., None]).reshape(query_rows, width).astype(jnp.bfloat16)
    every_image_att, every_text_att = (
        lax.all_gather(attended[:image_rows], "tok", axis=0, tiled=True),
        lax.all_gather(attended[image_rows:], "tok", axis=0, tiled=True),
    )
    image_back_cols = jnp.dot(
        every_image_att, image_from_heads[0], preferred_element_type=jnp.float32
    ).astype(jnp.bfloat16)
    text_back_cols = jnp.dot(
        every_text_att, text_from_heads[0], preferred_element_type=jnp.float32
    ).astype(jnp.bfloat16)
    image_back, text_back = (
        lax.all_to_all(image_back_cols, "tok", split_axis=0, concat_axis=1, tiled=True),
        lax.all_to_all(text_back_cols, "tok", split_axis=0, concat_axis=1, tiled=True),
    )
    image_mid = image_x + modul[2] * image_back.astype(jnp.float32)
    text_out = (text_x + text_mod[2] * text_back.astype(jnp.float32)).astype(jnp.bfloat16)
    mlp_normed = modulate(image_mid, modul[3], modul[4]).astype(jnp.bfloat16)
    up_weight = image_up[0]
    down_weight = image_down[0]
    hidden = jax.nn.gelu(
        jnp.dot(
            lax.all_gather(mlp_normed, "tok", axis=0, tiled=True),
            up_weight,
            preferred_element_type=jnp.float32,
        ),
        approximate=True,
    ).astype(jnp.bfloat16)
    reduced = lax.psum_scatter(
        jnp.dot(hidden, down_weight, preferred_element_type=jnp.float32),
        "tok",
        scatter_dimension=0,
        tiled=True,
    )
    image_out = (image_mid + modul[5] * reduced).astype(jnp.bfloat16)
    joined = from_behind(jnp.concatenate([image_out, text_out], axis=0), "section", 1)
    image_next = joined[:image_rows]
    text_next = joined[image_rows:]
    final_source = jnp.where(section == last_section, image_out, image_next)
    patch_last = entry_order[0, last_section]
    step_last = lax.dynamic_index_in_dim(step_index[0], patch_last, 0, False)
    final_mod = (
        lax.dynamic_index_in_dim(final_modulation, step_last, 0, False)
        .astype(jnp.float32)
        .reshape(2, width)
    )
    normed = modulate(final_source.astype(jnp.float32), final_mod[0], final_mod[1]).astype(
        jnp.bfloat16
    )
    velocity = jnp.dot(normed, final_weight, preferred_element_type=jnp.float32)
    latents_next = latents[0] + -1.0 / TSTEPS * velocity
    return (image_next[None, None], text_next[None, None], current[None, None], latents_next[None])


def solution(mesh):
    placed = (
        P("section", "grp", "tok", None),
        P("section", "grp", "tok", None),
        P("grp"),
        P("grp", None),
        P("grp", None),
        P("section", None, None),
        P("section", None, None),
        P("section", None, "tok"),
        P("section", None, "tok"),
        P("section", None, None),
        P("section", None, "tok"),
        P("section", None, "tok"),
        P("section", None, "tok"),
        P("section", "tok", None),
        P("section", "grp", "tok", None),
        P(),
        P(None, "section"),
        P("grp", "tok", "section"),
    )
    return jax.shard_map(
        shards,
        mesh=mesh,
        in_specs=placed,
        out_specs=(
            P("section", "grp", "tok", None),
            P("section", "grp", "tok", None),
            P("section", "grp", "tok", None),
            P("grp", "tok", "section"),
        ),
        check_vma=False,
    )
```

profile of v0, /device:TPU:2, one launch (start us, length us, event | category | flops | bytes accessed | tf_op | source)
XLA Modules:
  0.0 711.5 jit_solution(14484903372511090327)
XLA Ops:
  20.1 39.4 %all-gather = bf16[32,4,3072]{2,1,0:T(4,128)(2,1)S(1)} all-gather(bf16[1,4,3072]{2,1,0:T(4,128)(2,1)S(1)} %fusion.94), channel_id=1, replica_groups=mesh['section'=2,'grp'=4,'tok'=32] {'tok'}, dimensions={0}, use_global_device_ids=true | all-gather | bytes 811008 | tf_op jit(solution)/shard_map/all_gather | solution.py:112
  60.5 2.4 fusion.19
  63.7 3.9 all-to-all-start
  67.7 9.7 %all-to-all-done = bf16[32,4,288]{2,1,0:T(4,128)(2,1)S(1)} async-done(((bf16[32,4,288]{2,1,0:T(4,128)(2,1)}), bf16[32,4,288]{2,1,0:T(4,128)(2,1)S(1)}, u32[]{:S(2)}, u32[]{:S(2)}) %all-to-all-start) | async-done | bytes 73760 | tf_op jit(solution)/shard_map/all_to_all | solution.py:122
  81.8 58.1 %all-gather.18.cloned.1.call-done = bf16[32,4,6144]{2,1,0:T(4,128)(2,1)} async-done(((bf16[1,4,6144]{2,1,0:T(4,128)(2,1)}), bf16[32,4,6144]{2,1,0:T(4,128)(2,1)}) %all-gather.18.cloned.1.call-update) | async-done | bytes 1572880 | tf_op jit(solution)/shard_map/all_gather | solution.py:140
  139.8 3.7 reshape.266
  143.5 1.7 bitcast_select_fusion
  145.2 62.8 %all-gather.12.cloned.1.call-done = bf16[512,3072]{1,0:T(8,128)(2,1)} async-done(((bf16[16,3072]{1,0:T(8,128)(2,1)}), bf16[512,3072]{1,0:T(8,128)(2,1)}) %all-gather.12.cloned.1.call-update) | async-done | bytes 3145744 | tf_op jit(solution)/shard_map/all_gather | solution.py:113
  208.1 3.5 fusion.11
  212.5 6.6 all-to-all-start.1
  219.2 18.2 %all-to-all-done.1 = bf16[32,16,288]{2,1,0:T(8,128)(2,1)S(1)} async-done(((bf16[32,16,288]{2,1,0:T(8,128)(2,1)}), bf16[32,16,288]{2,1,0:T(8,128)(2,1)S(1)}, u32[]{:S(2)}, u32[]{:S(2)}) %all-to-all-start.1) | async-done | bytes 294944 | tf_op jit(solution)/shard_map/all_to_all | solution.py:123
  240.8 43.8 %all-gather.10.cloned.1.call-done = bf16[512,6144]{1,0:T(8,128)(2,1)} async-done(((bf16[16,6144]{1,0:T(8,128)(2,1)}), bf16[512,6144]{1,0:T(8,128)(2,1)}) %all-gather.10.cloned.1.call-update) | async-done | bytes 6291472 | tf_op jit(solution)/shard_map/all_gather | solution.py:151
  284.6 5.9 fusion.111
  290.5 4.8 copy.82
  295.3 4.7 copy.81
  300.0 2.6 fusion.115
  302.5 52.9 %all-gather.14.cloned.1.call-done = bf16[512,6144]{1,0:T(8,128)(2,1)} async-done(((bf16[16,6144]{1,0:T(8,128)(2,1)}), bf16[512,6144]{1,0:T(8,128)(2,1)}) %all-gather.14.cloned.1.call-update) | async-done | bytes 6291472 | tf_op jit(solution)/shard_map/all_gather | solution.py:155
  355.5 6.0 fusion.110
  361.4 4.7 copy.68
  366.1 4.7 copy.70
  370.8 2.7 fusion.116
  378.2 34.3 %all-gather.2 = bf16[32,4,3072]{2,1,0:T(4,128)(2,1)S(1)} all-gather(bf16[1,4,3072]{2,1,0:T(4,128)(2,1)S(1)} %slice_bitcast_fusion.2), channel_id=1, replica_groups=mesh['section'=2,'grp'=4,'tok'=32] {'tok'}, dimensions={0}, use_global_device_ids=true | all-gather | bytes 811008 | tf_op jit(solution)/shard_map/all_gather | solution.py:160
  413.6 1.7 convolution_convert_fusion.1
  415.4 12.7 %all_to_all.64 = bf16[32,4,96]{2,1,0:T(4,128)(2,1)S(1)} all-to-all(bf16[32,4,96]{2,1,0:T(4,128)(2,1)S(1)} %bitcast.220), channel_id=1, replica_groups=mesh['section'=2,'grp'=4,'tok'=32] {'tok'}, dimensions={0} | all-to-all | bytes 49152 | tf_op jit(solution)/shard_map/all_to_all | solution.py:170
  428.7 36.0 %all-gather.3 = bf16[32,4,3072]{2,1,0:T(4,128)(2,1)} all-gather(bf16[1,4,3072]{2,1,0:T(4,128)(2,1)S(1)} %fusion.92), channel_id=1, replica_groups=mesh['section'=2,'grp'=4,'tok'=32] {'tok'}, dimensions={0}, use_global_device_ids=true | all-gather | bytes 811008 | tf_op jit(solution)/shard_map/all_gather | solution.py:180
  464.7 1.6 reshape.270
  466.3 4.0 fusion
  473.7 3.0 convolution_convert_fusion
  477.5 3.9 all-to-all-start.3
  481.4 212.0 %all-reduce.3.cloned.1.call-done = f32[128,3072]{1,0:T(8,128)} async-done(((f32[128,3072]{1,0:T(8,128)}), f32[128,3072]{1,0:T(8,128)}) %all-reduce.3.cloned.1.call-update) | async-done | bytes 1572880
  694.7 2.8 collective-permute-start
  697.5 4.7 collective-permute-done
  (137 shorter events, 28.0 us)
Async XLA Ops:
  7.2 459.1 %copy-start = (bf16[1,384,3072]{2,1,0:T(8,128)(2,1)S(1)}, bf16[1,384,3072]{2,1,0:T(8,128)(2,1)}, u32[]{:S(2)}) copy-start(bf16[1,384,3072]{2,1,0:T(8,128)(2,1)} %param.31) | copy-start | bytes 7077892
  60.5 7.1 %copy-start.15 = (f32[1,4,128]{2,1,0:T(4,128)S(1)}, f32[1,4,128]{2,1,0:T(4,128)}, u32[]{:S(2)}) copy-start(f32[1,4,128]{2,1,0:T(4,128)} %param.27) | copy-start | bytes 6148
  60.5 18.7 %copy-start.3 = (bf16[1,1,16,3072]{3,2,1,0:T(8,128)(2,1)S(1)}, bf16[1,1,16,3072]{3,2,1,0:T(8,128)(2,1)}, u32[]{:S(2)}) copy-start(bf16[1,1,16,3072]{3,2,1,0:T(8,128)(2,1)} %param.19) | copy-start | bytes 294916
  60.5 19.1 %copy-start.13 = (bf16[1,4,9216]{2,1,0:T(4,128)(2,1)S(1)}, bf16[1,4,9216]{2,1,0:T(4,128)(2,1)}, u32[]{:S(2)}) copy-start(bf16[1,4,9216]{2,1,0:T(4,128)(2,1)} %param.24) | copy-start | bytes 221188
  63.7 13.6 %all-to-all-start = ((bf16[32,4,288]{2,1,0:T(4,128)(2,1)}), bf16[32,4,288]{2,1,0:T(4,128)(2,1)S(1)}, u32[]{:S(2)}, u32[]{:S(2)}) async-start(bf16[32,4,288]{2,1,0:T(4,128)(2,1)} %all_to_all.48), calls=%async_computation | async-start | bytes 196608 | tf_op jit(solution)/shard_map/all_to_all | solution.py:122
  67.6 72.3 %all-gather.18.cloned.1.call-start = ((), (), s32[]{:S(2)}) async-start(), calls=%async_computation.8 | async-start | bytes 1622016 | tf_op jit(solution)/shard_map/all_gather | solution.py:140
  79.2 128.9 %all-gather.12.cloned.1.call-start = ((), (), s32[]{:S(2)}) async-start(), calls=%async_computation.5 | async-start | bytes 3244032 | tf_op jit(solution)/shard_map/all_gather | solution.py:113
  79.7 63.8 %copy-start.7 = (bf16[1,1,16,6144]{3,2,1,0:T(8,128)(2,1)S(1)}, bf16[1,1,16,6144]{3,2,1,0:T(8,128)(2,1)}, u32[]{:S(2)}) copy-start(bf16[1,1,16,6144]{3,2,1,0:T(8,128)(2,1)} %param.32) | copy-start | bytes 589828
  81.1 203.6 %all-gather.10.cloned.1.call-start = ((), (), s32[]{:S(2)}) async-start(), calls=%async_computation.4 | async-start | bytes 6488064 | tf_op jit(solution)/shard_map/all_gather | solution.py:151
  212.5 24.9 %all-to-all-start.1 = ((bf16[32,16,288]{2,1,0:T(8,128)(2,1)}), bf16[32,16,288]{2,1,0:T(8,128)(2,1)S(1)}, u32[]{:S(2)}, u32[]{:S(2)}) async-start(bf16[32,16,288]{2,1,0:T(8,128)(2,1)} %bitcast.21), calls=%async_computation.1 | async-start | bytes 786432 | tf_op jit(solution)/shard_map/all_to_all | solution.py:123
  219.1 136.3 %all-gather.14.cloned.1.call-start = ((), (), s32[]{:S(2)}) async-start(), calls=%async_computation.6 | async-start | bytes 6488064 | tf_op jit(solution)/shard_map/all_gather | solution.py:155
  239.4 234.3 %all-gather.16.cloned.1.call-start = ((), (), s32[]{:S(2)}) async-start(), calls=%async_computation.7 | async-start | bytes 3244032 | tf_op jit(solution)/shard_map/all_gather | solution.py:161
  370.8 3.5 copy-start.1
  374.3 1.9 copy-start.2
  377.9 315.5 %all-reduce.3.cloned.1.call-start = ((), (), s32[]{:S(2)}) async-start(), calls=%async_computation.9 | async-start | bytes 3145728
  412.5 15.7 %copy-start.6 = (bf16[1,1,4,3072]{3,2,1,0:T(4,128)(2,1)S(1)}, bf16[1,1,4,3072]{3,2,1,0:T(4,128)(2,1)}, u32[]{:S(2)}) copy-start(bf16[1,1,4,3072]{3,2,1,0:T(4,128)(2,1)} %param.18) | copy-start | bytes 73732
  412.5 15.7 %copy-start.12 = (f32[1,1,3072]{2,1,0:T(1,128)S(1)}, f32[1,1,3072]{2,1,0:T(1,128)}, u32[]{:S(2)}) copy-start(f32[1,1,3072]{2,1,0:T(1,128)} %get-tuple-element.27) | copy-start | bytes 36868
  412.5 16.1 %copy-start.10 = (f32[1,1,3072]{2,1,0:T(1,128)S(1)}, f32[1,1,3072]{2,1,0:T(1,128)}, u32[]{:S(2)}) copy-start(f32[1,1,3072]{2,1,0:T(1,128)} %get-tuple-element.23) | copy-start | bytes 36868
  412.5 16.1 %copy-start.11 = (f32[1,1,3072]{2,1,0:T(1,128)S(1)}, f32[1,1,3072]{2,1,0:T(1,128)}, u32[]{:S(2)}) copy-start(f32[1,1,3072]{2,1,0:T(1,128)} %get-tuple-element.24) | copy-start | bytes 36868
  466.3 5.4 copy-start.18
  466.3 7.3 %copy-start.14 = (bf16[4,6144]{1,0:T(4,128)(2,1)S(1)}, bf16[4,6144]{1,0:T(4,128)(2,1)}, u32[]{:S(2)}) copy-start(bf16[4,6144]{1,0:T(4,128)(2,1)} %param.33) | copy-start | bytes 147460
  470.3 3.4 copy-start.5
  473.7 219.7 %copy-start.9 = (f32[1,1,3072]{2,1,0:T(1,128)S(1)}, f32[1,1,3072]{2,1,0:T(1,128)}, u32[]{:S(2)}) copy-start(f32[1,1,3072]{2,1,0:T(1,128)} %get-tuple-element.22) | copy-start | bytes 36868
  476.7 217.9 %copy-start.4 = (bf16[1,1,16,3072]{3,2,1,0:T(8,128)(2,1)S(1)}, bf16[1,1,16,3072]{3,2,1,0:T(8,128)(2,1)}, u32[]{:S(2)}) copy-start(bf16[1,1,16,3072]{3,2,1,0:T(8,128)(2,1)} %param.19) | copy-start | bytes 294916
  476.7 217.9 %copy-start.8 = (f32[1,1,3072]{2,1,0:T(1,128)S(1)}, f32[1,1,3072]{2,1,0:T(1,128)}, u32[]{:S(2)}) copy-start(f32[1,1,3072]{2,1,0:T(1,128)} %get-tuple-element.32) | copy-start | bytes 36868
  476.7 225.8 %copy-start.16 = (bf16[3072,32]{0,1:T(8,128)(2,1)S(1)}, bf16[3072,32]{0,1:T(8,128)(2,1)}, u32[]{:S(2)}) copy-start(bf16[3072,32]{0,1:T(8,128)(2,1)} %param.34) | copy-start | bytes 589828
  476.7 225.8 %copy-start.17 = (f32[1,4,32]{2,1,0:T(4,128)S(1)}, f32[1,4,32]{2,1,0:T(4,128)}, u32[]{:S(2)}) copy-start(f32[1,4,32]{2,1,0:T(4,128)} %param.35) | copy-start | bytes 1540
  477.5 216.8 %all-to-all-start.3 = ((bf16[32,16,96]{2,1,0:T(8,128)(2,1)}), bf16[32,16,96]{2,1,0:T(8,128)(2,1)S(1)}, u32[]{:S(2)}, u32[]{:S(2)}) async-start(bf16[32,16,96]{2,1,0:T(8,128)(2,1)} %bitcast.47), calls=%async_computation.3 | async-start | bytes 262144 | tf_op jit(solution)/shard_map/all_to_all | solution.py:171
  694.7 7.5 %collective-permute-start = (bf16[20,3072]{1,0:T(8,128)(2,1)S(1)}, bf16[20,3072]{1,0:T(8,128)(2,1)S(1)}, u32[]{:S(2)}, u32[]{:S(2)}) collective-permute-start(bf16[20,3072]{1,0:T(8,128)(2,1)S(1)} %pad_maximum_fusion.2), channel_id=1, source_target_pairs={{128,0},{0,128},{129,1},{1,129},{130,2},{2,130},{131,3},{3,131},{1... | collective-permute-start | bytes 368648 | tf_op jit(solution)/shard_map/ppermute | solution.py:17
Sparse Core Ops, SparseCore 0:
  79.3 60.4 all-gather.17
  142.3 65.7 all-gather.11
  210.5 74.0 all-gather.9
  286.4 69.0 all-gather.13
  378.0 66.5 all-gather.15
  470.5 222.8 all-reduce.2
where the time goes:
time: 713 us; the launch traced here: 711 us
  waiting for transfers between devices  462 us (65%)
  blocking collectives  122 us (17%)
  local copies, waits for them, and re-layouts  49.3 us (7%)
  between operations  24.4 us (3%)
  matrix products  22.6 us (3%)
  starting transfers between devices  17.5 us (2%)
  other arithmetic  13 us (2%)
    unnamed x7, waiting for transfers between devices  212 us
    all_gather x1, waiting for transfers between devices, shards(): lax.all_gather(text_normed, 'tok', axis=0, tiled=True)  62.8 us
    all_gather x1, waiting for transfers between devices, shards(): patch_rows = lax.all_gather(fresh_image, 'tok', axis=0, tiled=True)  58.1 us
    all_gather x1, waiting for transfers between devices, shards(): piece = lax.all_gather(fresh_text, 'tok', axis=0, tiled=True)  52.9 us
    all_gather x1, waiting for transfers between devices, shards(): piece = lax.all_gather(current, 'tok', axis=0, tiled=True)  43.8 us
    all_gather x1, blocking collectives, shards(): lax.all_gather(image_normed, 'tok', axis=0, tiled=True)  39.4 us
    all_gather x1, blocking collectives, shards(): lax.all_gather(mlp_normed, 'tok', axis=0, tiled=True)  36 us
    all_gather x1, blocking collectives, shards(): lax.all_gather(attended[:image_rows], 'tok', axis=0, tiled=True)  34.3 us
  transfers between devices with their start and end apart: 10, of which 8 were waited for; matrix products, arithmetic and copies ran while one was open for 6% of the time, Pallas kernels for 0%

commit v1 on v0

--- a/solution.py
+++ b/solution.py
@@ -35,35 +35,32 @@
     return (shaped * lax.rsqrt(power + eps) * gain).reshape(height, width)
 
 
-def attend(carry, queries, piece, valid):
-    highest, total, mixed = carry
+def attend(queries, keys, values, valid):
     height, width = queries.shape
     heads = width // HDIM
-    keys = piece[:, :width].reshape(-1, heads, HDIM)
-    values = piece[:, width:].reshape(-1, heads, HDIM)
     scores = jnp.einsum(
         "qhd,khd->qhk",
         queries.reshape(height, heads, HDIM),
-        keys,
+        keys.reshape(-1, heads, HDIM),
         preferred_element_type=jnp.float32,
     ) * HDIM ** (-0.5)
     scores = jnp.where(valid[None, None, :], scores, masked_score)
-    new_high = jnp.maximum(highest, jnp.max(scores, axis=-1))
-    expo = jnp.where(valid[None, None, :], jnp.exp(scores - new_high[..., None]), 0.0)
-    keep = jnp.exp(highest - new_high)
-    total = total * keep + jnp.sum(expo, axis=-1)
-    mixed = mixed * keep[..., None] + jnp.einsum(
-        "qhk,khd->qhd", expo.astype(jnp.bfloat16), values, preferred_element_type=jnp.float32
-    )
-    return (new_high, total, mixed)
-
-
-def empty_carry(height, heads):
-    return (
-        jnp.full((height, heads), masked_score, jnp.float32),
-        jnp.zeros((height, heads), jnp.float32),
-        jnp.zeros((height, heads, HDIM), jnp.float32),
-    )
+    highest = jnp.max(scores, axis=-1, keepdims=True)
+    expo = jnp.where(valid[None, None, :], jnp.exp(scores - highest), 0.0)
+    total = jnp.sum(expo, axis=-1)
+    mixed = jnp.einsum(
+        "qhk,khd->qhd",
+        expo.astype(jnp.bfloat16),
+        values.reshape(-1, heads, HDIM),
+        preferred_element_type=jnp.float32,
+    )
+    return (mixed / total[..., None]).reshape(height, width).astype(jnp.bfloat16)
+
+
+def cols_to_rows(cols):
+    got = lax.all_to_all(cols, "tok", split_axis=0, concat_axis=0, tiled=True)
+    count, rows, width = got.shape
+    return jnp.transpose(got, (1, 0, 2)).reshape(rows, count * width)
 
 
 def shards(
@@ -89,11 +86,12 @@
     section = lax.axis_index("section")
     last_section = lax.axis_size("section") - 1
     position = lax.axis_index("tok")
+    devices = lax.axis_size("tok")
     image_x = image_in[0, 0].astype(jnp.float32)
     text_x = text_in[0, 0].astype(jnp.float32)
     image_rows = image_x.shape[0]
+    text_rows = text_x.shape[0]
     width = image_x.shape[1]
-    heads = width // HDIM
     patch = lax.dynamic_index_in_dim(entry_order[0], section, 0, False)
     step_now = lax.dynamic_index_in_dim(step_index[0], patch, 0, False)
     modul = (
@@ -108,20 +106,26 @@
     )
     image_normed = modulate(image_x, modul[0], modul[1]).astype(jnp.bfloat16)
     text_normed = modulate(text_x, text_mod[0], text_mod[1]).astype(jnp.bfloat16)
-    every_image, every_text = (
-        lax.all_gather(image_normed, "tok", axis=0, tiled=True),
-        lax.all_gather(text_normed, "tok", axis=0, tiled=True),
-    )
-    image_cols = jnp.dot(every_image, image_to_heads[0], preferred_element_type=jnp.float32).astype(
-        jnp.bfloat16
-    )
-    text_cols = jnp.dot(every_text, text_to_heads[0], preferred_element_type=jnp.float32).astype(
-        jnp.bfloat16
-    )
-    image_proj, text_proj = (
-        lax.all_to_all(image_cols, "tok", split_axis=0, concat_axis=1, tiled=True),
-        lax.all_to_all(text_cols, "tok", split_axis=0, concat_axis=1, tiled=True),
-    )
+    every = lax.all_gather(
+        jnp.concatenate([image_normed, text_normed], axis=0), "tok", axis=0, tiled=False
+    )
+    image_cols = jnp.dot(
+        every[:, :image_rows].reshape(-1, width), image_to_heads[0], preferred_element_type=jnp.float32
+    ).astype(jnp.bfloat16)
+    text_cols = jnp.dot(
+        every[:, image_rows:].reshape(-1, width), text_to_heads[0], preferred_element_type=jnp.float32
+    ).astype(jnp.bfloat16)
+    proj = cols_to_rows(
+        jnp.concatenate(
+            [
+                image_cols.reshape(devices, image_rows, -1),
+                text_cols.reshape(devices, text_rows, -1),
+            ],
+            axis=1,
+        )
+    )
+    image_proj = proj[:image_rows]
+    text_proj = proj[image_rows:]
     gains = head_gain[0]
     image_query = head_norm(image_proj[:, :width].astype(jnp.float32), gains[0]).astype(
         jnp.bfloat16
@@ -136,40 +140,44 @@
     fresh_image = jnp.concatenate([image_key, image_proj[:, 2 * width :]], axis=1)
     fresh_text = jnp.concatenate([text_key, text_proj[:, 2 * width :]], axis=1)
     queries = jnp.concatenate([image_query, text_query], axis=0)
-    query_rows = queries.shape[0]
-    patch_rows = lax.all_gather(fresh_image, "tok", axis=0, tiled=True)
     stale = stale_cache[0, 0]
     cache_rows = stale.shape[0]
-    patch_len = patch_rows.shape[0]
-    first_row = position * cache_rows
-    begin = patch * patch_len
-    offset = jnp.clip(first_row - begin, 0, patch_len - cache_rows)
-    window = lax.dynamic_slice_in_dim(patch_rows, offset, cache_rows, 0)
-    inside = jnp.logical_and(first_row >= begin, first_row < begin + patch_len)
-    current = jnp.where(inside, window, stale)
+    gathered = lax.all_gather(
+        jnp.concatenate([stale, fresh_image, fresh_text], axis=0), "tok", axis=0, tiled=False
+    )
+    stale_all = gathered[:, :cache_rows].reshape(-1, 2 * width)
+    patch_all = gathered[:, cache_rows : cache_rows + image_rows].reshape(-1, 2 * width)
+    text_all = gathered[:, cache_rows + image_rows :].reshape(-1, 2 * width)
+    begin = patch * patch_all.shape[0]
+    cache_all = lax.dynamic_update_slice_in_dim(stale_all, patch_all, begin, 0)
+    current = lax.dynamic_slice_in_dim(cache_all, position * cache_rows, cache_rows, 0)
     text_count = text_length[0]
-    piece = lax.all_gather(current, "tok", axis=0, tiled=True)
-    carry = attend(
-        empty_carry(query_rows, heads), queries, piece, jnp.ones((piece.shape[0],), bool)
-    )
-    piece = lax.all_gather(fresh_text, "tok", axis=0, tiled=True)
-    where_text = jnp.arange(piece.shape[0], dtype=jnp.int32)
-    highest, total, mixed = attend(carry, queries, piece, where_text < text_count)
-    attended = (mixed / total[..., None]).reshape(query_rows, width).astype(jnp.bfloat16)
-    every_image_att, every_text_att = (
-        lax.all_gather(attended[:image_rows], "tok", axis=0, tiled=True),
-        lax.all_gather(attended[image_rows:], "tok", axis=0, tiled=True),
-    )
+    keys_all = jnp.concatenate([cache_all, text_all], axis=0)
+    valid = jnp.concatenate(
+        [
+            jnp.ones((cache_all.shape[0],), bool),
+            jnp.arange(text_all.shape[0], dtype=jnp.int32) < text_count,
+        ]
+    )
+    attended = attend(queries, keys_all[:, :width], keys_all[:, width:], valid)
+    every_att = lax.all_gather(attended, "tok", axis=0, tiled=False)
     image_back_cols = jnp.dot(
-        every_image_att, image_from_heads[0], preferred_element_type=jnp.float32
+        every_att[:, :image_rows].reshape(-1, width), image_from_heads[0], preferred_element_type=jnp.float32
     ).astype(jnp.bfloat16)
     text_back_cols = jnp.dot(
-        every_text_att, text_from_heads[0], preferred_element_type=jnp.float32
-    ).astype(jnp.bfloat16)
-    image_back, text_back = (
-        lax.all_to_all(image_back_cols, "tok", split_axis=0, concat_axis=1, tiled=True),
-        lax.all_to_all(text_back_cols, "tok", split_axis=0, concat_axis=1, tiled=True),
-    )
+        every_att[:, image_rows:].reshape(-1, width), text_from_heads[0], preferred_element_type=jnp.float32
+    ).astype(jnp.bfloat16)
+    back = cols_to_rows(
+        jnp.concatenate(
+            [
+                image_back_cols.reshape(devices, image_rows, -1),
+                text_back_cols.reshape(devices, text_rows, -1),
+            ],
+            axis=1,
+        )
+    )
+    image_back = back[:image_rows]
+    text_back = back[image_rows:]
     image_mid = image_x + modul[2] * image_back.astype(jnp.float32)
     text_out = (text_x + text_mod[2] * text_back.astype(jnp.float32)).astype(jnp.bfloat16)
     mlp_normed = modulate(image_mid, modul[3], modul[4]).astype(jnp.bfloat16)
@@ -183,11 +191,12 @@
         ),
         approximate=True,
     ).astype(jnp.bfloat16)
-    reduced = lax.psum_scatter(
-        jnp.dot(hidden, down_weight, preferred_element_type=jnp.float32),
-        "tok",
-        scatter_dimension=0,
-        tiled=True,
+    partial = jnp.dot(hidden, down_weight, preferred_element_type=jnp.float32)
+    reduced = jnp.sum(
+        lax.all_to_all(
+            partial.reshape(devices, image_rows, width), "tok", split_axis=0, concat_axis=0, tiled=True
+        ),
+        axis=0,
     )
     image_out = (image_mid + modul[5] * reduced).astype(jnp.bfloat16)
     joined = from_behind(jnp.concatenate([image_out, text_out], axis=0), "section", 1)

time: 713 us -> 490 us (0.69)
  waiting for transfers between devices: 462 us -> 286 us
  blocking collectives: 122 us -> 51 us
  other arithmetic: 13 us -> 32.5 us
  local copies, waits for them, and re-layouts: 49.3 us -> 62.9 us
    unnamed x7 -> x3, waiting for transfers between devices: 212 us -> 0.05 us
    all_gather x2 -> x0, blocking collectives: 73.7 us -> none  [the longest x1 39.4 us: shards(): lax.all_gather(image_normed, 'tok', axis=0, tiled=True)]
    all_to_all x3 -> x2, waiting for transfers between devices: 27.9 us -> 55.2 us  [the longest x1 37 us: shards(): lax.all_to_all(partial.reshape(devices, image_rows, width), 'tok', split_...]
    slice x5 -> x14, local copies, waits for them, and re-layouts: 21.9 us -> 41.8 us  [the longest x2 17.3 us: shards(): attended = attend(queries, keys_all[:, :width], keys_all[:, width:], valid)]
    concatenate x1 -> x3, other arithmetic: 0.69 us -> 15.3 us  [the longest x1 14.2 us: shards(): keys_all = jnp.concatenate([cache_all, text_all], axis=0)]
    unnamed x50 -> x35, local copies, waits for them, and re-layouts: 18.7 us -> 4.08 us
    all_gather x5 -> x3, waiting for transfers between devices: 218 us -> 229 us  [the longest x1 89.9 us: shards(): lax.all_gather(jnp.concatenate([stale, fresh_image, fresh_text], axis=0),...]
    dot_general x9 -> x8, matrix products: 21.8 us -> 14.9 us  [the longest x1 3.71 us: attend(): jnp.einsum('qhd,khd->qhk', queries.reshape(height, heads, HDIM), keys.res...]
  transfers between devices with their start and end apart: 10 -> 6, of which waited for: 8 -> 6; matrix products, arithmetic and copies ran while one was open for 6% -> 1% of each run, Pallas kernels for 0% -> 0%
where the time goes in v1:
time: 490 us; the launch traced here: 487 us
  waiting for transfers between devices  286 us (58%)
  local copies, waits for them, and re-layouts  62.9 us (13%)
  blocking collectives  51 us (10%)
  other arithmetic  32.5 us (7%)
  between operations  23.1 us (5%)
  matrix products  16.6 us (3%)
  starting transfers between devices  14.2 us (3%)
    all_gather x1, waiting for transfers between devices, shards(): lax.all_gather(jnp.concatenate([stale, fresh_image, fresh_text], axis=0),...  89.9 us
    all_gather x1, waiting for transfers between devices, shards(): lax.all_gather(jnp.concatenate([image_normed, text_normed], axis=0), 'tok...  70.7 us
    all_gather x1, waiting for transfers between devices, shards(): every_att = lax.all_gather(attended, 'tok', axis=0, tiled=False)  68.2 us
    all_to_all x1, waiting for transfers between devices, shards(): lax.all_to_all(partial.reshape(devices, image_rows, width), 'tok', split_...  37 us
    all_gather x1, blocking collectives, shards(): lax.all_gather(mlp_normed, 'tok', axis=0, tiled=True)  33.2 us
    all_to_all x1, waiting for transfers between devices, cols_to_rows(): got = lax.all_to_all(cols, 'tok', split_axis=0, concat_axis=0, tiled=True)  18.2 us
    all_to_all x1, blocking collectives, cols_to_rows(): got = lax.all_to_all(cols, 'tok', split_axis=0, concat_axis=0, tiled=True)  17.8 us
    slice x2, local copies, waits for them, and re-layouts, shards(): attended = attend(queries, keys_all[:, :width], keys_all[:, width:], valid)  17.3 us
  transfers between devices with their start and end apart: 6, of which 6 were waited for; matrix products, arithmetic and copies ran while one was open for 1% of the time, Pallas kernels for 0%

profile of v1, /device:TPU:2, one launch (start us, length us, event | category | flops | bytes accessed | tf_op | source)
XLA Modules:
  0.0 486.5 jit_solution(12383365515595446310)
XLA Ops:
  24.7 70.7 %all-gather.11.cloned.1.call-done = bf16[32,20,3072]{2,1,0:T(8,128)(2,1)} async-done(((bf16[1,20,3072]{2,1,0:T(8,128)(2,1)}), bf16[32,20,3072]{2,1,0:T(8,128)(2,1)}) %all-gather.11.cloned.1.call-update) | async-done | bytes 3932176 | tf_op jit(solution)/shard_map/all_gather | solution.py:109
  95.4 3.8 slice.211
  100.6 1.6 slice.210
  103.2 2.4 fusion.32
  106.8 6.2 %all-to-all-start = ((bf16[32,20,288]{2,1,0:T(8,128)(2,1)}), bf16[32,20,288]{2,1,0:T(8,128)(2,1)S(1)}, u32[]{:S(2)}, u32[]{:S(2)}) async-start(bf16[32,20,288]{2,1,0:T(8,128)(2,1)} %pad_maximum_fusion.1), calls=%async_computation | async-start | bytes 1179648 | tf_op jit(solution)/shard_map/all_to_all | solution.py:61
  114.3 18.2 %all-to-all-done = bf16[32,20,288]{2,1,0:T(8,128)(2,1)S(1)} async-done(((bf16[32,20,288]{2,1,0:T(8,128)(2,1)}), bf16[32,20,288]{2,1,0:T(8,128)(2,1)S(1)}, u32[]{:S(2)}, u32[]{:S(2)}) %all-to-all-start) | async-done | bytes 368672 | tf_op jit(solution)/shard_map/all_to_all | solution.py:61
  139.4 1.8 maximum_bitcast_fusion
  142.8 89.9 %all-gather.13.cloned.1.call-done = bf16[32,36,6144]{2,1,0:T(8,128)(2,1)} async-done(((bf16[1,36,6144]{2,1,0:T(8,128)(2,1)}), bf16[32,36,6144]{2,1,0:T(8,128)(2,1)}) %all-gather.13.cloned.1.call-update) | async-done | bytes 14155792 | tf_op jit(solution)/shard_map/all_gather | solution.py:145
  232.7 3.8 slice.219
  236.5 3.6 reshape.261
  240.1 7.3 %fusion.104 = (bf16[32,16,6144]{2,1,0:T(8,128)(2,1)S(1)}, bf16[32,16,6144]{2,1,0:T(8,128)(2,1)S(1)}) fusion(bf16[32,36,6144]{2,1,0:T(8,128)(2,1)} %all-gather.13.cloned.1.call-done), kind=kLoop, calls=%fused_computation.162 | loop fusion | bytes 25165824 | tf_op jit(solution)/shard_map/slice | solution.py:150
  247.6 14.2 %pad_maximum_fusion = (bf16[1024,3072]{1,0:T(8,128)(2,1)}, bf16[1024,3072]{1,0:T(8,128)(2,1)}) fusion(bf16[512,6144]{1,0:T(8,128)(2,1)S(1)} %bitcast.198, bf16[512,6144]{1,0:T(8,128)(2,1)S(1)} %constant_dynamic-update-slice_fusion), kind=kLoop, calls=%fused_computation.4 | loop fusion | flops 25165824 | bytes 25165824 | tf_op jit(solution)/shard_map/concatenate | solution.py:155
  261.8 8.6 %copy.90 = bf16[1024,3072]{0,1:T(8,128)(2,1)} copy(bf16[1024,3072]{1,0:T(8,128)(2,1)} %get-tuple-element.11) | data formatting | bytes 12582912 | tf_op jit(solution)/shard_map/slice | solution.py:162
  270.4 8.7 %copy.91 = bf16[1024,3072]{0,1:T(8,128)(2,1)} copy(bf16[1024,3072]{1,0:T(8,128)(2,1)} %get-tuple-element.10) | data formatting | bytes 12582912 | tf_op jit(solution)/shard_map/slice | solution.py:162
  279.1 3.7 fusion.66
  283.8 1.8 copy-done.2
  285.6 1.8 fusion.29
  288.2 68.2 %all-gather.9.cloned.1.call-done = bf16[32,20,3072]{2,1,0:T(8,128)(2,1)} async-done(((bf16[1,20,3072]{2,1,0:T(8,128)(2,1)}), bf16[32,20,3072]{2,1,0:T(8,128)(2,1)}) %all-gather.9.cloned.1.call-update) | async-done | bytes 3932176 | tf_op jit(solution)/shard_map/all_gather | solution.py:163
  356.3 3.7 slice.226
  361.3 1.6 slice.225
  364.0 1.7 convolution_convert_fusion.1
  365.9 17.8 %all_to_all.15 = bf16[32,20,96]{2,1,0:T(8,128)(2,1)S(1)} all-to-all(bf16[32,20,96]{2,1,0:T(8,128)(2,1)S(1)} %pad_maximum_fusion.2), channel_id=1, replica_groups=mesh['section'=2,'grp'=4,'tok'=32] {'tok'}, dimensions={0} | all-to-all | bytes 245760 | tf_op jit(solution)/shard_map/all_to_all | solution.py:61
  384.4 33.2 %all-gather.4 = bf16[32,4,3072]{2,1,0:T(4,128)(2,1)S(1)} all-gather(bf16[1,4,3072]{2,1,0:T(4,128)(2,1)S(1)} %fusion.92), channel_id=1, replica_groups=mesh['section'=2,'grp'=4,'tok'=32] {'tok'}, dimensions={0}, use_global_device_ids=true | all-gather | bytes 811008 | tf_op jit(solution)/shard_map/all_gather | solution.py:188
  418.7 2.5 fusion.63
  421.8 2.2 copy.100
  424.1 4.8 all-to-all-start.2
  431.2 37.0 %all-to-all-done.2 = f32[32,4,3072]{2,1,0:T(4,128)} async-done(((f32[32,4,3072]{2,1,0:T(4,128)}), f32[32,4,3072]{2,1,0:T(4,128)}, u32[]{:S(2)}, u32[]{:S(2)}) %all-to-all-start.2) | async-done | bytes 1572896 | tf_op jit(solution)/shard_map/all_to_all | solution.py:196
  468.1 1.6 reduce_sum.137
  469.9 2.9 collective-permute-start
  472.8 1.6 dynamic-slice_bitcast_fusion
  474.4 2.2 collective-permute-done
  477.0 1.7 fusion.36
  (122 shorter events, 32.5 us)
Async XLA Ops:
  7.2 414.1 %copy-start = (bf16[1,384,3072]{2,1,0:T(8,128)(2,1)S(1)}, bf16[1,384,3072]{2,1,0:T(8,128)(2,1)}, u32[]{:S(2)}) copy-start(bf16[1,384,3072]{2,1,0:T(8,128)(2,1)} %param.31) | copy-start | bytes 7077892
  7.2 88.2 %all-gather.11.cloned.1.call-start = ((), (), s32[]{:S(2)}) async-start(), calls=%async_computation.4 | async-start | bytes 4866048 | tf_op jit(solution)/shard_map/all_gather | solution.py:109
  95.4 3.8 copy-start.13
  103.2 9.8 %copy-start.12 = (f32[1,4,128]{2,1,0:T(4,128)S(1)}, f32[1,4,128]{2,1,0:T(4,128)}, u32[]{:S(2)}) copy-start(f32[1,4,128]{2,1,0:T(4,128)} %param.27) | copy-start | bytes 6148
  106.8 25.7 %all-to-all-start = ((bf16[32,20,288]{2,1,0:T(8,128)(2,1)}), bf16[32,20,288]{2,1,0:T(8,128)(2,1)S(1)}, u32[]{:S(2)}, u32[]{:S(2)}) async-start(bf16[32,20,288]{2,1,0:T(8,128)(2,1)} %pad_maximum_fusion.1), calls=%async_computation | async-start | bytes 1179648 | tf_op jit(solution)/shard_map/all_to_all | solution.py:61
  113.0 119.7 %all-gather.13.cloned.1.call-start = ((), (), s32[]{:S(2)}) async-start(), calls=%async_computation.5 | async-start | bytes 16220160 | tf_op jit(solution)/shard_map/all_gather | solution.py:145
  141.3 215.1 %all-gather.9.cloned.1.call-start = ((), (), s32[]{:S(2)}) async-start(), calls=%async_computation.3 | async-start | bytes 4866048 | tf_op jit(solution)/shard_map/all_gather | solution.py:163
  240.1 7.3 %copy-start.3 = (bf16[128,6144]{1,0:T(8,128)(2,1)S(1)}, bf16[128,6144]{1,0:T(8,128)(2,1)}, u32[]{:S(2)}) copy-start(bf16[128,6144]{1,0:T(8,128)(2,1)} %reshape.261) | copy-start | bytes 4718596
  247.6 14.2 %copy-start.1 = (bf16[512,6144]{1,0:T(8,128)(2,1)}, bf16[512,6144]{1,0:T(8,128)(2,1)S(1)}, u32[]{:S(2)}) copy-start(bf16[512,6144]{1,0:T(8,128)(2,1)S(1)} %constant_dynamic-update-slice_fusion) | copy-start | bytes 18874372
  282.8 2.8 copy-start.2
  288.2 71.9 %copy-start.5 = (bf16[1,3072,96]{1,2,0:T(8,128)(2,1)S(1)}, bf16[1,3072,96]{1,2,0:T(8,128)(2,1)}, u32[]{:S(2)}) copy-start(bf16[1,3072,96]{1,2,0:T(8,128)(2,1)} %param.29) | copy-start | bytes 1769476
  362.9 21.0 %copy-start.6 = (bf16[1,1,4,3072]{3,2,1,0:T(4,128)(2,1)S(1)}, bf16[1,1,4,3072]{3,2,1,0:T(4,128)(2,1)}, u32[]{:S(2)}) copy-start(bf16[1,1,4,3072]{3,2,1,0:T(4,128)(2,1)} %param.18) | copy-start | bytes 73732
  362.9 21.0 %copy-start.10 = (f32[1,1,3072]{2,1,0:T(1,128)S(1)}, f32[1,1,3072]{2,1,0:T(1,128)}, u32[]{:S(2)}) copy-start(f32[1,1,3072]{2,1,0:T(1,128)} %get-tuple-element.21) | copy-start | bytes 36868
  362.9 21.3 %copy-start.8 = (f32[1,1,3072]{2,1,0:T(1,128)S(1)}, f32[1,1,3072]{2,1,0:T(1,128)}, u32[]{:S(2)}) copy-start(f32[1,1,3072]{2,1,0:T(1,128)} %get-tuple-element.17) | copy-start | bytes 36868
  363.0 21.3 %copy-start.9 = (f32[1,1,3072]{2,1,0:T(1,128)S(1)}, f32[1,1,3072]{2,1,0:T(1,128)}, u32[]{:S(2)}) copy-start(f32[1,1,3072]{2,1,0:T(1,128)} %get-tuple-element.18) | copy-start | bytes 36868
  424.1 6.8 %copy-start.11 = (bf16[4,6144]{1,0:T(4,128)(2,1)S(1)}, bf16[4,6144]{1,0:T(4,128)(2,1)}, u32[]{:S(2)}) copy-start(bf16[4,6144]{1,0:T(4,128)(2,1)} %param.33) | copy-start | bytes 147460
  424.1 7.1 %copy-start.4 = (bf16[1,1,16,3072]{3,2,1,0:T(8,128)(2,1)S(1)}, bf16[1,1,16,3072]{3,2,1,0:T(8,128)(2,1)}, u32[]{:S(2)}) copy-start(bf16[1,1,16,3072]{3,2,1,0:T(8,128)(2,1)} %param.19) | copy-start | bytes 294916
  424.1 45.7 %copy-start.7 = (f32[1,1,3072]{2,1,0:T(1,128)S(1)}, f32[1,1,3072]{2,1,0:T(1,128)}, u32[]{:S(2)}) copy-start(f32[1,1,3072]{2,1,0:T(1,128)} %get-tuple-element.16) | copy-start | bytes 36868
  424.1 44.1 %all-to-all-start.2 = ((f32[32,4,3072]{2,1,0:T(4,128)}), f32[32,4,3072]{2,1,0:T(4,128)}, u32[]{:S(2)}, u32[]{:S(2)}) async-start(f32[32,4,3072]{2,1,0:T(4,128)} %copy.100), calls=%async_computation.2 | async-start | bytes 3145728 | tf_op jit(solution)/shard_map/all_to_all | solution.py:196
  428.9 48.1 %copy-start.14 = (f32[1,4,32]{2,1,0:T(4,128)S(1)}, f32[1,4,32]{2,1,0:T(4,128)}, u32[]{:S(2)}) copy-start(f32[1,4,32]{2,1,0:T(4,128)} %param.35) | copy-start | bytes 1540
  469.9 6.7 %collective-permute-start = (bf16[20,3072]{1,0:T(8,128)(2,1)S(1)}, bf16[20,3072]{1,0:T(8,128)(2,1)S(1)}, u32[]{:S(2)}, u32[]{:S(2)}) collective-permute-start(bf16[20,3072]{1,0:T(8,128)(2,1)S(1)} %pad_maximum_fusion.3), channel_id=1, source_target_pairs={{128,0},{0,128},{129,1},{1,129},{130,2},{2,130},{131,3},{3,131},{1... | collective-permute-start | bytes 368648 | tf_op jit(solution)/shard_map/ppermute | solution.py:17
Sparse Core Ops, SparseCore 0:
  24.8 70.5 all-gather.10
  141.4 91.2 all-gather.12
  288.3 68.0 all-gather.8

commit v2 on v1

--- a/solution.py
+++ b/solution.py
@@ -6,6 +6,9 @@
 HDIM = 128
 TSTEPS = 4
 
+
+TOK = ("ta", "tb")
+QUAD = 4
 
 eps = 1e-06
 masked_score = -1e30
@@ -58,7 +61,7 @@
 
 
 def cols_to_rows(cols):
-    got = lax.all_to_all(cols, "tok", split_axis=0, concat_axis=0, tiled=True)
+    got = lax.all_to_all(cols, TOK, split_axis=0, concat_axis=0, tiled=True)
     count, rows, width = got.shape
     return jnp.transpose(got, (1, 0, 2)).reshape(rows, count * width)
 
@@ -85,8 +88,8 @@
 ):
     section = lax.axis_index("section")
     last_section = lax.axis_size("section") - 1
-    position = lax.axis_index("tok")
-    devices = lax.axis_size("tok")
+    position = lax.axis_index("ta") * lax.axis_size("tb") + lax.axis_index("tb")
+    devices = lax.axis_size("ta") * lax.axis_size("tb")
     image_x = image_in[0, 0].astype(jnp.float32)
     text_x = text_in[0, 0].astype(jnp.float32)
     image_rows = image_x.shape[0]
@@ -107,7 +110,7 @@
     image_normed = modulate(image_x, modul[0], modul[1]).astype(jnp.bfloat16)
     text_normed = modulate(text_x, text_mod[0], text_mod[1]).astype(jnp.bfloat16)
     every = lax.all_gather(
-        jnp.concatenate([image_normed, text_normed], axis=0), "tok", axis=0, tiled=False
+        jnp.concatenate([image_normed, text_normed], axis=0), TOK, axis=0, tiled=False
     )
     image_cols = jnp.dot(
         every[:, :image_rows].reshape(-1, width), image_to_heads[0], preferred_element_type=jnp.float32
@@ -137,35 +140,60 @@
     text_key = head_norm(text_proj[:, width : 2 * width].astype(jnp.float32), gains[3]).astype(
         jnp.bfloat16
     )
-    fresh_image = jnp.concatenate([image_key, image_proj[:, 2 * width :]], axis=1)
-    fresh_text = jnp.concatenate([text_key, text_proj[:, 2 * width :]], axis=1)
-    queries = jnp.concatenate([image_query, text_query], axis=0)
+    image_value = image_proj[:, 2 * width :]
+    text_value = text_proj[:, 2 * width :]
     stale = stale_cache[0, 0]
     cache_rows = stale.shape[0]
-    gathered = lax.all_gather(
-        jnp.concatenate([stale, fresh_image, fresh_text], axis=0), "tok", axis=0, tiled=False
-    )
-    stale_all = gathered[:, :cache_rows].reshape(-1, 2 * width)
-    patch_all = gathered[:, cache_rows : cache_rows + image_rows].reshape(-1, 2 * width)
-    text_all = gathered[:, cache_rows + image_rows :].reshape(-1, 2 * width)
-    begin = patch * patch_all.shape[0]
-    cache_all = lax.dynamic_update_slice_in_dim(stale_all, patch_all, begin, 0)
-    current = lax.dynamic_slice_in_dim(cache_all, position * cache_rows, cache_rows, 0)
+    heads = width // HDIM
+    fresh_image = jnp.concatenate([image_key, image_value], axis=1)
+    quad = lax.all_gather(fresh_image, "tb", axis=0, tiled=True)
+    group = lax.axis_size("tb")
+    blocks = devices // group
+    route = [(j * group + b, j + blocks * b) for j in range(blocks) for b in range(group)]
+    moved = lax.ppermute(quad, TOK, route)
+    patch_len = image_rows * devices
+    per_patch = patch_len // cache_rows
+    current = jnp.where(position // per_patch == patch, moved, stale)
+    row_q = jnp.concatenate([image_query, text_query], axis=0)
+    row_k = jnp.concatenate([image_key, text_key], axis=0)
+    row_v = jnp.concatenate([image_value, text_value], axis=0)
+    pieces = [row_q, row_k, row_v, stale[:, :width], stale[:, width:]]
+    pack = jnp.concatenate([piece.reshape(piece.shape[0], heads, HDIM) for piece in pieces], axis=0)
+    pack = jnp.transpose(pack, (1, 0, 2))
+    pack = jnp.pad(pack, ((0, devices - heads), (0, 0), (0, 0)))
+    got = lax.all_to_all(pack, TOK, split_axis=0, concat_axis=0, tiled=True)
+    rows = image_rows + text_rows
+
+    def part(first, count):
+        return got[:, first : first + count].reshape(-1, HDIM)
+
+    queries = jnp.concatenate([part(0, image_rows), part(image_rows, text_rows)], axis=0)
+    fresh_k = part(rows, image_rows)
+    text_k = part(rows + image_rows, text_rows)
+    fresh_v = part(2 * rows, image_rows)
+    text_v = part(2 * rows + image_rows, text_rows)
+    cache_k = part(3 * rows, cache_rows)
+    cache_v = part(3 * rows + cache_rows, cache_rows)
+    begin = patch * patch_len
+    cache_k = lax.dynamic_update_slice_in_dim(cache_k, fresh_k, begin, 0)
+    cache_v = lax.dynamic_update_slice_in_dim(cache_v, fresh_v, begin, 0)
+    keys = jnp.concatenate([cache_k, text_k], axis=0)
+    values = jnp.concatenate([cache_v, text_v], axis=0)
     text_count = text_length[0]
-    keys_all = jnp.concatenate([cache_all, text_all], axis=0)
     valid = jnp.concatenate(
         [
-            jnp.ones((cache_all.shape[0],), bool),
-            jnp.arange(text_all.shape[0], dtype=jnp.int32) < text_count,
+            jnp.ones((cache_k.shape[0],), bool),
+            jnp.arange(text_k.shape[0], dtype=jnp.int32) < text_count,
         ]
     )
-    attended = attend(queries, keys_all[:, :width], keys_all[:, width:], valid)
-    every_att = lax.all_gather(attended, "tok", axis=0, tiled=False)
+    head_out = attend(queries, keys, values, valid)
+    every_head = lax.all_gather(head_out, TOK, axis=0, tiled=False)
+    every_att = jnp.transpose(every_head[:heads], (1, 0, 2)).reshape(-1, width)
     image_back_cols = jnp.dot(
-        every_att[:, :image_rows].reshape(-1, width), image_from_heads[0], preferred_element_type=jnp.float32
+        every_att[:patch_len], image_from_heads[0], preferred_element_type=jnp.float32
     ).astype(jnp.bfloat16)
     text_back_cols = jnp.dot(
-        every_att[:, image_rows:].reshape(-1, width), text_from_heads[0], preferred_element_type=jnp.float32
+        every_att[patch_len:], text_from_heads[0], preferred_element_type=jnp.float32
     ).astype(jnp.bfloat16)
     back = cols_to_rows(
         jnp.concatenate(
@@ -185,7 +213,7 @@
     down_weight = image_down[0]
     hidden = jax.nn.gelu(
         jnp.dot(
-            lax.all_gather(mlp_normed, "tok", axis=0, tiled=True),
+            lax.all_gather(mlp_normed, TOK, axis=0, tiled=True),
             up_weight,
             preferred_element_type=jnp.float32,
         ),
@@ -194,7 +222,7 @@
     partial = jnp.dot(hidden, down_weight, preferred_element_type=jnp.float32)
     reduced = jnp.sum(
         lax.all_to_all(
-            partial.reshape(devices, image_rows, width), "tok", split_axis=0, concat_axis=0, tiled=True
+            partial.reshape(devices, image_rows, width), TOK, split_axis=0, concat_axis=0, tiled=True
         ),
         axis=0,
     )
@@ -219,35 +247,40 @@
 
 
 def solution(mesh):
+    shape = mesh.devices.shape
+    split = jax.sharding.Mesh(
+        mesh.devices.reshape(shape[:2] + (shape[2] // QUAD, QUAD)),
+        ("section", "grp", "ta", "tb"),
+    )
     placed = (
-        P("section", "grp", "tok", None),
-        P("section", "grp", "tok", None),
+        P("section", "grp", TOK, None),
+        P("section", "grp", TOK, None),
         P("grp"),
         P("grp", None),
         P("grp", None),
         P("section", None, None),
         P("section", None, None),
-        P("section", None, "tok"),
-        P("section", None, "tok"),
+        P("section", None, TOK),
+        P("section", None, TOK),
         P("section", None, None),
-        P("section", None, "tok"),
-        P("section", None, "tok"),
-        P("section", None, "tok"),
-        P("section", "tok", None),
-        P("section", "grp", "tok", None),
+        P("section", None, TOK),
+        P("section", None, TOK),
+        P("section", None, TOK),
+        P("section", TOK, None),
+        P("section", "grp", TOK, None),
         P(),
         P(None, "section"),
-        P("grp", "tok", "section"),
+        P("grp", TOK, "section"),
     )
     return jax.shard_map(
         shards,
-        mesh=mesh,
+        mesh=split,
         in_specs=placed,
         out_specs=(
-            P("section", "grp", "tok", None),
-            P("section", "grp", "tok", None),
-            P("section", "grp", "tok", None),
-            P("grp", "tok", "section"),
+            P("section", "grp", TOK, None),
+            P("section", "grp", TOK, None),
+            P("section", "grp", TOK, None),
+            P("grp", TOK, "section"),
         ),
         check_vma=False,
     )

time: 490 us -> 379 us (0.77)
  waiting for transfers between devices: 286 us -> 179 us
  blocking collectives: 51 us -> 86.5 us
  local copies, waits for them, and re-layouts: 62.9 us -> 29 us
  other arithmetic: 32.5 us -> 21.1 us
  starting transfers between devices: 14.2 us -> 19.8 us
    all_gather x3 -> x2, waiting for transfers between devices: 229 us -> 135 us  [the longest x1 69.9 us: shards(): lax.all_gather(jnp.concatenate([image_normed, text_normed], axis=0), TOK,...]
    all_gather x1 -> x2, blocking collectives: 33.2 us -> 68.3 us  [the longest x1 35.1 us: shards(): quad = lax.all_gather(fresh_image, 'tb', axis=0, tiled=True)]
    slice x8 -> x9, local copies, waits for them, and re-layouts: 33.7 us -> 3.48 us  [the longest x3 2.77 us: shards(): every_att = jnp.transpose(every_head[:heads], (1, 0, 2)).reshape(-1, width)]
    all_to_all x2 -> x3, waiting for transfers between devices: 55.2 us -> 39.3 us  [the longest x1 21.7 us: shards(): got = lax.all_to_all(pack, TOK, split_axis=0, concat_axis=0, tiled=True)]
    concatenate x2 -> x1, other arithmetic: 14.9 us -> 0.05 us  [shards(): row_v = jnp.concatenate([image_value, text_value], axis=0)]
    all_to_all x2 -> x3, starting transfers between devices: 11 us -> 15 us  [the longest x1 6.22 us: cols_to_rows(): got = lax.all_to_all(cols, TOK, split_axis=0, concat_axis=0, tiled=True)]
  transfers between devices with their start and end apart: 6 -> 7, of which waited for: 6 -> 5; matrix products, arithmetic and copies ran while one was open for 1% -> 2% of each run, Pallas kernels for 0% -> 0%
where the time goes in v2:
time: 379 us; the launch traced here: 372 us
  waiting for transfers between devices  179 us (47%)
  blocking collectives  86.5 us (23%)
  local copies, waits for them, and re-layouts  29 us (8%)
  between operations  24.4 us (6%)
  other arithmetic  21.1 us (6%)
  starting transfers between devices  19.8 us (5%)
  matrix products  12.2 us (3%)
    all_gather x1, waiting for transfers between devices, shards(): lax.all_gather(jnp.concatenate([image_normed, text_normed], axis=0), TOK,...  69.9 us
    all_gather x1, waiting for transfers between devices, shards(): every_head = lax.all_gather(head_out, TOK, axis=0, tiled=False)  65.1 us
    all_gather x1, blocking collectives, shards(): quad = lax.all_gather(fresh_image, 'tb', axis=0, tiled=True)  35.1 us
    all_gather x1, blocking collectives, shards(): lax.all_gather(mlp_normed, TOK, axis=0, tiled=True)  33.2 us
    all_to_all x1, waiting for transfers between devices, shards(): got = lax.all_to_all(pack, TOK, split_axis=0, concat_axis=0, tiled=True)  21.7 us
    all_to_all x1, blocking collectives, cols_to_rows(): got = lax.all_to_all(cols, TOK, split_axis=0, concat_axis=0, tiled=True)  18.2 us
    all_to_all x1, waiting for transfers between devices, cols_to_rows(): got = lax.all_to_all(cols, TOK, split_axis=0, concat_axis=0, tiled=True)  17.6 us
  transfers between devices with their start and end apart: 7, of which 5 were waited for; matrix products, arithmetic and copies ran while one was open for 2% of the time, Pallas kernels for 0%

profile of v2, /device:TPU:2, one launch (start us, length us, event | category | flops | bytes accessed | tf_op | source)
XLA Modules:
  0.0 372.3 jit_solution(2466409942541169176)
XLA Ops:
  7.2 1.5 fusion.115
  12.8 1.3 constant_dynamic-slice_fusion
  21.0 1.0 convert_reduce_fusion
  22.1 1.1 fusion.48
  26.6 69.9 %all-gather.10.cloned.1.call-done = bf16[32,20,3072]{2,1,0:T(8,128)(2,1)} async-done(((bf16[1,20,3072]{2,1,0:T(8,128)(2,1)}), bf16[32,20,3072]{2,1,0:T(8,128)(2,1)}) %all-gather.10.cloned.1.call-update) | async-done | bytes 3932176 | tf_op jit(solution)/shard_map/all_gather | solution.py:112
  96.4 3.8 %slice.244 = bf16[32,16,3072]{2,1,0:T(8,128)(2,1)S(1)} slice(bf16[32,20,3072]{2,1,0:T(8,128)(2,1)} %all-gather.10.cloned.1.call-done), slice={[0:32], [4:20], [0:3072]} | slice | bytes 6291456 | tf_op jit(solution)/shard_map/slice | solution.py:119
  100.3 1.1 fusion.15
  101.6 1.6 slice.243
  103.2 1.1 reshape.300
  104.3 2.4 fusion.21
  106.8 1.0 pad_maximum_fusion
  107.9 6.2 %all-to-all-start = ((bf16[32,20,288]{2,1,0:T(8,128)(2,1)}), bf16[32,20,288]{2,1,0:T(8,128)(2,1)S(1)}, u32[]{:S(2)}, u32[]{:S(2)}) async-start(bf16[32,20,288]{2,1,0:T(8,128)(2,1)} %pad_maximum_fusion), calls=%async_computation | async-start | bytes 1179648 | tf_op jit(solution)/shard_map/all_to_all | solution.py:64
  116.1 17.6 %all-to-all-done = bf16[32,20,288]{2,1,0:T(8,128)(2,1)S(1)} async-done(((bf16[32,20,288]{2,1,0:T(8,128)(2,1)}), bf16[32,20,288]{2,1,0:T(8,128)(2,1)S(1)}, u32[]{:S(2)}, u32[]{:S(2)}) %all-to-all-start) | async-done | bytes 368672 | tf_op jit(solution)/shard_map/all_to_all | solution.py:64
  138.8 4.1 %concatenate.53 = bf16[92,24,128]{2,0,1:T(8,128)(2,1)S(1)} concatenate(bf16[4,24,128]{2,0,1:T(4,128)(2,1)S(1)} %get-tuple-element.29, bf16[16,24,128]{2,0,1:T(8,128)(2,1)S(1)} %bitcast.274, bf16[4,24,128]{2,0,1:T(4,128)(2,1)S(1)} %bitcast.275, bf16[16,24,128]{2,0,1:T(8,128)(2,1)S(1)} %bitcast.273, bf16[20,24,128]{2,0,1:T(8,128)(2,1)S(1)} %copy.99, ...), dimensions={0} | concatenate | bytes 1130496 | tf_op jit(solution)/shard_map/concatenate | solution.py:161
  143.8 3.9 %all-to-all-start.1 = ((bf16[32,92,128]{2,1,0:T(8,128)(2,1)}), bf16[32,92,128]{2,1,0:T(8,128)(2,1)S(1)}, u32[]{:S(2)}, u32[]{:S(2)}) async-start(bf16[32,92,128]{2,1,0:T(8,128)(2,1)} %pad.5), calls=%async_computation.1 | async-start | bytes 1572864 | tf_op jit(solution)/shard_map/all_to_all | solution.py:164
  149.3 21.7 %all-to-all-done.1 = bf16[32,92,128]{2,1,0:T(8,128)(2,1)S(1)} async-done(((bf16[32,92,128]{2,1,0:T(8,128)(2,1)}), bf16[32,92,128]{2,1,0:T(8,128)(2,1)S(1)}, u32[]{:S(2)}, u32[]{:S(2)}) %all-to-all-start.1) | async-done | bytes 753696 | tf_op jit(solution)/shard_map/all_to_all | solution.py:164
  172.6 1.6 fusion.32
  174.2 65.1 %all-gather.8.cloned.1.call-done = bf16[20480,1,128]{0,2,1:T(8,128)(2,1)} async-done(((bf16[640,1,128]{0,2,1:T(8,128)(2,1)}), bf16[20480,1,128]{0,2,1:T(8,128)(2,1)}) %all-gather.8.cloned.1.call-update) | async-done | bytes 5242896 | tf_op jit(solution)/shard_map/all_gather | solution.py:190
  239.2 2.1 slice-done
  244.6 1.4 convolution_convert_fusion.1
  246.2 18.2 %all_to_all.20 = bf16[32,20,96]{2,1,0:T(8,128)(2,1)S(1)} all-to-all(bf16[32,20,96]{2,1,0:T(8,128)(2,1)S(1)} %pad_maximum_fusion.1), channel_id=1, replica_groups=mesh['section'=2,'grp'=4,'ta'=8,'tb'=4] {'ta','tb'}, dimensions={0} | all-to-all | bytes 245760 | tf_op jit(solution)/shard_map/all_to_all | solution.py:64
  265.8 33.2 %all-gather.3 = bf16[32,4,3072]{2,1,0:T(4,128)(2,1)S(1)} all-gather(bf16[1,4,3072]{2,1,0:T(4,128)(2,1)S(1)} %fusion.97), channel_id=1, replica_groups=mesh['section'=2,'grp'=4,'ta'=8,'tb'=4] {'ta','tb'}, dimensions={0}, use_global_device_ids=true | all-gather | bytes 811008 | tf_op jit(solution)/shard_map/all_gather | solution.py:216
  299.0 1.1 reshape.326
  300.0 2.5 fusion.68
  303.2 2.2 copy.107
  305.4 4.8 %all-to-all-start.3 = ((f32[32,4,3072]{2,1,0:T(4,128)}), f32[32,4,3072]{2,1,0:T(4,128)}, u32[]{:S(2)}, u32[]{:S(2)}) async-start(f32[32,4,3072]{2,1,0:T(4,128)} %copy.107), calls=%async_computation.3 | async-start | bytes 3145728 | tf_op jit(solution)/shard_map/all_to_all | solution.py:224
  313.4 35.1 %all-gather.4 = bf16[4,4,6144]{2,1,0:T(4,128)(2,1)S(1)} all-gather(bf16[1,4,6144]{2,1,0:T(4,128)(2,1)S(1)} %maximum_bitcast_fusion.1), channel_id=1, replica_groups=mesh['section'=2,'grp'=4,'ta'=8,'tb'=4] {'tb'}, dimensions={0}, use_global_device_ids=true | all-gather | bytes 245760 | tf_op jit(solution)/shard_map/all_gather | solution.py:149
  348.5 1.3 collective-permute-start.1
  350.8 1.7 reduce_sum.137
  353.3 3.3 collective-permute-start
  357.3 5.0 %collective-permute-done = bf16[20,3072]{1,0:T(8,128)(2,1)S(1)} collective-permute-done((bf16[20,3072]{1,0:T(8,128)(2,1)S(1)}, bf16[20,3072]{1,0:T(8,128)(2,1)S(1)}, u32[]{:S(2)}, u32[]{:S(2)}) %collective-permute-start) | collective-permute-done | bytes 122912 | tf_op jit(solution)/shard_map/ppermute | solution.py:20
  362.7 1.5 fusion.25
  (128 shorter events, 28.5 us)
Async XLA Ops:
  7.2 295.4 %copy-start = (bf16[1,384,3072]{2,1,0:T(8,128)(2,1)S(1)}, bf16[1,384,3072]{2,1,0:T(8,128)(2,1)}, u32[]{:S(2)}) copy-start(bf16[1,384,3072]{2,1,0:T(8,128)(2,1)} %param.31) | copy-start | bytes 7077892
  7.2 89.2 %all-gather.10.cloned.1.call-start = ((), (), s32[]{:S(2)}) async-start(), calls=%async_computation.5 | async-start | bytes 4866048 | tf_op jit(solution)/shard_map/all_gather | solution.py:112
  96.4 3.8 %copy-start.11 = (bf16[1,3072,288]{1,2,0:T(8,128)(2,1)S(1)}, bf16[1,3072,288]{1,2,0:T(8,128)(2,1)}, u32[]{:S(2)}) copy-start(bf16[1,3072,288]{1,2,0:T(8,128)(2,1)} %param.26) | copy-start | bytes 5308420
  104.3 11.1 %copy-start.2 = (bf16[1,1,16,6144]{3,2,1,0:T(8,128)(2,1)S(1)}, bf16[1,1,16,6144]{3,2,1,0:T(8,128)(2,1)}, u32[]{:S(2)}) copy-start(bf16[1,1,16,6144]{3,2,1,0:T(8,128)(2,1)} %param.32) | copy-start | bytes 589828
  107.9 25.8 %all-to-all-start = ((bf16[32,20,288]{2,1,0:T(8,128)(2,1)}), bf16[32,20,288]{2,1,0:T(8,128)(2,1)S(1)}, u32[]{:S(2)}, u32[]{:S(2)}) async-start(bf16[32,20,288]{2,1,0:T(8,128)(2,1)} %pad_maximum_fusion), calls=%async_computation | async-start | bytes 1179648 | tf_op jit(solution)/shard_map/all_to_all | solution.py:64
  143.8 27.2 %all-to-all-start.1 = ((bf16[32,92,128]{2,1,0:T(8,128)(2,1)}), bf16[32,92,128]{2,1,0:T(8,128)(2,1)S(1)}, u32[]{:S(2)}, u32[]{:S(2)}) async-start(bf16[32,92,128]{2,1,0:T(8,128)(2,1)} %pad.5), calls=%async_computation.1 | async-start | bytes 1572864 | tf_op jit(solution)/shard_map/all_to_all | solution.py:164
  147.7 91.5 %all-gather.8.cloned.1.call-start = ((), (), s32[]{:S(2)}) async-start(), calls=%async_computation.4 | async-start | bytes 5406720 | tf_op jit(solution)/shard_map/all_gather | solution.py:190
  239.2 2.1 slice-start
  242.8 1.1 copy-start.4
  243.8 20.7 %copy-start.5 = (bf16[1,1,4,3072]{3,2,1,0:T(4,128)(2,1)S(1)}, bf16[1,1,4,3072]{3,2,1,0:T(4,128)(2,1)}, u32[]{:S(2)}) copy-start(bf16[1,1,4,3072]{3,2,1,0:T(4,128)(2,1)} %param.18) | copy-start | bytes 73732
  243.8 21.8 %copy-start.6 = (f32[1,1,3072]{2,1,0:T(1,128)S(1)}, f32[1,1,3072]{2,1,0:T(1,128)}, u32[]{:S(2)}) copy-start(f32[1,1,3072]{2,1,0:T(1,128)} %get-tuple-element.23) | copy-start | bytes 36868
  243.8 21.8 %copy-start.7 = (f32[1,1,3072]{2,1,0:T(1,128)S(1)}, f32[1,1,3072]{2,1,0:T(1,128)}, u32[]{:S(2)}) copy-start(f32[1,1,3072]{2,1,0:T(1,128)} %get-tuple-element.24) | copy-start | bytes 36868
  303.2 9.5 %copy-start.8 = (bf16[4,6144]{1,0:T(4,128)(2,1)S(1)}, bf16[4,6144]{1,0:T(4,128)(2,1)}, u32[]{:S(2)}) copy-start(bf16[4,6144]{1,0:T(4,128)(2,1)} %param.33) | copy-start | bytes 147460
  305.4 44.7 %copy-start.1 = (bf16[1,1,16,3072]{3,2,1,0:T(8,128)(2,1)S(1)}, bf16[1,1,16,3072]{3,2,1,0:T(8,128)(2,1)}, u32[]{:S(2)}) copy-start(bf16[1,1,16,3072]{3,2,1,0:T(8,128)(2,1)} %param.19) | copy-start | bytes 294916
  305.4 45.4 %all-to-all-start.3 = ((f32[32,4,3072]{2,1,0:T(4,128)}), f32[32,4,3072]{2,1,0:T(4,128)}, u32[]{:S(2)}, u32[]{:S(2)}) async-start(f32[32,4,3072]{2,1,0:T(4,128)} %copy.107), calls=%async_computation.3 | async-start | bytes 3145728 | tf_op jit(solution)/shard_map/all_to_all | solution.py:224
  310.2 46.4 %copy-start.3 = (bf16[1,1,16,6144]{3,2,1,0:T(8,128)(2,1)S(1)}, bf16[1,1,16,6144]{3,2,1,0:T(8,128)(2,1)}, u32[]{:S(2)}) copy-start(bf16[1,1,16,6144]{3,2,1,0:T(8,128)(2,1)} %param.32) | copy-start | bytes 589828
  348.5 8.1 %collective-permute-start.1 = (bf16[16,6144]{1,0:T(8,128)(2,1)S(1)}, bf16[16,6144]{1,0:T(8,128)(2,1)}, u32[]{:S(2)}, u32[]{:S(2)}) collective-permute-start(bf16[16,6144]{1,0:T(8,128)(2,1)S(1)} %reshape.328), channel_id=1, source_target_pairs={{0,0},{1,8},{2,16},{3,24},{4,1},{5,9},{6,17},{7,25},{8,2},{9,10},{... | collective-permute-start | bytes 589832 | tf_op jit(solution)/shard_map/ppermute | solution.py:153
  349.9 12.8 %copy-start.9 = (f32[1,3072]{1,0:T(1,128)S(1)}, f32[1,3072]{1,0:T(1,128)}, u32[]{:S(2)}) copy-start(f32[1,3072]{1,0:T(1,128)} %get-tuple-element.35) | copy-start | bytes 36868
  349.9 12.8 %copy-start.10 = (f32[1,3072]{1,0:T(1,128)S(1)}, f32[1,3072]{1,0:T(1,128)}, u32[]{:S(2)}) copy-start(f32[1,3072]{1,0:T(1,128)} %get-tuple-element.36) | copy-start | bytes 36868
  350.8 11.9 %copy-start.12 = (bf16[3072,32]{0,1:T(8,128)(2,1)S(1)}, bf16[3072,32]{0,1:T(8,128)(2,1)}, u32[]{:S(2)}) copy-start(bf16[3072,32]{0,1:T(8,128)(2,1)} %param.34) | copy-start | bytes 589828
  353.3 9.0 %collective-permute-start = (bf16[20,3072]{1,0:T(8,128)(2,1)S(1)}, bf16[20,3072]{1,0:T(8,128)(2,1)S(1)}, u32[]{:S(2)}, u32[]{:S(2)}) collective-permute-start(bf16[20,3072]{1,0:T(8,128)(2,1)S(1)} %pad_maximum_fusion.3), channel_id=1, source_target_pairs={{128,0},{0,128},{129,1},{1,129},{130,2},{2,130},{131,3},{3,131},{1... | collective-permute-start | bytes 368648 | tf_op jit(solution)/shard_map/ppermute | solution.py:20
Sparse Core Ops, SparseCore 0:
  25.9 70.5 all-gather.9
  174.3 64.9 all-gather.7

commit v3 on v2

--- a/solution.py
+++ b/solution.py
@@ -146,9 +146,16 @@
     cache_rows = stale.shape[0]
     heads = width // HDIM
     fresh_image = jnp.concatenate([image_key, image_value], axis=1)
-    quad = lax.all_gather(fresh_image, "tb", axis=0, tiled=True)
     group = lax.axis_size("tb")
     blocks = devices // group
+    mine = lax.axis_index("tb")
+    quad = [fresh_image]
+    for shift in range(1, group):
+        turn = [(j * group + b, j * group + (b + shift) % group) for j in range(blocks) for b in range(group)]
+        quad.append(lax.ppermute(fresh_image, TOK, turn))
+    quad = jnp.stack(quad)
+    order = (mine - jnp.arange(group)) % group
+    quad = jnp.zeros_like(quad).at[order].set(quad).reshape(-1, fresh_image.shape[1])
     route = [(j * group + b, j + blocks * b) for j in range(blocks) for b in range(group)]
     moved = lax.ppermute(quad, TOK, route)
     patch_len = image_rows * devices
@@ -187,25 +194,20 @@
         ]
     )
     head_out = attend(queries, keys, values, valid)
-    every_head = lax.all_gather(head_out, TOK, axis=0, tiled=False)
-    every_att = jnp.transpose(every_head[:heads], (1, 0, 2)).reshape(-1, width)
-    image_back_cols = jnp.dot(
-        every_att[:patch_len], image_from_heads[0], preferred_element_type=jnp.float32
-    ).astype(jnp.bfloat16)
-    text_back_cols = jnp.dot(
-        every_att[patch_len:], text_from_heads[0], preferred_element_type=jnp.float32
-    ).astype(jnp.bfloat16)
-    back = cols_to_rows(
-        jnp.concatenate(
-            [
-                image_back_cols.reshape(devices, image_rows, -1),
-                text_back_cols.reshape(devices, text_rows, -1),
-            ],
-            axis=1,
-        )
-    )
-    image_back = back[:image_rows]
-    text_back = back[image_rows:]
+    image_heads = lax.all_gather(head_out[:patch_len], TOK, axis=0, tiled=False)
+    text_heads = lax.all_gather(head_out[patch_len:], TOK, axis=0, tiled=False)
+    image_att = jnp.transpose(image_heads[:heads], (1, 0, 2)).reshape(-1, width)
+    text_att = jnp.transpose(text_heads[:heads], (1, 0, 2)).reshape(-1, width)
+    image_back = cols_to_rows(
+        jnp.dot(image_att, image_from_heads[0], preferred_element_type=jnp.float32)
+        .astype(jnp.bfloat16)
+        .reshape(devices, image_rows, -1)
+    )
+    text_back = cols_to_rows(
+        jnp.dot(text_att, text_from_heads[0], preferred_element_type=jnp.float32)
+        .astype(jnp.bfloat16)
+        .reshape(devices, text_rows, -1)
+    )
     image_mid = image_x + modul[2] * image_back.astype(jnp.float32)
     text_out = (text_x + text_mod[2] * text_back.astype(jnp.float32)).astype(jnp.bfloat16)
     mlp_normed = modulate(image_mid, modul[3], modul[4]).astype(jnp.bfloat16)
@@ -227,9 +229,8 @@
         axis=0,
     )
     image_out = (image_mid + modul[5] * reduced).astype(jnp.bfloat16)
-    joined = from_behind(jnp.concatenate([image_out, text_out], axis=0), "section", 1)
-    image_next = joined[:image_rows]
-    text_next = joined[image_rows:]
+    text_next = from_behind(text_out, "section", 1)
+    image_next = from_behind(image_out, "section", 1)
     final_source = jnp.where(section == last_section, image_out, image_next)
     patch_last = entry_order[0, last_section]
     step_last = lax.dynamic_index_in_dim(step_index[0], patch_last, 0, False)

time: 379 us -> 392 us (1.034); the launches traced: 372 us -> 390 us
  blocking collectives: 86.5 us -> 33.6 us
  waiting for transfers between devices: 179 us -> 224 us
  starting transfers between devices: 19.8 us -> 45 us
  local copies, waits for them, and re-layouts: 29 us -> 35.4 us
    ppermute x0 -> x3, waiting for transfers between devices: none -> 35.4 us  [shards(): quad.append(lax.ppermute(fresh_image, TOK, turn))]
    all_gather x1 -> x0, blocking collectives: 35.1 us -> none  [shards(): quad = lax.all_gather(fresh_image, 'tb', axis=0, tiled=True)]
    all_to_all x1 -> x3, starting transfers between devices: 6.22 us -> 25.5 us  [cols_to_rows(): got = lax.all_to_all(cols, TOK, split_axis=0, concat_axis=0, tiled=True)]
    all_to_all x1 -> x0, blocking collectives: 18.2 us -> none  [cols_to_rows(): got = lax.all_to_all(cols, TOK, split_axis=0, concat_axis=0, tiled=True)]
    all_to_all x1 -> x3, waiting for transfers between devices: 17.6 us -> 34.5 us  [cols_to_rows(): got = lax.all_to_all(cols, TOK, split_axis=0, concat_axis=0, tiled=True)]
    all_gather x1 -> x2, waiting for transfers between devices: 65.1 us -> 59.8 us  [the longest x1 59.8 us: shards(): image_heads = lax.all_gather(head_out[:patch_len], TOK, axis=0, tiled=False)]
  transfers between devices with their start and end apart: 7 -> 14, of which waited for: 5 -> 10; matrix products, arithmetic and copies ran while one was open for 2% -> 4% of each run, Pallas kernels for 0% -> 0%
where the time goes in v3:
time: 392 us; the launch traced here: 390 us
  waiting for transfers between devices  224 us (57%)
  starting transfers between devices  45 us (11%)
  local copies, waits for them, and re-layouts  35.4 us (9%)
  blocking collectives  33.6 us (9%)
  between operations  24 us (6%)
  other arithmetic  17.8 us (5%)
  matrix products  9.77 us (2%)
    all_gather x1, waiting for transfers between devices, shards(): lax.all_gather(jnp.concatenate([image_normed, text_normed], axis=0), TOK,...  69.3 us
    all_gather x1, waiting for transfers between devices, shards(): image_heads = lax.all_gather(head_out[:patch_len], TOK, axis=0, tiled=False)  59.8 us
    ppermute x3, waiting for transfers between devices, shards(): quad.append(lax.ppermute(fresh_image, TOK, turn))  35.4 us
    all_to_all x3, waiting for transfers between devices, cols_to_rows(): got = lax.all_to_all(cols, TOK, split_axis=0, concat_axis=0, tiled=True)  34.5 us
    all_gather x1, blocking collectives, shards(): lax.all_gather(mlp_normed, TOK, axis=0, tiled=True)  33.6 us
    all_to_all x3, starting transfers between devices, cols_to_rows(): got = lax.all_to_all(cols, TOK, split_axis=0, concat_axis=0, tiled=True)  25.5 us
    all_to_all x1, waiting for transfers between devices, shards(): got = lax.all_to_all(pack, TOK, split_axis=0, concat_axis=0, tiled=True)  22 us
  transfers between devices with their start and end apart: 14, of which 10 were waited for; matrix products, arithmetic and copies ran while one was open for 4% of the time, Pallas kernels for 0%

profile of v3, /device:TPU:2, one launch (start us, length us, event | category | flops | bytes accessed | tf_op | source)
XLA Modules:
  0.0 389.9 jit_solution(9079756252863896417)
XLA Ops:
  7.2 1.4 fusion.118
  12.4 1.3 constant_dynamic-slice_fusion
  24.9 1.4 slice_bitcast_fusion.3
  26.3 69.3 %all-gather.13.cloned.1.call-done = bf16[32,20,3072]{2,1,0:T(8,128)(2,1)} async-done(((bf16[1,20,3072]{2,1,0:T(8,128)(2,1)}), bf16[32,20,3072]{2,1,0:T(8,128)(2,1)}) %all-gather.13.cloned.1.call-update) | async-done | bytes 3932176 | tf_op jit(solution)/shard_map/all_gather | solution.py:112
  95.5 3.8 slice.225
  100.7 1.6 slice.224
  103.4 2.4 fusion.21
  107.0 6.2 %all-to-all-start = ((bf16[32,20,288]{2,1,0:T(8,128)(2,1)}), bf16[32,20,288]{2,1,0:T(8,128)(2,1)S(1)}, u32[]{:S(2)}, u32[]{:S(2)}) async-start(bf16[32,20,288]{2,1,0:T(8,128)(2,1)} %pad_maximum_fusion), calls=%async_computation | async-start | bytes 1179648 | tf_op jit(solution)/shard_map/all_to_all | solution.py:64
  113.2 1.3 broadcast_bitcast_fusion.2
  114.5 1.3 broadcast_bitcast_fusion.4
  116.5 16.2 %all-to-all-done = bf16[32,20,288]{2,1,0:T(8,128)(2,1)S(1)} async-done(((bf16[32,20,288]{2,1,0:T(8,128)(2,1)}), bf16[32,20,288]{2,1,0:T(8,128)(2,1)S(1)}, u32[]{:S(2)}, u32[]{:S(2)}) %all-to-all-start) | async-done | bytes 368672 | tf_op jit(solution)/shard_map/all_to_all | solution.py:64
  137.9 4.1 %concatenate.47 = bf16[92,24,128]{2,0,1:T(8,128)(2,1)S(1)} concatenate(bf16[4,24,128]{2,0,1:T(4,128)(2,1)S(1)} %get-tuple-element.29, bf16[16,24,128]{2,0,1:T(8,128)(2,1)S(1)} %bitcast.281, bf16[4,24,128]{2,0,1:T(4,128)(2,1)S(1)} %bitcast.282, bf16[16,24,128]{2,0,1:T(8,128)(2,1)S(1)} %bitcast.280, bf16[20,24,128]{2,0,1:T(8,128)(2,1)S(1)} %copy.65, ...), dimensions={0} | concatenate | bytes 1130496 | tf_op jit(solution)/shard_map/concatenate | solution.py:168
  143.0 3.9 %all-to-all-start.1 = ((bf16[32,92,128]{2,1,0:T(8,128)(2,1)}), bf16[32,92,128]{2,1,0:T(8,128)(2,1)S(1)}, u32[]{:S(2)}, u32[]{:S(2)}) async-start(bf16[32,92,128]{2,1,0:T(8,128)(2,1)} %pad.5), calls=%async_computation.1 | async-start | bytes 1572864 | tf_op jit(solution)/shard_map/all_to_all | solution.py:171
  148.2 22.0 %all-to-all-done.1 = bf16[32,92,128]{2,1,0:T(8,128)(2,1)S(1)} async-done(((bf16[32,92,128]{2,1,0:T(8,128)(2,1)}), bf16[32,92,128]{2,1,0:T(8,128)(2,1)S(1)}, u32[]{:S(2)}, u32[]{:S(2)}) %all-to-all-start.1) | async-done | bytes 753696 | tf_op jit(solution)/shard_map/all_to_all | solution.py:171
  173.3 59.8 %all-gather.9.cloned.1.call-done = bf16[4096,1,128]{0,2,1:T(8,128)(2,1)} async-done(((bf16[128,1,128]{0,2,1:T(8,128)(2,1)}), bf16[4096,1,128]{0,2,1:T(8,128)(2,1)}) %all-gather.9.cloned.1.call-update) | async-done | bytes 1048592 | tf_op jit(solution)/shard_map/all_gather | solution.py:197
  235.6 4.9 %all-to-all-start.2 = ((bf16[32,4,96]{2,1,0:T(4,128)(2,1)}), bf16[32,4,96]{2,1,0:T(4,128)(2,1)S(1)}, u32[]{:S(2)}, u32[]{:S(2)}) async-start(bf16[32,4,96]{2,1,0:T(4,128)(2,1)} %bitcast.44), calls=%async_computation.2 | async-start | bytes 65536 | tf_op jit(solution)/shard_map/all_to_all | solution.py:64
  241.3 7.9 %all-to-all-done.2 = bf16[32,4,96]{2,1,0:T(4,128)(2,1)S(1)} async-done(((bf16[32,4,96]{2,1,0:T(4,128)(2,1)}), bf16[32,4,96]{2,1,0:T(4,128)(2,1)S(1)}, u32[]{:S(2)}, u32[]{:S(2)}) %all-to-all-start.2) | async-done | bytes 24608 | tf_op jit(solution)/shard_map/all_to_all | solution.py:64
  249.8 33.6 %all-gather.4 = bf16[32,4,3072]{2,1,0:T(4,128)(2,1)S(1)} all-gather(bf16[1,4,3072]{2,1,0:T(4,128)(2,1)S(1)} %fusion.97), channel_id=1, replica_groups=mesh['section'=2,'grp'=4,'ta'=8,'tb'=4] {'ta','tb'}, dimensions={0}, use_global_device_ids=true | all-gather | bytes 811008 | tf_op jit(solution)/shard_map/all_gather | solution.py:218
  284.5 2.5 fusion.68
  287.7 2.2 copy.72
  289.9 4.8 %all-to-all-start.3 = ((f32[32,4,3072]{2,1,0:T(4,128)}), f32[32,4,3072]{2,1,0:T(4,128)}, u32[]{:S(2)}, u32[]{:S(2)}) async-start(f32[32,4,3072]{2,1,0:T(4,128)} %copy.72), calls=%async_computation.3 | async-start | bytes 3145728 | tf_op jit(solution)/shard_map/all_to_all | solution.py:226
  296.9 1.6 collective-permute-start.3
  298.6 1.3 collective-permute-start.4
  300.5 35.2 %collective-permute-done.2 = bf16[4,6144]{1,0:T(4,128)(2,1)S(1)} collective-permute-done((bf16[4,6144]{1,0:T(4,128)(2,1)S(1)}, bf16[4,6144]{1,0:T(4,128)(2,1)S(1)}, u32[]{:S(2)}, u32[]{:S(2)}) %collective-permute-start.2) | collective-permute-done | bytes 49184 | tf_op jit(solution)/shard_map/ppermute | solution.py:155
  337.6 1.6 reduce_sum.137
  339.3 3.5 collective-permute-start
  345.1 1.9 slice-done
  346.9 1.3 copy.90
  350.7 14.4 %all-to-all-start.4 = ((bf16[32,16,96]{2,1,0:T(8,128)(2,1)}), bf16[32,16,96]{2,1,0:T(8,128)(2,1)S(1)}, u32[]{:S(2)}, u32[]{:S(2)}) async-start(bf16[32,16,96]{2,1,0:T(8,128)(2,1)} %bitcast.58), calls=%async_computation.4 | async-start | bytes 262144 | tf_op jit(solution)/shard_map/all_to_all | solution.py:64
  365.1 10.4 %all-to-all-done.4 = bf16[32,16,96]{2,1,0:T(8,128)(2,1)S(1)} async-done(((bf16[32,16,96]{2,1,0:T(8,128)(2,1)}), bf16[32,16,96]{2,1,0:T(8,128)(2,1)S(1)}, u32[]{:S(2)}, u32[]{:S(2)}) %all-to-all-start.4) | async-done | bytes 98336 | tf_op jit(solution)/shard_map/all_to_all | solution.py:64
  375.9 3.3 collective-permute-start.1
  380.0 2.1 collective-permute-done.1
  (151 shorter events, 37.3 us)
Async XLA Ops:
  7.2 279.9 %copy-start = (bf16[1,384,3072]{2,1,0:T(8,128)(2,1)S(1)}, bf16[1,384,3072]{2,1,0:T(8,128)(2,1)}, u32[]{:S(2)}) copy-start(bf16[1,384,3072]{2,1,0:T(8,128)(2,1)} %param.31) | copy-start | bytes 7077892
  7.2 88.4 %all-gather.13.cloned.1.call-start = ((), (), s32[]{:S(2)}) async-start(), calls=%async_computation.7 | async-start | bytes 4866048 | tf_op jit(solution)/shard_map/all_gather | solution.py:112
  95.5 3.8 copy-start.12
  103.4 12.4 %copy-start.2 = (bf16[1,1,16,6144]{3,2,1,0:T(8,128)(2,1)S(1)}, bf16[1,1,16,6144]{3,2,1,0:T(8,128)(2,1)}, u32[]{:S(2)}) copy-start(bf16[1,1,16,6144]{3,2,1,0:T(8,128)(2,1)} %param.32) | copy-start | bytes 589828
  107.0 25.8 %all-to-all-start = ((bf16[32,20,288]{2,1,0:T(8,128)(2,1)}), bf16[32,20,288]{2,1,0:T(8,128)(2,1)S(1)}, u32[]{:S(2)}, u32[]{:S(2)}) async-start(bf16[32,20,288]{2,1,0:T(8,128)(2,1)} %pad_maximum_fusion), calls=%async_computation | async-start | bytes 1179648 | tf_op jit(solution)/shard_map/all_to_all | solution.py:64
  143.0 27.2 %all-to-all-start.1 = ((bf16[32,92,128]{2,1,0:T(8,128)(2,1)}), bf16[32,92,128]{2,1,0:T(8,128)(2,1)S(1)}, u32[]{:S(2)}, u32[]{:S(2)}) async-start(bf16[32,92,128]{2,1,0:T(8,128)(2,1)} %pad.5), calls=%async_computation.1 | async-start | bytes 1572864 | tf_op jit(solution)/shard_map/all_to_all | solution.py:171
  146.9 86.2 %all-gather.9.cloned.1.call-start = ((), (), s32[]{:S(2)}) async-start(), calls=%async_computation.5 | async-start | bytes 1081344 | tf_op jit(solution)/shard_map/all_gather | solution.py:197
  172.6 62.0 %copy-start.4 = (bf16[1,3072,96]{1,2,0:T(8,128)(2,1)S(1)}, bf16[1,3072,96]{1,2,0:T(8,128)(2,1)}, u32[]{:S(2)}) copy-start(bf16[1,3072,96]{1,2,0:T(8,128)(2,1)} %param.28) | copy-start | bytes 1769476
  234.2 15.1 %copy-start.6 = (bf16[1,1,4,3072]{3,2,1,0:T(4,128)(2,1)S(1)}, bf16[1,1,4,3072]{3,2,1,0:T(4,128)(2,1)}, u32[]{:S(2)}) copy-start(bf16[1,1,4,3072]{3,2,1,0:T(4,128)(2,1)} %param.18) | copy-start | bytes 73732
  234.2 15.1 %copy-start.10 = (f32[1,1,3072]{2,1,0:T(1,128)S(1)}, f32[1,1,3072]{2,1,0:T(1,128)}, u32[]{:S(2)}) copy-start(f32[1,1,3072]{2,1,0:T(1,128)} %get-tuple-element.27) | copy-start | bytes 36868
  234.2 15.5 %copy-start.8 = (f32[1,1,3072]{2,1,0:T(1,128)S(1)}, f32[1,1,3072]{2,1,0:T(1,128)}, u32[]{:S(2)}) copy-start(f32[1,1,3072]{2,1,0:T(1,128)} %get-tuple-element.23) | copy-start | bytes 36868
  234.2 15.5 %copy-start.9 = (f32[1,1,3072]{2,1,0:T(1,128)S(1)}, f32[1,1,3072]{2,1,0:T(1,128)}, u32[]{:S(2)}) copy-start(f32[1,1,3072]{2,1,0:T(1,128)} %get-tuple-element.24) | copy-start | bytes 36868
  235.6 13.5 %all-to-all-start.2 = ((bf16[32,4,96]{2,1,0:T(4,128)(2,1)}), bf16[32,4,96]{2,1,0:T(4,128)(2,1)S(1)}, u32[]{:S(2)}, u32[]{:S(2)}) async-start(bf16[32,4,96]{2,1,0:T(4,128)(2,1)} %bitcast.44), calls=%async_computation.2 | async-start | bytes 65536 | tf_op jit(solution)/shard_map/all_to_all | solution.py:64
  240.6 104.5 %all-gather.11.cloned.1.call-start = ((), (), s32[]{:S(2)}) async-start(), calls=%async_computation.6 | async-start | bytes 4325376 | tf_op jit(solution)/shard_map/all_gather | solution.py:198
  287.7 8.9 %copy-start.11 = (bf16[4,6144]{1,0:T(4,128)(2,1)S(1)}, bf16[4,6144]{1,0:T(4,128)(2,1)}, u32[]{:S(2)}) copy-start(bf16[4,6144]{1,0:T(4,128)(2,1)} %param.33) | copy-start | bytes 147460
  289.9 49.4 %copy-start.7 = (f32[1,1,3072]{2,1,0:T(1,128)S(1)}, f32[1,1,3072]{2,1,0:T(1,128)}, u32[]{:S(2)}) copy-start(f32[1,1,3072]{2,1,0:T(1,128)} %get-tuple-element.22) | copy-start | bytes 36868
  289.9 52.9 %copy-start.3 = (bf16[1,1,16,6144]{3,2,1,0:T(8,128)(2,1)S(1)}, bf16[1,1,16,6144]{3,2,1,0:T(8,128)(2,1)}, u32[]{:S(2)}) copy-start(bf16[1,1,16,6144]{3,2,1,0:T(8,128)(2,1)} %param.32) | copy-start | bytes 589828
  289.9 47.7 %all-to-all-start.3 = ((f32[32,4,3072]{2,1,0:T(4,128)}), f32[32,4,3072]{2,1,0:T(4,128)}, u32[]{:S(2)}, u32[]{:S(2)}) async-start(f32[32,4,3072]{2,1,0:T(4,128)} %copy.72), calls=%async_computation.3 | async-start | bytes 3145728 | tf_op jit(solution)/shard_map/all_to_all | solution.py:226
  296.7 39.0 %collective-permute-start.2 = (bf16[4,6144]{1,0:T(4,128)(2,1)S(1)}, bf16[4,6144]{1,0:T(4,128)(2,1)S(1)}, u32[]{:S(2)}, u32[]{:S(2)}) collective-permute-start(bf16[4,6144]{1,0:T(4,128)(2,1)S(1)} %get-tuple-element.33), channel_id=1, source_target_pairs={{0,1},{1,2},{2,3},{3,0},{4,5},{5,6},{6,7},{7,4},{8,9},{9,10},{10,1... | collective-permute-start | bytes 147464 | tf_op jit(solution)/shard_map/ppermute | solution.py:155
  296.9 38.9 %collective-permute-start.3 = (bf16[4,6144]{1,0:T(4,128)(2,1)S(1)}, bf16[4,6144]{1,0:T(4,128)(2,1)S(1)}, u32[]{:S(2)}, u32[]{:S(2)}) collective-permute-start(bf16[4,6144]{1,0:T(4,128)(2,1)S(1)} %get-tuple-element.33), channel_id=1, source_target_pairs={{0,2},{1,3},{2,0},{3,1},{4,6},{5,7},{6,4},{7,5},{8,10},{9,11},{10,... | collective-permute-start | bytes 147464 | tf_op jit(solution)/shard_map/ppermute | solution.py:155
  298.6 37.3 %collective-permute-start.4 = (bf16[4,6144]{1,0:T(4,128)(2,1)S(1)}, bf16[4,6144]{1,0:T(4,128)(2,1)S(1)}, u32[]{:S(2)}, u32[]{:S(2)}) collective-permute-start(bf16[4,6144]{1,0:T(4,128)(2,1)S(1)} %get-tuple-element.33), channel_id=1, source_target_pairs={{0,3},{1,0},{2,1},{3,2},{4,7},{5,4},{6,5},{7,6},{8,11},{9,8},{10,9... | collective-permute-start | bytes 147464 | tf_op jit(solution)/shard_map/ppermute | solution.py:155
  336.9 5.9 %collective-permute-start.5 = (bf16[16,6144]{1,0:T(8,128)(2,1)S(1)}, bf16[16,6144]{1,0:T(8,128)(2,1)S(1)}, u32[]{:S(2)}, u32[]{:S(2)}) collective-permute-start(bf16[16,6144]{1,0:T(8,128)(2,1)S(1)} %reshape.368), channel_id=1, source_target_pairs={{0,0},{1,8},{2,16},{3,24},{4,1},{5,9},{6,17},{7,25},{8,2},{9,10},{... | collective-permute-start | bytes 589832 | tf_op jit(solution)/shard_map/ppermute | solution.py:160
  339.3 5.4 %collective-permute-start = (bf16[4,3072]{1,0:T(4,128)(2,1)S(1)}, bf16[4,3072]{1,0:T(4,128)(2,1)S(1)}, u32[]{:S(2)}, u32[]{:S(2)}) collective-permute-start(bf16[4,3072]{1,0:T(4,128)(2,1)S(1)} %add_convert_fusion), channel_id=1, source_target_pairs={{128,0},{0,128},{129,1},{1,129},{130,2},{2,130},{131,3},{3,131},{1... | collective-permute-start | bytes 73736 | tf_op jit(solution)/shard_map/ppermute | solution.py:20
  345.1 1.9 slice-start
  348.2 1.1 copy-start.5
  349.3 26.5 %copy-start.1 = (bf16[1,1,16,3072]{3,2,1,0:T(8,128)(2,1)S(1)}, bf16[1,1,16,3072]{3,2,1,0:T(8,128)(2,1)}, u32[]{:S(2)}) copy-start(bf16[1,1,16,3072]{3,2,1,0:T(8,128)(2,1)} %param.19) | copy-start | bytes 294916
  349.3 29.9 %copy-start.13 = (bf16[3072,32]{0,1:T(8,128)(2,1)S(1)}, bf16[3072,32]{0,1:T(8,128)(2,1)}, u32[]{:S(2)}) copy-start(bf16[3072,32]{0,1:T(8,128)(2,1)} %param.34) | copy-start | bytes 589828
  349.3 29.8 %copy-start.14 = (f32[1,4,32]{2,1,0:T(4,128)S(1)}, f32[1,4,32]{2,1,0:T(4,128)}, u32[]{:S(2)}) copy-start(f32[1,4,32]{2,1,0:T(4,128)} %param.35) | copy-start | bytes 1540
  350.7 24.8 %all-to-all-start.4 = ((bf16[32,16,96]{2,1,0:T(8,128)(2,1)}), bf16[32,16,96]{2,1,0:T(8,128)(2,1)S(1)}, u32[]{:S(2)}, u32[]{:S(2)}) async-start(bf16[32,16,96]{2,1,0:T(8,128)(2,1)} %bitcast.58), calls=%async_computation.4 | async-start | bytes 262144 | tf_op jit(solution)/shard_map/all_to_all | solution.py:64
  375.9 6.2 %collective-permute-start.1 = (bf16[16,3072]{1,0:T(8,128)(2,1)S(1)}, bf16[16,3072]{1,0:T(8,128)(2,1)S(1)}, u32[]{:S(2)}, u32[]{:S(2)}) collective-permute-start(bf16[16,3072]{1,0:T(8,128)(2,1)S(1)} %fusion.52), channel_id=1, source_target_pairs={{128,0},{0,128},{129,1},{1,129},{130,2},{2,130},{131,3},{3,131},{1... | collective-permute-start | bytes 294920 | tf_op jit(solution)/shard_map/ppermute | solution.py:20
Sparse Core Ops, SparseCore 0:
  25.0 70.5 all-gather.12
  173.4 59.5 all-gather.8
  243.3 75.5 all-gather.10

commit v4 on v3

--- a/solution.py
+++ b/solution.py
@@ -164,23 +164,28 @@
     row_q = jnp.concatenate([image_query, text_query], axis=0)
     row_k = jnp.concatenate([image_key, text_key], axis=0)
     row_v = jnp.concatenate([image_value, text_value], axis=0)
-    pieces = [row_q, row_k, row_v, stale[:, :width], stale[:, width:]]
-    pack = jnp.concatenate([piece.reshape(piece.shape[0], heads, HDIM) for piece in pieces], axis=0)
-    pack = jnp.transpose(pack, (1, 0, 2))
-    pack = jnp.pad(pack, ((0, devices - heads), (0, 0), (0, 0)))
-    got = lax.all_to_all(pack, TOK, split_axis=0, concat_axis=0, tiled=True)
+    def by_head(pieces):
+        pack = jnp.concatenate(
+            [piece.reshape(piece.shape[0], heads, HDIM) for piece in pieces], axis=0
+        )
+        pack = jnp.transpose(pack, (1, 0, 2))
+        pack = jnp.pad(pack, ((0, devices - heads), (0, 0), (0, 0)))
+        return lax.all_to_all(pack, TOK, split_axis=0, concat_axis=0, tiled=True)
+
+    got_cache = by_head([stale[:, :width], stale[:, width:]])
+    got = by_head([row_q, row_k, row_v])
     rows = image_rows + text_rows
 
-    def part(first, count):
-        return got[:, first : first + count].reshape(-1, HDIM)
+    def part(first, count, source=got):
+        return source[:, first : first + count].reshape(-1, HDIM)
 
     queries = jnp.concatenate([part(0, image_rows), part(image_rows, text_rows)], axis=0)
     fresh_k = part(rows, image_rows)
     text_k = part(rows + image_rows, text_rows)
     fresh_v = part(2 * rows, image_rows)
     text_v = part(2 * rows + image_rows, text_rows)
-    cache_k = part(3 * rows, cache_rows)
-    cache_v = part(3 * rows + cache_rows, cache_rows)
+    cache_k = part(0, cache_rows, got_cache)
+    cache_v = part(cache_rows, cache_rows, got_cache)
     begin = patch * patch_len
     cache_k = lax.dynamic_update_slice_in_dim(cache_k, fresh_k, begin, 0)
     cache_v = lax.dynamic_update_slice_in_dim(cache_v, fresh_v, begin, 0)
@@ -194,7 +199,14 @@
         ]
     )
     head_out = attend(queries, keys, values, valid)
-    image_heads = lax.all_gather(head_out[:patch_len], TOK, axis=0, tiled=False)
+    image_block = head_out[:patch_len]
+    image_heads = lax.all_to_all(
+        jnp.broadcast_to(image_block[None], (devices,) + image_block.shape),
+        TOK,
+        split_axis=0,
+        concat_axis=0,
+        tiled=True,
+    )
     text_heads = lax.all_gather(head_out[patch_len:], TOK, axis=0, tiled=False)
     image_att = jnp.transpose(image_heads[:heads], (1, 0, 2)).reshape(-1, width)
     text_att = jnp.transpose(text_heads[:heads], (1, 0, 2)).reshape(-1, width)

time: 392 us -> 366 us (0.934)
  waiting for transfers between devices: 224 us -> 163 us
  blocking collectives: 33.6 us -> 65.1 us
  starting transfers between devices: 45 us -> 49 us
    all_gather x1 -> x0, waiting for transfers between devices: 59.8 us -> none  [shards(): image_heads = lax.all_gather(head_out[:patch_len], TOK, axis=0, tiled=False)]
    all_to_all x0 -> x1, blocking collectives: none -> 31.5 us  [shards(): lax.all_to_all(jnp.broadcast_to(image_block[None], (devices,) + image_blo...]
    all_to_all x1 -> x2, starting transfers between devices: 3.91 us -> 9.58 us  [by_head(): return lax.all_to_all(pack, TOK, split_axis=0, concat_axis=0, tiled=True)]
    concatenate x3 -> x1, local copies, waits for them, and re-layouts: 4.12 us -> 0.02 us  [by_head(): jnp.concatenate([piece.reshape(piece.shape[0], heads, HDIM) for piece in...]
    all_to_all x1 -> x2, waiting for transfers between devices: 22 us -> 19 us  [by_head(): return lax.all_to_all(pack, TOK, split_axis=0, concat_axis=0, tiled=True)]
  transfers between devices with their start and end apart: 14 -> 14, of which waited for: 10 -> 10; matrix products, arithmetic and copies ran while one was open for 4% -> 7% of each run, Pallas kernels for 0% -> 0%
where the time goes in v4:
time: 366 us; the launch traced here: 365 us
  waiting for transfers between devices  163 us (45%)
  blocking collectives  65.1 us (18%)
  starting transfers between devices  49 us (13%)
  local copies, waits for them, and re-layouts  33.7 us (9%)
  between operations  24.5 us (7%)
  other arithmetic  18.8 us (5%)
  matrix products  10.7 us (3%)
    all_gather x1, waiting for transfers between devices, shards(): lax.all_gather(jnp.concatenate([image_normed, text_normed], axis=0), TOK,...  68.4 us
    ppermute x3, waiting for transfers between devices, shards(): quad.append(lax.ppermute(fresh_image, TOK, turn))  35.9 us
    all_to_all x3, waiting for transfers between devices, cols_to_rows(): got = lax.all_to_all(cols, TOK, split_axis=0, concat_axis=0, tiled=True)  35.6 us
    all_gather x1, blocking collectives, shards(): lax.all_gather(mlp_normed, TOK, axis=0, tiled=True)  33.6 us
    all_to_all x1, blocking collectives, shards(): lax.all_to_all(jnp.broadcast_to(image_block[None], (devices,) + image_blo...  31.5 us
    all_to_all x3, starting transfers between devices, cols_to_rows(): got = lax.all_to_all(cols, TOK, split_axis=0, concat_axis=0, tiled=True)  24.5 us
    all_to_all x2, waiting for transfers between devices, by_head(): return lax.all_to_all(pack, TOK, split_axis=0, concat_axis=0, tiled=True)  19 us
    all_to_all x2, starting transfers between devices, by_head(): return lax.all_to_all(pack, TOK, split_axis=0, concat_axis=0, tiled=True)  9.58 us
  transfers between devices with their start and end apart: 14, of which 10 were waited for; matrix products, arithmetic and copies ran while one was open for 7% of the time, Pallas kernels for 0%

profile of v4, /device:TPU:2, one launch (start us, length us, event | category | flops | bytes accessed | tf_op | source)
XLA Modules:
  0.0 364.9 jit_solution(10899027873529506643)
XLA Ops:
  7.2 1.5 fusion.119
  12.7 1.3 constant_dynamic-slice_fusion
  27.3 68.4 %all-gather.9.cloned.1.call-done = bf16[32,20,3072]{2,1,0:T(8,128)(2,1)} async-done(((bf16[1,20,3072]{2,1,0:T(8,128)(2,1)}), bf16[32,20,3072]{2,1,0:T(8,128)(2,1)}) %all-gather.9.cloned.1.call-update) | async-done | bytes 3932176 | tf_op jit(solution)/shard_map/all_gather | solution.py:112
  95.8 3.8 %slice.230 = bf16[32,16,3072]{2,1,0:T(8,128)(2,1)S(1)} slice(bf16[32,20,3072]{2,1,0:T(8,128)(2,1)} %all-gather.9.cloned.1.call-done), slice={[0:32], [4:20], [0:3072]} | slice | bytes 6291456 | tf_op jit(solution)/shard_map/slice | solution.py:119
  100.9 1.6 slice.229
  103.6 2.4 fusion.21
  107.2 6.2 %all-to-all-start.1 = ((bf16[32,20,288]{2,1,0:T(8,128)(2,1)}), bf16[32,20,288]{2,1,0:T(8,128)(2,1)S(1)}, u32[]{:S(2)}, u32[]{:S(2)}) async-start(bf16[32,20,288]{2,1,0:T(8,128)(2,1)} %pad_maximum_fusion), calls=%async_computation.1 | async-start | bytes 1179648 | tf_op jit(solution)/shard_map/all_to_all | solution.py:64
  115.5 17.5 %all-to-all-done.1 = bf16[32,20,288]{2,1,0:T(8,128)(2,1)S(1)} async-done(((bf16[32,20,288]{2,1,0:T(8,128)(2,1)}), bf16[32,20,288]{2,1,0:T(8,128)(2,1)S(1)}, u32[]{:S(2)}, u32[]{:S(2)}) %all-to-all-start.1) | async-done | bytes 368672 | tf_op jit(solution)/shard_map/all_to_all | solution.py:64
  133.0 3.9 %all-to-all-start = ((bf16[32,32,128]{2,1,0:T(8,128)(2,1)}), bf16[32,32,128]{2,1,0:T(8,128)(2,1)S(1)}, u32[]{:S(2)}, u32[]{:S(2)}) async-start(bf16[32,32,128]{2,1,0:T(8,128)(2,1)} %pad.9.clone), calls=%async_computation | async-start | bytes 524288 | tf_op jit(solution)/shard_map/all_to_all | solution.py:173
  147.4 2.6 all-to-all-done
  150.0 5.7 %all-to-all-start.2 = ((bf16[32,60,128]{2,1,0:T(8,128)(2,1)}), bf16[32,60,128]{2,1,0:T(8,128)(2,1)S(1)}, u32[]{:S(2)}, u32[]{:S(2)}) async-start(bf16[32,60,128]{2,1,0:T(8,128)(2,1)} %pad.10.clone), calls=%async_computation.2 | async-start | bytes 1048576 | tf_op jit(solution)/shard_map/all_to_all | solution.py:173
  157.8 16.4 %all-to-all-done.2 = bf16[32,60,128]{2,1,0:T(8,128)(2,1)S(1)} async-done(((bf16[32,60,128]{2,1,0:T(8,128)(2,1)}), bf16[32,60,128]{2,1,0:T(8,128)(2,1)S(1)}, u32[]{:S(2)}, u32[]{:S(2)}) %all-to-all-start.2) | async-done | bytes 491552 | tf_op jit(solution)/shard_map/all_to_all | solution.py:173
  175.0 1.5 fusion.4
  178.3 31.5 %all_to_all.35 = bf16[32,128,128]{1,2,0:T(8,128)(2,1)S(1)} all-to-all(bf16[32,128,128]{1,2,0:T(8,128)(2,1)S(1)} %broadcast_in_dim.36), channel_id=1, replica_groups=mesh['section'=2,'grp'=4,'ta'=8,'tb'=4] {'ta','tb'}, dimensions={0} | all-to-all | bytes 2097152 | tf_op jit(solution)/shard_map/all_to_all | solution.py:203
  211.0 4.1 %all-to-all-start.4 = ((bf16[32,4,96]{2,1,0:T(4,128)(2,1)}), bf16[32,4,96]{2,1,0:T(4,128)(2,1)S(1)}, u32[]{:S(2)}, u32[]{:S(2)}) async-start(bf16[32,4,96]{2,1,0:T(4,128)(2,1)} %bitcast.44), calls=%async_computation.4 | async-start | bytes 65536 | tf_op jit(solution)/shard_map/all_to_all | solution.py:64
  216.0 7.7 %all-to-all-done.4 = bf16[32,4,96]{2,1,0:T(4,128)(2,1)S(1)} async-done(((bf16[32,4,96]{2,1,0:T(4,128)(2,1)}), bf16[32,4,96]{2,1,0:T(4,128)(2,1)S(1)}, u32[]{:S(2)}, u32[]{:S(2)}) %all-to-all-start.4) | async-done | bytes 24608 | tf_op jit(solution)/shard_map/all_to_all | solution.py:64
  224.3 33.6 %all-gather.3 = bf16[32,4,3072]{2,1,0:T(4,128)(2,1)S(1)} all-gather(bf16[1,4,3072]{2,1,0:T(4,128)(2,1)S(1)} %fusion.97), channel_id=1, replica_groups=mesh['section'=2,'grp'=4,'ta'=8,'tb'=4] {'ta','tb'}, dimensions={0}, use_global_device_ids=true | all-gather | bytes 811008 | tf_op jit(solution)/shard_map/all_gather | solution.py:230
  259.0 2.5 fusion.68
  262.1 2.2 copy.65
  264.3 4.8 %all-to-all-start.5 = ((f32[32,4,3072]{2,1,0:T(4,128)}), f32[32,4,3072]{2,1,0:T(4,128)}, u32[]{:S(2)}, u32[]{:S(2)}) async-start(f32[32,4,3072]{2,1,0:T(4,128)} %copy.65), calls=%async_computation.5 | async-start | bytes 3145728 | tf_op jit(solution)/shard_map/all_to_all | solution.py:238
  271.2 1.6 collective-permute-start.3
  272.9 1.3 collective-permute-start.4
  274.9 35.3 %collective-permute-done.2 = bf16[4,6144]{1,0:T(4,128)(2,1)S(1)} collective-permute-done((bf16[4,6144]{1,0:T(4,128)(2,1)S(1)}, bf16[4,6144]{1,0:T(4,128)(2,1)S(1)}, u32[]{:S(2)}, u32[]{:S(2)}) %collective-permute-start.2) | collective-permute-done | bytes 49184 | tf_op jit(solution)/shard_map/ppermute | solution.py:155
  312.5 1.6 reduce_sum.137
  314.1 2.9 collective-permute-start
  317.8 1.8 collective-permute-done
  319.9 1.9 slice-done
  321.8 1.3 copy.86
  325.6 14.2 %all-to-all-start.6 = ((bf16[32,16,96]{2,1,0:T(8,128)(2,1)}), bf16[32,16,96]{2,1,0:T(8,128)(2,1)S(1)}, u32[]{:S(2)}, u32[]{:S(2)}) async-start(bf16[32,16,96]{2,1,0:T(8,128)(2,1)} %bitcast.58), calls=%async_computation.6 | async-start | bytes 262144 | tf_op jit(solution)/shard_map/all_to_all | solution.py:64
  339.8 10.4 %all-to-all-done.6 = bf16[32,16,96]{2,1,0:T(8,128)(2,1)S(1)} async-done(((bf16[32,16,96]{2,1,0:T(8,128)(2,1)}), bf16[32,16,96]{2,1,0:T(8,128)(2,1)S(1)}, u32[]{:S(2)}, u32[]{:S(2)}) %all-to-all-start.6) | async-done | bytes 98336 | tf_op jit(solution)/shard_map/all_to_all | solution.py:64
  350.6 3.1 collective-permute-start.1
  354.5 2.3 collective-permute-done.1
  (166 shorter events, 43.4 us)
Async XLA Ops:
  7.2 254.4 %copy-start = (bf16[1,384,3072]{2,1,0:T(8,128)(2,1)S(1)}, bf16[1,384,3072]{2,1,0:T(8,128)(2,1)}, u32[]{:S(2)}) copy-start(bf16[1,384,3072]{2,1,0:T(8,128)(2,1)} %param.31) | copy-start | bytes 7077892
  7.2 88.6 %all-gather.9.cloned.1.call-start = ((), (), s32[]{:S(2)}) async-start(), calls=%async_computation.8 | async-start | bytes 4866048 | tf_op jit(solution)/shard_map/all_gather | solution.py:112
  95.8 3.8 %copy-start.16 = (bf16[1,3072,288]{1,2,0:T(8,128)(2,1)S(1)}, bf16[1,3072,288]{1,2,0:T(8,128)(2,1)}, u32[]{:S(2)}) copy-start(bf16[1,3072,288]{1,2,0:T(8,128)(2,1)} %param.26) | copy-start | bytes 5308420
  103.6 9.8 %copy-start.7 = (bf16[2,8,24,128]{3,2,1,0:T(8,128)(2,1)S(1)}, bf16[2,8,24,128]{3,2,1,0:T(8,128)(2,1)}, u32[]{:S(2)}) copy-start(bf16[2,8,24,128]{3,2,1,0:T(8,128)(2,1)} %copy.71) | copy-start | bytes 294916
  103.6 9.8 %copy-start.8 = (bf16[2,8,24,128]{3,2,1,0:T(8,128)(2,1)S(1)}, bf16[2,8,24,128]{3,2,1,0:T(8,128)(2,1)}, u32[]{:S(2)}) copy-start(bf16[2,8,24,128]{3,2,1,0:T(8,128)(2,1)} %copy.72) | copy-start | bytes 294916
  103.6 10.6 %copy-start.15 = (f32[1,4,128]{2,1,0:T(4,128)S(1)}, f32[1,4,128]{2,1,0:T(4,128)}, u32[]{:S(2)}) copy-start(f32[1,4,128]{2,1,0:T(4,128)} %param.27) | copy-start | bytes 6148
  107.2 25.7 %all-to-all-start.1 = ((bf16[32,20,288]{2,1,0:T(8,128)(2,1)}), bf16[32,20,288]{2,1,0:T(8,128)(2,1)S(1)}, u32[]{:S(2)}, u32[]{:S(2)}) async-start(bf16[32,20,288]{2,1,0:T(8,128)(2,1)} %pad_maximum_fusion), calls=%async_computation.1 | async-start | bytes 1179648 | tf_op jit(solution)/shard_map/all_to_all | solution.py:64
  133.0 17.1 %all-to-all-start = ((bf16[32,32,128]{2,1,0:T(8,128)(2,1)}), bf16[32,32,128]{2,1,0:T(8,128)(2,1)S(1)}, u32[]{:S(2)}, u32[]{:S(2)}) async-start(bf16[32,32,128]{2,1,0:T(8,128)(2,1)} %pad.9.clone), calls=%async_computation | async-start | bytes 524288 | tf_op jit(solution)/shard_map/all_to_all | solution.py:173
  143.0 3.5 copy-start.6
  150.0 24.2 %all-to-all-start.2 = ((bf16[32,60,128]{2,1,0:T(8,128)(2,1)}), bf16[32,60,128]{2,1,0:T(8,128)(2,1)S(1)}, u32[]{:S(2)}, u32[]{:S(2)}) async-start(bf16[32,60,128]{2,1,0:T(8,128)(2,1)} %pad.10.clone), calls=%async_computation.2 | async-start | bytes 1048576 | tf_op jit(solution)/shard_map/all_to_all | solution.py:173
  178.0 31.9 %copy-start.3 = (bf16[1,3072,96]{1,2,0:T(8,128)(2,1)S(1)}, bf16[1,3072,96]{1,2,0:T(8,128)(2,1)}, u32[]{:S(2)}) copy-start(bf16[1,3072,96]{1,2,0:T(8,128)(2,1)} %param.28) | copy-start | bytes 1769476
  178.3 45.5 %copy-start.9 = (bf16[1,1,4,3072]{3,2,1,0:T(4,128)(2,1)S(1)}, bf16[1,1,4,3072]{3,2,1,0:T(4,128)(2,1)}, u32[]{:S(2)}) copy-start(bf16[1,1,4,3072]{3,2,1,0:T(4,128)(2,1)} %param.18) | copy-start | bytes 73732
  178.3 45.5 %copy-start.13 = (f32[1,1,3072]{2,1,0:T(1,128)S(1)}, f32[1,1,3072]{2,1,0:T(1,128)}, u32[]{:S(2)}) copy-start(f32[1,1,3072]{2,1,0:T(1,128)} %get-tuple-element.27) | copy-start | bytes 36868
  178.3 45.9 %copy-start.11 = (f32[1,1,3072]{2,1,0:T(1,128)S(1)}, f32[1,1,3072]{2,1,0:T(1,128)}, u32[]{:S(2)}) copy-start(f32[1,1,3072]{2,1,0:T(1,128)} %get-tuple-element.23) | copy-start | bytes 36868
  178.3 45.9 %copy-start.12 = (f32[1,1,3072]{2,1,0:T(1,128)S(1)}, f32[1,1,3072]{2,1,0:T(1,128)}, u32[]{:S(2)}) copy-start(f32[1,1,3072]{2,1,0:T(1,128)} %get-tuple-element.24) | copy-start | bytes 36868
  211.0 12.7 %all-to-all-start.4 = ((bf16[32,4,96]{2,1,0:T(4,128)(2,1)}), bf16[32,4,96]{2,1,0:T(4,128)(2,1)S(1)}, u32[]{:S(2)}, u32[]{:S(2)}) async-start(bf16[32,4,96]{2,1,0:T(4,128)(2,1)} %bitcast.44), calls=%async_computation.4 | async-start | bytes 65536 | tf_op jit(solution)/shard_map/all_to_all | solution.py:64
  215.1 104.9 %all-gather.7.cloned.1.call-start = ((), (), s32[]{:S(2)}) async-start(), calls=%async_computation.7 | async-start | bytes 4325376 | tf_op jit(solution)/shard_map/all_gather | solution.py:210
  262.1 8.8 %copy-start.14 = (bf16[4,6144]{1,0:T(4,128)(2,1)S(1)}, bf16[4,6144]{1,0:T(4,128)(2,1)}, u32[]{:S(2)}) copy-start(bf16[4,6144]{1,0:T(4,128)(2,1)} %param.33) | copy-start | bytes 147460
  264.3 49.8 %copy-start.10 = (f32[1,1,3072]{2,1,0:T(1,128)S(1)}, f32[1,1,3072]{2,1,0:T(1,128)}, u32[]{:S(2)}) copy-start(f32[1,1,3072]{2,1,0:T(1,128)} %get-tuple-element.22) | copy-start | bytes 36868
  264.3 52.7 %copy-start.2 = (bf16[1,1,16,6144]{3,2,1,0:T(8,128)(2,1)S(1)}, bf16[1,1,16,6144]{3,2,1,0:T(8,128)(2,1)}, u32[]{:S(2)}) copy-start(bf16[1,1,16,6144]{3,2,1,0:T(8,128)(2,1)} %param.32) | copy-start | bytes 589828
  264.3 48.1 %all-to-all-start.5 = ((f32[32,4,3072]{2,1,0:T(4,128)}), f32[32,4,3072]{2,1,0:T(4,128)}, u32[]{:S(2)}, u32[]{:S(2)}) async-start(f32[32,4,3072]{2,1,0:T(4,128)} %copy.65), calls=%async_computation.5 | async-start | bytes 3145728 | tf_op jit(solution)/shard_map/all_to_all | solution.py:238
  271.0 39.2 %collective-permute-start.2 = (bf16[4,6144]{1,0:T(4,128)(2,1)S(1)}, bf16[4,6144]{1,0:T(4,128)(2,1)S(1)}, u32[]{:S(2)}, u32[]{:S(2)}) collective-permute-start(bf16[4,6144]{1,0:T(4,128)(2,1)S(1)} %get-tuple-element.33), channel_id=1, source_target_pairs={{0,1},{1,2},{2,3},{3,0},{4,5},{5,6},{6,7},{7,4},{8,9},{9,10},{10,1... | collective-permute-start | bytes 147464 | tf_op jit(solution)/shard_map/ppermute | solution.py:155
  271.2 39.5 %collective-permute-start.3 = (bf16[4,6144]{1,0:T(4,128)(2,1)S(1)}, bf16[4,6144]{1,0:T(4,128)(2,1)S(1)}, u32[]{:S(2)}, u32[]{:S(2)}) collective-permute-start(bf16[4,6144]{1,0:T(4,128)(2,1)S(1)} %get-tuple-element.33), channel_id=1, source_target_pairs={{0,2},{1,3},{2,0},{3,1},{4,6},{5,7},{6,4},{7,5},{8,10},{9,11},{10,... | collective-permute-start | bytes 147464 | tf_op jit(solution)/shard_map/ppermute | solution.py:155
  272.9 37.9 %collective-permute-start.4 = (bf16[4,6144]{1,0:T(4,128)(2,1)S(1)}, bf16[4,6144]{1,0:T(4,128)(2,1)S(1)}, u32[]{:S(2)}, u32[]{:S(2)}) collective-permute-start(bf16[4,6144]{1,0:T(4,128)(2,1)S(1)} %get-tuple-element.33), channel_id=1, source_target_pairs={{0,3},{1,0},{2,1},{3,2},{4,7},{5,4},{6,5},{7,6},{8,11},{9,8},{10,9... | collective-permute-start | bytes 147464 | tf_op jit(solution)/shard_map/ppermute | solution.py:155
  311.8 5.3 %collective-permute-start.5 = (bf16[16,6144]{1,0:T(8,128)(2,1)S(1)}, bf16[16,6144]{1,0:T(8,128)(2,1)S(1)}, u32[]{:S(2)}, u32[]{:S(2)}) collective-permute-start(bf16[16,6144]{1,0:T(8,128)(2,1)S(1)} %reshape.368), channel_id=1, source_target_pairs={{0,0},{1,8},{2,16},{3,24},{4,1},{5,9},{6,17},{7,25},{8,2},{9,10},{... | collective-permute-start | bytes 589832 | tf_op jit(solution)/shard_map/ppermute | solution.py:160
  314.1 5.4 %collective-permute-start = (bf16[4,3072]{1,0:T(4,128)(2,1)S(1)}, bf16[4,3072]{1,0:T(4,128)(2,1)S(1)}, u32[]{:S(2)}, u32[]{:S(2)}) collective-permute-start(bf16[4,3072]{1,0:T(4,128)(2,1)S(1)} %add_convert_fusion), channel_id=1, source_target_pairs={{128,0},{0,128},{129,1},{1,129},{130,2},{2,130},{131,3},{3,131},{1... | collective-permute-start | bytes 73736 | tf_op jit(solution)/shard_map/ppermute | solution.py:20
  319.9 1.9 slice-start
  324.2 26.3 %copy-start.1 = (bf16[1,1,16,3072]{3,2,1,0:T(8,128)(2,1)S(1)}, bf16[1,1,16,3072]{3,2,1,0:T(8,128)(2,1)}, u32[]{:S(2)}) copy-start(bf16[1,1,16,3072]{3,2,1,0:T(8,128)(2,1)} %param.19) | copy-start | bytes 294916
  324.2 29.5 %copy-start.17 = (bf16[3072,32]{0,1:T(8,128)(2,1)S(1)}, bf16[3072,32]{0,1:T(8,128)(2,1)}, u32[]{:S(2)}) copy-start(bf16[3072,32]{0,1:T(8,128)(2,1)} %param.34) | copy-start | bytes 589828
  324.2 29.5 %copy-start.18 = (f32[1,4,32]{2,1,0:T(4,128)S(1)}, f32[1,4,32]{2,1,0:T(4,128)}, u32[]{:S(2)}) copy-start(f32[1,4,32]{2,1,0:T(4,128)} %param.35) | copy-start | bytes 1540
  325.6 24.6 %all-to-all-start.6 = ((bf16[32,16,96]{2,1,0:T(8,128)(2,1)}), bf16[32,16,96]{2,1,0:T(8,128)(2,1)S(1)}, u32[]{:S(2)}, u32[]{:S(2)}) async-start(bf16[32,16,96]{2,1,0:T(8,128)(2,1)} %bitcast.58), calls=%async_computation.6 | async-start | bytes 262144 | tf_op jit(solution)/shard_map/all_to_all | solution.py:64
  350.6 6.2 %collective-permute-start.1 = (bf16[16,3072]{1,0:T(8,128)(2,1)S(1)}, bf16[16,3072]{1,0:T(8,128)(2,1)S(1)}, u32[]{:S(2)}, u32[]{:S(2)}) collective-permute-start(bf16[16,3072]{1,0:T(8,128)(2,1)S(1)} %fusion.52), channel_id=1, source_target_pairs={{128,0},{0,128},{129,1},{1,129},{130,2},{2,130},{131,3},{3,131},{1... | collective-permute-start | bytes 294920 | tf_op jit(solution)/shard_map/ppermute | solution.py:20
  (2 other events, 1.7 us)
Sparse Core Ops, SparseCore 0:
  25.2 70.5 all-gather.8
  217.8 75.8 all-gather.6

commit v5 on v3

--- a/solution.py
+++ b/solution.py
@@ -64,6 +64,12 @@
     got = lax.all_to_all(cols, TOK, split_axis=0, concat_axis=0, tiled=True)
     count, rows, width = got.shape
     return jnp.transpose(got, (1, 0, 2)).reshape(rows, count * width)
+
+
+def broadcast_rows(block, devices):
+    copies = jnp.broadcast_to(block[None], (devices,) + block.shape)
+    got = lax.all_to_all(copies, TOK, split_axis=0, concat_axis=0, tiled=True)
+    return got.reshape(-1, block.shape[-1])
 
 
 def shards(
@@ -109,6 +115,22 @@
     )
     image_normed = modulate(image_x, modul[0], modul[1]).astype(jnp.bfloat16)
     text_normed = modulate(text_x, text_mod[0], text_mod[1]).astype(jnp.bfloat16)
+    stale = stale_cache[0, 0]
+    cache_rows = stale.shape[0]
+    heads = width // HDIM
+
+    def by_head(pieces):
+        pack = jnp.concatenate(
+            [piece.reshape(piece.shape[0], heads, HDIM) for piece in pieces], axis=0
+        )
+        pack = jnp.transpose(pack, (1, 0, 2))
+        pack = jnp.pad(pack, ((0, devices - heads), (0, 0), (0, 0)))
+        return lax.all_to_all(pack, TOK, split_axis=0, concat_axis=0, tiled=True)
+
+    got_cache = by_head([stale[:, :width], stale[:, width:]])
+    got_cache, image_normed, text_normed = lax.optimization_barrier(
+        (got_cache, image_normed, text_normed)
+    )
     every = lax.all_gather(
         jnp.concatenate([image_normed, text_normed], axis=0), TOK, axis=0, tiled=False
     )
@@ -142,9 +164,6 @@
     )
     image_value = image_proj[:, 2 * width :]
     text_value = text_proj[:, 2 * width :]
-    stale = stale_cache[0, 0]
-    cache_rows = stale.shape[0]
-    heads = width // HDIM
     fresh_image = jnp.concatenate([image_key, image_value], axis=1)
     group = lax.axis_size("tb")
     blocks = devices // group
@@ -164,23 +183,19 @@
     row_q = jnp.concatenate([image_query, text_query], axis=0)
     row_k = jnp.concatenate([image_key, text_key], axis=0)
     row_v = jnp.concatenate([image_value, text_value], axis=0)
-    pieces = [row_q, row_k, row_v, stale[:, :width], stale[:, width:]]
-    pack = jnp.concatenate([piece.reshape(piece.shape[0], heads, HDIM) for piece in pieces], axis=0)
-    pack = jnp.transpose(pack, (1, 0, 2))
-    pack = jnp.pad(pack, ((0, devices - heads), (0, 0), (0, 0)))
-    got = lax.all_to_all(pack, TOK, split_axis=0, concat_axis=0, tiled=True)
+    got = by_head([row_q, row_k, row_v])
     rows = image_rows + text_rows
 
-    def part(first, count):
-        return got[:, first : first + count].reshape(-1, HDIM)
+    def part(first, count, source=got):
+        return source[:, first : first + count].reshape(-1, HDIM)
 
     queries = jnp.concatenate([part(0, image_rows), part(image_rows, text_rows)], axis=0)
     fresh_k = part(rows, image_rows)
     text_k = part(rows + image_rows, text_rows)
     fresh_v = part(2 * rows, image_rows)
     text_v = part(2 * rows + image_rows, text_rows)
-    cache_k = part(3 * rows, cache_rows)
-    cache_v = part(3 * rows + cache_rows, cache_rows)
+    cache_k = part(0, cache_rows, got_cache)
+    cache_v = part(cache_rows, cache_rows, got_cache)
     begin = patch * patch_len
     cache_k = lax.dynamic_update_slice_in_dim(cache_k, fresh_k, begin, 0)
     cache_v = lax.dynamic_update_slice_in_dim(cache_v, fresh_v, begin, 0)
@@ -194,7 +209,7 @@
         ]
     )
     head_out = attend(queries, keys, values, valid)
-    image_heads = lax.all_gather(head_out[:patch_len], TOK, axis=0, tiled=False)
+    image_heads = broadcast_rows(head_out[:patch_len], devices).reshape(devices, patch_len, HDIM)
     text_heads = lax.all_gather(head_out[patch_len:], TOK, axis=0, tiled=False)
     image_att = jnp.transpose(image_heads[:heads], (1, 0, 2)).reshape(-1, width)
     text_att = jnp.transpose(text_heads[:heads], (1, 0, 2)).reshape(-1, width)
@@ -215,7 +230,7 @@
     down_weight = image_down[0]
     hidden = jax.nn.gelu(
         jnp.dot(
-            lax.all_gather(mlp_normed, TOK, axis=0, tiled=True),
+            broadcast_rows(mlp_normed, devices),
             up_weight,
             preferred_element_type=jnp.float32,
         ),

time: 392 us -> 366 us (0.934)
  waiting for transfers between devices: 224 us -> 166 us
  blocking collectives: 33.6 us -> 64 us
  starting transfers between devices: 45 us -> 53.2 us
  other arithmetic: 17.8 us -> 13.4 us
    all_to_all x0 -> x2, blocking collectives: none -> 64 us  [broadcast_rows(): got = lax.all_to_all(copies, TOK, split_axis=0, concat_axis=0, tiled=True)]
    all_gather x1 -> x0, waiting for transfers between devices: 59.8 us -> none  [shards(): image_heads = lax.all_gather(head_out[:patch_len], TOK, axis=0, tiled=False)]
    all_gather x1 -> x0, blocking collectives: 33.6 us -> none  [shards(): lax.all_gather(mlp_normed, TOK, axis=0, tiled=True)]
    all_to_all x1 -> x2, starting transfers between devices: 3.91 us -> 13.8 us  [by_head(): return lax.all_to_all(pack, TOK, split_axis=0, concat_axis=0, tiled=True)]
    concatenate x3 -> x1, local copies, waits for them, and re-layouts: 4.12 us -> 0.02 us  [by_head(): jnp.concatenate([piece.reshape(piece.shape[0], heads, HDIM) for piece in...]
    ppermute x3, waiting for transfers between devices: 35.4 us -> 39.4 us  [shards(): quad.append(lax.ppermute(fresh_image, TOK, turn))]
    all_to_all x1 -> x2, waiting for transfers between devices: 22 us -> 19.1 us  [by_head(): return lax.all_to_all(pack, TOK, split_axis=0, concat_axis=0, tiled=True)]
  transfers between devices with their start and end apart: 14 -> 14, of which waited for: 10 -> 10; matrix products, arithmetic and copies ran while one was open for 4% -> 5% of each run, Pallas kernels for 0% -> 0%
where the time goes in v5:
time: 366 us; the launch traced here: 365 us
  waiting for transfers between devices  166 us (45%)
  blocking collectives  64 us (17%)
  starting transfers between devices  53.2 us (15%)
  local copies, waits for them, and re-layouts  32.8 us (9%)
  between operations  24.3 us (7%)
  other arithmetic  13.4 us (4%)
  matrix products  11.6 us (3%)
    all_gather x1, waiting for transfers between devices, shards(): lax.all_gather(jnp.concatenate([image_normed, text_normed], axis=0), TOK,...  66.4 us
    all_to_all x2, blocking collectives, broadcast_rows(): got = lax.all_to_all(copies, TOK, split_axis=0, concat_axis=0, tiled=True)  64 us
    ppermute x3, waiting for transfers between devices, shards(): quad.append(lax.ppermute(fresh_image, TOK, turn))  39.4 us
    all_to_all x3, waiting for transfers between devices, cols_to_rows(): got = lax.all_to_all(cols, TOK, split_axis=0, concat_axis=0, tiled=True)  36.4 us
    all_to_all x3, starting transfers between devices, cols_to_rows(): got = lax.all_to_all(cols, TOK, split_axis=0, concat_axis=0, tiled=True)  24.4 us
    all_to_all x2, waiting for transfers between devices, by_head(): return lax.all_to_all(pack, TOK, split_axis=0, concat_axis=0, tiled=True)  19.1 us
    all_to_all x2, starting transfers between devices, by_head(): return lax.all_to_all(pack, TOK, split_axis=0, concat_axis=0, tiled=True)  13.8 us
  transfers between devices with their start and end apart: 14, of which 10 were waited for; matrix products, arithmetic and copies ran while one was open for 5% of the time, Pallas kernels for 0%

profile of v5, /device:TPU:2, one launch (start us, length us, event | category | flops | bytes accessed | tf_op | source)
XLA Modules:
  0.0 364.8 jit_solution(11934359471738366556)
XLA Ops:
  9.2 9.9 %all-to-all-start = ((bf16[32,32,128]{2,1,0:T(8,128)(2,1)}), bf16[32,32,128]{2,1,0:T(8,128)(2,1)S(1)}, u32[]{:S(2)}, u32[]{:S(2)}) async-start(bf16[32,32,128]{2,1,0:T(8,128)(2,1)} %pad.9.clone), calls=%async_computation | async-start | bytes 524288 | tf_op jit(solution)/shard_map/all_to_all | solution.py:128
  19.1 1.3 fusion.118
  24.0 1.4 constant_dynamic-slice_fusion
  29.7 2.5 all-to-all-done
  32.9 66.4 %all-gather.8.cloned.1.call-done = bf16[32,20,3072]{2,1,0:T(8,128)(2,1)} async-done(((bf16[1,20,3072]{2,1,0:T(8,128)(2,1)}), bf16[32,20,3072]{2,1,0:T(8,128)(2,1)}) %all-gather.8.cloned.1.call-update) | async-done | bytes 3932176 | tf_op jit(solution)/shard_map/all_gather | solution.py:134
  99.4 3.8 %slice.229 = bf16[32,16,3072]{2,1,0:T(8,128)(2,1)S(1)} slice(bf16[32,20,3072]{2,1,0:T(8,128)(2,1)} %all-gather.8.cloned.1.call-done), slice={[0:32], [4:20], [0:3072]} | slice | bytes 6291456 | tf_op jit(solution)/shard_map/slice | solution.py:141
  105.3 1.6 slice.228
  107.9 2.4 fusion.21
  111.6 6.2 %all-to-all-start.1 = ((bf16[32,20,288]{2,1,0:T(8,128)(2,1)}), bf16[32,20,288]{2,1,0:T(8,128)(2,1)S(1)}, u32[]{:S(2)}, u32[]{:S(2)}) async-start(bf16[32,20,288]{2,1,0:T(8,128)(2,1)} %pad_maximum_fusion), calls=%async_computation.1 | async-start | bytes 1179648 | tf_op jit(solution)/shard_map/all_to_all | solution.py:64
  119.0 18.3 %all-to-all-done.1 = bf16[32,20,288]{2,1,0:T(8,128)(2,1)S(1)} async-done(((bf16[32,20,288]{2,1,0:T(8,128)(2,1)}), bf16[32,20,288]{2,1,0:T(8,128)(2,1)S(1)}, u32[]{:S(2)}, u32[]{:S(2)}) %all-to-all-start.1) | async-done | bytes 368672 | tf_op jit(solution)/shard_map/all_to_all | solution.py:64
  147.3 3.9 %all-to-all-start.2 = ((bf16[32,60,128]{2,1,0:T(8,128)(2,1)}), bf16[32,60,128]{2,1,0:T(8,128)(2,1)S(1)}, u32[]{:S(2)}, u32[]{:S(2)}) async-start(bf16[32,60,128]{2,1,0:T(8,128)(2,1)} %pad.10.clone), calls=%async_computation.2 | async-start | bytes 1048576 | tf_op jit(solution)/shard_map/all_to_all | solution.py:128
  153.1 16.6 %all-to-all-done.2 = bf16[32,60,128]{2,1,0:T(8,128)(2,1)S(1)} async-done(((bf16[32,60,128]{2,1,0:T(8,128)(2,1)}), bf16[32,60,128]{2,1,0:T(8,128)(2,1)S(1)}, u32[]{:S(2)}, u32[]{:S(2)}) %all-to-all-start.2) | async-done | bytes 491552 | tf_op jit(solution)/shard_map/all_to_all | solution.py:128
  170.4 1.5 fusion.4
  173.3 1.8 fusion.32
  175.4 31.5 %all_to_all.40 = bf16[32,128,128]{1,2,0:T(8,128)(2,1)S(1)} all-to-all(bf16[32,128,128]{1,2,0:T(8,128)(2,1)S(1)} %broadcast_in_dim.38), channel_id=1, replica_groups=mesh['section'=2,'grp'=4,'ta'=8,'tb'=4] {'ta','tb'}, dimensions={0} | all-to-all | bytes 2097152 | tf_op jit(solution)/shard_map/all_to_all | solution.py:71
  208.0 4.1 %all-to-all-start.4 = ((bf16[32,4,96]{2,1,0:T(4,128)(2,1)}), bf16[32,4,96]{2,1,0:T(4,128)(2,1)S(1)}, u32[]{:S(2)}, u32[]{:S(2)}) async-start(bf16[32,4,96]{2,1,0:T(4,128)(2,1)} %bitcast.44), calls=%async_computation.4 | async-start | bytes 65536 | tf_op jit(solution)/shard_map/all_to_all | solution.py:64
  213.0 7.7 %all-to-all-done.4 = bf16[32,4,96]{2,1,0:T(4,128)(2,1)S(1)} async-done(((bf16[32,4,96]{2,1,0:T(4,128)(2,1)}), bf16[32,4,96]{2,1,0:T(4,128)(2,1)S(1)}, u32[]{:S(2)}, u32[]{:S(2)}) %all-to-all-start.4) | async-done | bytes 24608 | tf_op jit(solution)/shard_map/all_to_all | solution.py:64
  221.5 32.5 %all_to_all.41 = bf16[32,4,3072]{2,1,0:T(4,128)(2,1)S(1)} all-to-all(bf16[32,4,3072]{2,1,0:T(4,128)(2,1)S(1)} %broadcast_in_dim.39), channel_id=1, replica_groups=mesh['section'=2,'grp'=4,'ta'=8,'tb'=4] {'ta','tb'}, dimensions={0} | all-to-all | bytes 1572864 | tf_op jit(solution)/shard_map/all_to_all | solution.py:71
  255.1 2.5 fusion.68
  258.3 2.2 copy.65
  260.5 4.8 %all-to-all-start.6 = ((f32[32,4,3072]{2,1,0:T(4,128)}), f32[32,4,3072]{2,1,0:T(4,128)}, u32[]{:S(2)}, u32[]{:S(2)}) async-start(f32[32,4,3072]{2,1,0:T(4,128)} %copy.65), calls=%async_computation.6 | async-start | bytes 3145728 | tf_op jit(solution)/shard_map/all_to_all | solution.py:241
  267.7 1.8 collective-permute-start.3
  269.4 1.4 collective-permute-start.4
  271.4 38.5 %collective-permute-done.2 = bf16[4,6144]{1,0:T(4,128)(2,1)S(1)} collective-permute-done((bf16[4,6144]{1,0:T(4,128)(2,1)S(1)}, bf16[4,6144]{1,0:T(4,128)(2,1)S(1)}, u32[]{:S(2)}, u32[]{:S(2)}) %collective-permute-start.2) | collective-permute-done | bytes 49184 | tf_op jit(solution)/shard_map/ppermute | solution.py:174
  312.5 1.6 reduce_sum.137
  314.1 2.9 collective-permute-start
  317.7 1.8 collective-permute-done
  320.0 1.9 slice-done
  325.6 14.1 %all-to-all-start.7 = ((bf16[32,16,96]{2,1,0:T(8,128)(2,1)}), bf16[32,16,96]{2,1,0:T(8,128)(2,1)S(1)}, u32[]{:S(2)}, u32[]{:S(2)}) async-start(bf16[32,16,96]{2,1,0:T(8,128)(2,1)} %bitcast.57), calls=%async_computation.7 | async-start | bytes 262144 | tf_op jit(solution)/shard_map/all_to_all | solution.py:64
  339.7 10.4 %all-to-all-done.7 = bf16[32,16,96]{2,1,0:T(8,128)(2,1)S(1)} async-done(((bf16[32,16,96]{2,1,0:T(8,128)(2,1)}), bf16[32,16,96]{2,1,0:T(8,128)(2,1)S(1)}, u32[]{:S(2)}, u32[]{:S(2)}) %all-to-all-start.7) | async-done | bytes 98336 | tf_op jit(solution)/shard_map/all_to_all | solution.py:64
  350.5 3.1 collective-permute-start.1
  354.4 2.3 collective-permute-done.1
  (175 shorter events, 37.8 us)
Async XLA Ops:
  7.2 250.5 %copy-start = (bf16[1,384,3072]{2,1,0:T(8,128)(2,1)S(1)}, bf16[1,384,3072]{2,1,0:T(8,128)(2,1)}, u32[]{:S(2)}) copy-start(bf16[1,384,3072]{2,1,0:T(8,128)(2,1)} %param.31) | copy-start | bytes 7077892
  7.2 20.1 %copy-start.16 = (bf16[1,4,18432]{2,1,0:T(4,128)(2,1)S(1)}, bf16[1,4,18432]{2,1,0:T(4,128)(2,1)}, u32[]{:S(2)}) copy-start(bf16[1,4,18432]{2,1,0:T(4,128)(2,1)} %param.23) | copy-start | bytes 442372
  7.2 20.9 %copy-start.7 = (bf16[1,1,4,3072]{3,2,1,0:T(4,128)(2,1)S(1)}, bf16[1,1,4,3072]{3,2,1,0:T(4,128)(2,1)}, u32[]{:S(2)}) copy-start(bf16[1,1,4,3072]{3,2,1,0:T(4,128)(2,1)} %param.18) | copy-start | bytes 73732
  7.2 21.2 %copy-start.17 = (bf16[1,4,9216]{2,1,0:T(4,128)(2,1)S(1)}, bf16[1,4,9216]{2,1,0:T(4,128)(2,1)}, u32[]{:S(2)}) copy-start(bf16[1,4,9216]{2,1,0:T(4,128)(2,1)} %param.24) | copy-start | bytes 221188
  7.2 21.9 %copy-start.1 = (bf16[1,1,16,3072]{3,2,1,0:T(8,128)(2,1)S(1)}, bf16[1,1,16,3072]{3,2,1,0:T(8,128)(2,1)}, u32[]{:S(2)}) copy-start(bf16[1,1,16,3072]{3,2,1,0:T(8,128)(2,1)} %param.19) | copy-start | bytes 294916
  9.2 23.1 %all-to-all-start = ((bf16[32,32,128]{2,1,0:T(8,128)(2,1)}), bf16[32,32,128]{2,1,0:T(8,128)(2,1)S(1)}, u32[]{:S(2)}, u32[]{:S(2)}) async-start(bf16[32,32,128]{2,1,0:T(8,128)(2,1)} %pad.9.clone), calls=%async_computation | async-start | bytes 524288 | tf_op jit(solution)/shard_map/all_to_all | solution.py:128
  19.0 80.3 %all-gather.8.cloned.1.call-start = ((), (), s32[]{:S(2)}) async-start(), calls=%async_computation.9 | async-start | bytes 4866048 | tf_op jit(solution)/shard_map/all_gather | solution.py:134
  107.9 9.8 %copy-start.19 = (f32[1,4,128]{2,1,0:T(4,128)S(1)}, f32[1,4,128]{2,1,0:T(4,128)}, u32[]{:S(2)}) copy-start(f32[1,4,128]{2,1,0:T(4,128)} %param.27) | copy-start | bytes 6148
  111.6 25.7 %all-to-all-start.1 = ((bf16[32,20,288]{2,1,0:T(8,128)(2,1)}), bf16[32,20,288]{2,1,0:T(8,128)(2,1)S(1)}, u32[]{:S(2)}, u32[]{:S(2)}) async-start(bf16[32,20,288]{2,1,0:T(8,128)(2,1)} %pad_maximum_fusion), calls=%async_computation.1 | async-start | bytes 1179648 | tf_op jit(solution)/shard_map/all_to_all | solution.py:64
  146.2 24.3 %copy-start.8 = (bf16[4,3072]{1,0:T(4,128)(2,1)}, bf16[4,3072]{1,0:T(4,128)(2,1)S(1)}, u32[]{:S(2)}) copy-start(bf16[4,3072]{1,0:T(4,128)(2,1)S(1)} %get-tuple-element.34) | copy-start | bytes 73732
  147.3 22.4 %all-to-all-start.2 = ((bf16[32,60,128]{2,1,0:T(8,128)(2,1)}), bf16[32,60,128]{2,1,0:T(8,128)(2,1)S(1)}, u32[]{:S(2)}, u32[]{:S(2)}) async-start(bf16[32,60,128]{2,1,0:T(8,128)(2,1)} %pad.10.clone), calls=%async_computation.2 | async-start | bytes 1048576 | tf_op jit(solution)/shard_map/all_to_all | solution.py:128
  175.1 31.9 %copy-start.4 = (bf16[1,3072,96]{1,2,0:T(8,128)(2,1)S(1)}, bf16[1,3072,96]{1,2,0:T(8,128)(2,1)}, u32[]{:S(2)}) copy-start(bf16[1,3072,96]{1,2,0:T(8,128)(2,1)} %param.28) | copy-start | bytes 1769476
  175.3 45.5 %copy-start.15 = (f32[1,1,3072]{2,1,0:T(1,128)S(1)}, f32[1,1,3072]{2,1,0:T(1,128)}, u32[]{:S(2)}) copy-start(f32[1,1,3072]{2,1,0:T(1,128)} %get-tuple-element.33) | copy-start | bytes 36868
  175.4 45.9 %copy-start.13 = (f32[1,1,3072]{2,1,0:T(1,128)S(1)}, f32[1,1,3072]{2,1,0:T(1,128)}, u32[]{:S(2)}) copy-start(f32[1,1,3072]{2,1,0:T(1,128)} %get-tuple-element.29) | copy-start | bytes 36868
  175.4 45.9 %copy-start.14 = (f32[1,1,3072]{2,1,0:T(1,128)S(1)}, f32[1,1,3072]{2,1,0:T(1,128)}, u32[]{:S(2)}) copy-start(f32[1,1,3072]{2,1,0:T(1,128)} %get-tuple-element.30) | copy-start | bytes 36868
  208.0 12.7 %all-to-all-start.4 = ((bf16[32,4,96]{2,1,0:T(4,128)(2,1)}), bf16[32,4,96]{2,1,0:T(4,128)(2,1)S(1)}, u32[]{:S(2)}, u32[]{:S(2)}) async-start(bf16[32,4,96]{2,1,0:T(4,128)(2,1)} %bitcast.44), calls=%async_computation.4 | async-start | bytes 65536 | tf_op jit(solution)/shard_map/all_to_all | solution.py:64
  212.1 107.8 %all-gather.6.cloned.1.call-start = ((), (), s32[]{:S(2)}) async-start(), calls=%async_computation.8 | async-start | bytes 4325376 | tf_op jit(solution)/shard_map/all_gather | solution.py:213
  258.3 9.1 %copy-start.18 = (bf16[4,6144]{1,0:T(4,128)(2,1)S(1)}, bf16[4,6144]{1,0:T(4,128)(2,1)}, u32[]{:S(2)}) copy-start(bf16[4,6144]{1,0:T(4,128)(2,1)} %param.33) | copy-start | bytes 147460
  258.3 9.1 %copy-start.9 = (bf16[4,3072]{1,0:T(4,128)(2,1)S(1)}, bf16[4,3072]{1,0:T(4,128)(2,1)}, u32[]{:S(2)}) copy-start(bf16[4,3072]{1,0:T(4,128)(2,1)} %copy-done.8) | copy-start | bytes 73732
  260.5 53.6 %copy-start.12 = (f32[1,1,3072]{2,1,0:T(1,128)S(1)}, f32[1,1,3072]{2,1,0:T(1,128)}, u32[]{:S(2)}) copy-start(f32[1,1,3072]{2,1,0:T(1,128)} %get-tuple-element.28) | copy-start | bytes 36868
  260.5 56.6 %copy-start.3 = (bf16[1,1,16,6144]{3,2,1,0:T(8,128)(2,1)S(1)}, bf16[1,1,16,6144]{3,2,1,0:T(8,128)(2,1)}, u32[]{:S(2)}) copy-start(bf16[1,1,16,6144]{3,2,1,0:T(8,128)(2,1)} %param.32) | copy-start | bytes 589828
  260.5 52.0 %all-to-all-start.6 = ((f32[32,4,3072]{2,1,0:T(4,128)}), f32[32,4,3072]{2,1,0:T(4,128)}, u32[]{:S(2)}, u32[]{:S(2)}) async-start(f32[32,4,3072]{2,1,0:T(4,128)} %copy.65), calls=%async_computation.6 | async-start | bytes 3145728 | tf_op jit(solution)/shard_map/all_to_all | solution.py:241
  267.5 42.4 %collective-permute-start.2 = (bf16[4,6144]{1,0:T(4,128)(2,1)S(1)}, bf16[4,6144]{1,0:T(4,128)(2,1)S(1)}, u32[]{:S(2)}, u32[]{:S(2)}) collective-permute-start(bf16[4,6144]{1,0:T(4,128)(2,1)S(1)} %get-tuple-element.39), channel_id=1, source_target_pairs={{0,1},{1,2},{2,3},{3,0},{4,5},{5,6},{6,7},{7,4},{8,9},{9,10},{10,1... | collective-permute-start | bytes 147464 | tf_op jit(solution)/shard_map/ppermute | solution.py:174
  267.7 43.1 %collective-permute-start.3 = (bf16[4,6144]{1,0:T(4,128)(2,1)S(1)}, bf16[4,6144]{1,0:T(4,128)(2,1)S(1)}, u32[]{:S(2)}, u32[]{:S(2)}) collective-permute-start(bf16[4,6144]{1,0:T(4,128)(2,1)S(1)} %get-tuple-element.39), channel_id=1, source_target_pairs={{0,2},{1,3},{2,0},{3,1},{4,6},{5,7},{6,4},{7,5},{8,10},{9,11},{10,... | collective-permute-start | bytes 147464 | tf_op jit(solution)/shard_map/ppermute | solution.py:174
  269.4 41.3 %collective-permute-start.4 = (bf16[4,6144]{1,0:T(4,128)(2,1)S(1)}, bf16[4,6144]{1,0:T(4,128)(2,1)S(1)}, u32[]{:S(2)}, u32[]{:S(2)}) collective-permute-start(bf16[4,6144]{1,0:T(4,128)(2,1)S(1)} %get-tuple-element.39), channel_id=1, source_target_pairs={{0,3},{1,0},{2,1},{3,2},{4,7},{5,4},{6,5},{7,6},{8,11},{9,8},{10,9... | collective-permute-start | bytes 147464 | tf_op jit(solution)/shard_map/ppermute | solution.py:174
  311.8 5.3 %collective-permute-start.5 = (bf16[16,6144]{1,0:T(8,128)(2,1)S(1)}, bf16[16,6144]{1,0:T(8,128)(2,1)S(1)}, u32[]{:S(2)}, u32[]{:S(2)}) collective-permute-start(bf16[16,6144]{1,0:T(8,128)(2,1)S(1)} %reshape.455), channel_id=1, source_target_pairs={{0,0},{1,8},{2,16},{3,24},{4,1},{5,9},{6,17},{7,25},{8,2},{9,10},{... | collective-permute-start | bytes 589832 | tf_op jit(solution)/shard_map/ppermute | solution.py:179
  314.1 5.4 %collective-permute-start = (bf16[4,3072]{1,0:T(4,128)(2,1)S(1)}, bf16[4,3072]{1,0:T(4,128)(2,1)S(1)}, u32[]{:S(2)}, u32[]{:S(2)}) collective-permute-start(bf16[4,3072]{1,0:T(4,128)(2,1)S(1)} %add_convert_fusion), channel_id=1, source_target_pairs={{128,0},{0,128},{129,1},{1,129},{130,2},{2,130},{131,3},{3,131},{1... | collective-permute-start | bytes 73736 | tf_op jit(solution)/shard_map/ppermute | solution.py:20
  324.2 26.2 %copy-start.11 = (f32[1,1,3072]{2,1,0:T(1,128)S(1)}, f32[1,1,3072]{2,1,0:T(1,128)}, u32[]{:S(2)}) copy-start(f32[1,1,3072]{2,1,0:T(1,128)} %get-tuple-element.40) | copy-start | bytes 36868
  324.2 29.4 %copy-start.21 = (bf16[3072,32]{0,1:T(8,128)(2,1)S(1)}, bf16[3072,32]{0,1:T(8,128)(2,1)}, u32[]{:S(2)}) copy-start(bf16[3072,32]{0,1:T(8,128)(2,1)} %param.34) | copy-start | bytes 589828
  324.2 29.4 %copy-start.22 = (f32[1,4,32]{2,1,0:T(4,128)S(1)}, f32[1,4,32]{2,1,0:T(4,128)}, u32[]{:S(2)}) copy-start(f32[1,4,32]{2,1,0:T(4,128)} %param.35) | copy-start | bytes 1540
  325.6 24.5 %all-to-all-start.7 = ((bf16[32,16,96]{2,1,0:T(8,128)(2,1)}), bf16[32,16,96]{2,1,0:T(8,128)(2,1)S(1)}, u32[]{:S(2)}, u32[]{:S(2)}) async-start(bf16[32,16,96]{2,1,0:T(8,128)(2,1)} %bitcast.57), calls=%async_computation.7 | async-start | bytes 262144 | tf_op jit(solution)/shard_map/all_to_all | solution.py:64
  350.5 6.2 %collective-permute-start.1 = (bf16[16,3072]{1,0:T(8,128)(2,1)S(1)}, bf16[16,3072]{1,0:T(8,128)(2,1)S(1)}, u32[]{:S(2)}, u32[]{:S(2)}) collective-permute-start(bf16[16,3072]{1,0:T(8,128)(2,1)S(1)} %fusion.52), channel_id=1, source_target_pairs={{128,0},{0,128},{129,1},{1,129},{130,2},{2,130},{131,3},{3,131},{1... | collective-permute-start | bytes 294920 | tf_op jit(solution)/shard_map/ppermute | solution.py:20
  (6 other events, 13.1 us)
Sparse Core Ops, SparseCore 0:
  33.1 66.2 all-gather.7
  214.8 87.2 all-gather.5

commit v6 on v5

--- a/solution.py
+++ b/solution.py
@@ -165,21 +165,8 @@
     image_value = image_proj[:, 2 * width :]
     text_value = text_proj[:, 2 * width :]
     fresh_image = jnp.concatenate([image_key, image_value], axis=1)
-    group = lax.axis_size("tb")
-    blocks = devices // group
-    mine = lax.axis_index("tb")
-    quad = [fresh_image]
-    for shift in range(1, group):
-        turn = [(j * group + b, j * group + (b + shift) % group) for j in range(blocks) for b in range(group)]
-        quad.append(lax.ppermute(fresh_image, TOK, turn))
-    quad = jnp.stack(quad)
-    order = (mine - jnp.arange(group)) % group
-    quad = jnp.zeros_like(quad).at[order].set(quad).reshape(-1, fresh_image.shape[1])
-    route = [(j * group + b, j + blocks * b) for j in range(blocks) for b in range(group)]
-    moved = lax.ppermute(quad, TOK, route)
     patch_len = image_rows * devices
     per_patch = patch_len // cache_rows
-    current = jnp.where(position // per_patch == patch, moved, stale)
     row_q = jnp.concatenate([image_query, text_query], axis=0)
     row_k = jnp.concatenate([image_key, text_key], axis=0)
     row_v = jnp.concatenate([image_value, text_value], axis=0)
@@ -210,7 +197,17 @@
     )
     head_out = attend(queries, keys, values, valid)
     image_heads = broadcast_rows(head_out[:patch_len], devices).reshape(devices, patch_len, HDIM)
-    text_heads = lax.all_gather(head_out[patch_len:], TOK, axis=0, tiled=False)
+    riders = fresh_image.reshape(-1, HDIM)
+    text_heads = lax.all_gather(
+        jnp.concatenate([head_out[patch_len:], riders], axis=0), TOK, axis=0, tiled=False
+    )
+    text_len = head_out.shape[0] - patch_len
+    fresh_all = text_heads[:, text_len:].reshape(patch_len, -1)
+    text_heads = text_heads[:, :text_len]
+    moved = lax.dynamic_slice_in_dim(
+        fresh_all, (position % per_patch) * cache_rows, cache_rows, 0
+    )
+    current = jnp.where(position // per_patch == patch, moved, stale)
     image_att = jnp.transpose(image_heads[:heads], (1, 0, 2)).reshape(-1, width)
     text_att = jnp.transpose(text_heads[:heads], (1, 0, 2)).reshape(-1, width)
     image_back = cols_to_rows(

time: 366 us -> 367 us (level)
  blocking collectives: 64 us -> 84.8 us
  starting transfers between devices: 53.2 us -> 35 us
  waiting for transfers between devices: 166 us -> 148 us
  local copies, waits for them, and re-layouts: 32.8 us -> 46.4 us
    ppermute x4 -> x0, waiting for transfers between devices: 39.4 us -> none  [the longest x3 39.4 us: shards(): quad.append(lax.ppermute(fresh_image, TOK, turn))]
    all_to_all x1, waiting for transfers between devices: 0.01 us -> 37.5 us  [shards(): lax.all_to_all(partial.reshape(devices, image_rows, width), TOK, split_ax...]
    all_to_all x3 -> x2, waiting for transfers between devices: 36.4 us -> 21 us  [cols_to_rows(): got = lax.all_to_all(cols, TOK, split_axis=0, concat_axis=0, tiled=True)]
    all_to_all x3 -> x2, starting transfers between devices: 24.4 us -> 10.7 us  [cols_to_rows(): got = lax.all_to_all(cols, TOK, split_axis=0, concat_axis=0, tiled=True)]
    all_to_all x0 -> x1, blocking collectives: none -> 13.3 us  [cols_to_rows(): got = lax.all_to_all(cols, TOK, split_axis=0, concat_axis=0, tiled=True)]
    transpose x0 -> x2, local copies, waits for them, and re-layouts: none -> 8.64 us  [shards(): text_att = jnp.transpose(text_heads[:heads], (1, 0, 2)).reshape(-1, width)]
    all_to_all x2, blocking collectives: 64 us -> 71.6 us  [broadcast_rows(): got = lax.all_to_all(copies, TOK, split_axis=0, concat_axis=0, tiled=True)]
    ppermute x4 -> x0, starting transfers between devices: 4 us -> none  [the longest x3 3.33 us: shards(): quad.append(lax.ppermute(fresh_image, TOK, turn))]
  transfers between devices with their start and end apart: 14 -> 9, of which waited for: 10 -> 8; matrix products, arithmetic and copies ran while one was open for 5% -> 7% of each run, Pallas kernels for 0% -> 0%
where the time goes in v6:
time: 367 us; the launch traced here: 365 us
  waiting for transfers between devices  148 us (40%)
  blocking collectives  84.8 us (23%)
  local copies, waits for them, and re-layouts  46.4 us (13%)
  starting transfers between devices  35 us (10%)
  between operations  24.6 us (7%)
  matrix products  13.5 us (4%)
  other arithmetic  12.6 us (3%)
    all_to_all x2, blocking collectives, broadcast_rows(): got = lax.all_to_all(copies, TOK, split_axis=0, concat_axis=0, tiled=True)  71.6 us
    all_gather x1, waiting for transfers between devices, shards(): lax.all_gather(jnp.concatenate([image_normed, text_normed], axis=0), TOK,...  66.3 us
    all_to_all x1, waiting for transfers between devices, shards(): lax.all_to_all(partial.reshape(devices, image_rows, width), TOK, split_ax...  37.5 us
    all_to_all x2, waiting for transfers between devices, cols_to_rows(): got = lax.all_to_all(cols, TOK, split_axis=0, concat_axis=0, tiled=True)  21 us
    all_to_all x2, waiting for transfers between devices, by_head(): return lax.all_to_all(pack, TOK, split_axis=0, concat_axis=0, tiled=True)  19.5 us
    all_to_all x2, starting transfers between devices, by_head(): return lax.all_to_all(pack, TOK, split_axis=0, concat_axis=0, tiled=True)  13.8 us
    all_to_all x1, blocking collectives, cols_to_rows(): got = lax.all_to_all(cols, TOK, split_axis=0, concat_axis=0, tiled=True)  13.3 us
    all_to_all x2, starting transfers between devices, cols_to_rows(): got = lax.all_to_all(cols, TOK, split_axis=0, concat_axis=0, tiled=True)  10.7 us
  transfers between devices with their start and end apart: 9, of which 8 were waited for; matrix products, arithmetic and copies ran while one was open for 7% of the time, Pallas kernels for 0%

profile of v6, /device:TPU:2, one launch (start us, length us, event | category | flops | bytes accessed | tf_op | source)
XLA Modules:
  0.0 365.3 jit_solution(9763289717324515974)
XLA Ops:
  9.2 9.9 %all-to-all-start = ((bf16[32,32,128]{2,1,0:T(8,128)(2,1)}), bf16[32,32,128]{2,1,0:T(8,128)(2,1)S(1)}, u32[]{:S(2)}, u32[]{:S(2)}) async-start(bf16[32,32,128]{2,1,0:T(8,128)(2,1)} %pad.9.clone), calls=%async_computation | async-start | bytes 524288 | tf_op jit(solution)/shard_map/all_to_all | solution.py:128
  29.5 2.7 all-to-all-done
  33.0 66.3 %all-gather.8.cloned.1.call-done = bf16[32,20,3072]{2,1,0:T(8,128)(2,1)} async-done(((bf16[1,20,3072]{2,1,0:T(8,128)(2,1)}), bf16[32,20,3072]{2,1,0:T(8,128)(2,1)}) %all-gather.8.cloned.1.call-update) | async-done | bytes 3932176 | tf_op jit(solution)/shard_map/all_gather | solution.py:134
  99.3 1.6 slice.236
  102.0 2.3 fusion.21
  104.5 3.8 %slice.237 = bf16[32,16,3072]{2,1,0:T(8,128)(2,1)S(1)} slice(bf16[32,20,3072]{2,1,0:T(8,128)(2,1)} %all-gather.8.cloned.1.call-done), slice={[0:32], [4:20], [0:3072]} | slice | bytes 6291456 | tf_op jit(solution)/shard_map/slice | solution.py:141
  110.7 6.2 %all-to-all-start.1 = ((bf16[32,20,288]{2,1,0:T(8,128)(2,1)}), bf16[32,20,288]{2,1,0:T(8,128)(2,1)S(1)}, u32[]{:S(2)}, u32[]{:S(2)}) async-start(bf16[32,20,288]{2,1,0:T(8,128)(2,1)} %pad_maximum_fusion), calls=%async_computation.1 | async-start | bytes 1179648 | tf_op jit(solution)/shard_map/all_to_all | solution.py:64
  118.8 17.6 %all-to-all-done.1 = bf16[32,20,288]{2,1,0:T(8,128)(2,1)S(1)} async-done(((bf16[32,20,288]{2,1,0:T(8,128)(2,1)}), bf16[32,20,288]{2,1,0:T(8,128)(2,1)S(1)}, u32[]{:S(2)}, u32[]{:S(2)}) %all-to-all-start.1) | async-done | bytes 368672 | tf_op jit(solution)/shard_map/all_to_all | solution.py:64
  147.2 1.6 slice_dynamic-update-slice_fusion
  150.7 3.9 %all-to-all-start.2 = ((bf16[32,60,128]{2,1,0:T(8,128)(2,1)}), bf16[32,60,128]{2,1,0:T(8,128)(2,1)S(1)}, u32[]{:S(2)}, u32[]{:S(2)}) async-start(bf16[32,60,128]{2,1,0:T(8,128)(2,1)} %pad.10.clone), calls=%async_computation.2 | async-start | bytes 1048576 | tf_op jit(solution)/shard_map/all_to_all | solution.py:128
  156.2 16.8 %all-to-all-done.2 = bf16[32,60,128]{2,1,0:T(8,128)(2,1)S(1)} async-done(((bf16[32,60,128]{2,1,0:T(8,128)(2,1)}), bf16[32,60,128]{2,1,0:T(8,128)(2,1)S(1)}, u32[]{:S(2)}, u32[]{:S(2)}) %all-to-all-start.2) | async-done | bytes 491552 | tf_op jit(solution)/shard_map/all_to_all | solution.py:128
  176.0 1.8 fusion.32
  179.0 40.3 %all_to_all.40 = bf16[32,128,128]{1,2,0:T(8,128)(2,1)S(1)} all-to-all(bf16[32,128,128]{1,2,0:T(8,128)(2,1)S(1)} %broadcast_in_dim.36), channel_id=1, replica_groups=mesh['section'=2,'grp'=4,'ta'=8,'tb'=4] {'ta','tb'}, dimensions={0} | all-to-all | bytes 2097152 | tf_op jit(solution)/shard_map/all_to_all | solution.py:71
  219.7 13.3 %all_to_all.41 = bf16[32,4,96]{2,1,0:T(4,128)(2,1)S(1)} all-to-all(bf16[32,4,96]{2,1,0:T(4,128)(2,1)S(1)} %bitcast.269), channel_id=1, replica_groups=mesh['section'=2,'grp'=4,'ta'=8,'tb'=4] {'ta','tb'}, dimensions={0} | all-to-all | bytes 49152 | tf_op jit(solution)/shard_map/all_to_all | solution.py:64
  233.9 31.3 %all_to_all.42 = bf16[32,4,3072]{2,1,0:T(4,128)(2,1)S(1)} all-to-all(bf16[32,4,3072]{2,1,0:T(4,128)(2,1)S(1)} %broadcast_in_dim.37), channel_id=1, replica_groups=mesh['section'=2,'grp'=4,'ta'=8,'tb'=4] {'ta','tb'}, dimensions={0} | all-to-all | bytes 1572864 | tf_op jit(solution)/shard_map/all_to_all | solution.py:71
  266.2 2.5 fusion.68
  269.4 2.3 copy.68
  271.7 5.5 %all-to-all-start.6 = ((f32[32,4,3072]{2,1,0:T(4,128)}), f32[32,4,3072]{2,1,0:T(4,128)}, u32[]{:S(2)}, u32[]{:S(2)}) async-start(f32[32,4,3072]{2,1,0:T(4,128)} %copy.68), calls=%async_computation.6 | async-start | bytes 3145728 | tf_op jit(solution)/shard_map/all_to_all | solution.py:238
  278.9 37.5 %all-to-all-done.6 = f32[32,4,3072]{2,1,0:T(4,128)} async-done(((f32[32,4,3072]{2,1,0:T(4,128)}), f32[32,4,3072]{2,1,0:T(4,128)}, u32[]{:S(2)}, u32[]{:S(2)}) %all-to-all-start.6) | async-done | bytes 1572896 | tf_op jit(solution)/shard_map/all_to_all | solution.py:238
  316.4 1.6 reduce_sum.137
  318.0 2.5 collective-permute-start
  321.3 2.2 collective-permute-done
  323.8 3.9 %slice_bitcast_fusion = bf16[512,24,128]{2,0,1:T(8,128)(2,1)} fusion(bf16[32,704,128]{2,1,0:T(8,128)(2,1)} %bitcast.249), kind=kLoop, calls=%fused_computation | loop fusion | bytes 6291456 | tf_op jit(solution)/shard_map/transpose | solution.py:212
  327.8 4.7 %copy.71 = bf16[512,24,128]{0,2,1:T(8,128)(2,1)} copy(bf16[512,24,128]{2,0,1:T(8,128)(2,1)} %slice_bitcast_fusion) | data formatting | bytes 6291456 | tf_op jit(solution)/shard_map/transpose | solution.py:212
  332.5 2.6 convolution_convert_fusion
  335.8 4.4 %all-to-all-start.7 = ((bf16[32,16,96]{2,1,0:T(8,128)(2,1)}), bf16[32,16,96]{2,1,0:T(8,128)(2,1)S(1)}, u32[]{:S(2)}, u32[]{:S(2)}) async-start(bf16[32,16,96]{2,1,0:T(8,128)(2,1)} %bitcast.59), calls=%async_computation.7 | async-start | bytes 262144 | tf_op jit(solution)/shard_map/all_to_all | solution.py:64
  341.1 2.7 slice.260
  343.8 3.6 reshape.409
  347.4 3.3 all-to-all-done.7
  351.0 2.5 collective-permute-start.1
  353.6 1.7 select_bitcast_fusion
  355.2 2.0 collective-permute-done.1
  (165 shorter events, 35.9 us)
Async XLA Ops:
  7.2 261.6 %copy-start = (bf16[1,384,3072]{2,1,0:T(8,128)(2,1)S(1)}, bf16[1,384,3072]{2,1,0:T(8,128)(2,1)}, u32[]{:S(2)}) copy-start(bf16[1,384,3072]{2,1,0:T(8,128)(2,1)} %param.31) | copy-start | bytes 7077892
  7.2 19.9 %copy-start.7 = (bf16[1,1,4,3072]{3,2,1,0:T(4,128)(2,1)S(1)}, bf16[1,1,4,3072]{3,2,1,0:T(4,128)(2,1)}, u32[]{:S(2)}) copy-start(bf16[1,1,4,3072]{3,2,1,0:T(4,128)(2,1)} %param.18) | copy-start | bytes 73732
  7.2 20.3 %copy-start.1 = (bf16[1,1,16,3072]{3,2,1,0:T(8,128)(2,1)S(1)}, bf16[1,1,16,3072]{3,2,1,0:T(8,128)(2,1)}, u32[]{:S(2)}) copy-start(bf16[1,1,16,3072]{3,2,1,0:T(8,128)(2,1)} %param.19) | copy-start | bytes 294916
  7.2 21.3 %copy-start.17 = (bf16[1,4,9216]{2,1,0:T(4,128)(2,1)S(1)}, bf16[1,4,9216]{2,1,0:T(4,128)(2,1)}, u32[]{:S(2)}) copy-start(bf16[1,4,9216]{2,1,0:T(4,128)(2,1)} %param.24) | copy-start | bytes 221188
  7.2 21.4 %copy-start.16 = (bf16[1,4,18432]{2,1,0:T(4,128)(2,1)S(1)}, bf16[1,4,18432]{2,1,0:T(4,128)(2,1)}, u32[]{:S(2)}) copy-start(bf16[1,4,18432]{2,1,0:T(4,128)(2,1)} %param.23) | copy-start | bytes 442372
  9.2 23.1 %all-to-all-start = ((bf16[32,32,128]{2,1,0:T(8,128)(2,1)}), bf16[32,32,128]{2,1,0:T(8,128)(2,1)S(1)}, u32[]{:S(2)}, u32[]{:S(2)}) async-start(bf16[32,32,128]{2,1,0:T(8,128)(2,1)} %pad.9.clone), calls=%async_computation | async-start | bytes 524288 | tf_op jit(solution)/shard_map/all_to_all | solution.py:128
  19.0 80.2 %all-gather.8.cloned.1.call-start = ((), (), s32[]{:S(2)}) async-start(), calls=%async_computation.9 | async-start | bytes 4866048 | tf_op jit(solution)/shard_map/all_gather | solution.py:134
  32.2 0.8 copy-start.2
  104.5 3.8 %copy-start.20 = (bf16[1,3072,288]{1,2,0:T(8,128)(2,1)S(1)}, bf16[1,3072,288]{1,2,0:T(8,128)(2,1)}, u32[]{:S(2)}) copy-start(bf16[1,3072,288]{1,2,0:T(8,128)(2,1)} %param.26) | copy-start | bytes 5308420
  109.5 8.1 %copy-start.19 = (f32[1,4,128]{2,1,0:T(4,128)S(1)}, f32[1,4,128]{2,1,0:T(4,128)}, u32[]{:S(2)}) copy-start(f32[1,4,128]{2,1,0:T(4,128)} %param.27) | copy-start | bytes 6148
  110.7 25.8 %all-to-all-start.1 = ((bf16[32,20,288]{2,1,0:T(8,128)(2,1)}), bf16[32,20,288]{2,1,0:T(8,128)(2,1)S(1)}, u32[]{:S(2)}, u32[]{:S(2)}) async-start(bf16[32,20,288]{2,1,0:T(8,128)(2,1)} %pad_maximum_fusion), calls=%async_computation.1 | async-start | bytes 1179648 | tf_op jit(solution)/shard_map/all_to_all | solution.py:64
  136.9 6.9 %copy-start.8 = (bf16[4,3072]{1,0:T(4,128)(2,1)}, bf16[4,3072]{1,0:T(4,128)(2,1)S(1)}, u32[]{:S(2)}) copy-start(bf16[4,3072]{1,0:T(4,128)(2,1)S(1)} %slice.244) | copy-start | bytes 73732
  143.1 2.8 copy-start.10
  144.0 11.4 %copy-start.3 = (bf16[32,32,128]{2,1,0:T(8,128)(2,1)S(1)}, bf16[32,32,128]{2,1,0:T(8,128)(2,1)}, u32[]{:S(2)}) copy-start(bf16[32,32,128]{2,1,0:T(8,128)(2,1)} %copy-done.2) | copy-start | bytes 786436
  144.4 11.7 %copy-start.9 = (bf16[4,3072]{1,0:T(4,128)(2,1)S(1)}, bf16[4,3072]{1,0:T(4,128)(2,1)}, u32[]{:S(2)}) copy-start(bf16[4,3072]{1,0:T(4,128)(2,1)} %copy-done.8) | copy-start | bytes 73732
  150.7 22.4 %all-to-all-start.2 = ((bf16[32,60,128]{2,1,0:T(8,128)(2,1)}), bf16[32,60,128]{2,1,0:T(8,128)(2,1)S(1)}, u32[]{:S(2)}, u32[]{:S(2)}) async-start(bf16[32,60,128]{2,1,0:T(8,128)(2,1)} %pad.10.clone), calls=%async_computation.2 | async-start | bytes 1048576 | tf_op jit(solution)/shard_map/all_to_all | solution.py:128
  154.6 169.3 %all-gather.6.cloned.1.call-start = ((), (), s32[]{:S(2)}) async-start(), calls=%async_computation.8 | async-start | bytes 5947392 | tf_op jit(solution)/shard_map/all_gather | solution.py:201
  173.7 2.3 copy-start.11
  177.8 41.5 %copy-start.5 = (bf16[1,3072,96]{1,2,0:T(8,128)(2,1)S(1)}, bf16[1,3072,96]{1,2,0:T(8,128)(2,1)}, u32[]{:S(2)}) copy-start(bf16[1,3072,96]{1,2,0:T(8,128)(2,1)} %param.28) | copy-start | bytes 1769476
  178.9 54.2 %copy-start.15 = (f32[1,1,3072]{2,1,0:T(1,128)S(1)}, f32[1,1,3072]{2,1,0:T(1,128)}, u32[]{:S(2)}) copy-start(f32[1,1,3072]{2,1,0:T(1,128)} %get-tuple-element.33) | copy-start | bytes 36868
  179.0 54.6 %copy-start.13 = (f32[1,1,3072]{2,1,0:T(1,128)S(1)}, f32[1,1,3072]{2,1,0:T(1,128)}, u32[]{:S(2)}) copy-start(f32[1,1,3072]{2,1,0:T(1,128)} %get-tuple-element.29) | copy-start | bytes 36868
  179.0 54.6 %copy-start.14 = (f32[1,1,3072]{2,1,0:T(1,128)S(1)}, f32[1,1,3072]{2,1,0:T(1,128)}, u32[]{:S(2)}) copy-start(f32[1,1,3072]{2,1,0:T(1,128)} %get-tuple-element.30) | copy-start | bytes 36868
  269.4 9.4 %copy-start.18 = (bf16[4,6144]{1,0:T(4,128)(2,1)S(1)}, bf16[4,6144]{1,0:T(4,128)(2,1)}, u32[]{:S(2)}) copy-start(bf16[4,6144]{1,0:T(4,128)(2,1)} %param.33) | copy-start | bytes 147460
  271.7 46.3 %copy-start.12 = (f32[1,1,3072]{2,1,0:T(1,128)S(1)}, f32[1,1,3072]{2,1,0:T(1,128)}, u32[]{:S(2)}) copy-start(f32[1,1,3072]{2,1,0:T(1,128)} %get-tuple-element.28) | copy-start | bytes 36868
  271.7 44.7 %all-to-all-start.6 = ((f32[32,4,3072]{2,1,0:T(4,128)}), f32[32,4,3072]{2,1,0:T(4,128)}, u32[]{:S(2)}, u32[]{:S(2)}) async-start(f32[32,4,3072]{2,1,0:T(4,128)} %copy.68), calls=%async_computation.6 | async-start | bytes 3145728 | tf_op jit(solution)/shard_map/all_to_all | solution.py:238
  318.0 5.4 %collective-permute-start = (bf16[4,3072]{1,0:T(4,128)(2,1)S(1)}, bf16[4,3072]{1,0:T(4,128)(2,1)S(1)}, u32[]{:S(2)}, u32[]{:S(2)}) collective-permute-start(bf16[4,3072]{1,0:T(4,128)(2,1)S(1)} %add_convert_fusion), channel_id=1, source_target_pairs={{128,0},{0,128},{129,1},{1,129},{130,2},{2,130},{131,3},{3,131},{1... | collective-permute-start | bytes 73736 | tf_op jit(solution)/shard_map/ppermute | solution.py:20
  327.8 4.7 %copy-start.6 = (bf16[1,3072,96]{1,2,0:T(8,128)(2,1)S(1)}, bf16[1,3072,96]{1,2,0:T(8,128)(2,1)}, u32[]{:S(2)}) copy-start(bf16[1,3072,96]{1,2,0:T(8,128)(2,1)} %param.29) | copy-start | bytes 1769476
  332.5 7.8 %copy-start.21 = (bf16[3072,32]{0,1:T(8,128)(2,1)S(1)}, bf16[3072,32]{0,1:T(8,128)(2,1)}, u32[]{:S(2)}) copy-start(bf16[3072,32]{0,1:T(8,128)(2,1)} %param.34) | copy-start | bytes 589828
  332.5 7.8 %copy-start.22 = (f32[1,4,32]{2,1,0:T(4,128)S(1)}, f32[1,4,32]{2,1,0:T(4,128)}, u32[]{:S(2)}) copy-start(f32[1,4,32]{2,1,0:T(4,128)} %param.35) | copy-start | bytes 1540
  335.8 14.9 %all-to-all-start.7 = ((bf16[32,16,96]{2,1,0:T(8,128)(2,1)}), bf16[32,16,96]{2,1,0:T(8,128)(2,1)S(1)}, u32[]{:S(2)}, u32[]{:S(2)}) async-start(bf16[32,16,96]{2,1,0:T(8,128)(2,1)} %bitcast.59), calls=%async_computation.7 | async-start | bytes 262144 | tf_op jit(solution)/shard_map/all_to_all | solution.py:64
  343.8 9.8 %copy-start.4 = (bf16[1,1,16,6144]{3,2,1,0:T(8,128)(2,1)S(1)}, bf16[1,1,16,6144]{3,2,1,0:T(8,128)(2,1)}, u32[]{:S(2)}) copy-start(bf16[1,1,16,6144]{3,2,1,0:T(8,128)(2,1)} %param.32) | copy-start | bytes 589828
  351.0 6.2 %collective-permute-start.1 = (bf16[16,3072]{1,0:T(8,128)(2,1)S(1)}, bf16[16,3072]{1,0:T(8,128)(2,1)S(1)}, u32[]{:S(2)}, u32[]{:S(2)}) collective-permute-start(bf16[16,3072]{1,0:T(8,128)(2,1)S(1)} %fusion.52), channel_id=1, source_target_pairs={{128,0},{0,128},{129,1},{1,129},{130,2},{2,130},{131,3},{3,131},{1... | collective-permute-start | bytes 294920 | tf_op jit(solution)/shard_map/ppermute | solution.py:20
Sparse Core Ops, SparseCore 0:
  33.1 66.1 all-gather.7
  178.8 86.4 all-gather.5

commit v7 on v6

--- a/solution.py
+++ b/solution.py
@@ -236,8 +236,12 @@
     partial = jnp.dot(hidden, down_weight, preferred_element_type=jnp.float32)
     reduced = jnp.sum(
         lax.all_to_all(
-            partial.reshape(devices, image_rows, width), TOK, split_axis=0, concat_axis=0, tiled=True
-        ),
+            partial.astype(jnp.bfloat16).reshape(devices, image_rows, width),
+            TOK,
+            split_axis=0,
+            concat_axis=0,
+            tiled=True,
+        ).astype(jnp.float32),
         axis=0,
     )
     image_out = (image_mid + modul[5] * reduced).astype(jnp.bfloat16)

time: 367 us -> 350 us (0.954)
  waiting for transfers between devices: 148 us -> 132 us
    all_to_all x1, waiting for transfers between devices: 37.5 us -> 21.4 us  [shards(): lax.all_to_all(partial.astype(jnp.bfloat16).reshape(devices, image_rows,...]
where the time goes in v7:
time: 350 us; the launch traced here: 348 us
  waiting for transfers between devices  132 us (38%)
  blocking collectives  84.5 us (24%)
  local copies, waits for them, and re-layouts  46.9 us (13%)
  starting transfers between devices  34.8 us (10%)
  between operations  24.4 us (7%)
  matrix products  14.1 us (4%)
  other arithmetic  11.3 us (3%)
    all_to_all x2, blocking collectives, broadcast_rows(): got = lax.all_to_all(copies, TOK, split_axis=0, concat_axis=0, tiled=True)  71.3 us
    all_gather x1, waiting for transfers between devices, shards(): lax.all_gather(jnp.concatenate([image_normed, text_normed], axis=0), TOK,...  66.1 us
    all_to_all x1, waiting for transfers between devices, shards(): lax.all_to_all(partial.astype(jnp.bfloat16).reshape(devices, image_rows,...  21.4 us
    all_to_all x2, waiting for transfers between devices, cols_to_rows(): got = lax.all_to_all(cols, TOK, split_axis=0, concat_axis=0, tiled=True)  20.9 us
    all_to_all x2, waiting for transfers between devices, by_head(): return lax.all_to_all(pack, TOK, split_axis=0, concat_axis=0, tiled=True)  19.8 us
    all_to_all x2, starting transfers between devices, by_head(): return lax.all_to_all(pack, TOK, split_axis=0, concat_axis=0, tiled=True)  13.8 us
    all_to_all x1, blocking collectives, cols_to_rows(): got = lax.all_to_all(cols, TOK, split_axis=0, concat_axis=0, tiled=True)  13.2 us
    all_to_all x2, starting transfers between devices, cols_to_rows(): got = lax.all_to_all(cols, TOK, split_axis=0, concat_axis=0, tiled=True)  10.1 us
  transfers between devices with their start and end apart: 9, of which 8 were waited for; matrix products, arithmetic and copies ran while one was open for 7% of the time, Pallas kernels for 0%

profile of v7, /device:TPU:2, one launch (start us, length us, event | category | flops | bytes accessed | tf_op | source)
XLA Modules:
  0.0 348.4 jit_solution(4453954649677889589)
XLA Ops:
  9.2 9.9 %all-to-all-start = ((bf16[32,32,128]{2,1,0:T(8,128)(2,1)}), bf16[32,32,128]{2,1,0:T(8,128)(2,1)S(1)}, u32[]{:S(2)}, u32[]{:S(2)}) async-start(bf16[32,32,128]{2,1,0:T(8,128)(2,1)} %pad.9.clone), calls=%async_computation | async-start | bytes 524288 | tf_op jit(solution)/shard_map/all_to_all | solution.py:128
  29.3 2.9 all-to-all-done
  33.0 66.1 %all-gather.8.cloned.1.call-done = bf16[32,20,3072]{2,1,0:T(8,128)(2,1)} async-done(((bf16[1,20,3072]{2,1,0:T(8,128)(2,1)}), bf16[32,20,3072]{2,1,0:T(8,128)(2,1)}) %all-gather.8.cloned.1.call-update) | async-done | bytes 3932176 | tf_op jit(solution)/shard_map/all_gather | solution.py:134
  99.1 1.6 slice.236
  101.8 2.3 fusion.20
  104.3 3.8 %slice.237 = bf16[32,16,3072]{2,1,0:T(8,128)(2,1)S(1)} slice(bf16[32,20,3072]{2,1,0:T(8,128)(2,1)} %all-gather.8.cloned.1.call-done), slice={[0:32], [4:20], [0:3072]} | slice | bytes 6291456 | tf_op jit(solution)/shard_map/slice | solution.py:141
  110.5 6.2 %all-to-all-start.1 = ((bf16[32,20,288]{2,1,0:T(8,128)(2,1)}), bf16[32,20,288]{2,1,0:T(8,128)(2,1)S(1)}, u32[]{:S(2)}, u32[]{:S(2)}) async-start(bf16[32,20,288]{2,1,0:T(8,128)(2,1)} %pad_maximum_fusion), calls=%async_computation.1 | async-start | bytes 1179648 | tf_op jit(solution)/shard_map/all_to_all | solution.py:64
  118.6 17.6 %all-to-all-done.1 = bf16[32,20,288]{2,1,0:T(8,128)(2,1)S(1)} async-done(((bf16[32,20,288]{2,1,0:T(8,128)(2,1)}), bf16[32,20,288]{2,1,0:T(8,128)(2,1)S(1)}, u32[]{:S(2)}, u32[]{:S(2)}) %all-to-all-start.1) | async-done | bytes 368672 | tf_op jit(solution)/shard_map/all_to_all | solution.py:64
  147.0 1.6 slice_dynamic-update-slice_fusion
  150.5 3.9 %all-to-all-start.2 = ((bf16[32,60,128]{2,1,0:T(8,128)(2,1)}), bf16[32,60,128]{2,1,0:T(8,128)(2,1)S(1)}, u32[]{:S(2)}, u32[]{:S(2)}) async-start(bf16[32,60,128]{2,1,0:T(8,128)(2,1)} %pad.10.clone), calls=%async_computation.2 | async-start | bytes 1048576 | tf_op jit(solution)/shard_map/all_to_all | solution.py:128
  156.0 16.9 %all-to-all-done.2 = bf16[32,60,128]{2,1,0:T(8,128)(2,1)S(1)} async-done(((bf16[32,60,128]{2,1,0:T(8,128)(2,1)}), bf16[32,60,128]{2,1,0:T(8,128)(2,1)S(1)}, u32[]{:S(2)}, u32[]{:S(2)}) %all-to-all-start.2) | async-done | bytes 491552 | tf_op jit(solution)/shard_map/all_to_all | solution.py:128
  175.8 1.8 fusion.31
  178.8 40.3 %all_to_all.40 = bf16[32,128,128]{1,2,0:T(8,128)(2,1)S(1)} all-to-all(bf16[32,128,128]{1,2,0:T(8,128)(2,1)S(1)} %broadcast_in_dim.36), channel_id=1, replica_groups=mesh['section'=2,'grp'=4,'ta'=8,'tb'=4] {'ta','tb'}, dimensions={0} | all-to-all | bytes 2097152 | tf_op jit(solution)/shard_map/all_to_all | solution.py:71
  219.5 13.2 %all_to_all.41 = bf16[32,4,96]{2,1,0:T(4,128)(2,1)S(1)} all-to-all(bf16[32,4,96]{2,1,0:T(4,128)(2,1)S(1)} %bitcast.270), channel_id=1, replica_groups=mesh['section'=2,'grp'=4,'ta'=8,'tb'=4] {'ta','tb'}, dimensions={0} | all-to-all | bytes 49152 | tf_op jit(solution)/shard_map/all_to_all | solution.py:64
  233.6 31.0 %all_to_all.42 = bf16[32,4,3072]{2,1,0:T(4,128)(2,1)} all-to-all(bf16[32,4,3072]{2,1,0:T(4,128)(2,1)S(1)} %broadcast_in_dim.37), channel_id=1, replica_groups=mesh['section'=2,'grp'=4,'ta'=8,'tb'=4] {'ta','tb'}, dimensions={0} | all-to-all | bytes 1572864 | tf_op jit(solution)/shard_map/all_to_all | solution.py:71
  264.7 1.6 reshape.406
  266.3 3.7 %convolution_convert_fusion = bf16[128,3072]{1,0:T(8,128)(2,1)} fusion(bf16[1,384,3072]{2,1,0:T(8,128)(2,1)S(1)} %copy-done, bf16[128,3072]{1,0:T(8,128)(2,1)S(1)} %reshape.406, bf16[1,3072,384]{2,1,0:T(8,128)(2,1)} %param.30), kind=kOutput, calls=%fused_computation | convolution fusion | flops 604815360 | bytes 6291456 | tf_op jit(solution)/shard_map/dot_general | solution.py:236
  270.0 2.4 reshape.407
  272.4 5.7 %all-to-all-start.6 = ((bf16[32,4,3072]{2,1,0:T(4,128)(2,1)}), bf16[32,4,3072]{2,1,0:T(4,128)(2,1)S(1)}, u32[]{:S(2)}, u32[]{:S(2)}) async-start(bf16[32,4,3072]{2,1,0:T(4,128)(2,1)} %reshape.407), calls=%async_computation.6 | async-start | bytes 1572864 | tf_op jit(solution)/shard_map/all_to_all | solution.py:238
  279.9 21.4 %all-to-all-done.6 = bf16[32,4,3072]{2,1,0:T(4,128)(2,1)S(1)} async-done(((bf16[32,4,3072]{2,1,0:T(4,128)(2,1)}), bf16[32,4,3072]{2,1,0:T(4,128)(2,1)S(1)}, u32[]{:S(2)}, u32[]{:S(2)}) %all-to-all-start.6) | async-done | bytes 786464 | tf_op jit(solution)/shard_map/all_to_all | solution.py:238
  301.7 2.6 collective-permute-start
  305.0 2.1 collective-permute-done
  307.5 3.9 %slice_bitcast_fusion = bf16[512,24,128]{2,0,1:T(8,128)(2,1)} fusion(bf16[32,704,128]{2,1,0:T(8,128)(2,1)} %bitcast.250), kind=kLoop, calls=%fused_computation.1 | loop fusion | bytes 6291456 | tf_op jit(solution)/shard_map/transpose | solution.py:212
  311.4 4.7 %copy.66 = bf16[512,24,128]{0,2,1:T(8,128)(2,1)} copy(bf16[512,24,128]{2,0,1:T(8,128)(2,1)} %slice_bitcast_fusion) | data formatting | bytes 6291456 | tf_op jit(solution)/shard_map/transpose | solution.py:212
  316.1 2.6 convolution_convert_fusion.1
  319.5 3.9 %all-to-all-start.7 = ((bf16[32,16,96]{2,1,0:T(8,128)(2,1)}), bf16[32,16,96]{2,1,0:T(8,128)(2,1)S(1)}, u32[]{:S(2)}, u32[]{:S(2)}) async-start(bf16[32,16,96]{2,1,0:T(8,128)(2,1)} %bitcast.58), calls=%async_computation.7 | async-start | bytes 262144 | tf_op jit(solution)/shard_map/all_to_all | solution.py:64
  324.2 2.7 slice.260
  326.9 3.6 %reshape.411 = bf16[128,6144]{1,0:T(8,128)(2,1)} reshape(bf16[32,192,128]{2,1,0:T(8,128)(2,1)} %slice.260) | data formatting | bytes 3145728 | tf_op jit(solution)/shard_map/reshape | solution.py:205
  330.5 3.3 all-to-all-done.7
  334.1 2.6 collective-permute-start.1
  336.7 1.7 select_bitcast_fusion
  338.4 1.9 collective-permute-done.1
  (163 shorter events, 34.5 us)
Async XLA Ops:
  7.2 259.1 %copy-start = (bf16[1,384,3072]{2,1,0:T(8,128)(2,1)S(1)}, bf16[1,384,3072]{2,1,0:T(8,128)(2,1)}, u32[]{:S(2)}) copy-start(bf16[1,384,3072]{2,1,0:T(8,128)(2,1)} %param.31) | copy-start | bytes 7077892
  7.2 19.7 %copy-start.7 = (bf16[1,1,4,3072]{3,2,1,0:T(4,128)(2,1)S(1)}, bf16[1,1,4,3072]{3,2,1,0:T(4,128)(2,1)}, u32[]{:S(2)}) copy-start(bf16[1,1,4,3072]{3,2,1,0:T(4,128)(2,1)} %param.18) | copy-start | bytes 73732
  7.2 20.1 %copy-start.1 = (bf16[1,1,16,3072]{3,2,1,0:T(8,128)(2,1)S(1)}, bf16[1,1,16,3072]{3,2,1,0:T(8,128)(2,1)}, u32[]{:S(2)}) copy-start(bf16[1,1,16,3072]{3,2,1,0:T(8,128)(2,1)} %param.19) | copy-start | bytes 294916
  7.2 21.1 %copy-start.17 = (bf16[1,4,9216]{2,1,0:T(4,128)(2,1)S(1)}, bf16[1,4,9216]{2,1,0:T(4,128)(2,1)}, u32[]{:S(2)}) copy-start(bf16[1,4,9216]{2,1,0:T(4,128)(2,1)} %param.24) | copy-start | bytes 221188
  7.2 21.2 %copy-start.16 = (bf16[1,4,18432]{2,1,0:T(4,128)(2,1)S(1)}, bf16[1,4,18432]{2,1,0:T(4,128)(2,1)}, u32[]{:S(2)}) copy-start(bf16[1,4,18432]{2,1,0:T(4,128)(2,1)} %param.23) | copy-start | bytes 442372
  9.2 23.1 %all-to-all-start = ((bf16[32,32,128]{2,1,0:T(8,128)(2,1)}), bf16[32,32,128]{2,1,0:T(8,128)(2,1)S(1)}, u32[]{:S(2)}, u32[]{:S(2)}) async-start(bf16[32,32,128]{2,1,0:T(8,128)(2,1)} %pad.9.clone), calls=%async_computation | async-start | bytes 524288 | tf_op jit(solution)/shard_map/all_to_all | solution.py:128
  19.0 80.0 %all-gather.8.cloned.1.call-start = ((), (), s32[]{:S(2)}) async-start(), calls=%async_computation.9 | async-start | bytes 4866048 | tf_op jit(solution)/shard_map/all_gather | solution.py:134
  32.2 0.8 copy-start.2
  104.3 3.8 %copy-start.20 = (bf16[1,3072,288]{1,2,0:T(8,128)(2,1)S(1)}, bf16[1,3072,288]{1,2,0:T(8,128)(2,1)}, u32[]{:S(2)}) copy-start(bf16[1,3072,288]{1,2,0:T(8,128)(2,1)} %param.26) | copy-start | bytes 5308420
  109.3 8.1 %copy-start.19 = (f32[1,4,128]{2,1,0:T(4,128)S(1)}, f32[1,4,128]{2,1,0:T(4,128)}, u32[]{:S(2)}) copy-start(f32[1,4,128]{2,1,0:T(4,128)} %param.27) | copy-start | bytes 6148
  110.5 25.8 %all-to-all-start.1 = ((bf16[32,20,288]{2,1,0:T(8,128)(2,1)}), bf16[32,20,288]{2,1,0:T(8,128)(2,1)S(1)}, u32[]{:S(2)}, u32[]{:S(2)}) async-start(bf16[32,20,288]{2,1,0:T(8,128)(2,1)} %pad_maximum_fusion), calls=%async_computation.1 | async-start | bytes 1179648 | tf_op jit(solution)/shard_map/all_to_all | solution.py:64
  136.7 6.9 %copy-start.8 = (bf16[4,3072]{1,0:T(4,128)(2,1)}, bf16[4,3072]{1,0:T(4,128)(2,1)S(1)}, u32[]{:S(2)}) copy-start(bf16[4,3072]{1,0:T(4,128)(2,1)S(1)} %slice.244) | copy-start | bytes 73732
  142.9 2.8 copy-start.10
  143.8 11.3 %copy-start.3 = (bf16[32,32,128]{2,1,0:T(8,128)(2,1)S(1)}, bf16[32,32,128]{2,1,0:T(8,128)(2,1)}, u32[]{:S(2)}) copy-start(bf16[32,32,128]{2,1,0:T(8,128)(2,1)} %copy-done.2) | copy-start | bytes 786436
  144.2 11.6 %copy-start.9 = (bf16[4,3072]{1,0:T(4,128)(2,1)S(1)}, bf16[4,3072]{1,0:T(4,128)(2,1)}, u32[]{:S(2)}) copy-start(bf16[4,3072]{1,0:T(4,128)(2,1)} %copy-done.8) | copy-start | bytes 73732
  150.5 22.4 %all-to-all-start.2 = ((bf16[32,60,128]{2,1,0:T(8,128)(2,1)}), bf16[32,60,128]{2,1,0:T(8,128)(2,1)S(1)}, u32[]{:S(2)}, u32[]{:S(2)}) async-start(bf16[32,60,128]{2,1,0:T(8,128)(2,1)} %pad.10.clone), calls=%async_computation.2 | async-start | bytes 1048576 | tf_op jit(solution)/shard_map/all_to_all | solution.py:128
  154.4 153.1 %all-gather.6.cloned.1.call-start = ((), (), s32[]{:S(2)}) async-start(), calls=%async_computation.8 | async-start | bytes 5947392 | tf_op jit(solution)/shard_map/all_gather | solution.py:201
  173.5 2.3 copy-start.11
  177.6 41.5 %copy-start.5 = (bf16[1,3072,96]{1,2,0:T(8,128)(2,1)S(1)}, bf16[1,3072,96]{1,2,0:T(8,128)(2,1)}, u32[]{:S(2)}) copy-start(bf16[1,3072,96]{1,2,0:T(8,128)(2,1)} %param.28) | copy-start | bytes 1769476
  178.7 54.2 %copy-start.15 = (f32[1,1,3072]{2,1,0:T(1,128)S(1)}, f32[1,1,3072]{2,1,0:T(1,128)}, u32[]{:S(2)}) copy-start(f32[1,1,3072]{2,1,0:T(1,128)} %get-tuple-element.33) | copy-start | bytes 36868
  178.7 54.6 %copy-start.13 = (f32[1,1,3072]{2,1,0:T(1,128)S(1)}, f32[1,1,3072]{2,1,0:T(1,128)}, u32[]{:S(2)}) copy-start(f32[1,1,3072]{2,1,0:T(1,128)} %get-tuple-element.29) | copy-start | bytes 36868
  178.8 54.6 %copy-start.14 = (f32[1,1,3072]{2,1,0:T(1,128)S(1)}, f32[1,1,3072]{2,1,0:T(1,128)}, u32[]{:S(2)}) copy-start(f32[1,1,3072]{2,1,0:T(1,128)} %get-tuple-element.30) | copy-start | bytes 36868
  270.0 9.9 %copy-start.18 = (bf16[4,6144]{1,0:T(4,128)(2,1)S(1)}, bf16[4,6144]{1,0:T(4,128)(2,1)}, u32[]{:S(2)}) copy-start(bf16[4,6144]{1,0:T(4,128)(2,1)} %param.33) | copy-start | bytes 147460
  270.0 31.7 %copy-start.12 = (f32[1,1,3072]{2,1,0:T(1,128)S(1)}, f32[1,1,3072]{2,1,0:T(1,128)}, u32[]{:S(2)}) copy-start(f32[1,1,3072]{2,1,0:T(1,128)} %get-tuple-element.28) | copy-start | bytes 36868
  272.4 29.0 %all-to-all-start.6 = ((bf16[32,4,3072]{2,1,0:T(4,128)(2,1)}), bf16[32,4,3072]{2,1,0:T(4,128)(2,1)S(1)}, u32[]{:S(2)}, u32[]{:S(2)}) async-start(bf16[32,4,3072]{2,1,0:T(4,128)(2,1)} %reshape.407), calls=%async_computation.6 | async-start | bytes 1572864 | tf_op jit(solution)/shard_map/all_to_all | solution.py:238
  301.7 5.4 %collective-permute-start = (bf16[4,3072]{1,0:T(4,128)(2,1)S(1)}, bf16[4,3072]{1,0:T(4,128)(2,1)S(1)}, u32[]{:S(2)}, u32[]{:S(2)}) collective-permute-start(bf16[4,3072]{1,0:T(4,128)(2,1)S(1)} %add_convert_fusion), channel_id=1, source_target_pairs={{128,0},{0,128},{129,1},{1,129},{130,2},{2,130},{131,3},{3,131},{1... | collective-permute-start | bytes 73736 | tf_op jit(solution)/shard_map/ppermute | solution.py:20
  311.4 4.7 %copy-start.6 = (bf16[1,3072,96]{1,2,0:T(8,128)(2,1)S(1)}, bf16[1,3072,96]{1,2,0:T(8,128)(2,1)}, u32[]{:S(2)}) copy-start(bf16[1,3072,96]{1,2,0:T(8,128)(2,1)} %param.29) | copy-start | bytes 1769476
  316.1 7.2 %copy-start.21 = (bf16[3072,32]{0,1:T(8,128)(2,1)S(1)}, bf16[3072,32]{0,1:T(8,128)(2,1)}, u32[]{:S(2)}) copy-start(bf16[3072,32]{0,1:T(8,128)(2,1)} %param.34) | copy-start | bytes 589828
  316.1 7.2 %copy-start.22 = (f32[1,4,32]{2,1,0:T(4,128)S(1)}, f32[1,4,32]{2,1,0:T(4,128)}, u32[]{:S(2)}) copy-start(f32[1,4,32]{2,1,0:T(4,128)} %param.35) | copy-start | bytes 1540
  319.5 14.3 %all-to-all-start.7 = ((bf16[32,16,96]{2,1,0:T(8,128)(2,1)}), bf16[32,16,96]{2,1,0:T(8,128)(2,1)S(1)}, u32[]{:S(2)}, u32[]{:S(2)}) async-start(bf16[32,16,96]{2,1,0:T(8,128)(2,1)} %bitcast.58), calls=%async_computation.7 | async-start | bytes 262144 | tf_op jit(solution)/shard_map/all_to_all | solution.py:64
  326.9 9.8 %copy-start.4 = (bf16[1,1,16,6144]{3,2,1,0:T(8,128)(2,1)S(1)}, bf16[1,1,16,6144]{3,2,1,0:T(8,128)(2,1)}, u32[]{:S(2)}) copy-start(bf16[1,1,16,6144]{3,2,1,0:T(8,128)(2,1)} %param.32) | copy-start | bytes 589828
  334.1 6.2 %collective-permute-start.1 = (bf16[16,3072]{1,0:T(8,128)(2,1)S(1)}, bf16[16,3072]{1,0:T(8,128)(2,1)S(1)}, u32[]{:S(2)}, u32[]{:S(2)}) collective-permute-start(bf16[16,3072]{1,0:T(8,128)(2,1)S(1)} %fusion.51), channel_id=1, source_target_pairs={{128,0},{0,128},{129,1},{1,129},{130,2},{2,130},{131,3},{3,131},{1... | collective-permute-start | bytes 294920 | tf_op jit(solution)/shard_map/ppermute | solution.py:20
Sparse Core Ops, SparseCore 0:
  33.1 65.9 all-gather.7
  178.6 86.1 all-gather.5

commit v8 on v7

--- a/solution.py
+++ b/solution.py
@@ -58,6 +58,16 @@
         preferred_element_type=jnp.float32,
     )
     return (mixed / total[..., None]).reshape(height, width).astype(jnp.bfloat16)
+
+
+def attend_columns(queries, keys, values, valid):
+    scores = jnp.dot(queries, keys.T, preferred_element_type=jnp.float32) * HDIM ** (-0.5)
+    scores = jnp.where(valid[None, :], scores, masked_score)
+    highest = jnp.max(scores, axis=-1, keepdims=True)
+    expo = jnp.where(valid[None, :], jnp.exp(scores - highest), 0.0)
+    total = jnp.sum(expo, axis=-1, keepdims=True)
+    mixed = jnp.dot(expo.astype(jnp.bfloat16), values, preferred_element_type=jnp.float32)
+    return mixed / total
 
 
 def cols_to_rows(cols):
@@ -119,15 +129,20 @@
     cache_rows = stale.shape[0]
     heads = width // HDIM
 
-    def by_head(pieces):
-        pack = jnp.concatenate(
-            [piece.reshape(piece.shape[0], heads, HDIM) for piece in pieces], axis=0
-        )
-        pack = jnp.transpose(pack, (1, 0, 2))
-        pack = jnp.pad(pack, ((0, devices - heads), (0, 0), (0, 0)))
+    span = width // devices
+    first = [span * t // HDIM for t in range(devices)]
+    second = [(span * t + span - 1) // HDIM for t in range(devices)]
+
+    def by_columns(head_pieces, column_pieces):
+        parts = []
+        for piece in head_pieces:
+            shaped = piece.reshape(piece.shape[0], heads, HDIM)
+            parts += [shaped[:, jnp.array(first)], shaped[:, jnp.array(second)]]
+        parts += [piece.reshape(piece.shape[0], devices, span) for piece in column_pieces]
+        pack = jnp.transpose(jnp.concatenate(parts, axis=-1), (1, 0, 2))
         return lax.all_to_all(pack, TOK, split_axis=0, concat_axis=0, tiled=True)
 
-    got_cache = by_head([stale[:, :width], stale[:, width:]])
+    got_cache = by_columns([stale[:, :width]], [stale[:, width:]])
     got_cache, image_normed, text_normed = lax.optimization_barrier(
         (got_cache, image_normed, text_normed)
     )
@@ -170,34 +185,44 @@
     row_q = jnp.concatenate([image_query, text_query], axis=0)
     row_k = jnp.concatenate([image_key, text_key], axis=0)
     row_v = jnp.concatenate([image_value, text_value], axis=0)
-    got = by_head([row_q, row_k, row_v])
-    rows = image_rows + text_rows
-
-    def part(first, count, source=got):
-        return source[:, first : first + count].reshape(-1, HDIM)
-
-    queries = jnp.concatenate([part(0, image_rows), part(image_rows, text_rows)], axis=0)
-    fresh_k = part(rows, image_rows)
-    text_k = part(rows + image_rows, text_rows)
-    fresh_v = part(2 * rows, image_rows)
-    text_v = part(2 * rows + image_rows, text_rows)
-    cache_k = part(0, cache_rows, got_cache)
-    cache_v = part(cache_rows, cache_rows, got_cache)
+    got = by_columns([row_q, row_k], [row_v])
+
+    def part(source, first_col, count, first_row, row_count):
+        block = source[:, first_row : first_row + row_count, first_col : first_col + count]
+        return block.reshape(-1, count)
+
+    def rows_of(first_col, count):
+        return (
+            part(got, first_col, count, 0, image_rows),
+            part(got, first_col, count, image_rows, text_rows),
+        )
+
     begin = patch * patch_len
-    cache_k = lax.dynamic_update_slice_in_dim(cache_k, fresh_k, begin, 0)
-    cache_v = lax.dynamic_update_slice_in_dim(cache_v, fresh_v, begin, 0)
-    keys = jnp.concatenate([cache_k, text_k], axis=0)
-    values = jnp.concatenate([cache_v, text_v], axis=0)
     text_count = text_length[0]
+    cache_len = cache_rows * devices
     valid = jnp.concatenate(
         [
-            jnp.ones((cache_k.shape[0],), bool),
-            jnp.arange(text_k.shape[0], dtype=jnp.int32) < text_count,
+            jnp.ones((cache_len,), bool),
+            jnp.arange(text_rows * devices, dtype=jnp.int32) < text_count,
         ]
     )
-    head_out = attend(queries, keys, values, valid)
-    image_heads = broadcast_rows(head_out[:patch_len], devices).reshape(devices, patch_len, HDIM)
-    riders = fresh_image.reshape(-1, HDIM)
+
+    def keys_of(first_col, count, cache_col):
+        fresh, text = rows_of(first_col, count)
+        cache = part(got_cache, cache_col, count, 0, cache_rows)
+        cache = lax.dynamic_update_slice_in_dim(cache, fresh, begin, 0)
+        return jnp.concatenate([cache, text], axis=0)
+
+    values = keys_of(4 * HDIM, span, 2 * HDIM)
+    mixed = []
+    for which in range(2):
+        queries = jnp.concatenate(rows_of(which * HDIM, HDIM), axis=0)
+        keys = keys_of(2 * HDIM + which * HDIM, HDIM, which * HDIM)
+        mixed.append(attend_columns(queries, keys, values, valid))
+    split = jnp.minimum(span, HDIM * (span * position // HDIM + 1) - span * position)
+    head_out = jnp.where(jnp.arange(span) < split, mixed[0], mixed[1]).astype(jnp.bfloat16)
+    image_heads = broadcast_rows(head_out[:patch_len], devices).reshape(devices, patch_len, span)
+    riders = fresh_image.reshape(-1, span)
     text_heads = lax.all_gather(
         jnp.concatenate([head_out[patch_len:], riders], axis=0), TOK, axis=0, tiled=False
     )
@@ -208,8 +233,8 @@
         fresh_all, (position % per_patch) * cache_rows, cache_rows, 0
     )
     current = jnp.where(position // per_patch == patch, moved, stale)
-    image_att = jnp.transpose(image_heads[:heads], (1, 0, 2)).reshape(-1, width)
-    text_att = jnp.transpose(text_heads[:heads], (1, 0, 2)).reshape(-1, width)
+    image_att = jnp.transpose(image_heads, (1, 0, 2)).reshape(-1, width)
+    text_att = jnp.transpose(text_heads, (1, 0, 2)).reshape(-1, width)
     image_back = cols_to_rows(
         jnp.dot(image_att, image_from_heads[0], preferred_element_type=jnp.float32)
         .astype(jnp.bfloat16)

time: 350 us -> 359 us (1.026)
  local copies, waits for them, and re-layouts: 46.9 us -> 59.6 us
  blocking collectives: 84.5 us -> 76.2 us
    unnamed x64, local copies, waits for them, and re-layouts: 7.04 us -> 19.7 us
    transpose x2 -> x0, local copies, waits for them, and re-layouts: 8.64 us -> none  [shards(): text_att = jnp.transpose(text_heads[:heads], (1, 0, 2)).reshape(-1, width)]
    all_to_all x2, waiting for transfers between devices: 19.8 us -> 27.3 us  [by_columns(): return lax.all_to_all(pack, TOK, split_axis=0, concat_axis=0, tiled=True)]
    all_to_all x2, blocking collectives: 71.3 us -> 63.9 us  [broadcast_rows(): got = lax.all_to_all(copies, TOK, split_axis=0, concat_axis=0, tiled=True)]
    gather x0 -> x6, local copies, waits for them, and re-layouts: none -> 6.23 us  [by_columns(): parts += [shaped[:, jnp.array(first)], shaped[:, jnp.array(second)]]]
  transfers between devices with their start and end apart: 9 -> 9, of which waited for: 8 -> 7; matrix products, arithmetic and copies ran while one was open for 7% -> 10% of each run, Pallas kernels for 0% -> 0%
where the time goes in v8:
time: 359 us; the launch traced here: 356 us
  waiting for transfers between devices  135 us (38%)
  blocking collectives  76.2 us (21%)
  local copies, waits for them, and re-layouts  59.6 us (17%)
  starting transfers between devices  35.4 us (10%)
  between operations  24.3 us (7%)
  matrix products  13.3 us (4%)
  other arithmetic  12.2 us (3%)
    all_gather x1, waiting for transfers between devices, shards(): lax.all_gather(jnp.concatenate([image_normed, text_normed], axis=0), TOK,...  64 us
    all_to_all x2, blocking collectives, broadcast_rows(): got = lax.all_to_all(copies, TOK, split_axis=0, concat_axis=0, tiled=True)  63.9 us
    all_to_all x2, waiting for transfers between devices, by_columns(): return lax.all_to_all(pack, TOK, split_axis=0, concat_axis=0, tiled=True)  27.3 us
    all_to_all x1, waiting for transfers between devices, shards(): lax.all_to_all(partial.astype(jnp.bfloat16).reshape(devices, image_rows,...  21.6 us
    unnamed x64, local copies, waits for them, and re-layouts  19.7 us
    all_to_all x2, waiting for transfers between devices, cols_to_rows(): got = lax.all_to_all(cols, TOK, split_axis=0, concat_axis=0, tiled=True)  18.3 us
    all_to_all x2, starting transfers between devices, by_columns(): return lax.all_to_all(pack, TOK, split_axis=0, concat_axis=0, tiled=True)  13.8 us
    all_to_all x1, blocking collectives, cols_to_rows(): got = lax.all_to_all(cols, TOK, split_axis=0, concat_axis=0, tiled=True)  12.4 us
  transfers between devices with their start and end apart: 9, of which 7 were waited for; matrix products, arithmetic and copies ran while one was open for 10% of the time, Pallas kernels for 0%

profile of v8, /device:TPU:2, one launch (start us, length us, event | category | flops | bytes accessed | tf_op | source)
XLA Modules:
  0.0 356.2 jit_solution(8156413456399321336)
XLA Ops:
  11.3 9.9 %all-to-all-start = ((bf16[32,16,352]{2,1,0:T(8,128)(2,1)}), bf16[32,16,352]{2,1,0:T(8,128)(2,1)S(1)}, u32[]{:S(2)}, u32[]{:S(2)}) async-start(bf16[32,16,352]{2,1,0:T(8,128)(2,1)} %maximum_bitcast_fusion), calls=%async_computation | async-start | bytes 786432 | tf_op jit(solution)/shard_map/all_to_all | solution.py:143
  30.6 6.5 %all-to-all-done = bf16[32,16,352]{2,1,0:T(8,128)(2,1)S(1)} async-done(((bf16[32,16,352]{2,1,0:T(8,128)(2,1)}), bf16[32,16,352]{2,1,0:T(8,128)(2,1)S(1)}, u32[]{:S(2)}, u32[]{:S(2)}) %all-to-all-start) | async-done | bytes 360480 | tf_op jit(solution)/shard_map/all_to_all | solution.py:143
  37.9 64.0 %all-gather.8.cloned.1.call-done = bf16[32,20,3072]{2,1,0:T(8,128)(2,1)} async-done(((bf16[1,20,3072]{2,1,0:T(8,128)(2,1)}), bf16[32,20,3072]{2,1,0:T(8,128)(2,1)}) %all-gather.8.cloned.1.call-update) | async-done | bytes 3932176 | tf_op jit(solution)/shard_map/all_gather | solution.py:149
  101.9 1.6 slice.254
  104.6 2.3 fusion.22
  107.2 3.8 %slice.255 = bf16[32,16,3072]{2,1,0:T(8,128)(2,1)S(1)} slice(bf16[32,20,3072]{2,1,0:T(8,128)(2,1)} %all-gather.8.cloned.1.call-done), slice={[0:32], [4:20], [0:3072]} | slice | bytes 6291456 | tf_op jit(solution)/shard_map/slice | solution.py:156
  113.4 6.2 %all-to-all-start.1 = ((bf16[32,20,288]{2,1,0:T(8,128)(2,1)}), bf16[32,20,288]{2,1,0:T(8,128)(2,1)S(1)}, u32[]{:S(2)}, u32[]{:S(2)}) async-start(bf16[32,20,288]{2,1,0:T(8,128)(2,1)} %pad_maximum_fusion), calls=%async_computation.1 | async-start | bytes 1179648 | tf_op jit(solution)/shard_map/all_to_all | solution.py:74
  120.8 18.3 %all-to-all-done.1 = bf16[32,20,288]{2,1,0:T(8,128)(2,1)S(1)} async-done(((bf16[32,20,288]{2,1,0:T(8,128)(2,1)}), bf16[32,20,288]{2,1,0:T(8,128)(2,1)S(1)}, u32[]{:S(2)}, u32[]{:S(2)}) %all-to-all-start.1) | async-done | bytes 368672 | tf_op jit(solution)/shard_map/all_to_all | solution.py:74
  156.6 3.9 %all-to-all-start.2 = ((bf16[32,20,608]{2,1,0:T(8,128)(2,1)}), bf16[32,20,608]{2,1,0:T(8,128)(2,1)S(1)}, u32[]{:S(2)}, u32[]{:S(2)}) async-start(bf16[32,20,608]{2,1,0:T(8,128)(2,1)} %bitcast.225), calls=%async_computation.2 | async-start | bytes 1966080 | tf_op jit(solution)/shard_map/all_to_all | solution.py:143
  162.0 1.7 fusion.134
  164.4 1.5 reshape.399
  166.8 20.8 %all-to-all-done.2 = bf16[32,20,608]{2,1,0:T(8,128)(2,1)S(1)} async-done(((bf16[32,20,608]{2,1,0:T(8,128)(2,1)}), bf16[32,20,608]{2,1,0:T(8,128)(2,1)S(1)}, u32[]{:S(2)}, u32[]{:S(2)}) %all-to-all-start.2) | async-done | bytes 778272 | tf_op jit(solution)/shard_map/all_to_all | solution.py:143
  195.3 32.5 %all_to_all.40 = bf16[32,128,96]{1,2,0:T(8,128)(2,1)S(1)} all-to-all(bf16[32,128,96]{1,2,0:T(8,128)(2,1)S(1)} %broadcast_in_dim.107), channel_id=1, replica_groups=mesh['section'=2,'grp'=4,'ta'=8,'tb'=4] {'ta','tb'}, dimensions={0} | all-to-all | bytes 1572864 | tf_op jit(solution)/shard_map/all_to_all | solution.py:81
  228.2 12.4 %all_to_all.41 = bf16[32,4,96]{2,1,0:T(4,128)(2,1)S(1)} all-to-all(bf16[32,4,96]{2,1,0:T(4,128)(2,1)S(1)} %bitcast.238), channel_id=1, replica_groups=mesh['section'=2,'grp'=4,'ta'=8,'tb'=4] {'ta','tb'}, dimensions={0} | all-to-all | bytes 49152 | tf_op jit(solution)/shard_map/all_to_all | solution.py:74
  241.4 31.4 %all_to_all.42 = bf16[32,4,3072]{2,1,0:T(4,128)(2,1)} all-to-all(bf16[32,4,3072]{2,1,0:T(4,128)(2,1)S(1)} %broadcast_in_dim.108), channel_id=1, replica_groups=mesh['section'=2,'grp'=4,'ta'=8,'tb'=4] {'ta','tb'}, dimensions={0} | all-to-all | bytes 1572864 | tf_op jit(solution)/shard_map/all_to_all | solution.py:81
  272.8 1.6 reshape.397
  274.4 3.7 %convolution_convert_fusion = bf16[128,3072]{1,0:T(8,128)(2,1)} fusion(bf16[1,384,3072]{2,1,0:T(8,128)(2,1)S(1)} %copy-done, bf16[128,3072]{1,0:T(8,128)(2,1)S(1)} %reshape.397, bf16[1,3072,384]{2,1,0:T(8,128)(2,1)} %param.36), kind=kOutput, calls=%fused_computation.6 | convolution fusion | flops 604815360 | bytes 6291456 | tf_op jit(solution)/shard_map/dot_general | solution.py:261
  278.1 2.4 reshape.398
  280.5 5.3 %all-to-all-start.6 = ((bf16[32,4,3072]{2,1,0:T(4,128)(2,1)}), bf16[32,4,3072]{2,1,0:T(4,128)(2,1)S(1)}, u32[]{:S(2)}, u32[]{:S(2)}) async-start(bf16[32,4,3072]{2,1,0:T(4,128)(2,1)} %reshape.398), calls=%async_computation.6 | async-start | bytes 1572864 | tf_op jit(solution)/shard_map/all_to_all | solution.py:263
  287.6 21.6 %all-to-all-done.6 = bf16[32,4,3072]{2,1,0:T(4,128)(2,1)S(1)} async-done(((bf16[32,4,3072]{2,1,0:T(4,128)(2,1)}), bf16[32,4,3072]{2,1,0:T(4,128)(2,1)S(1)}, u32[]{:S(2)}, u32[]{:S(2)}) %all-to-all-start.6) | async-done | bytes 786464 | tf_op jit(solution)/shard_map/all_to_all | solution.py:263
  309.5 3.1 collective-permute-start
  313.3 1.9 collective-permute-done
  315.5 3.6 %copy.88 = bf16[12,8,32,768]{3,2,1,0:T(8,128)(2,1)S(1)} copy(bf16[12,8,32,768]{3,1,2,0:T(8,128)(2,1)} %bitcast.218) | data formatting | bytes 9437184
  319.5 1.8 copy-done.1
  321.3 1.7 copy.75
  324.5 3.9 %all-to-all-start.7 = ((bf16[32,16,96]{2,1,0:T(8,128)(2,1)}), bf16[32,16,96]{2,1,0:T(8,128)(2,1)S(1)}, u32[]{:S(2)}, u32[]{:S(2)}) async-start(bf16[32,16,96]{2,1,0:T(8,128)(2,1)} %bitcast.63), calls=%async_computation.7 | async-start | bytes 262144 | tf_op jit(solution)/shard_map/all_to_all | solution.py:74
  329.2 2.7 slice.281
  331.9 4.3 %copy.76 = bf16[32,256,96]{2,1,0:T(8,128)(2,1)} copy(bf16[32,256,96]{1,0,2:T(8,128)(2,1)} %slice.281) | data formatting | bytes 3145728
  336.2 5.1 %reshape.402 = bf16[128,6144]{1,0:T(8,128)(2,1)} reshape(bf16[32,256,96]{2,1,0:T(8,128)(2,1)} %copy.76) | data formatting | bytes 3145728 | tf_op jit(solution)/shard_map/reshape | solution.py:230
  341.6 2.9 collective-permute-start.1
  344.5 1.7 select_bitcast_fusion
  346.2 1.9 collective-permute-done.1
  (182 shorter events, 45.9 us)
Async XLA Ops:
  7.2 267.2 %copy-start = (bf16[1,384,3072]{2,1,0:T(8,128)(2,1)S(1)}, bf16[1,384,3072]{2,1,0:T(8,128)(2,1)}, u32[]{:S(2)}) copy-start(bf16[1,384,3072]{2,1,0:T(8,128)(2,1)} %param.37) | copy-start | bytes 7077892
  7.2 14.0 %copy-start.21 = (s32[1,4]{1,0:T(1,128)S(1)}, s32[1,4]{1,0:T(1,128)}, u32[]{:S(2)}) copy-start(s32[1,4]{1,0:T(1,128)} %param.27) | copy-start | bytes 52
  7.2 18.5 %copy-start.19 = (s32[1,4]{1,0:T(1,128)S(1)}, s32[1,4]{1,0:T(1,128)}, u32[]{:S(2)}) copy-start(s32[1,4]{1,0:T(1,128)} %param.28) | copy-start | bytes 52
  7.2 20.4 %copy-start.9 = (bf16[1,1,4,3072]{3,2,1,0:T(4,128)(2,1)S(1)}, bf16[1,1,4,3072]{3,2,1,0:T(4,128)(2,1)}, u32[]{:S(2)}) copy-start(bf16[1,1,4,3072]{3,2,1,0:T(4,128)(2,1)} %param.24) | copy-start | bytes 73732
  7.2 20.7 %copy-start.3 = (bf16[1,1,16,3072]{3,2,1,0:T(8,128)(2,1)S(1)}, bf16[1,1,16,3072]{3,2,1,0:T(8,128)(2,1)}, u32[]{:S(2)}) copy-start(bf16[1,1,16,3072]{3,2,1,0:T(8,128)(2,1)} %param.25) | copy-start | bytes 294916
  7.2 21.8 %copy-start.17 = (bf16[1,4,9216]{2,1,0:T(4,128)(2,1)S(1)}, bf16[1,4,9216]{2,1,0:T(4,128)(2,1)}, u32[]{:S(2)}) copy-start(bf16[1,4,9216]{2,1,0:T(4,128)(2,1)} %param.30) | copy-start | bytes 221188
  7.2 22.4 %copy-start.16 = (bf16[1,4,18432]{2,1,0:T(4,128)(2,1)S(1)}, bf16[1,4,18432]{2,1,0:T(4,128)(2,1)}, u32[]{:S(2)}) copy-start(bf16[1,4,18432]{2,1,0:T(4,128)(2,1)} %param.29) | copy-start | bytes 442372
  11.3 25.8 %all-to-all-start = ((bf16[32,16,352]{2,1,0:T(8,128)(2,1)}), bf16[32,16,352]{2,1,0:T(8,128)(2,1)S(1)}, u32[]{:S(2)}, u32[]{:S(2)}) async-start(bf16[32,16,352]{2,1,0:T(8,128)(2,1)} %maximum_bitcast_fusion), calls=%async_computation | async-start | bytes 786432 | tf_op jit(solution)/shard_map/all_to_all | solution.py:143
  21.2 80.8 %all-gather.8.cloned.1.call-start = ((), (), s32[]{:S(2)}) async-start(), calls=%async_computation.9 | async-start | bytes 4866048 | tf_op jit(solution)/shard_map/all_gather | solution.py:149
  107.2 3.8 %copy-start.22 = (bf16[1,3072,288]{1,2,0:T(8,128)(2,1)S(1)}, bf16[1,3072,288]{1,2,0:T(8,128)(2,1)}, u32[]{:S(2)}) copy-start(bf16[1,3072,288]{1,2,0:T(8,128)(2,1)} %param.32) | copy-start | bytes 5308420
  112.1 7.5 %copy-start.20 = (f32[1,4,128]{2,1,0:T(4,128)S(1)}, f32[1,4,128]{2,1,0:T(4,128)}, u32[]{:S(2)}) copy-start(f32[1,4,128]{2,1,0:T(4,128)} %param.33) | copy-start | bytes 6148
  113.4 25.8 %all-to-all-start.1 = ((bf16[32,20,288]{2,1,0:T(8,128)(2,1)}), bf16[32,20,288]{2,1,0:T(8,128)(2,1)S(1)}, u32[]{:S(2)}, u32[]{:S(2)}) async-start(bf16[32,20,288]{2,1,0:T(8,128)(2,1)} %pad_maximum_fusion), calls=%async_computation.1 | async-start | bytes 1179648 | tf_op jit(solution)/shard_map/all_to_all | solution.py:74
  150.6 37.1 %slice-start = ((bf16[32,16,352]{2,1,0:T(8,128)(2,1)}), bf16[32,16,96]{2,1,0:T(8,128)(2,1)S(1)}, s32[]{:S(2)}) async-start(bf16[32,16,352]{2,1,0:T(8,128)(2,1)} %copy-done.2), calls=%async_computation.10 | async-start | bytes 262144 | tf_op jit(solution)/shard_map/slice | solution.py:191
  156.6 31.1 %all-to-all-start.2 = ((bf16[32,20,608]{2,1,0:T(8,128)(2,1)}), bf16[32,20,608]{2,1,0:T(8,128)(2,1)S(1)}, u32[]{:S(2)}, u32[]{:S(2)}) async-start(bf16[32,20,608]{2,1,0:T(8,128)(2,1)} %bitcast.225), calls=%async_computation.2 | async-start | bytes 1966080 | tf_op jit(solution)/shard_map/all_to_all | solution.py:143
  160.5 155.0 %all-gather.6.cloned.1.call-start = ((), (), s32[]{:S(2)}) async-start(), calls=%async_computation.8 | async-start | bytes 4866048 | tf_op jit(solution)/shard_map/all_gather | solution.py:226
  194.4 33.4 %copy-start.7 = (bf16[1,3072,96]{1,2,0:T(8,128)(2,1)S(1)}, bf16[1,3072,96]{1,2,0:T(8,128)(2,1)}, u32[]{:S(2)}) copy-start(bf16[1,3072,96]{1,2,0:T(8,128)(2,1)} %param.34) | copy-start | bytes 1769476
  194.4 46.3 %copy-start.15 = (f32[1,1,3072]{2,1,0:T(1,128)S(1)}, f32[1,1,3072]{2,1,0:T(1,128)}, u32[]{:S(2)}) copy-start(f32[1,1,3072]{2,1,0:T(1,128)} %get-tuple-element.37) | copy-start | bytes 36868
  194.4 46.7 %copy-start.13 = (f32[1,1,3072]{2,1,0:T(1,128)S(1)}, f32[1,1,3072]{2,1,0:T(1,128)}, u32[]{:S(2)}) copy-start(f32[1,1,3072]{2,1,0:T(1,128)} %get-tuple-element.33) | copy-start | bytes 36868
  194.4 46.7 %copy-start.14 = (f32[1,1,3072]{2,1,0:T(1,128)S(1)}, f32[1,1,3072]{2,1,0:T(1,128)}, u32[]{:S(2)}) copy-start(f32[1,1,3072]{2,1,0:T(1,128)} %get-tuple-element.34) | copy-start | bytes 36868
  278.1 9.5 %copy-start.18 = (bf16[4,6144]{1,0:T(4,128)(2,1)S(1)}, bf16[4,6144]{1,0:T(4,128)(2,1)}, u32[]{:S(2)}) copy-start(bf16[4,6144]{1,0:T(4,128)(2,1)} %param.39) | copy-start | bytes 147460
  278.1 31.4 %copy-start.12 = (f32[1,1,3072]{2,1,0:T(1,128)S(1)}, f32[1,1,3072]{2,1,0:T(1,128)}, u32[]{:S(2)}) copy-start(f32[1,1,3072]{2,1,0:T(1,128)} %get-tuple-element.32) | copy-start | bytes 36868
  280.5 28.7 %all-to-all-start.6 = ((bf16[32,4,3072]{2,1,0:T(4,128)(2,1)}), bf16[32,4,3072]{2,1,0:T(4,128)(2,1)S(1)}, u32[]{:S(2)}, u32[]{:S(2)}) async-start(bf16[32,4,3072]{2,1,0:T(4,128)(2,1)} %reshape.398), calls=%async_computation.6 | async-start | bytes 1572864 | tf_op jit(solution)/shard_map/all_to_all | solution.py:263
  309.5 5.6 %collective-permute-start = (bf16[4,3072]{1,0:T(4,128)(2,1)S(1)}, bf16[4,3072]{1,0:T(4,128)(2,1)S(1)}, u32[]{:S(2)}, u32[]{:S(2)}) collective-permute-start(bf16[4,3072]{1,0:T(4,128)(2,1)S(1)} %add_convert_fusion), channel_id=1, source_target_pairs={{128,0},{0,128},{129,1},{1,129},{130,2},{2,130},{131,3},{3,131},{1... | collective-permute-start | bytes 73736 | tf_op jit(solution)/shard_map/ppermute | solution.py:20
  319.2 2.1 copy-start.1
  321.3 1.8 copy-start.8
  323.1 5.3 %copy-start.23 = (bf16[3072,32]{0,1:T(8,128)(2,1)S(1)}, bf16[3072,32]{0,1:T(8,128)(2,1)}, u32[]{:S(2)}) copy-start(bf16[3072,32]{0,1:T(8,128)(2,1)} %param.40) | copy-start | bytes 589828
  323.1 5.3 %copy-start.24 = (f32[1,4,32]{2,1,0:T(4,128)S(1)}, f32[1,4,32]{2,1,0:T(4,128)}, u32[]{:S(2)}) copy-start(f32[1,4,32]{2,1,0:T(4,128)} %param.41) | copy-start | bytes 1540
  324.5 16.8 %all-to-all-start.7 = ((bf16[32,16,96]{2,1,0:T(8,128)(2,1)}), bf16[32,16,96]{2,1,0:T(8,128)(2,1)S(1)}, u32[]{:S(2)}, u32[]{:S(2)}) async-start(bf16[32,16,96]{2,1,0:T(8,128)(2,1)} %bitcast.63), calls=%async_computation.7 | async-start | bytes 262144 | tf_op jit(solution)/shard_map/all_to_all | solution.py:74
  336.2 5.4 %copy-start.4 = (bf16[1,1,16,3072]{3,2,1,0:T(8,128)(2,1)S(1)}, bf16[1,1,16,3072]{3,2,1,0:T(8,128)(2,1)}, u32[]{:S(2)}) copy-start(bf16[1,1,16,3072]{3,2,1,0:T(8,128)(2,1)} %param.25) | copy-start | bytes 294916
  336.2 5.4 %copy-start.11 = (f32[1,1,3072]{2,1,0:T(1,128)S(1)}, f32[1,1,3072]{2,1,0:T(1,128)}, u32[]{:S(2)}) copy-start(f32[1,1,3072]{2,1,0:T(1,128)} %get-tuple-element.42) | copy-start | bytes 36868
  336.2 8.3 %copy-start.6 = (bf16[1,1,16,6144]{3,2,1,0:T(8,128)(2,1)S(1)}, bf16[1,1,16,6144]{3,2,1,0:T(8,128)(2,1)}, u32[]{:S(2)}) copy-start(bf16[1,1,16,6144]{3,2,1,0:T(8,128)(2,1)} %param.38) | copy-start | bytes 589828
  341.6 6.5 %collective-permute-start.1 = (bf16[16,3072]{1,0:T(8,128)(2,1)S(1)}, bf16[16,3072]{1,0:T(8,128)(2,1)S(1)}, u32[]{:S(2)}, u32[]{:S(2)}) collective-permute-start(bf16[16,3072]{1,0:T(8,128)(2,1)S(1)} %fusion.57), channel_id=1, source_target_pairs={{128,0},{0,128},{129,1},{1,129},{130,2},{2,130},{131,3},{3,131},{1... | collective-permute-start | bytes 294920 | tf_op jit(solution)/shard_map/ppermute | solution.py:20
  (3 other events, 3.5 us)
Sparse Core Ops, SparseCore 0:
  38.0 63.8 all-gather.7
  195.3 78.9 all-gather.5

commit v9 on v7

--- a/solution.py
+++ b/solution.py
@@ -234,6 +234,7 @@
         approximate=True,
     ).astype(jnp.bfloat16)
     partial = jnp.dot(hidden, down_weight, preferred_element_type=jnp.float32)
+    partial, text_back = lax.optimization_barrier((partial, text_back))
     reduced = jnp.sum(
         lax.all_to_all(
             partial.astype(jnp.bfloat16).reshape(devices, image_rows, width),

time: 350 us -> 345 us (0.986)
  blocking collectives: 84.5 us -> 53.5 us
  waiting for transfers between devices: 132 us -> 148 us
  starting transfers between devices: 34.8 us -> 38.8 us
    all_to_all x2 -> x1, blocking collectives: 71.3 us -> 40.3 us  [broadcast_rows(): got = lax.all_to_all(copies, TOK, split_axis=0, concat_axis=0, tiled=True)]
    all_to_all x0 -> x1, waiting for transfers between devices: none -> 25.4 us  [broadcast_rows(): got = lax.all_to_all(copies, TOK, split_axis=0, concat_axis=0, tiled=True)]
    all_to_all x1, waiting for transfers between devices: 21.4 us -> 11.9 us  [shards(): lax.all_to_all(partial.astype(jnp.bfloat16).reshape(devices, image_rows,...]
    all_to_all x0 -> x1, starting transfers between devices: none -> 4.63 us  [broadcast_rows(): got = lax.all_to_all(copies, TOK, split_axis=0, concat_axis=0, tiled=True)]
    unnamed x64 -> x58, local copies, waits for them, and re-layouts: 7.04 us -> 7.68 us
  transfers between devices with their start and end apart: 9 -> 10, of which waited for: 8 -> 8; matrix products, arithmetic and copies ran while one was open for 7% -> 7% of each run, Pallas kernels for 0% -> 0%
where the time goes in v9:
time: 345 us; the launch traced here: 343 us
  waiting for transfers between devices  148 us (43%)
  blocking collectives  53.5 us (16%)
  local copies, waits for them, and re-layouts  49.3 us (14%)
  starting transfers between devices  38.8 us (11%)
  between operations  24.8 us (7%)
  matrix products  15.2 us (4%)
  other arithmetic  12.8 us (4%)
    all_gather x1, waiting for transfers between devices, shards(): lax.all_gather(jnp.concatenate([image_normed, text_normed], axis=0), TOK,...  66.3 us
    all_to_all x1, blocking collectives, broadcast_rows(): got = lax.all_to_all(copies, TOK, split_axis=0, concat_axis=0, tiled=True)  40.3 us
    all_to_all x1, waiting for transfers between devices, broadcast_rows(): got = lax.all_to_all(copies, TOK, split_axis=0, concat_axis=0, tiled=True)  25.4 us
    all_to_all x2, waiting for transfers between devices, cols_to_rows(): got = lax.all_to_all(cols, TOK, split_axis=0, concat_axis=0, tiled=True)  24.4 us
    all_to_all x2, waiting for transfers between devices, by_head(): return lax.all_to_all(pack, TOK, split_axis=0, concat_axis=0, tiled=True)  19.5 us
    all_to_all x2, starting transfers between devices, by_head(): return lax.all_to_all(pack, TOK, split_axis=0, concat_axis=0, tiled=True)  13.8 us
    all_to_all x1, blocking collectives, cols_to_rows(): got = lax.all_to_all(cols, TOK, split_axis=0, concat_axis=0, tiled=True)  13.2 us
    all_to_all x1, waiting for transfers between devices, shards(): lax.all_to_all(partial.astype(jnp.bfloat16).reshape(devices, image_rows,...  11.9 us
  transfers between devices with their start and end apart: 10, of which 8 were waited for; matrix products, arithmetic and copies ran while one was open for 7% of the time, Pallas kernels for 0%

profile of v9, /device:TPU:2, one launch (start us, length us, event | category | flops | bytes accessed | tf_op | source)
XLA Modules:
  0.0 342.6 jit_solution(7488993244899926928)
XLA Ops:
  9.2 9.9 %all-to-all-start = ((bf16[32,32,128]{2,1,0:T(8,128)(2,1)}), bf16[32,32,128]{2,1,0:T(8,128)(2,1)S(1)}, u32[]{:S(2)}, u32[]{:S(2)}) async-start(bf16[32,32,128]{2,1,0:T(8,128)(2,1)} %pad.9.clone), calls=%async_computation | async-start | bytes 524288 | tf_op jit(solution)/shard_map/all_to_all | solution.py:128
  29.5 2.7 all-to-all-done
  33.0 66.3 %all-gather.8.cloned.1.call-done = bf16[32,20,3072]{2,1,0:T(8,128)(2,1)} async-done(((bf16[1,20,3072]{2,1,0:T(8,128)(2,1)}), bf16[32,20,3072]{2,1,0:T(8,128)(2,1)}) %all-gather.8.cloned.1.call-update) | async-done | bytes 3932176 | tf_op jit(solution)/shard_map/all_gather | solution.py:134
  99.3 1.6 slice.236
  102.0 2.3 fusion.21
  104.5 3.8 %slice.237 = bf16[32,16,3072]{2,1,0:T(8,128)(2,1)S(1)} slice(bf16[32,20,3072]{2,1,0:T(8,128)(2,1)} %all-gather.8.cloned.1.call-done), slice={[0:32], [4:20], [0:3072]} | slice | bytes 6291456 | tf_op jit(solution)/shard_map/slice | solution.py:141
  110.7 6.2 %all-to-all-start.1 = ((bf16[32,20,288]{2,1,0:T(8,128)(2,1)}), bf16[32,20,288]{2,1,0:T(8,128)(2,1)S(1)}, u32[]{:S(2)}, u32[]{:S(2)}) async-start(bf16[32,20,288]{2,1,0:T(8,128)(2,1)} %pad_maximum_fusion), calls=%async_computation.1 | async-start | bytes 1179648 | tf_op jit(solution)/shard_map/all_to_all | solution.py:64
  118.9 17.6 %all-to-all-done.1 = bf16[32,20,288]{2,1,0:T(8,128)(2,1)S(1)} async-done(((bf16[32,20,288]{2,1,0:T(8,128)(2,1)}), bf16[32,20,288]{2,1,0:T(8,128)(2,1)S(1)}, u32[]{:S(2)}, u32[]{:S(2)}) %all-to-all-start.1) | async-done | bytes 368672 | tf_op jit(solution)/shard_map/all_to_all | solution.py:64
  147.2 1.6 slice_dynamic-update-slice_fusion
  150.7 3.9 %all-to-all-start.2 = ((bf16[32,60,128]{2,1,0:T(8,128)(2,1)}), bf16[32,60,128]{2,1,0:T(8,128)(2,1)S(1)}, u32[]{:S(2)}, u32[]{:S(2)}) async-start(bf16[32,60,128]{2,1,0:T(8,128)(2,1)} %pad.10.clone), calls=%async_computation.2 | async-start | bytes 1048576 | tf_op jit(solution)/shard_map/all_to_all | solution.py:128
  156.2 16.8 %all-to-all-done.2 = bf16[32,60,128]{2,1,0:T(8,128)(2,1)S(1)} async-done(((bf16[32,60,128]{2,1,0:T(8,128)(2,1)}), bf16[32,60,128]{2,1,0:T(8,128)(2,1)S(1)}, u32[]{:S(2)}, u32[]{:S(2)}) %all-to-all-start.2) | async-done | bytes 491552 | tf_op jit(solution)/shard_map/all_to_all | solution.py:128
  176.0 1.8 fusion.32
  179.0 40.3 %all_to_all.40 = bf16[32,128,128]{1,2,0:T(8,128)(2,1)S(1)} all-to-all(bf16[32,128,128]{1,2,0:T(8,128)(2,1)S(1)} %broadcast_in_dim.36), channel_id=1, replica_groups=mesh['section'=2,'grp'=4,'ta'=8,'tb'=4] {'ta','tb'}, dimensions={0} | all-to-all | bytes 2097152 | tf_op jit(solution)/shard_map/all_to_all | solution.py:71
  219.7 13.2 %all_to_all.41 = bf16[32,4,96]{2,1,0:T(4,128)(2,1)S(1)} all-to-all(bf16[32,4,96]{2,1,0:T(4,128)(2,1)S(1)} %bitcast.270), channel_id=1, replica_groups=mesh['section'=2,'grp'=4,'ta'=8,'tb'=4] {'ta','tb'}, dimensions={0} | all-to-all | bytes 49152 | tf_op jit(solution)/shard_map/all_to_all | solution.py:64
  234.7 4.6 %all-to-all-start.5 = ((bf16[32,4,3072]{2,1,0:T(4,128)(2,1)}), bf16[32,4,3072]{2,1,0:T(4,128)(2,1)}, u32[]{:S(2)}, u32[]{:S(2)}) async-start(bf16[32,4,3072]{2,1,0:T(4,128)(2,1)} %broadcast_in_dim.37), calls=%async_computation.5 | async-start | bytes 1572864 | tf_op jit(solution)/shard_map/all_to_all | solution.py:71
  241.4 25.4 %all-to-all-done.5 = bf16[32,4,3072]{2,1,0:T(4,128)(2,1)} async-done(((bf16[32,4,3072]{2,1,0:T(4,128)(2,1)}), bf16[32,4,3072]{2,1,0:T(4,128)(2,1)}, u32[]{:S(2)}, u32[]{:S(2)}) %all-to-all-start.5) | async-done | bytes 786464 | tf_op jit(solution)/shard_map/all_to_all | solution.py:71
  266.8 1.6 reshape.406
  268.4 3.9 %slice_bitcast_fusion = bf16[512,24,128]{2,0,1:T(8,128)(2,1)} fusion(bf16[32,704,128]{2,1,0:T(8,128)(2,1)} %bitcast.249), kind=kLoop, calls=%fused_computation | loop fusion | bytes 6291456 | tf_op jit(solution)/shard_map/transpose | solution.py:212
  272.4 4.6 %copy.66 = bf16[512,24,128]{0,2,1:T(8,128)(2,1)} copy(bf16[512,24,128]{2,0,1:T(8,128)(2,1)} %slice_bitcast_fusion) | data formatting | bytes 6291456 | tf_op jit(solution)/shard_map/transpose | solution.py:212
  277.0 2.7 convolution_convert_fusion
  280.5 4.3 %all-to-all-start.6 = ((bf16[32,16,96]{2,1,0:T(8,128)(2,1)}), bf16[32,16,96]{2,1,0:T(8,128)(2,1)S(1)}, u32[]{:S(2)}, u32[]{:S(2)}) async-start(bf16[32,16,96]{2,1,0:T(8,128)(2,1)} %bitcast.56), calls=%async_computation.6 | async-start | bytes 262144 | tf_op jit(solution)/shard_map/all_to_all | solution.py:64
  284.8 3.7 %fusion = bf16[128,3072]{1,0:T(8,128)(2,1)} fusion(bf16[1,384,3072]{2,1,0:T(8,128)(2,1)S(1)} %copy-done, bf16[128,3072]{1,0:T(8,128)(2,1)S(1)} %reshape.406, bf16[1,3072,384]{2,1,0:T(8,128)(2,1)} %param.30), kind=kOutput, calls=%fused_computation.3 | convolution fusion | flops 604422144 | bytes 6291456 | tf_op jit(solution)/shard_map/dot_general | solution.py:236
  288.5 6.7 %all-to-all-done.6 = bf16[32,16,96]{2,1,0:T(8,128)(2,1)S(1)} async-done(((bf16[32,16,96]{2,1,0:T(8,128)(2,1)}), bf16[32,16,96]{2,1,0:T(8,128)(2,1)S(1)}, u32[]{:S(2)}, u32[]{:S(2)}) %all-to-all-start.6) | async-done | bytes 98336 | tf_op jit(solution)/shard_map/all_to_all | solution.py:64
  297.0 2.4 reshape.411
  299.4 3.9 %all-to-all-start.7 = ((bf16[32,4,3072]{2,1,0:T(4,128)(2,1)}), bf16[32,4,3072]{2,1,0:T(4,128)(2,1)S(1)}, u32[]{:S(2)}, u32[]{:S(2)}) async-start(bf16[32,4,3072]{2,1,0:T(4,128)(2,1)} %reshape.411), calls=%async_computation.7 | async-start | bytes 1572864 | tf_op jit(solution)/shard_map/all_to_all | solution.py:239
  304.9 2.7 slice.260
  307.6 3.6 %reshape.412 = bf16[128,6144]{1,0:T(8,128)(2,1)} reshape(bf16[32,192,128]{2,1,0:T(8,128)(2,1)} %slice.260) | data formatting | bytes 3145728 | tf_op jit(solution)/shard_map/reshape | solution.py:205
  311.8 2.9 collective-permute-start.1
  314.7 11.9 %all-to-all-done.7 = bf16[32,4,3072]{2,1,0:T(4,128)(2,1)S(1)} async-done(((bf16[32,4,3072]{2,1,0:T(4,128)(2,1)}), bf16[32,4,3072]{2,1,0:T(4,128)(2,1)S(1)}, u32[]{:S(2)}, u32[]{:S(2)}) %all-to-all-start.7) | async-done | bytes 786464 | tf_op jit(solution)/shard_map/all_to_all | solution.py:239
  327.0 3.0 collective-permute-start
  330.0 1.7 select_bitcast_fusion
  332.8 1.7 fusion.25
  (157 shorter events, 38.3 us)
Async XLA Ops:
  7.2 277.6 %copy-start = (bf16[1,384,3072]{2,1,0:T(8,128)(2,1)S(1)}, bf16[1,384,3072]{2,1,0:T(8,128)(2,1)}, u32[]{:S(2)}) copy-start(bf16[1,384,3072]{2,1,0:T(8,128)(2,1)} %param.31) | copy-start | bytes 7077892
  7.2 19.9 %copy-start.6 = (bf16[1,1,4,3072]{3,2,1,0:T(4,128)(2,1)S(1)}, bf16[1,1,4,3072]{3,2,1,0:T(4,128)(2,1)}, u32[]{:S(2)}) copy-start(bf16[1,1,4,3072]{3,2,1,0:T(4,128)(2,1)} %param.18) | copy-start | bytes 73732
  7.2 20.3 %copy-start.1 = (bf16[1,1,16,3072]{3,2,1,0:T(8,128)(2,1)S(1)}, bf16[1,1,16,3072]{3,2,1,0:T(8,128)(2,1)}, u32[]{:S(2)}) copy-start(bf16[1,1,16,3072]{3,2,1,0:T(8,128)(2,1)} %param.19) | copy-start | bytes 294916
  7.2 21.3 %copy-start.16 = (bf16[1,4,9216]{2,1,0:T(4,128)(2,1)S(1)}, bf16[1,4,9216]{2,1,0:T(4,128)(2,1)}, u32[]{:S(2)}) copy-start(bf16[1,4,9216]{2,1,0:T(4,128)(2,1)} %param.24) | copy-start | bytes 221188
  7.2 21.4 %copy-start.15 = (bf16[1,4,18432]{2,1,0:T(4,128)(2,1)S(1)}, bf16[1,4,18432]{2,1,0:T(4,128)(2,1)}, u32[]{:S(2)}) copy-start(bf16[1,4,18432]{2,1,0:T(4,128)(2,1)} %param.23) | copy-start | bytes 442372
  9.2 23.1 %all-to-all-start = ((bf16[32,32,128]{2,1,0:T(8,128)(2,1)}), bf16[32,32,128]{2,1,0:T(8,128)(2,1)S(1)}, u32[]{:S(2)}, u32[]{:S(2)}) async-start(bf16[32,32,128]{2,1,0:T(8,128)(2,1)} %pad.9.clone), calls=%async_computation | async-start | bytes 524288 | tf_op jit(solution)/shard_map/all_to_all | solution.py:128
  19.0 80.2 %all-gather.8.cloned.1.call-start = ((), (), s32[]{:S(2)}) async-start(), calls=%async_computation.9 | async-start | bytes 4866048 | tf_op jit(solution)/shard_map/all_gather | solution.py:134
  32.2 0.8 copy-start.2
  104.5 3.8 %copy-start.18 = (bf16[1,3072,288]{1,2,0:T(8,128)(2,1)S(1)}, bf16[1,3072,288]{1,2,0:T(8,128)(2,1)}, u32[]{:S(2)}) copy-start(bf16[1,3072,288]{1,2,0:T(8,128)(2,1)} %param.26) | copy-start | bytes 5308420
  109.5 8.1 %copy-start.17 = (f32[1,4,128]{2,1,0:T(4,128)S(1)}, f32[1,4,128]{2,1,0:T(4,128)}, u32[]{:S(2)}) copy-start(f32[1,4,128]{2,1,0:T(4,128)} %param.27) | copy-start | bytes 6148
  110.7 25.8 %all-to-all-start.1 = ((bf16[32,20,288]{2,1,0:T(8,128)(2,1)}), bf16[32,20,288]{2,1,0:T(8,128)(2,1)S(1)}, u32[]{:S(2)}, u32[]{:S(2)}) async-start(bf16[32,20,288]{2,1,0:T(8,128)(2,1)} %pad_maximum_fusion), calls=%async_computation.1 | async-start | bytes 1179648 | tf_op jit(solution)/shard_map/all_to_all | solution.py:64
  136.9 6.9 %copy-start.7 = (bf16[4,3072]{1,0:T(4,128)(2,1)}, bf16[4,3072]{1,0:T(4,128)(2,1)S(1)}, u32[]{:S(2)}) copy-start(bf16[4,3072]{1,0:T(4,128)(2,1)S(1)} %slice.244) | copy-start | bytes 73732
  143.1 2.8 copy-start.9
  144.0 11.3 %copy-start.3 = (bf16[32,32,128]{2,1,0:T(8,128)(2,1)S(1)}, bf16[32,32,128]{2,1,0:T(8,128)(2,1)}, u32[]{:S(2)}) copy-start(bf16[32,32,128]{2,1,0:T(8,128)(2,1)} %copy-done.2) | copy-start | bytes 786436
  144.4 11.6 %copy-start.8 = (bf16[4,3072]{1,0:T(4,128)(2,1)S(1)}, bf16[4,3072]{1,0:T(4,128)(2,1)}, u32[]{:S(2)}) copy-start(bf16[4,3072]{1,0:T(4,128)(2,1)} %copy-done.7) | copy-start | bytes 73732
  150.7 22.4 %all-to-all-start.2 = ((bf16[32,60,128]{2,1,0:T(8,128)(2,1)}), bf16[32,60,128]{2,1,0:T(8,128)(2,1)S(1)}, u32[]{:S(2)}, u32[]{:S(2)}) async-start(bf16[32,60,128]{2,1,0:T(8,128)(2,1)} %pad.10.clone), calls=%async_computation.2 | async-start | bytes 1048576 | tf_op jit(solution)/shard_map/all_to_all | solution.py:128
  154.6 113.9 %all-gather.6.cloned.1.call-start = ((), (), s32[]{:S(2)}) async-start(), calls=%async_computation.8 | async-start | bytes 5947392 | tf_op jit(solution)/shard_map/all_gather | solution.py:201
  173.7 2.3 copy-start.10
  177.8 41.5 %copy-start.4 = (bf16[1,3072,96]{1,2,0:T(8,128)(2,1)S(1)}, bf16[1,3072,96]{1,2,0:T(8,128)(2,1)}, u32[]{:S(2)}) copy-start(bf16[1,3072,96]{1,2,0:T(8,128)(2,1)} %param.28) | copy-start | bytes 1769476
  178.9 54.2 %copy-start.14 = (f32[1,1,3072]{2,1,0:T(1,128)S(1)}, f32[1,1,3072]{2,1,0:T(1,128)}, u32[]{:S(2)}) copy-start(f32[1,1,3072]{2,1,0:T(1,128)} %get-tuple-element.35) | copy-start | bytes 36868
  178.9 54.6 %copy-start.12 = (f32[1,1,3072]{2,1,0:T(1,128)S(1)}, f32[1,1,3072]{2,1,0:T(1,128)}, u32[]{:S(2)}) copy-start(f32[1,1,3072]{2,1,0:T(1,128)} %get-tuple-element.31) | copy-start | bytes 36868
  179.0 54.6 %copy-start.13 = (f32[1,1,3072]{2,1,0:T(1,128)S(1)}, f32[1,1,3072]{2,1,0:T(1,128)}, u32[]{:S(2)}) copy-start(f32[1,1,3072]{2,1,0:T(1,128)} %get-tuple-element.32) | copy-start | bytes 36868
  234.7 32.1 %all-to-all-start.5 = ((bf16[32,4,3072]{2,1,0:T(4,128)(2,1)}), bf16[32,4,3072]{2,1,0:T(4,128)(2,1)}, u32[]{:S(2)}, u32[]{:S(2)}) async-start(bf16[32,4,3072]{2,1,0:T(4,128)(2,1)} %broadcast_in_dim.37), calls=%async_computation.5 | async-start | bytes 1572864 | tf_op jit(solution)/shard_map/all_to_all | solution.py:71
  280.5 14.8 %all-to-all-start.6 = ((bf16[32,16,96]{2,1,0:T(8,128)(2,1)}), bf16[32,16,96]{2,1,0:T(8,128)(2,1)S(1)}, u32[]{:S(2)}, u32[]{:S(2)}) async-start(bf16[32,16,96]{2,1,0:T(8,128)(2,1)} %bitcast.56), calls=%async_computation.6 | async-start | bytes 262144 | tf_op jit(solution)/shard_map/all_to_all | solution.py:64
  295.2 0.7 copy-start.5
  299.4 27.2 %all-to-all-start.7 = ((bf16[32,4,3072]{2,1,0:T(4,128)(2,1)}), bf16[32,4,3072]{2,1,0:T(4,128)(2,1)S(1)}, u32[]{:S(2)}, u32[]{:S(2)}) async-start(bf16[32,4,3072]{2,1,0:T(4,128)(2,1)} %reshape.411), calls=%async_computation.7 | async-start | bytes 1572864 | tf_op jit(solution)/shard_map/all_to_all | solution.py:239
  307.6 19.4 %copy-start.11 = (f32[1,1,3072]{2,1,0:T(1,128)S(1)}, f32[1,1,3072]{2,1,0:T(1,128)}, u32[]{:S(2)}) copy-start(f32[1,1,3072]{2,1,0:T(1,128)} %get-tuple-element.30) | copy-start | bytes 36868
  307.6 25.2 %copy-start.19 = (f32[1,4,32]{2,1,0:T(4,128)S(1)}, f32[1,4,32]{2,1,0:T(4,128)}, u32[]{:S(2)}) copy-start(f32[1,4,32]{2,1,0:T(4,128)} %param.35) | copy-start | bytes 1540
  311.8 19.9 %collective-permute-start.1 = (bf16[16,3072]{1,0:T(8,128)(2,1)}, bf16[16,3072]{1,0:T(8,128)(2,1)S(1)}, u32[]{:S(2)}, u32[]{:S(2)}) collective-permute-start(bf16[16,3072]{1,0:T(8,128)(2,1)} %fusion.52), channel_id=1, source_target_pairs={{128,0},{0,128},{129,1},{1,129},{130,2},{2,130},{131,3},{3,131},{1... | collective-permute-start | bytes 294920 | tf_op jit(solution)/shard_map/ppermute | solution.py:20
  327.0 5.4 %collective-permute-start = (bf16[4,3072]{1,0:T(4,128)(2,1)S(1)}, bf16[4,3072]{1,0:T(4,128)(2,1)S(1)}, u32[]{:S(2)}, u32[]{:S(2)}) collective-permute-start(bf16[4,3072]{1,0:T(4,128)(2,1)S(1)} %add_convert_fusion), channel_id=1, source_target_pairs={{128,0},{0,128},{129,1},{1,129},{130,2},{2,130},{131,3},{3,131},{1... | collective-permute-start | bytes 73736 | tf_op jit(solution)/shard_map/ppermute | solution.py:20
Sparse Core Ops, SparseCore 0:
  33.1 66.1 all-gather.7
  178.8 85.9 all-gather.5

commit v10 on v9

--- a/solution.py
+++ b/solution.py
@@ -134,20 +134,16 @@
     every = lax.all_gather(
         jnp.concatenate([image_normed, text_normed], axis=0), TOK, axis=0, tiled=False
     )
-    image_cols = jnp.dot(
-        every[:, :image_rows].reshape(-1, width), image_to_heads[0], preferred_element_type=jnp.float32
-    ).astype(jnp.bfloat16)
-    text_cols = jnp.dot(
-        every[:, image_rows:].reshape(-1, width), text_to_heads[0], preferred_element_type=jnp.float32
-    ).astype(jnp.bfloat16)
+    flat = every.reshape(-1, width)
+    image_cols = jnp.dot(flat, image_to_heads[0], preferred_element_type=jnp.float32)
+    text_cols = jnp.dot(flat, text_to_heads[0], preferred_element_type=jnp.float32)
+    is_image = (jnp.arange(image_rows + text_rows) < image_rows)[None, :, None]
     proj = cols_to_rows(
-        jnp.concatenate(
-            [
-                image_cols.reshape(devices, image_rows, -1),
-                text_cols.reshape(devices, text_rows, -1),
-            ],
-            axis=1,
-        )
+        jnp.where(
+            is_image,
+            image_cols.reshape(devices, image_rows + text_rows, -1),
+            text_cols.reshape(devices, image_rows + text_rows, -1),
+        ).astype(jnp.bfloat16)
     )
     image_proj = proj[:image_rows]
     text_proj = proj[image_rows:]
@@ -208,17 +204,19 @@
         fresh_all, (position % per_patch) * cache_rows, cache_rows, 0
     )
     current = jnp.where(position // per_patch == patch, moved, stale)
-    image_att = jnp.transpose(image_heads[:heads], (1, 0, 2)).reshape(-1, width)
-    text_att = jnp.transpose(text_heads[:heads], (1, 0, 2)).reshape(-1, width)
+    def from_heads(blocks, weight):
+        return jnp.einsum(
+            "hrd,hdc->rc",
+            blocks[:heads],
+            weight.reshape(heads, HDIM, -1),
+            preferred_element_type=jnp.float32,
+        ).astype(jnp.bfloat16)
+
     image_back = cols_to_rows(
-        jnp.dot(image_att, image_from_heads[0], preferred_element_type=jnp.float32)
-        .astype(jnp.bfloat16)
-        .reshape(devices, image_rows, -1)
+        from_heads(image_heads, image_from_heads[0]).reshape(devices, image_rows, -1)
     )
     text_back = cols_to_rows(
-        jnp.dot(text_att, text_from_heads[0], preferred_element_type=jnp.float32)
-        .astype(jnp.bfloat16)
-        .reshape(devices, text_rows, -1)
+        from_heads(text_heads, text_from_heads[0]).reshape(devices, text_rows, -1)
     )
     image_mid = image_x + modul[2] * image_back.astype(jnp.float32)
     text_out = (text_x + text_mod[2] * text_back.astype(jnp.float32)).astype(jnp.bfloat16)

time: 345 us -> 340 us (0.986)
  blocking collectives: 53.5 us -> 13.5 us
  waiting for transfers between devices: 148 us -> 181 us
  local copies, waits for them, and re-layouts: 49.3 us -> 38.7 us
  matrix products: 15.2 us -> 21.5 us
  starting transfers between devices: 38.8 us -> 43.4 us
    all_to_all x1 -> x0, blocking collectives: 40.3 us -> none  [broadcast_rows(): got = lax.all_to_all(copies, TOK, split_axis=0, concat_axis=0, tiled=True)]
    all_to_all x1 -> x2, waiting for transfers between devices: 25.4 us -> 58.4 us  [broadcast_rows(): got = lax.all_to_all(copies, TOK, split_axis=0, concat_axis=0, tiled=True)]
    transpose x2 -> x0, local copies, waits for them, and re-layouts: 8.56 us -> none  [shards(): text_att = jnp.transpose(text_heads[:heads], (1, 0, 2)).reshape(-1, width)]
    dot_general x4, matrix products: 6.47 us -> 13.7 us  [the longest x1 5.66 us: shards(): jnp.dot(flat, text_to_heads[0], preferred_element_type=jnp.float32)]
    slice x3 -> x0, local copies, waits for them, and re-layouts: 5.5 us -> none  [the longest x1 3.82 us: shards(): every[:, image_rows:].reshape(-1, width)]
    all_to_all x1 -> x2, starting transfers between devices: 4.63 us -> 8.55 us  [broadcast_rows(): got = lax.all_to_all(copies, TOK, split_axis=0, concat_axis=0, tiled=True)]
    unnamed x58 -> x56, local copies, waits for them, and re-layouts: 7.68 us -> 11.6 us
  transfers between devices with their start and end apart: 10 -> 11, of which waited for: 8 -> 9; matrix products, arithmetic and copies ran while one was open for 7% -> 9% of each run, Pallas kernels for 0% -> 0%
where the time goes in v10:
time: 340 us; the launch traced here: 337 us
  waiting for transfers between devices  181 us (53%)
  starting transfers between devices  43.4 us (13%)
  local copies, waits for them, and re-layouts  38.7 us (11%)
  between operations  24 us (7%)
  matrix products  21.5 us (6%)
  other arithmetic  14.9 us (4%)
  blocking collectives  13.5 us (4%)
    all_gather x1, waiting for transfers between devices, shards(): lax.all_gather(jnp.concatenate([image_normed, text_normed], axis=0), TOK,...  66.4 us
    all_to_all x2, waiting for transfers between devices, broadcast_rows(): got = lax.all_to_all(copies, TOK, split_axis=0, concat_axis=0, tiled=True)  58.4 us
    all_to_all x2, waiting for transfers between devices, cols_to_rows(): got = lax.all_to_all(cols, TOK, split_axis=0, concat_axis=0, tiled=True)  24.4 us
    all_to_all x2, waiting for transfers between devices, by_head(): return lax.all_to_all(pack, TOK, split_axis=0, concat_axis=0, tiled=True)  19.2 us
    all_to_all x2, starting transfers between devices, by_head(): return lax.all_to_all(pack, TOK, split_axis=0, concat_axis=0, tiled=True)  13.8 us
    all_to_all x1, blocking collectives, cols_to_rows(): got = lax.all_to_all(cols, TOK, split_axis=0, concat_axis=0, tiled=True)  13.5 us
    all_to_all x1, waiting for transfers between devices, shards(): lax.all_to_all(partial.astype(jnp.bfloat16).reshape(devices, image_rows,...  11.7 us
    unnamed x56, local copies, waits for them, and re-layouts  11.6 us
  transfers between devices with their start and end apart: 11, of which 9 were waited for; matrix products, arithmetic and copies ran while one was open for 9% of the time, Pallas kernels for 0%

profile of v10, /device:TPU:2, one launch (start us, length us, event | category | flops | bytes accessed | tf_op | source)
XLA Modules:
  0.0 337.0 jit_solution(17351460633258674306)
XLA Ops:
  9.2 9.9 %all-to-all-start = ((bf16[32,32,128]{2,1,0:T(8,128)(2,1)}), bf16[32,32,128]{2,1,0:T(8,128)(2,1)S(1)}, u32[]{:S(2)}, u32[]{:S(2)}) async-start(bf16[32,32,128]{2,1,0:T(8,128)(2,1)} %pad.9.clone), calls=%async_computation | async-start | bytes 524288 | tf_op jit(solution)/shard_map/all_to_all | solution.py:128
  29.7 2.5 all-to-all-done
  33.0 66.4 %all-gather.8.cloned.1.call-done = bf16[32,20,3072]{2,1,0:T(8,128)(2,1)} async-done(((bf16[1,20,3072]{2,1,0:T(8,128)(2,1)}), bf16[32,20,3072]{2,1,0:T(8,128)(2,1)}) %all-gather.8.cloned.1.call-update) | async-done | bytes 3932176 | tf_op jit(solution)/shard_map/all_gather | solution.py:134
  99.4 5.7 %fusion.9 = bf16[32,20,288]{2,1,0:T(8,128)(2,1)S(1)} fusion(bf16[32,20,3072]{2,1,0:T(8,128)(2,1)} %all-gather.8.cloned.1.call-done, bf16[1,3072,288]{1,2,0:T(8,128)(2,1)} %param.26), kind=kOutput, calls=%fused_computation.11 | convolution fusion | flops 1132462080 | bytes 6070272 | tf_op jit(solution)/shard_map/dot_general | solution.py:139
  105.1 3.5 %fusion.16 = bf16[32,20,288]{2,1,0:T(8,128)(2,1)} fusion(bf16[32,20,288]{2,1,0:T(8,128)(2,1)S(1)} %fusion.9, bf16[32,20,3072]{2,1,0:T(8,128)(2,1)S(1)} %copy-done.15, bf16[1,3072,288]{1,2,0:T(8,128)(2,1)S(1)} %copy-done.16, pred[20]{0:T(512)(128)(4,1)S(1)} %iota_compare_fusion.1), kind=kOutput, calls=%fused_computation.17 | convolution fusion | flops 1132646400 | bytes 6438932 | tf_op jit(solution)/shard_map/dot_general | solution.py:138
  108.6 6.2 %all-to-all-start.1 = ((bf16[32,20,288]{2,1,0:T(8,128)(2,1)}), bf16[32,20,288]{2,1,0:T(8,128)(2,1)S(1)}, u32[]{:S(2)}, u32[]{:S(2)}) async-start(bf16[32,20,288]{2,1,0:T(8,128)(2,1)} %fusion.16), calls=%async_computation.1 | async-start | bytes 1179648 | tf_op jit(solution)/shard_map/all_to_all | solution.py:64
  116.7 17.6 %all-to-all-done.1 = bf16[32,20,288]{2,1,0:T(8,128)(2,1)S(1)} async-done(((bf16[32,20,288]{2,1,0:T(8,128)(2,1)}), bf16[32,20,288]{2,1,0:T(8,128)(2,1)S(1)}, u32[]{:S(2)}, u32[]{:S(2)}) %all-to-all-start.1) | async-done | bytes 368672 | tf_op jit(solution)/shard_map/all_to_all | solution.py:64
  149.3 3.9 %all-to-all-start.2 = ((bf16[32,60,128]{2,1,0:T(8,128)(2,1)}), bf16[32,60,128]{2,1,0:T(8,128)(2,1)S(1)}, u32[]{:S(2)}, u32[]{:S(2)}) async-start(bf16[32,60,128]{2,1,0:T(8,128)(2,1)} %pad.10.clone), calls=%async_computation.2 | async-start | bytes 1048576 | tf_op jit(solution)/shard_map/all_to_all | solution.py:128
  155.0 16.7 %all-to-all-done.2 = bf16[32,60,128]{2,1,0:T(8,128)(2,1)S(1)} async-done(((bf16[32,60,128]{2,1,0:T(8,128)(2,1)}), bf16[32,60,128]{2,1,0:T(8,128)(2,1)S(1)}, u32[]{:S(2)}, u32[]{:S(2)}) %all-to-all-start.2) | async-done | bytes 491552 | tf_op jit(solution)/shard_map/all_to_all | solution.py:128
  173.1 1.5 fusion.6
  178.4 3.9 %all-to-all-start.3 = ((bf16[32,128,128]{2,1,0:T(8,128)(2,1)}), bf16[32,128,128]{2,1,0:T(8,128)(2,1)S(1)}, u32[]{:S(2)}, u32[]{:S(2)}) async-start(bf16[32,128,128]{2,1,0:T(8,128)(2,1)} %broadcast_in_dim.45), calls=%async_computation.3 | async-start | bytes 2097152 | tf_op jit(solution)/shard_map/all_to_all | solution.py:71
  182.3 2.0 copy.101
  184.3 35.7 %all-to-all-done.3 = bf16[32,128,128]{2,1,0:T(8,128)(2,1)S(1)} async-done(((bf16[32,128,128]{2,1,0:T(8,128)(2,1)}), bf16[32,128,128]{2,1,0:T(8,128)(2,1)S(1)}, u32[]{:S(2)}, u32[]{:S(2)}) %all-to-all-start.3) | async-done | bytes 1048608 | tf_op jit(solution)/shard_map/all_to_all | solution.py:71
  220.0 1.4 fusion.32
  221.6 13.5 %all_to_all.40 = bf16[32,4,96]{2,1,0:T(4,128)(2,1)S(1)} all-to-all(bf16[32,4,96]{2,1,0:T(4,128)(2,1)S(1)} %bitcast.275), channel_id=1, replica_groups=mesh['section'=2,'grp'=4,'ta'=8,'tb'=4] {'ta','tb'}, dimensions={0} | all-to-all | bytes 49152 | tf_op jit(solution)/shard_map/all_to_all | solution.py:64
  238.2 4.6 %all-to-all-start.5 = ((bf16[32,4,3072]{2,1,0:T(4,128)(2,1)}), bf16[32,4,3072]{2,1,0:T(4,128)(2,1)}, u32[]{:S(2)}, u32[]{:S(2)}) async-start(bf16[32,4,3072]{2,1,0:T(4,128)(2,1)} %broadcast_in_dim.46), calls=%async_computation.5 | async-start | bytes 1572864 | tf_op jit(solution)/shard_map/all_to_all | solution.py:71
  245.6 22.7 %all-to-all-done.5 = bf16[32,4,3072]{2,1,0:T(4,128)(2,1)} async-done(((bf16[32,4,3072]{2,1,0:T(4,128)(2,1)}), bf16[32,4,3072]{2,1,0:T(4,128)(2,1)}, u32[]{:S(2)}, u32[]{:S(2)}) %all-to-all-start.5) | async-done | bytes 786464 | tf_op jit(solution)/shard_map/all_to_all | solution.py:71
  268.4 1.6 reshape.394
  270.0 3.1 fusion.29
  273.8 4.6 %all-to-all-start.6 = ((bf16[32,16,96]{2,1,0:T(8,128)(2,1)}), bf16[32,16,96]{2,1,0:T(8,128)(2,1)S(1)}, u32[]{:S(2)}, u32[]{:S(2)}) async-start(bf16[32,16,96]{2,1,0:T(8,128)(2,1)} %bitcast.52), calls=%async_computation.6 | async-start | bytes 262144 | tf_op jit(solution)/shard_map/all_to_all | solution.py:64
  278.5 3.7 %fusion.2 = bf16[128,3072]{1,0:T(8,128)(2,1)} fusion(bf16[1,384,3072]{2,1,0:T(8,128)(2,1)S(1)} %copy-done, bf16[128,3072]{1,0:T(8,128)(2,1)S(1)} %reshape.394, bf16[1,3072,384]{2,1,0:T(8,128)(2,1)} %param.30), kind=kOutput, calls=%fused_computation.4 | convolution fusion | flops 604422144 | bytes 6291456 | tf_op jit(solution)/shard_map/dot_general | solution.py:234
  282.2 6.7 %all-to-all-done.6 = bf16[32,16,96]{2,1,0:T(8,128)(2,1)S(1)} async-done(((bf16[32,16,96]{2,1,0:T(8,128)(2,1)}), bf16[32,16,96]{2,1,0:T(8,128)(2,1)S(1)}, u32[]{:S(2)}, u32[]{:S(2)}) %all-to-all-start.6) | async-done | bytes 98336 | tf_op jit(solution)/shard_map/all_to_all | solution.py:64
  291.4 2.4 reshape.398
  293.7 3.9 %all-to-all-start.7 = ((bf16[32,4,3072]{2,1,0:T(4,128)(2,1)}), bf16[32,4,3072]{2,1,0:T(4,128)(2,1)S(1)}, u32[]{:S(2)}, u32[]{:S(2)}) async-start(bf16[32,4,3072]{2,1,0:T(4,128)(2,1)} %reshape.398), calls=%async_computation.7 | async-start | bytes 1572864 | tf_op jit(solution)/shard_map/all_to_all | solution.py:237
  298.3 2.7 slice.249
  301.0 3.6 %reshape.399 = bf16[128,6144]{1,0:T(8,128)(2,1)} reshape(bf16[32,192,128]{2,1,0:T(8,128)(2,1)} %slice.249) | data formatting | bytes 3145728 | tf_op jit(solution)/shard_map/reshape | solution.py:201
  304.7 1.6 fusion.61
  306.2 3.0 collective-permute-start.1
  309.2 11.7 %all-to-all-done.7 = bf16[32,4,3072]{2,1,0:T(4,128)(2,1)S(1)} async-done(((bf16[32,4,3072]{2,1,0:T(4,128)(2,1)}), bf16[32,4,3072]{2,1,0:T(4,128)(2,1)S(1)}, u32[]{:S(2)}, u32[]{:S(2)}) %all-to-all-start.7) | async-done | bytes 786464 | tf_op jit(solution)/shard_map/all_to_all | solution.py:237
  321.3 3.1 collective-permute-start
  324.4 1.7 select_bitcast_fusion
  327.1 1.7 fusion.34
  (148 shorter events, 40.0 us)
Async XLA Ops:
  7.2 271.3 %copy-start = (bf16[1,384,3072]{2,1,0:T(8,128)(2,1)S(1)}, bf16[1,384,3072]{2,1,0:T(8,128)(2,1)}, u32[]{:S(2)}) copy-start(bf16[1,384,3072]{2,1,0:T(8,128)(2,1)} %param.31) | copy-start | bytes 7077892
  7.2 20.2 %copy-start.11 = (bf16[1,4,18432]{2,1,0:T(4,128)(2,1)S(1)}, bf16[1,4,18432]{2,1,0:T(4,128)(2,1)}, u32[]{:S(2)}) copy-start(bf16[1,4,18432]{2,1,0:T(4,128)(2,1)} %param.23) | copy-start | bytes 442372
  7.2 20.9 %copy-start.6 = (bf16[1,1,4,3072]{3,2,1,0:T(4,128)(2,1)S(1)}, bf16[1,1,4,3072]{3,2,1,0:T(4,128)(2,1)}, u32[]{:S(2)}) copy-start(bf16[1,1,4,3072]{3,2,1,0:T(4,128)(2,1)} %param.18) | copy-start | bytes 73732
  7.2 21.3 %copy-start.12 = (bf16[1,4,9216]{2,1,0:T(4,128)(2,1)S(1)}, bf16[1,4,9216]{2,1,0:T(4,128)(2,1)}, u32[]{:S(2)}) copy-start(bf16[1,4,9216]{2,1,0:T(4,128)(2,1)} %param.24) | copy-start | bytes 221188
  7.2 21.9 %copy-start.1 = (bf16[1,1,16,3072]{3,2,1,0:T(8,128)(2,1)S(1)}, bf16[1,1,16,3072]{3,2,1,0:T(8,128)(2,1)}, u32[]{:S(2)}) copy-start(bf16[1,1,16,3072]{3,2,1,0:T(8,128)(2,1)} %param.19) | copy-start | bytes 294916
  9.2 23.1 %all-to-all-start = ((bf16[32,32,128]{2,1,0:T(8,128)(2,1)}), bf16[32,32,128]{2,1,0:T(8,128)(2,1)S(1)}, u32[]{:S(2)}, u32[]{:S(2)}) async-start(bf16[32,32,128]{2,1,0:T(8,128)(2,1)} %pad.9.clone), calls=%async_computation | async-start | bytes 524288 | tf_op jit(solution)/shard_map/all_to_all | solution.py:128
  19.0 80.4 %all-gather.8.cloned.1.call-start = ((), (), s32[]{:S(2)}) async-start(), calls=%async_computation.9 | async-start | bytes 4866048 | tf_op jit(solution)/shard_map/all_gather | solution.py:134
  99.4 5.7 %copy-start.15 = (bf16[32,20,3072]{2,1,0:T(8,128)(2,1)S(1)}, bf16[32,20,3072]{2,1,0:T(8,128)(2,1)}, u32[]{:S(2)}) copy-start(bf16[32,20,3072]{2,1,0:T(8,128)(2,1)} %all-gather.8.cloned.1.call-done) | copy-start | bytes 11796484
  99.4 5.7 %copy-start.16 = (bf16[1,3072,288]{1,2,0:T(8,128)(2,1)S(1)}, bf16[1,3072,288]{1,2,0:T(8,128)(2,1)}, u32[]{:S(2)}) copy-start(bf16[1,3072,288]{1,2,0:T(8,128)(2,1)} %param.25) | copy-start | bytes 5308420
  105.1 10.4 %copy-start.14 = (f32[1,4,128]{2,1,0:T(4,128)S(1)}, f32[1,4,128]{2,1,0:T(4,128)}, u32[]{:S(2)}) copy-start(f32[1,4,128]{2,1,0:T(4,128)} %param.27) | copy-start | bytes 6148
  108.6 25.7 %all-to-all-start.1 = ((bf16[32,20,288]{2,1,0:T(8,128)(2,1)}), bf16[32,20,288]{2,1,0:T(8,128)(2,1)S(1)}, u32[]{:S(2)}, u32[]{:S(2)}) async-start(bf16[32,20,288]{2,1,0:T(8,128)(2,1)} %fusion.16), calls=%async_computation.1 | async-start | bytes 1179648 | tf_op jit(solution)/shard_map/all_to_all | solution.py:64
  138.4 5.6 %copy-start.5 = (bf16[16,3072]{1,0:T(8,128)(2,1)S(1)}, bf16[16,3072]{1,0:T(8,128)(2,1)}, u32[]{:S(2)}) copy-start(bf16[16,3072]{1,0:T(8,128)(2,1)} %slice.235) | copy-start | bytes 294916
  143.9 10.9 %copy-start.7 = (bf16[4,3072]{1,0:T(4,128)(2,1)S(1)}, bf16[4,3072]{1,0:T(4,128)(2,1)}, u32[]{:S(2)}) copy-start(bf16[4,3072]{1,0:T(4,128)(2,1)} %get-tuple-element.36) | copy-start | bytes 73732
  149.3 22.4 %all-to-all-start.2 = ((bf16[32,60,128]{2,1,0:T(8,128)(2,1)}), bf16[32,60,128]{2,1,0:T(8,128)(2,1)S(1)}, u32[]{:S(2)}, u32[]{:S(2)}) async-start(bf16[32,60,128]{2,1,0:T(8,128)(2,1)} %pad.10.clone), calls=%async_computation.2 | async-start | bytes 1048576 | tf_op jit(solution)/shard_map/all_to_all | solution.py:128
  153.2 116.7 %all-gather.6.cloned.1.call-start = ((), (), s32[]{:S(2)}) async-start(), calls=%async_computation.8 | async-start | bytes 5947392 | tf_op jit(solution)/shard_map/all_gather | solution.py:197
  173.1 2.2 copy-start.8
  178.4 41.6 %all-to-all-start.3 = ((bf16[32,128,128]{2,1,0:T(8,128)(2,1)}), bf16[32,128,128]{2,1,0:T(8,128)(2,1)S(1)}, u32[]{:S(2)}, u32[]{:S(2)}) async-start(bf16[32,128,128]{2,1,0:T(8,128)(2,1)} %broadcast_in_dim.45), calls=%async_computation.3 | async-start | bytes 2097152 | tf_op jit(solution)/shard_map/all_to_all | solution.py:71
  221.5 22.6 %copy-start.3 = (bf16[1,3072,96]{1,2,0:T(8,128)(2,1)S(1)}, bf16[1,3072,96]{1,2,0:T(8,128)(2,1)}, u32[]{:S(2)}) copy-start(bf16[1,3072,96]{1,2,0:T(8,128)(2,1)} %param.29) | copy-start | bytes 1769476
  238.2 30.2 %all-to-all-start.5 = ((bf16[32,4,3072]{2,1,0:T(4,128)(2,1)}), bf16[32,4,3072]{2,1,0:T(4,128)(2,1)}, u32[]{:S(2)}, u32[]{:S(2)}) async-start(bf16[32,4,3072]{2,1,0:T(4,128)(2,1)} %broadcast_in_dim.46), calls=%async_computation.5 | async-start | bytes 1572864 | tf_op jit(solution)/shard_map/all_to_all | solution.py:71
  273.8 15.1 %all-to-all-start.6 = ((bf16[32,16,96]{2,1,0:T(8,128)(2,1)}), bf16[32,16,96]{2,1,0:T(8,128)(2,1)S(1)}, u32[]{:S(2)}, u32[]{:S(2)}) async-start(bf16[32,16,96]{2,1,0:T(8,128)(2,1)} %bitcast.52), calls=%async_computation.6 | async-start | bytes 262144 | tf_op jit(solution)/shard_map/all_to_all | solution.py:64
  282.2 15.5 %copy-start.13 = (bf16[4,6144]{1,0:T(4,128)(2,1)S(1)}, bf16[4,6144]{1,0:T(4,128)(2,1)}, u32[]{:S(2)}) copy-start(bf16[4,6144]{1,0:T(4,128)(2,1)} %param.33) | copy-start | bytes 147460
  288.9 0.7 copy-start.4
  293.7 27.2 %all-to-all-start.7 = ((bf16[32,4,3072]{2,1,0:T(4,128)(2,1)}), bf16[32,4,3072]{2,1,0:T(4,128)(2,1)S(1)}, u32[]{:S(2)}, u32[]{:S(2)}) async-start(bf16[32,4,3072]{2,1,0:T(4,128)(2,1)} %reshape.398), calls=%async_computation.7 | async-start | bytes 1572864 | tf_op jit(solution)/shard_map/all_to_all | solution.py:237
  298.3 6.3 %copy-start.9 = (f32[1,1,3072]{2,1,0:T(1,128)S(1)}, f32[1,1,3072]{2,1,0:T(1,128)}, u32[]{:S(2)}) copy-start(f32[1,1,3072]{2,1,0:T(1,128)} %get-tuple-element.40) | copy-start | bytes 36868
  301.0 20.3 %copy-start.10 = (f32[1,1,3072]{2,1,0:T(1,128)S(1)}, f32[1,1,3072]{2,1,0:T(1,128)}, u32[]{:S(2)}) copy-start(f32[1,1,3072]{2,1,0:T(1,128)} %get-tuple-element.30) | copy-start | bytes 36868
  301.0 23.4 %copy-start.2 = (bf16[1,1,16,6144]{3,2,1,0:T(8,128)(2,1)S(1)}, bf16[1,1,16,6144]{3,2,1,0:T(8,128)(2,1)}, u32[]{:S(2)}) copy-start(bf16[1,1,16,6144]{3,2,1,0:T(8,128)(2,1)} %param.32) | copy-start | bytes 589828
  301.0 26.1 %copy-start.17 = (f32[1,4,32]{2,1,0:T(4,128)S(1)}, f32[1,4,32]{2,1,0:T(4,128)}, u32[]{:S(2)}) copy-start(f32[1,4,32]{2,1,0:T(4,128)} %param.35) | copy-start | bytes 1540
  306.2 19.8 %collective-permute-start.1 = (bf16[16,3072]{1,0:T(8,128)(2,1)}, bf16[16,3072]{1,0:T(8,128)(2,1)S(1)}, u32[]{:S(2)}, u32[]{:S(2)}) collective-permute-start(bf16[16,3072]{1,0:T(8,128)(2,1)} %fusion.61), channel_id=1, source_target_pairs={{128,0},{0,128},{129,1},{1,129},{130,2},{2,130},{131,3},{3,131},{1... | collective-permute-start | bytes 294920 | tf_op jit(solution)/shard_map/ppermute | solution.py:20
  321.3 5.4 %collective-permute-start = (bf16[4,3072]{1,0:T(4,128)(2,1)S(1)}, bf16[4,3072]{1,0:T(4,128)(2,1)S(1)}, u32[]{:S(2)}, u32[]{:S(2)}) collective-permute-start(bf16[4,3072]{1,0:T(4,128)(2,1)S(1)} %add_convert_fusion), channel_id=1, source_target_pairs={{128,0},{0,128},{129,1},{1,129},{130,2},{2,130},{131,3},{3,131},{1... | collective-permute-start | bytes 73736 | tf_op jit(solution)/shard_map/ppermute | solution.py:20
Sparse Core Ops, SparseCore 0:
  33.1 66.2 all-gather.7
  177.2 84.9 all-gather.5

commit v11 on v10

--- a/solution.py
+++ b/solution.py
@@ -161,12 +161,25 @@
     image_value = image_proj[:, 2 * width :]
     text_value = text_proj[:, 2 * width :]
     fresh_image = jnp.concatenate([image_key, image_value], axis=1)
+    group = lax.axis_size("tb")
+    blocks = devices // group
+    mine = lax.axis_index("tb")
+    quad = [fresh_image]
+    for shift in range(1, group):
+        turn = [(j * group + b, j * group + (b + shift) % group) for j in range(blocks) for b in range(group)]
+        quad.append(lax.ppermute(fresh_image, TOK, turn))
+    quad = jnp.stack(quad)
+    quad = jnp.take(quad, (mine - jnp.arange(group)) % group, axis=0).reshape(-1, fresh_image.shape[1])
+    route = [(j * group + b, j + blocks * b) for j in range(blocks) for b in range(group)]
+    moved = lax.ppermute(quad, TOK, route)
     patch_len = image_rows * devices
     per_patch = patch_len // cache_rows
+    current = jnp.where(position // per_patch == patch, moved, stale)
     row_q = jnp.concatenate([image_query, text_query], axis=0)
     row_k = jnp.concatenate([image_key, text_key], axis=0)
     row_v = jnp.concatenate([image_value, text_value], axis=0)
     got = by_head([row_q, row_k, row_v])
+    got, current = lax.optimization_barrier((got, current))
     rows = image_rows + text_rows
 
     def part(first, count, source=got):
@@ -193,17 +206,7 @@
     )
     head_out = attend(queries, keys, values, valid)
     image_heads = broadcast_rows(head_out[:patch_len], devices).reshape(devices, patch_len, HDIM)
-    riders = fresh_image.reshape(-1, HDIM)
-    text_heads = lax.all_gather(
-        jnp.concatenate([head_out[patch_len:], riders], axis=0), TOK, axis=0, tiled=False
-    )
-    text_len = head_out.shape[0] - patch_len
-    fresh_all = text_heads[:, text_len:].reshape(patch_len, -1)
-    text_heads = text_heads[:, :text_len]
-    moved = lax.dynamic_slice_in_dim(
-        fresh_all, (position % per_patch) * cache_rows, cache_rows, 0
-    )
-    current = jnp.where(position // per_patch == patch, moved, stale)
+    text_heads = lax.all_gather(head_out[patch_len:], TOK, axis=0, tiled=False)
     def from_heads(blocks, weight):
         return jnp.einsum(
             "hrd,hdc->rc",

time: 340 us -> 337 us (level)
  starting transfers between devices: 43.4 us -> 50.2 us
  local copies, waits for them, and re-layouts: 38.7 us -> 33.1 us
    all_to_all x1, waiting for transfers between devices: 11.7 us -> 18 us  [shards(): lax.all_to_all(partial.astype(jnp.bfloat16).reshape(devices, image_rows,...]
    ppermute x0 -> x4, starting transfers between devices: none -> 5.87 us  [the longest x1 2.98 us: shards(): moved = lax.ppermute(quad, TOK, route)]
    reshape x3 -> x0, local copies, waits for them, and re-layouts: 3.76 us -> none  [the longest x1 3.62 us: shards(): fresh_all = text_heads[:, text_len:].reshape(patch_len, -1)]
    all_to_all x2, waiting for transfers between devices: 58.4 us -> 54.9 us  [broadcast_rows(): got = lax.all_to_all(copies, TOK, split_axis=0, concat_axis=0, tiled=True)]
    unnamed x56 -> x59, local copies, waits for them, and re-layouts: 11.6 us -> 9.68 us
  transfers between devices with their start and end apart: 11 -> 15, of which waited for: 9 -> 9; matrix products, arithmetic and copies ran while one was open for 9% -> 10% of each run, Pallas kernels for 0% -> 0%
where the time goes in v11:
time: 337 us; the launch traced here: 336 us
  waiting for transfers between devices  183 us (54%)
  starting transfers between devices  50.2 us (15%)
  local copies, waits for them, and re-layouts  33.1 us (10%)
  between operations  24.4 us (7%)
  matrix products  18.1 us (5%)
  other arithmetic  13.7 us (4%)
  blocking collectives  13.4 us (4%)
    all_gather x1, waiting for transfers between devices, shards(): lax.all_gather(jnp.concatenate([image_normed, text_normed], axis=0), TOK,...  66.3 us
    all_to_all x2, waiting for transfers between devices, broadcast_rows(): got = lax.all_to_all(copies, TOK, split_axis=0, concat_axis=0, tiled=True)  54.9 us
    all_to_all x2, waiting for transfers between devices, cols_to_rows(): got = lax.all_to_all(cols, TOK, split_axis=0, concat_axis=0, tiled=True)  21.8 us
    all_to_all x2, waiting for transfers between devices, by_head(): return lax.all_to_all(pack, TOK, split_axis=0, concat_axis=0, tiled=True)  19 us
    all_to_all x1, waiting for transfers between devices, shards(): lax.all_to_all(partial.astype(jnp.bfloat16).reshape(devices, image_rows,...  18 us
    all_to_all x2, starting transfers between devices, by_head(): return lax.all_to_all(pack, TOK, split_axis=0, concat_axis=0, tiled=True)  15.8 us
    all_to_all x1, blocking collectives, cols_to_rows(): got = lax.all_to_all(cols, TOK, split_axis=0, concat_axis=0, tiled=True)  13.4 us
    all_to_all x2, starting transfers between devices, cols_to_rows(): got = lax.all_to_all(cols, TOK, split_axis=0, concat_axis=0, tiled=True)  10.5 us
  transfers between devices with their start and end apart: 15, of which 9 were waited for; matrix products, arithmetic and copies ran while one was open for 10% of the time, Pallas kernels for 0%

profile of v11, /device:TPU:2, one launch (start us, length us, event | category | flops | bytes accessed | tf_op | source)
XLA Modules:
  0.0 335.7 jit_solution(9138543983739386717)
XLA Ops:
  9.2 9.9 %all-to-all-start = ((bf16[32,32,128]{2,1,0:T(8,128)(2,1)}), bf16[32,32,128]{2,1,0:T(8,128)(2,1)S(1)}, u32[]{:S(2)}, u32[]{:S(2)}) async-start(bf16[32,32,128]{2,1,0:T(8,128)(2,1)} %pad.9.clone), calls=%async_computation | async-start | bytes 524288 | tf_op jit(solution)/shard_map/all_to_all | solution.py:128
  30.8 1.4 all-to-all-done
  34.2 66.3 %all-gather.8.cloned.1.call-done = bf16[32,20,3072]{2,1,0:T(8,128)(2,1)} async-done(((bf16[1,20,3072]{2,1,0:T(8,128)(2,1)}), bf16[32,20,3072]{2,1,0:T(8,128)(2,1)}) %all-gather.8.cloned.1.call-update) | async-done | bytes 3932176 | tf_op jit(solution)/shard_map/all_gather | solution.py:134
  100.5 5.7 %fusion.7 = bf16[32,20,288]{2,1,0:T(8,128)(2,1)S(1)} fusion(bf16[32,20,3072]{2,1,0:T(8,128)(2,1)} %all-gather.8.cloned.1.call-done, bf16[1,3072,288]{1,2,0:T(8,128)(2,1)} %param.26), kind=kOutput, calls=%fused_computation.10 | convolution fusion | flops 1132462080 | bytes 6070272 | tf_op jit(solution)/shard_map/dot_general | solution.py:139
  106.2 3.5 %fusion.14 = bf16[32,20,288]{2,1,0:T(8,128)(2,1)} fusion(bf16[32,20,288]{2,1,0:T(8,128)(2,1)S(1)} %fusion.7, bf16[32,20,3072]{2,1,0:T(8,128)(2,1)S(1)} %copy-done.16, bf16[1,3072,288]{1,2,0:T(8,128)(2,1)S(1)} %copy-done.17, pred[20]{0:T(512)(128)(4,1)S(1)} %iota_compare_fusion.1), kind=kOutput, calls=%fused_computation.16 | convolution fusion | flops 1132646400 | bytes 6438932 | tf_op jit(solution)/shard_map/dot_general | solution.py:138
  109.7 6.2 %all-to-all-start.1 = ((bf16[32,20,288]{2,1,0:T(8,128)(2,1)}), bf16[32,20,288]{2,1,0:T(8,128)(2,1)S(1)}, u32[]{:S(2)}, u32[]{:S(2)}) async-start(bf16[32,20,288]{2,1,0:T(8,128)(2,1)} %fusion.14), calls=%async_computation.1 | async-start | bytes 1179648 | tf_op jit(solution)/shard_map/all_to_all | solution.py:64
  120.4 15.0 %all-to-all-done.1 = bf16[32,20,288]{2,1,0:T(8,128)(2,1)S(1)} async-done(((bf16[32,20,288]{2,1,0:T(8,128)(2,1)}), bf16[32,20,288]{2,1,0:T(8,128)(2,1)S(1)}, u32[]{:S(2)}, u32[]{:S(2)}) %all-to-all-start.1) | async-done | bytes 368672 | tf_op jit(solution)/shard_map/all_to_all | solution.py:64
  136.8 1.5 collective-permute-start.1
  138.2 1.4 collective-permute-start.2
  146.1 3.0 collective-permute-start.3
  151.7 5.9 %all-to-all-start.2 = ((bf16[32,60,128]{2,1,0:T(8,128)(2,1)}), bf16[32,60,128]{2,1,0:T(8,128)(2,1)S(1)}, u32[]{:S(2)}, u32[]{:S(2)}) async-start(bf16[32,60,128]{2,1,0:T(8,128)(2,1)} %pad.10.clone), calls=%async_computation.2 | async-start | bytes 1048576 | tf_op jit(solution)/shard_map/all_to_all | solution.py:128
  158.4 17.7 %all-to-all-done.2 = bf16[32,60,128]{2,1,0:T(8,128)(2,1)S(1)} async-done(((bf16[32,60,128]{2,1,0:T(8,128)(2,1)}), bf16[32,60,128]{2,1,0:T(8,128)(2,1)S(1)}, u32[]{:S(2)}, u32[]{:S(2)}) %all-to-all-start.2) | async-done | bytes 491552 | tf_op jit(solution)/shard_map/all_to_all | solution.py:128
  180.5 3.9 %all-to-all-start.3 = ((bf16[32,128,128]{2,1,0:T(8,128)(2,1)}), bf16[32,128,128]{2,1,0:T(8,128)(2,1)S(1)}, u32[]{:S(2)}, u32[]{:S(2)}) async-start(bf16[32,128,128]{2,1,0:T(8,128)(2,1)} %broadcast_in_dim.97), calls=%async_computation.3 | async-start | bytes 2097152 | tf_op jit(solution)/shard_map/all_to_all | solution.py:71
  184.5 2.0 copy.93
  186.5 34.2 %all-to-all-done.3 = bf16[32,128,128]{2,1,0:T(8,128)(2,1)S(1)} async-done(((bf16[32,128,128]{2,1,0:T(8,128)(2,1)}), bf16[32,128,128]{2,1,0:T(8,128)(2,1)S(1)}, u32[]{:S(2)}, u32[]{:S(2)}) %all-to-all-start.3) | async-done | bytes 1048608 | tf_op jit(solution)/shard_map/all_to_all | solution.py:71
  220.7 1.4 fusion.25
  222.2 13.4 %all_to_all.40 = bf16[32,4,96]{2,1,0:T(4,128)(2,1)S(1)} all-to-all(bf16[32,4,96]{2,1,0:T(4,128)(2,1)S(1)} %bitcast.286), channel_id=1, replica_groups=mesh['section'=2,'grp'=4,'ta'=8,'tb'=4] {'ta','tb'}, dimensions={0} | all-to-all | bytes 49152 | tf_op jit(solution)/shard_map/all_to_all | solution.py:64
  238.8 4.6 %all-to-all-start.5 = ((bf16[32,4,3072]{2,1,0:T(4,128)(2,1)}), bf16[32,4,3072]{2,1,0:T(4,128)(2,1)}, u32[]{:S(2)}, u32[]{:S(2)}) async-start(bf16[32,4,3072]{2,1,0:T(4,128)(2,1)} %broadcast_in_dim.98), calls=%async_computation.5 | async-start | bytes 1572864 | tf_op jit(solution)/shard_map/all_to_all | solution.py:71
  244.6 1.4 copy.73
  246.0 20.7 %all-to-all-done.5 = bf16[32,4,3072]{2,1,0:T(4,128)(2,1)} async-done(((bf16[32,4,3072]{2,1,0:T(4,128)(2,1)}), bf16[32,4,3072]{2,1,0:T(4,128)(2,1)}, u32[]{:S(2)}, u32[]{:S(2)}) %all-to-all-start.5) | async-done | bytes 786464 | tf_op jit(solution)/shard_map/all_to_all | solution.py:71
  266.7 1.6 reshape.446
  268.3 1.9 slice-done
  272.9 4.3 %all-to-all-start.6 = ((bf16[32,16,96]{2,1,0:T(8,128)(2,1)}), bf16[32,16,96]{2,1,0:T(8,128)(2,1)S(1)}, u32[]{:S(2)}, u32[]{:S(2)}) async-start(bf16[32,16,96]{2,1,0:T(8,128)(2,1)} %bitcast.55), calls=%async_computation.6 | async-start | bytes 262144 | tf_op jit(solution)/shard_map/all_to_all | solution.py:64
  277.2 3.7 %fusion = bf16[128,3072]{1,0:T(8,128)(2,1)} fusion(bf16[1,384,3072]{2,1,0:T(8,128)(2,1)S(1)} %copy-done, bf16[128,3072]{1,0:T(8,128)(2,1)S(1)} %reshape.446, bf16[1,3072,384]{2,1,0:T(8,128)(2,1)} %param.30), kind=kOutput, calls=%fused_computation.3 | convolution fusion | flops 604422144 | bytes 6291456 | tf_op jit(solution)/shard_map/dot_general | solution.py:237
  280.9 6.7 %all-to-all-done.6 = bf16[32,16,96]{2,1,0:T(8,128)(2,1)S(1)} async-done(((bf16[32,16,96]{2,1,0:T(8,128)(2,1)}), bf16[32,16,96]{2,1,0:T(8,128)(2,1)S(1)}, u32[]{:S(2)}, u32[]{:S(2)}) %all-to-all-start.6) | async-done | bytes 98336 | tf_op jit(solution)/shard_map/all_to_all | solution.py:64
  290.0 2.4 reshape.449
  292.5 3.9 %all-to-all-start.7 = ((bf16[32,4,3072]{2,1,0:T(4,128)(2,1)}), bf16[32,4,3072]{2,1,0:T(4,128)(2,1)S(1)}, u32[]{:S(2)}, u32[]{:S(2)}) async-start(bf16[32,4,3072]{2,1,0:T(4,128)(2,1)} %reshape.449), calls=%async_computation.7 | async-start | bytes 1572864 | tf_op jit(solution)/shard_map/all_to_all | solution.py:240
  298.9 2.7 collective-permute-start.5
  301.7 18.0 %all-to-all-done.7 = bf16[32,4,3072]{2,1,0:T(4,128)(2,1)S(1)} async-done(((bf16[32,4,3072]{2,1,0:T(4,128)(2,1)}), bf16[32,4,3072]{2,1,0:T(4,128)(2,1)S(1)}, u32[]{:S(2)}, u32[]{:S(2)}) %all-to-all-start.7) | async-done | bytes 786464 | tf_op jit(solution)/shard_map/all_to_all | solution.py:240
  320.0 2.8 collective-permute-start.4
  322.9 2.6 collective-permute-done.4
  325.8 1.7 fusion.27
  (165 shorter events, 39.7 us)
Async XLA Ops:
  7.2 270.0 %copy-start = (bf16[1,384,3072]{2,1,0:T(8,128)(2,1)S(1)}, bf16[1,384,3072]{2,1,0:T(8,128)(2,1)}, u32[]{:S(2)}) copy-start(bf16[1,384,3072]{2,1,0:T(8,128)(2,1)} %param.31) | copy-start | bytes 7077892
  7.2 20.4 %copy-start.12 = (bf16[1,4,18432]{2,1,0:T(4,128)(2,1)S(1)}, bf16[1,4,18432]{2,1,0:T(4,128)(2,1)}, u32[]{:S(2)}) copy-start(bf16[1,4,18432]{2,1,0:T(4,128)(2,1)} %param.23) | copy-start | bytes 442372
  7.2 21.2 %copy-start.7 = (bf16[1,1,4,3072]{3,2,1,0:T(4,128)(2,1)S(1)}, bf16[1,1,4,3072]{3,2,1,0:T(4,128)(2,1)}, u32[]{:S(2)}) copy-start(bf16[1,1,4,3072]{3,2,1,0:T(4,128)(2,1)} %param.18) | copy-start | bytes 73732
  7.2 23.1 %copy-start.1 = (bf16[1,1,16,3072]{3,2,1,0:T(8,128)(2,1)S(1)}, bf16[1,1,16,3072]{3,2,1,0:T(8,128)(2,1)}, u32[]{:S(2)}) copy-start(bf16[1,1,16,3072]{3,2,1,0:T(8,128)(2,1)} %param.19) | copy-start | bytes 294916
  7.2 27.0 %copy-start.15 = (f32[1,4,128]{2,1,0:T(4,128)S(1)}, f32[1,4,128]{2,1,0:T(4,128)}, u32[]{:S(2)}) copy-start(f32[1,4,128]{2,1,0:T(4,128)} %param.27) | copy-start | bytes 6148
  9.2 23.1 %all-to-all-start = ((bf16[32,32,128]{2,1,0:T(8,128)(2,1)}), bf16[32,32,128]{2,1,0:T(8,128)(2,1)S(1)}, u32[]{:S(2)}, u32[]{:S(2)}) async-start(bf16[32,32,128]{2,1,0:T(8,128)(2,1)} %pad.9.clone), calls=%async_computation | async-start | bytes 524288 | tf_op jit(solution)/shard_map/all_to_all | solution.py:128
  19.0 81.5 %all-gather.8.cloned.1.call-start = ((), (), s32[]{:S(2)}) async-start(), calls=%async_computation.9 | async-start | bytes 4866048 | tf_op jit(solution)/shard_map/all_gather | solution.py:134
  100.5 5.7 %copy-start.16 = (bf16[32,20,3072]{2,1,0:T(8,128)(2,1)S(1)}, bf16[32,20,3072]{2,1,0:T(8,128)(2,1)}, u32[]{:S(2)}) copy-start(bf16[32,20,3072]{2,1,0:T(8,128)(2,1)} %all-gather.8.cloned.1.call-done) | copy-start | bytes 11796484
  100.5 5.7 %copy-start.17 = (bf16[1,3072,288]{1,2,0:T(8,128)(2,1)S(1)}, bf16[1,3072,288]{1,2,0:T(8,128)(2,1)}, u32[]{:S(2)}) copy-start(bf16[1,3072,288]{1,2,0:T(8,128)(2,1)} %param.25) | copy-start | bytes 5308420
  109.7 25.8 %all-to-all-start.1 = ((bf16[32,20,288]{2,1,0:T(8,128)(2,1)}), bf16[32,20,288]{2,1,0:T(8,128)(2,1)S(1)}, u32[]{:S(2)}, u32[]{:S(2)}) async-start(bf16[32,20,288]{2,1,0:T(8,128)(2,1)} %fusion.14), calls=%async_computation.1 | async-start | bytes 1179648 | tf_op jit(solution)/shard_map/all_to_all | solution.py:64
  136.8 5.3 %collective-permute-start = (bf16[4,6144]{1,0:T(4,128)(2,1)}, bf16[4,6144]{1,0:T(4,128)(2,1)}, u32[]{:S(2)}, u32[]{:S(2)}) collective-permute-start(bf16[4,6144]{1,0:T(4,128)(2,1)} %get-tuple-element.45), channel_id=1, source_target_pairs={{0,1},{1,2},{2,3},{3,0},{4,5},{5,6},{6,7},{7,4},{8,9},{9,10},{10,1... | collective-permute-start | bytes 147464 | tf_op jit(solution)/shard_map/ppermute | solution.py:170
  136.8 5.3 %collective-permute-start.1 = (bf16[4,6144]{1,0:T(4,128)(2,1)}, bf16[4,6144]{1,0:T(4,128)(2,1)}, u32[]{:S(2)}, u32[]{:S(2)}) collective-permute-start(bf16[4,6144]{1,0:T(4,128)(2,1)} %get-tuple-element.45), channel_id=1, source_target_pairs={{0,2},{1,3},{2,0},{3,1},{4,6},{5,7},{6,4},{7,5},{8,10},{9,11},{10,... | collective-permute-start | bytes 147464 | tf_op jit(solution)/shard_map/ppermute | solution.py:170
  138.2 3.9 %collective-permute-start.2 = (bf16[4,6144]{1,0:T(4,128)(2,1)}, bf16[4,6144]{1,0:T(4,128)(2,1)}, u32[]{:S(2)}, u32[]{:S(2)}) collective-permute-start(bf16[4,6144]{1,0:T(4,128)(2,1)} %get-tuple-element.45), channel_id=1, source_target_pairs={{0,3},{1,0},{2,1},{3,2},{4,7},{5,4},{6,5},{7,6},{8,11},{9,8},{10,9... | collective-permute-start | bytes 147464 | tf_op jit(solution)/shard_map/ppermute | solution.py:170
  142.0 15.7 %copy-start.2 = (bf16[1,1,16,6144]{3,2,1,0:T(8,128)(2,1)S(1)}, bf16[1,1,16,6144]{3,2,1,0:T(8,128)(2,1)}, u32[]{:S(2)}) copy-start(bf16[1,1,16,6144]{3,2,1,0:T(8,128)(2,1)} %param.32) | copy-start | bytes 589828
  144.7 31.5 %copy-start.9 = (bf16[32,16,128]{2,1,0:T(8,128)(2,1)S(1)}, bf16[32,16,128]{2,1,0:T(8,128)(2,1)}, u32[]{:S(2)}) copy-start(bf16[32,16,128]{2,1,0:T(8,128)(2,1)} %get-tuple-element.31) | copy-start | bytes 393220
  144.7 31.6 %copy-start.14 = (pred[1024]{0:T(1024)(128)(4,1)S(1)}, pred[1024]{0:T(1024)(128)(4,1)}, u32[]{:S(2)}) copy-start(pred[1024]{0:T(1024)(128)(4,1)} %concatenate.50) | copy-start | bytes 3076
  146.1 11.6 %collective-permute-start.3 = (bf16[16,6144]{1,0:T(8,128)(2,1)}, bf16[16,6144]{1,0:T(8,128)(2,1)}, u32[]{:S(2)}, u32[]{:S(2)}) collective-permute-start(bf16[16,6144]{1,0:T(8,128)(2,1)} %broadcast_select_fusion), channel_id=1, source_target_pairs={{0,0},{1,8},{2,16},{3,24},{4,1},{5,9},{6,17},{7,25},{8,2},{9,10},{... | collective-permute-start | bytes 589832 | tf_op jit(solution)/shard_map/ppermute | solution.py:174
  151.7 24.4 %all-to-all-start.2 = ((bf16[32,60,128]{2,1,0:T(8,128)(2,1)}), bf16[32,60,128]{2,1,0:T(8,128)(2,1)S(1)}, u32[]{:S(2)}, u32[]{:S(2)}) async-start(bf16[32,60,128]{2,1,0:T(8,128)(2,1)} %pad.10.clone), calls=%async_computation.2 | async-start | bytes 1048576 | tf_op jit(solution)/shard_map/all_to_all | solution.py:128
  157.6 110.7 %all-gather.6.cloned.1.call-start = ((), (), s32[]{:S(2)}) async-start(), calls=%async_computation.8 | async-start | bytes 4325376 | tf_op jit(solution)/shard_map/all_gather | solution.py:209
  180.5 40.1 %all-to-all-start.3 = ((bf16[32,128,128]{2,1,0:T(8,128)(2,1)}), bf16[32,128,128]{2,1,0:T(8,128)(2,1)S(1)}, u32[]{:S(2)}, u32[]{:S(2)}) async-start(bf16[32,128,128]{2,1,0:T(8,128)(2,1)} %broadcast_in_dim.97), calls=%async_computation.3 | async-start | bytes 2097152 | tf_op jit(solution)/shard_map/all_to_all | solution.py:71
  238.8 27.9 %all-to-all-start.5 = ((bf16[32,4,3072]{2,1,0:T(4,128)(2,1)}), bf16[32,4,3072]{2,1,0:T(4,128)(2,1)}, u32[]{:S(2)}, u32[]{:S(2)}) async-start(bf16[32,4,3072]{2,1,0:T(4,128)(2,1)} %broadcast_in_dim.98), calls=%async_computation.5 | async-start | bytes 1572864 | tf_op jit(solution)/shard_map/all_to_all | solution.py:71
  268.3 1.9 slice-start
  270.2 1.3 copy-start.3
  272.9 14.8 %all-to-all-start.6 = ((bf16[32,16,96]{2,1,0:T(8,128)(2,1)}), bf16[32,16,96]{2,1,0:T(8,128)(2,1)S(1)}, u32[]{:S(2)}, u32[]{:S(2)}) async-start(bf16[32,16,96]{2,1,0:T(8,128)(2,1)} %bitcast.55), calls=%async_computation.6 | async-start | bytes 262144 | tf_op jit(solution)/shard_map/all_to_all | solution.py:64
  280.9 17.3 %copy-start.13 = (bf16[4,6144]{1,0:T(4,128)(2,1)S(1)}, bf16[4,6144]{1,0:T(4,128)(2,1)}, u32[]{:S(2)}) copy-start(bf16[4,6144]{1,0:T(4,128)(2,1)} %param.33) | copy-start | bytes 147460
  280.9 17.4 %copy-start.10 = (f32[1,1,3072]{2,1,0:T(1,128)S(1)}, f32[1,1,3072]{2,1,0:T(1,128)}, u32[]{:S(2)}) copy-start(f32[1,1,3072]{2,1,0:T(1,128)} %get-tuple-element.46) | copy-start | bytes 36868
  280.9 39.1 %copy-start.11 = (f32[1,1,3072]{2,1,0:T(1,128)S(1)}, f32[1,1,3072]{2,1,0:T(1,128)}, u32[]{:S(2)}) copy-start(f32[1,1,3072]{2,1,0:T(1,128)} %get-tuple-element.34) | copy-start | bytes 36868
  280.9 45.0 %copy-start.18 = (f32[1,4,32]{2,1,0:T(4,128)S(1)}, f32[1,4,32]{2,1,0:T(4,128)}, u32[]{:S(2)}) copy-start(f32[1,4,32]{2,1,0:T(4,128)} %param.35) | copy-start | bytes 1540
  290.0 8.2 %copy-start.6 = (bf16[16,3072]{1,0:T(8,128)(2,1)S(1)}, bf16[16,3072]{1,0:T(8,128)(2,1)}, u32[]{:S(2)}) copy-start(bf16[16,3072]{1,0:T(8,128)(2,1)} %reshape.448) | copy-start | bytes 294916
  292.5 27.2 %all-to-all-start.7 = ((bf16[32,4,3072]{2,1,0:T(4,128)(2,1)}), bf16[32,4,3072]{2,1,0:T(4,128)(2,1)S(1)}, u32[]{:S(2)}, u32[]{:S(2)}) async-start(bf16[32,4,3072]{2,1,0:T(4,128)(2,1)} %reshape.449), calls=%async_computation.7 | async-start | bytes 1572864 | tf_op jit(solution)/shard_map/all_to_all | solution.py:240
  298.9 23.9 %collective-permute-start.5 = (bf16[16,3072]{1,0:T(8,128)(2,1)}, bf16[16,3072]{1,0:T(8,128)(2,1)S(1)}, u32[]{:S(2)}, u32[]{:S(2)}) collective-permute-start(bf16[16,3072]{1,0:T(8,128)(2,1)} %fusion.53), channel_id=1, source_target_pairs={{128,0},{0,128},{129,1},{1,129},{130,2},{2,130},{131,3},{3,131},{1... | collective-permute-start | bytes 294920 | tf_op jit(solution)/shard_map/ppermute | solution.py:20
  320.0 5.4 %collective-permute-start.4 = (bf16[4,3072]{1,0:T(4,128)(2,1)S(1)}, bf16[4,3072]{1,0:T(4,128)(2,1)S(1)}, u32[]{:S(2)}, u32[]{:S(2)}) collective-permute-start(bf16[4,3072]{1,0:T(4,128)(2,1)S(1)} %add_convert_fusion), channel_id=1, source_target_pairs={{128,0},{0,128},{129,1},{1,129},{130,2},{2,130},{131,3},{3,131},{1... | collective-permute-start | bytes 73736 | tf_op jit(solution)/shard_map/ppermute | solution.py:20
  (3 other events, 2.7 us)
Sparse Core Ops, SparseCore 0:
  33.1 67.4 all-gather.7
  179.3 74.7 all-gather.5

commit v12 on v11

--- a/solution.py
+++ b/solution.py
@@ -218,11 +218,8 @@
     image_back = cols_to_rows(
         from_heads(image_heads, image_from_heads[0]).reshape(devices, image_rows, -1)
     )
-    text_back = cols_to_rows(
-        from_heads(text_heads, text_from_heads[0]).reshape(devices, text_rows, -1)
-    )
+    text_back_cols = from_heads(text_heads, text_from_heads[0]).reshape(devices, -1)
     image_mid = image_x + modul[2] * image_back.astype(jnp.float32)
-    text_out = (text_x + text_mod[2] * text_back.astype(jnp.float32)).astype(jnp.bfloat16)
     mlp_normed = modulate(image_mid, modul[3], modul[4]).astype(jnp.bfloat16)
     up_weight = image_up[0]
     down_weight = image_down[0]
@@ -235,17 +232,21 @@
         approximate=True,
     ).astype(jnp.bfloat16)
     partial = jnp.dot(hidden, down_weight, preferred_element_type=jnp.float32)
-    partial, text_back = lax.optimization_barrier((partial, text_back))
+    sums = partial.astype(jnp.bfloat16).reshape(devices, -1)
+    both = lax.all_to_all(
+        jnp.concatenate([sums, text_back_cols], axis=1),
+        TOK,
+        split_axis=0,
+        concat_axis=0,
+        tiled=True,
+    )
     reduced = jnp.sum(
-        lax.all_to_all(
-            partial.astype(jnp.bfloat16).reshape(devices, image_rows, width),
-            TOK,
-            split_axis=0,
-            concat_axis=0,
-            tiled=True,
-        ).astype(jnp.float32),
-        axis=0,
-    )
+        both[:, : sums.shape[1]].reshape(devices, image_rows, width).astype(jnp.float32), axis=0
+    )
+    text_back = jnp.transpose(
+        both[:, sums.shape[1] :].reshape(devices, text_rows, -1), (1, 0, 2)
+    ).reshape(text_rows, width)
+    text_out = (text_x + text_mod[2] * text_back.astype(jnp.float32)).astype(jnp.bfloat16)
     image_out = (image_mid + modul[5] * reduced).astype(jnp.bfloat16)
     text_next = from_behind(text_out, "section", 1)
     image_next = from_behind(image_out, "section", 1)

time: 337 us -> 341 us (1.012)
  local copies, waits for them, and re-layouts: 33.1 us -> 40.5 us
  starting transfers between devices: 50.2 us -> 43.4 us
    unnamed x59 -> x62, local copies, waits for them, and re-layouts: 9.68 us -> 17.7 us
    all_to_all x2 -> x1, waiting for transfers between devices: 21.8 us -> 15.6 us  [cols_to_rows(): got = lax.all_to_all(cols, TOK, split_axis=0, concat_axis=0, tiled=True)]
    all_to_all x1, waiting for transfers between devices: 18 us -> 23.6 us  [shards(): lax.all_to_all(jnp.concatenate([sums, text_back_cols], axis=1), TOK, spli...]
    all_to_all x2 -> x1, starting transfers between devices: 10.5 us -> 6.21 us  [cols_to_rows(): got = lax.all_to_all(cols, TOK, split_axis=0, concat_axis=0, tiled=True)]
  transfers between devices with their start and end apart: 15 -> 14, of which waited for: 9 -> 9; matrix products, arithmetic and copies ran while one was open for 10% -> 11% of each run, Pallas kernels for 0% -> 0%
where the time goes in v12:
time: 341 us; the launch traced here: 339 us
  waiting for transfers between devices  184 us (54%)
  starting transfers between devices  43.4 us (13%)
  local copies, waits for them, and re-layouts  40.5 us (12%)
  between operations  24.2 us (7%)
  matrix products  18.1 us (5%)
  other arithmetic  15.5 us (5%)
  blocking collectives  13.3 us (4%)
    all_gather x1, waiting for transfers between devices, shards(): lax.all_gather(jnp.concatenate([image_normed, text_normed], axis=0), TOK,...  66.2 us
    all_to_all x2, waiting for transfers between devices, broadcast_rows(): got = lax.all_to_all(copies, TOK, split_axis=0, concat_axis=0, tiled=True)  54.9 us
    all_to_all x1, waiting for transfers between devices, shards(): lax.all_to_all(jnp.concatenate([sums, text_back_cols], axis=1), TOK, spli...  23.6 us
    all_to_all x2, waiting for transfers between devices, by_head(): return lax.all_to_all(pack, TOK, split_axis=0, concat_axis=0, tiled=True)  19.1 us
    unnamed x62, local copies, waits for them, and re-layouts  17.7 us
    all_to_all x2, starting transfers between devices, by_head(): return lax.all_to_all(pack, TOK, split_axis=0, concat_axis=0, tiled=True)  15.8 us
    all_to_all x1, waiting for transfers between devices, cols_to_rows(): got = lax.all_to_all(cols, TOK, split_axis=0, concat_axis=0, tiled=True)  15.6 us
    all_to_all x1, blocking collectives, cols_to_rows(): got = lax.all_to_all(cols, TOK, split_axis=0, concat_axis=0, tiled=True)  13.3 us
  transfers between devices with their start and end apart: 14, of which 9 were waited for; matrix products, arithmetic and copies ran while one was open for 11% of the time, Pallas kernels for 0%

profile of v12, /device:TPU:2, one launch (start us, length us, event | category | flops | bytes accessed | tf_op | source)
XLA Modules:
  0.0 338.7 jit_solution(14529360220003753941)
XLA Ops:
  9.2 9.9 %all-to-all-start = ((bf16[32,32,128]{2,1,0:T(8,128)(2,1)}), bf16[32,32,128]{2,1,0:T(8,128)(2,1)S(1)}, u32[]{:S(2)}, u32[]{:S(2)}) async-start(bf16[32,32,128]{2,1,0:T(8,128)(2,1)} %pad.9.clone), calls=%async_computation | async-start | bytes 524288 | tf_op jit(solution)/shard_map/all_to_all | solution.py:128
  30.8 1.4 all-to-all-done
  34.3 66.2 %all-gather.8.cloned.1.call-done = bf16[32,20,3072]{2,1,0:T(8,128)(2,1)} async-done(((bf16[1,20,3072]{2,1,0:T(8,128)(2,1)}), bf16[32,20,3072]{2,1,0:T(8,128)(2,1)}) %all-gather.8.cloned.1.call-update) | async-done | bytes 3932176 | tf_op jit(solution)/shard_map/all_gather | solution.py:134
  100.5 5.7 %fusion.6 = bf16[32,20,288]{2,1,0:T(8,128)(2,1)S(1)} fusion(bf16[32,20,3072]{2,1,0:T(8,128)(2,1)} %all-gather.8.cloned.1.call-done, bf16[1,3072,288]{1,2,0:T(8,128)(2,1)} %param.26), kind=kOutput, calls=%fused_computation.10 | convolution fusion | flops 1132462080 | bytes 6070272 | tf_op jit(solution)/shard_map/dot_general | solution.py:139
  106.2 3.5 %fusion.13 = bf16[32,20,288]{2,1,0:T(8,128)(2,1)} fusion(bf16[32,20,288]{2,1,0:T(8,128)(2,1)S(1)} %fusion.6, bf16[32,20,3072]{2,1,0:T(8,128)(2,1)S(1)} %copy-done.15, bf16[1,3072,288]{1,2,0:T(8,128)(2,1)S(1)} %copy-done.16, pred[20]{0:T(512)(128)(4,1)S(1)} %iota_compare_fusion.1), kind=kOutput, calls=%fused_computation.16 | convolution fusion | flops 1132646400 | bytes 6438932 | tf_op jit(solution)/shard_map/dot_general | solution.py:138
  109.7 6.2 %all-to-all-start.1 = ((bf16[32,20,288]{2,1,0:T(8,128)(2,1)}), bf16[32,20,288]{2,1,0:T(8,128)(2,1)S(1)}, u32[]{:S(2)}, u32[]{:S(2)}) async-start(bf16[32,20,288]{2,1,0:T(8,128)(2,1)} %fusion.13), calls=%async_computation.1 | async-start | bytes 1179648 | tf_op jit(solution)/shard_map/all_to_all | solution.py:64
  119.9 15.6 %all-to-all-done.1 = bf16[32,20,288]{2,1,0:T(8,128)(2,1)S(1)} async-done(((bf16[32,20,288]{2,1,0:T(8,128)(2,1)}), bf16[32,20,288]{2,1,0:T(8,128)(2,1)S(1)}, u32[]{:S(2)}, u32[]{:S(2)}) %all-to-all-start.1) | async-done | bytes 368672 | tf_op jit(solution)/shard_map/all_to_all | solution.py:64
  138.2 1.4 collective-permute-start.1
  146.7 3.0 collective-permute-start.3
  152.3 5.9 %all-to-all-start.2 = ((bf16[32,60,128]{2,1,0:T(8,128)(2,1)}), bf16[32,60,128]{2,1,0:T(8,128)(2,1)S(1)}, u32[]{:S(2)}, u32[]{:S(2)}) async-start(bf16[32,60,128]{2,1,0:T(8,128)(2,1)} %pad.10.clone), calls=%async_computation.2 | async-start | bytes 1048576 | tf_op jit(solution)/shard_map/all_to_all | solution.py:128
  159.0 17.7 %all-to-all-done.2 = bf16[32,60,128]{2,1,0:T(8,128)(2,1)S(1)} async-done(((bf16[32,60,128]{2,1,0:T(8,128)(2,1)}), bf16[32,60,128]{2,1,0:T(8,128)(2,1)S(1)}, u32[]{:S(2)}, u32[]{:S(2)}) %all-to-all-start.2) | async-done | bytes 491552 | tf_op jit(solution)/shard_map/all_to_all | solution.py:128
  177.4 1.5 fusion.3
  182.5 3.9 %all-to-all-start.3 = ((bf16[32,128,128]{2,1,0:T(8,128)(2,1)}), bf16[32,128,128]{2,1,0:T(8,128)(2,1)S(1)}, u32[]{:S(2)}, u32[]{:S(2)}) async-start(bf16[32,128,128]{2,1,0:T(8,128)(2,1)} %broadcast_in_dim.97), calls=%async_computation.3 | async-start | bytes 2097152 | tf_op jit(solution)/shard_map/all_to_all | solution.py:71
  186.5 2.0 copy.94
  188.5 34.2 %all-to-all-done.3 = bf16[32,128,128]{2,1,0:T(8,128)(2,1)S(1)} async-done(((bf16[32,128,128]{2,1,0:T(8,128)(2,1)}), bf16[32,128,128]{2,1,0:T(8,128)(2,1)S(1)}, u32[]{:S(2)}, u32[]{:S(2)}) %all-to-all-start.3) | async-done | bytes 1048608 | tf_op jit(solution)/shard_map/all_to_all | solution.py:71
  222.7 1.4 fusion.24
  224.3 13.3 %all_to_all.42 = bf16[32,4,96]{2,1,0:T(4,128)(2,1)S(1)} all-to-all(bf16[32,4,96]{2,1,0:T(4,128)(2,1)S(1)} %bitcast.292), channel_id=1, replica_groups=mesh['section'=2,'grp'=4,'ta'=8,'tb'=4] {'ta','tb'}, dimensions={0} | all-to-all | bytes 49152 | tf_op jit(solution)/shard_map/all_to_all | solution.py:64
  240.7 4.6 %all-to-all-start.5 = ((bf16[32,4,3072]{2,1,0:T(4,128)(2,1)}), bf16[32,4,3072]{2,1,0:T(4,128)(2,1)}, u32[]{:S(2)}, u32[]{:S(2)}) async-start(bf16[32,4,3072]{2,1,0:T(4,128)(2,1)} %broadcast_in_dim.98), calls=%async_computation.5 | async-start | bytes 1572864 | tf_op jit(solution)/shard_map/all_to_all | solution.py:71
  246.5 1.5 copy.72
  248.0 20.6 %all-to-all-done.5 = bf16[32,4,3072]{2,1,0:T(4,128)(2,1)} async-done(((bf16[32,4,3072]{2,1,0:T(4,128)(2,1)}), bf16[32,4,3072]{2,1,0:T(4,128)(2,1)}, u32[]{:S(2)}, u32[]{:S(2)}) %all-to-all-start.5) | async-done | bytes 786464 | tf_op jit(solution)/shard_map/all_to_all | solution.py:71
  268.6 1.6 reshape.453
  270.2 3.7 %convolution_convert_fusion = bf16[128,3072]{1,0:T(8,128)(2,1)} fusion(bf16[1,384,3072]{2,1,0:T(8,128)(2,1)S(1)} %copy-done, bf16[128,3072]{1,0:T(8,128)(2,1)S(1)} %reshape.453, bf16[1,3072,384]{2,1,0:T(8,128)(2,1)} %param.30), kind=kOutput, calls=%fused_computation.1 | convolution fusion | flops 604815360 | bytes 6291456 | tf_op jit(solution)/shard_map/dot_general | solution.py:234
  273.9 2.5 reshape.454
  276.4 1.9 slice-done
  282.2 2.0 reduce.7
  284.2 3.1 reshape.477
  287.3 4.4 %all-to-all-start.6 = ((bf16[32,2,6912]{2,1,0:T(2,128)(2,1)}), bf16[32,2,6912]{2,1,0:T(2,128)(2,1)S(1)}, u32[]{:S(2)}, u32[]{:S(2)}) async-start(bf16[32,2,6912]{2,1,0:T(2,128)(2,1)} %reshape.477), calls=%async_computation.6 | async-start | bytes 1769472 | tf_op jit(solution)/shard_map/all_to_all | solution.py:236
  293.4 23.6 %all-to-all-done.6 = bf16[32,2,6912]{2,1,0:T(2,128)(2,1)S(1)} async-done(((bf16[32,2,6912]{2,1,0:T(2,128)(2,1)}), bf16[32,2,6912]{2,1,0:T(2,128)(2,1)S(1)}, u32[]{:S(2)}, u32[]{:S(2)}) %all-to-all-start.6) | async-done | bytes 884768 | tf_op jit(solution)/shard_map/all_to_all | solution.py:236
  316.9 2.1 reshape.478
  319.0 1.6 copy.114
  320.9 3.0 collective-permute-start.4
  327.6 3.0 collective-permute-done.5
  (173 shorter events, 42.4 us)
Async XLA Ops:
  7.2 263.0 %copy-start = (bf16[1,384,3072]{2,1,0:T(8,128)(2,1)S(1)}, bf16[1,384,3072]{2,1,0:T(8,128)(2,1)}, u32[]{:S(2)}) copy-start(bf16[1,384,3072]{2,1,0:T(8,128)(2,1)} %param.31) | copy-start | bytes 7077892
  7.2 20.4 %copy-start.10 = (bf16[1,4,18432]{2,1,0:T(4,128)(2,1)S(1)}, bf16[1,4,18432]{2,1,0:T(4,128)(2,1)}, u32[]{:S(2)}) copy-start(bf16[1,4,18432]{2,1,0:T(4,128)(2,1)} %param.23) | copy-start | bytes 442372
  7.2 21.1 %copy-start.5 = (bf16[1,1,4,3072]{3,2,1,0:T(4,128)(2,1)S(1)}, bf16[1,1,4,3072]{3,2,1,0:T(4,128)(2,1)}, u32[]{:S(2)}) copy-start(bf16[1,1,4,3072]{3,2,1,0:T(4,128)(2,1)} %param.18) | copy-start | bytes 73732
  7.2 23.0 %copy-start.1 = (bf16[1,1,16,3072]{3,2,1,0:T(8,128)(2,1)S(1)}, bf16[1,1,16,3072]{3,2,1,0:T(8,128)(2,1)}, u32[]{:S(2)}) copy-start(bf16[1,1,16,3072]{3,2,1,0:T(8,128)(2,1)} %param.19) | copy-start | bytes 294916
  7.2 27.0 %copy-start.13 = (f32[1,4,128]{2,1,0:T(4,128)S(1)}, f32[1,4,128]{2,1,0:T(4,128)}, u32[]{:S(2)}) copy-start(f32[1,4,128]{2,1,0:T(4,128)} %param.27) | copy-start | bytes 6148
  9.2 23.1 %all-to-all-start = ((bf16[32,32,128]{2,1,0:T(8,128)(2,1)}), bf16[32,32,128]{2,1,0:T(8,128)(2,1)S(1)}, u32[]{:S(2)}, u32[]{:S(2)}) async-start(bf16[32,32,128]{2,1,0:T(8,128)(2,1)} %pad.9.clone), calls=%async_computation | async-start | bytes 524288 | tf_op jit(solution)/shard_map/all_to_all | solution.py:128
  19.0 81.4 %all-gather.8.cloned.1.call-start = ((), (), s32[]{:S(2)}) async-start(), calls=%async_computation.8 | async-start | bytes 4866048 | tf_op jit(solution)/shard_map/all_gather | solution.py:134
  100.5 5.7 %copy-start.15 = (bf16[32,20,3072]{2,1,0:T(8,128)(2,1)S(1)}, bf16[32,20,3072]{2,1,0:T(8,128)(2,1)}, u32[]{:S(2)}) copy-start(bf16[32,20,3072]{2,1,0:T(8,128)(2,1)} %all-gather.8.cloned.1.call-done) | copy-start | bytes 11796484
  100.5 5.7 %copy-start.16 = (bf16[1,3072,288]{1,2,0:T(8,128)(2,1)S(1)}, bf16[1,3072,288]{1,2,0:T(8,128)(2,1)}, u32[]{:S(2)}) copy-start(bf16[1,3072,288]{1,2,0:T(8,128)(2,1)} %param.25) | copy-start | bytes 5308420
  109.7 25.8 %all-to-all-start.1 = ((bf16[32,20,288]{2,1,0:T(8,128)(2,1)}), bf16[32,20,288]{2,1,0:T(8,128)(2,1)S(1)}, u32[]{:S(2)}, u32[]{:S(2)}) async-start(bf16[32,20,288]{2,1,0:T(8,128)(2,1)} %fusion.13), calls=%async_computation.1 | async-start | bytes 1179648 | tf_op jit(solution)/shard_map/all_to_all | solution.py:64
  137.5 4.4 %copy-start.4 = (bf16[16,3072]{1,0:T(8,128)(2,1)S(1)}, bf16[16,3072]{1,0:T(8,128)(2,1)}, u32[]{:S(2)}) copy-start(bf16[16,3072]{1,0:T(8,128)(2,1)} %slice.237) | copy-start | bytes 294916
  137.5 8.4 %copy-start.14 = (pred[16]{0:T(512)(128)(4,1)S(1)}, pred[16]{0:T(512)(128)(4,1)}, u32[]{:S(2)}) copy-start(pred[16]{0:T(512)(128)(4,1)} %broadcast_in_dim.90) | copy-start | bytes 52
  138.2 5.7 %collective-permute-start.2 = (bf16[4,6144]{1,0:T(4,128)(2,1)}, bf16[4,6144]{1,0:T(4,128)(2,1)}, u32[]{:S(2)}, u32[]{:S(2)}) collective-permute-start(bf16[4,6144]{1,0:T(4,128)(2,1)} %get-tuple-element.43), channel_id=1, source_target_pairs={{0,3},{1,0},{2,1},{3,2},{4,7},{5,4},{6,5},{7,6},{8,11},{9,8},{10,9... | collective-permute-start | bytes 147464 | tf_op jit(solution)/shard_map/ppermute | solution.py:170
  138.2 5.8 %collective-permute-start.1 = (bf16[4,6144]{1,0:T(4,128)(2,1)}, bf16[4,6144]{1,0:T(4,128)(2,1)}, u32[]{:S(2)}, u32[]{:S(2)}) collective-permute-start(bf16[4,6144]{1,0:T(4,128)(2,1)} %get-tuple-element.43), channel_id=1, source_target_pairs={{0,2},{1,3},{2,0},{3,1},{4,6},{5,7},{6,4},{7,5},{8,10},{9,11},{10,... | collective-permute-start | bytes 147464 | tf_op jit(solution)/shard_map/ppermute | solution.py:170
  139.6 4.3 %collective-permute-start = (bf16[4,6144]{1,0:T(4,128)(2,1)}, bf16[4,6144]{1,0:T(4,128)(2,1)}, u32[]{:S(2)}, u32[]{:S(2)}) collective-permute-start(bf16[4,6144]{1,0:T(4,128)(2,1)} %get-tuple-element.43), channel_id=1, source_target_pairs={{0,1},{1,2},{2,3},{3,0},{4,5},{5,6},{6,7},{7,4},{8,9},{9,10},{10,1... | collective-permute-start | bytes 147464 | tf_op jit(solution)/shard_map/ppermute | solution.py:170
  140.8 3.2 copy-start.6
  142.0 16.3 %copy-start.2 = (bf16[1,1,16,6144]{3,2,1,0:T(8,128)(2,1)S(1)}, bf16[1,1,16,6144]{3,2,1,0:T(8,128)(2,1)}, u32[]{:S(2)}) copy-start(bf16[1,1,16,6144]{3,2,1,0:T(8,128)(2,1)} %param.32) | copy-start | bytes 589828
  145.8 31.6 %copy-start.7 = (bf16[32,16,128]{2,1,0:T(8,128)(2,1)S(1)}, bf16[32,16,128]{2,1,0:T(8,128)(2,1)}, u32[]{:S(2)}) copy-start(bf16[32,16,128]{2,1,0:T(8,128)(2,1)} %get-tuple-element.28) | copy-start | bytes 393220
  145.9 31.5 %copy-start.12 = (pred[1024]{0:T(1024)(128)(4,1)S(1)}, pred[1024]{0:T(1024)(128)(4,1)}, u32[]{:S(2)}) copy-start(pred[1024]{0:T(1024)(128)(4,1)} %concatenate.53) | copy-start | bytes 3076
  146.7 11.6 %collective-permute-start.3 = (bf16[16,6144]{1,0:T(8,128)(2,1)}, bf16[16,6144]{1,0:T(8,128)(2,1)}, u32[]{:S(2)}, u32[]{:S(2)}) collective-permute-start(bf16[16,6144]{1,0:T(8,128)(2,1)} %broadcast_select_fusion), channel_id=1, source_target_pairs={{0,0},{1,8},{2,16},{3,24},{4,1},{5,9},{6,17},{7,25},{8,2},{9,10},{... | collective-permute-start | bytes 589832 | tf_op jit(solution)/shard_map/ppermute | solution.py:174
  152.3 24.3 %all-to-all-start.2 = ((bf16[32,60,128]{2,1,0:T(8,128)(2,1)}), bf16[32,60,128]{2,1,0:T(8,128)(2,1)S(1)}, u32[]{:S(2)}, u32[]{:S(2)}) async-start(bf16[32,60,128]{2,1,0:T(8,128)(2,1)} %pad.10.clone), calls=%async_computation.2 | async-start | bytes 1048576 | tf_op jit(solution)/shard_map/all_to_all | solution.py:128
  158.2 118.2 %all-gather.6.cloned.1.call-start = ((), (), s32[]{:S(2)}) async-start(), calls=%async_computation.7 | async-start | bytes 4325376 | tf_op jit(solution)/shard_map/all_gather | solution.py:209
  182.5 40.2 %all-to-all-start.3 = ((bf16[32,128,128]{2,1,0:T(8,128)(2,1)}), bf16[32,128,128]{2,1,0:T(8,128)(2,1)S(1)}, u32[]{:S(2)}, u32[]{:S(2)}) async-start(bf16[32,128,128]{2,1,0:T(8,128)(2,1)} %broadcast_in_dim.97), calls=%async_computation.3 | async-start | bytes 2097152 | tf_op jit(solution)/shard_map/all_to_all | solution.py:71
  240.7 27.9 %all-to-all-start.5 = ((bf16[32,4,3072]{2,1,0:T(4,128)(2,1)}), bf16[32,4,3072]{2,1,0:T(4,128)(2,1)}, u32[]{:S(2)}, u32[]{:S(2)}) async-start(bf16[32,4,3072]{2,1,0:T(4,128)(2,1)} %broadcast_in_dim.98), calls=%async_computation.5 | async-start | bytes 1572864 | tf_op jit(solution)/shard_map/all_to_all | solution.py:71
  282.2 11.2 %copy-start.11 = (bf16[4,6144]{1,0:T(4,128)(2,1)S(1)}, bf16[4,6144]{1,0:T(4,128)(2,1)}, u32[]{:S(2)}) copy-start(bf16[4,6144]{1,0:T(4,128)(2,1)} %param.33) | copy-start | bytes 147460
  287.3 29.6 %all-to-all-start.6 = ((bf16[32,2,6912]{2,1,0:T(2,128)(2,1)}), bf16[32,2,6912]{2,1,0:T(2,128)(2,1)S(1)}, u32[]{:S(2)}, u32[]{:S(2)}) async-start(bf16[32,2,6912]{2,1,0:T(2,128)(2,1)} %reshape.477), calls=%async_computation.6 | async-start | bytes 1769472 | tf_op jit(solution)/shard_map/all_to_all | solution.py:236
  293.4 27.5 %copy-start.9 = (f32[1,1,3072]{2,1,0:T(1,128)S(1)}, f32[1,1,3072]{2,1,0:T(1,128)}, u32[]{:S(2)}) copy-start(f32[1,1,3072]{2,1,0:T(1,128)} %get-tuple-element.32) | copy-start | bytes 36868
  319.0 5.3 %copy-start.8 = (f32[1,1,3072]{2,1,0:T(1,128)S(1)}, f32[1,1,3072]{2,1,0:T(1,128)}, u32[]{:S(2)}) copy-start(f32[1,1,3072]{2,1,0:T(1,128)} %get-tuple-element.44) | copy-start | bytes 36868
  319.0 7.7 %copy-start.17 = (bf16[3072,32]{0,1:T(8,128)(2,1)S(1)}, bf16[3072,32]{0,1:T(8,128)(2,1)}, u32[]{:S(2)}) copy-start(bf16[3072,32]{0,1:T(8,128)(2,1)} %param.34) | copy-start | bytes 589828
  319.0 7.7 %copy-start.18 = (f32[1,4,32]{2,1,0:T(4,128)S(1)}, f32[1,4,32]{2,1,0:T(4,128)}, u32[]{:S(2)}) copy-start(f32[1,4,32]{2,1,0:T(4,128)} %param.35) | copy-start | bytes 1540
  320.9 5.4 %collective-permute-start.4 = (bf16[4,3072]{1,0:T(4,128)(2,1)S(1)}, bf16[4,3072]{1,0:T(4,128)(2,1)S(1)}, u32[]{:S(2)}, u32[]{:S(2)}) collective-permute-start(bf16[4,3072]{1,0:T(4,128)(2,1)S(1)} %add_convert_fusion), channel_id=1, source_target_pairs={{128,0},{0,128},{129,1},{1,129},{130,2},{2,130},{131,3},{3,131},{1... | collective-permute-start | bytes 73736 | tf_op jit(solution)/shard_map/ppermute | solution.py:20
  324.4 6.2 %collective-permute-start.5 = (bf16[16,3072]{1,0:T(8,128)(2,1)S(1)}, bf16[16,3072]{1,0:T(8,128)(2,1)S(1)}, u32[]{:S(2)}, u32[]{:S(2)}) collective-permute-start(bf16[16,3072]{1,0:T(8,128)(2,1)S(1)} %fusion.52), channel_id=1, source_target_pairs={{128,0},{0,128},{129,1},{1,129},{130,2},{2,130},{131,3},{3,131},{1... | collective-permute-start | bytes 294920 | tf_op jit(solution)/shard_map/ppermute | solution.py:20
  (2 other events, 3.2 us)
Sparse Core Ops, SparseCore 0:
  33.1 67.3 all-gather.7
  181.3 76.1 all-gather.5

commit v13 on v11

--- a/solution.py
+++ b/solution.py
@@ -131,18 +131,17 @@
     got_cache, image_normed, text_normed = lax.optimization_barrier(
         (got_cache, image_normed, text_normed)
     )
-    every = lax.all_gather(
-        jnp.concatenate([image_normed, text_normed], axis=0), TOK, axis=0, tiled=False
-    )
-    flat = every.reshape(-1, width)
-    image_cols = jnp.dot(flat, image_to_heads[0], preferred_element_type=jnp.float32)
-    text_cols = jnp.dot(flat, text_to_heads[0], preferred_element_type=jnp.float32)
-    is_image = (jnp.arange(image_rows + text_rows) < image_rows)[None, :, None]
+    every_text = lax.all_gather(text_normed, TOK, axis=0, tiled=True)
+    every_image = broadcast_rows(image_normed, devices)
+    image_cols = jnp.dot(every_image, image_to_heads[0], preferred_element_type=jnp.float32)
+    text_cols = jnp.dot(every_text, text_to_heads[0], preferred_element_type=jnp.float32)
     proj = cols_to_rows(
-        jnp.where(
-            is_image,
-            image_cols.reshape(devices, image_rows + text_rows, -1),
-            text_cols.reshape(devices, image_rows + text_rows, -1),
+        jnp.concatenate(
+            [
+                image_cols.reshape(devices, image_rows, -1),
+                text_cols.reshape(devices, text_rows, -1),
+            ],
+            axis=1,
         ).astype(jnp.bfloat16)
     )
     image_proj = proj[:image_rows]

time: 337 us -> 337 us (level)
  waiting for transfers between devices: 183 us -> 175 us
  starting transfers between devices: 50.2 us -> 57.1 us
    all_gather x1, waiting for transfers between devices: 66.3 us -> 31.5 us  [shards(): every_text = lax.all_gather(text_normed, TOK, axis=0, tiled=True)]
    all_to_all x2 -> x3, waiting for transfers between devices: 54.9 us -> 82 us  [broadcast_rows(): got = lax.all_to_all(copies, TOK, split_axis=0, concat_axis=0, tiled=True)]
    all_to_all x2 -> x3, starting transfers between devices: 8.55 us -> 15.4 us  [broadcast_rows(): got = lax.all_to_all(copies, TOK, split_axis=0, concat_axis=0, tiled=True)]
    unnamed x59 -> x61, local copies, waits for them, and re-layouts: 9.68 us -> 10.4 us
  transfers between devices with their start and end apart: 15 -> 16, of which waited for: 9 -> 10; matrix products, arithmetic and copies ran while one was open for 10% -> 11% of each run, Pallas kernels for 0% -> 0%
where the time goes in v13:
time: 337 us; the launch traced here: 334 us
  waiting for transfers between devices  175 us (52%)
  starting transfers between devices  57.1 us (17%)
  local copies, waits for them, and re-layouts  34.6 us (10%)
  between operations  24.7 us (7%)
  matrix products  15.7 us (5%)
  other arithmetic  14.5 us (4%)
  blocking collectives  13.1 us (4%)
    all_to_all x3, waiting for transfers between devices, broadcast_rows(): got = lax.all_to_all(copies, TOK, split_axis=0, concat_axis=0, tiled=True)  82 us
    all_gather x1, waiting for transfers between devices, shards(): every_text = lax.all_gather(text_normed, TOK, axis=0, tiled=True)  31.5 us
    all_to_all x2, waiting for transfers between devices, cols_to_rows(): got = lax.all_to_all(cols, TOK, split_axis=0, concat_axis=0, tiled=True)  22.3 us
    all_to_all x2, waiting for transfers between devices, by_head(): return lax.all_to_all(pack, TOK, split_axis=0, concat_axis=0, tiled=True)  19.1 us
    all_to_all x1, waiting for transfers between devices, shards(): lax.all_to_all(partial.astype(jnp.bfloat16).reshape(devices, image_rows,...  17.5 us
    all_to_all x2, starting transfers between devices, by_head(): return lax.all_to_all(pack, TOK, split_axis=0, concat_axis=0, tiled=True)  15.8 us
    all_to_all x3, starting transfers between devices, broadcast_rows(): got = lax.all_to_all(copies, TOK, split_axis=0, concat_axis=0, tiled=True)  15.4 us
    all_to_all x1, blocking collectives, cols_to_rows(): got = lax.all_to_all(cols, TOK, split_axis=0, concat_axis=0, tiled=True)  13.1 us
  transfers between devices with their start and end apart: 16, of which 10 were waited for; matrix products, arithmetic and copies ran while one was open for 11% of the time, Pallas kernels for 0%

profile of v13, /device:TPU:2, one launch (start us, length us, event | category | flops | bytes accessed | tf_op | source)
XLA Modules:
  0.0 334.5 jit_solution(8781687223198665789)
XLA Ops:
  9.2 9.9 %all-to-all-start = ((bf16[32,32,128]{2,1,0:T(8,128)(2,1)}), bf16[32,32,128]{2,1,0:T(8,128)(2,1)S(1)}, u32[]{:S(2)}, u32[]{:S(2)}) async-start(bf16[32,32,128]{2,1,0:T(8,128)(2,1)} %pad.9.clone), calls=%async_computation | async-start | bytes 524288 | tf_op jit(solution)/shard_map/all_to_all | solution.py:128
  30.6 1.6 all-to-all-done
  33.3 6.8 %all-to-all-start.1 = ((bf16[32,4,3072]{2,1,0:T(4,128)(2,1)}), bf16[32,4,3072]{2,1,0:T(4,128)(2,1)}, u32[]{:S(2)}, u32[]{:S(2)}) async-start(bf16[32,4,3072]{2,1,0:T(4,128)(2,1)} %broadcast_in_dim.48), calls=%async_computation.1 | async-start | bytes 1572864 | tf_op jit(solution)/shard_map/all_to_all | solution.py:71
  41.5 26.7 %all-to-all-done.1 = bf16[32,4,3072]{2,1,0:T(4,128)(2,1)} async-done(((bf16[32,4,3072]{2,1,0:T(4,128)(2,1)}), bf16[32,4,3072]{2,1,0:T(4,128)(2,1)}, u32[]{:S(2)}, u32[]{:S(2)}) %all-to-all-start.1) | async-done | bytes 786464 | tf_op jit(solution)/shard_map/all_to_all | solution.py:71
  68.2 2.6 fusion.22
  70.8 31.5 %all-gather.4.cloned.1.call-done = bf16[512,3072]{1,0:T(8,128)(2,1)} async-done(((bf16[16,3072]{1,0:T(8,128)(2,1)}), bf16[512,3072]{1,0:T(8,128)(2,1)}) %all-gather.4.cloned.1.call-update) | async-done | bytes 3145744 | tf_op jit(solution)/shard_map/all_gather | solution.py:134
  102.4 4.2 %fusion.15 = bf16[32,16,288]{2,1,0:T(8,128)(2,1)S(1)} fusion(bf16[32,16,3072]{2,1,0:T(8,128)(2,1)} %bitcast.306, bf16[1,3072,288]{1,2,0:T(8,128)(2,1)} %param.26), kind=kOutput, calls=%fused_computation.18 | convolution fusion | flops 906117120 | bytes 5210112 | tf_op jit(solution)/shard_map/dot_general | solution.py:137
  107.7 5.6 %all-to-all-start.2 = ((bf16[32,20,288]{2,1,0:T(8,128)(2,1)}), bf16[32,20,288]{2,1,0:T(8,128)(2,1)S(1)}, u32[]{:S(2)}, u32[]{:S(2)}) async-start(bf16[32,20,288]{2,1,0:T(8,128)(2,1)} %pad_maximum_fusion), calls=%async_computation.2 | async-start | bytes 1179648 | tf_op jit(solution)/shard_map/all_to_all | solution.py:64
  117.2 15.6 %all-to-all-done.2 = bf16[32,20,288]{2,1,0:T(8,128)(2,1)S(1)} async-done(((bf16[32,20,288]{2,1,0:T(8,128)(2,1)}), bf16[32,20,288]{2,1,0:T(8,128)(2,1)S(1)}, u32[]{:S(2)}, u32[]{:S(2)}) %all-to-all-start.2) | async-done | bytes 368672 | tf_op jit(solution)/shard_map/all_to_all | solution.py:64
  134.7 1.5 collective-permute-start.1
  144.9 3.0 collective-permute-start.3
  150.5 5.9 %all-to-all-start.3 = ((bf16[32,60,128]{2,1,0:T(8,128)(2,1)}), bf16[32,60,128]{2,1,0:T(8,128)(2,1)S(1)}, u32[]{:S(2)}, u32[]{:S(2)}) async-start(bf16[32,60,128]{2,1,0:T(8,128)(2,1)} %pad.10.clone), calls=%async_computation.3 | async-start | bytes 1048576 | tf_op jit(solution)/shard_map/all_to_all | solution.py:128
  157.4 17.5 %all-to-all-done.3 = bf16[32,60,128]{2,1,0:T(8,128)(2,1)S(1)} async-done(((bf16[32,60,128]{2,1,0:T(8,128)(2,1)}), bf16[32,60,128]{2,1,0:T(8,128)(2,1)S(1)}, u32[]{:S(2)}, u32[]{:S(2)}) %all-to-all-start.3) | async-done | bytes 491552 | tf_op jit(solution)/shard_map/all_to_all | solution.py:128
  179.3 3.9 %all-to-all-start.4 = ((bf16[32,128,128]{2,1,0:T(8,128)(2,1)}), bf16[32,128,128]{2,1,0:T(8,128)(2,1)S(1)}, u32[]{:S(2)}, u32[]{:S(2)}) async-start(bf16[32,128,128]{2,1,0:T(8,128)(2,1)} %broadcast_in_dim.94), calls=%async_computation.4 | async-start | bytes 2097152 | tf_op jit(solution)/shard_map/all_to_all | solution.py:71
  183.2 2.0 copy.88
  185.2 34.4 %all-to-all-done.4 = bf16[32,128,128]{2,1,0:T(8,128)(2,1)S(1)} async-done(((bf16[32,128,128]{2,1,0:T(8,128)(2,1)}), bf16[32,128,128]{2,1,0:T(8,128)(2,1)S(1)}, u32[]{:S(2)}, u32[]{:S(2)}) %all-to-all-start.4) | async-done | bytes 1048608 | tf_op jit(solution)/shard_map/all_to_all | solution.py:71
  219.6 1.4 fusion.25
  221.2 13.1 %all_to_all.45 = bf16[32,4,96]{2,1,0:T(4,128)(2,1)S(1)} all-to-all(bf16[32,4,96]{2,1,0:T(4,128)(2,1)S(1)} %bitcast.284), channel_id=1, replica_groups=mesh['section'=2,'grp'=4,'ta'=8,'tb'=4] {'ta','tb'}, dimensions={0} | all-to-all | bytes 49152 | tf_op jit(solution)/shard_map/all_to_all | solution.py:64
  237.3 4.6 %all-to-all-start.6 = ((bf16[32,4,3072]{2,1,0:T(4,128)(2,1)}), bf16[32,4,3072]{2,1,0:T(4,128)(2,1)}, u32[]{:S(2)}, u32[]{:S(2)}) async-start(bf16[32,4,3072]{2,1,0:T(4,128)(2,1)} %broadcast_in_dim.95), calls=%async_computation.6 | async-start | bytes 1572864 | tf_op jit(solution)/shard_map/all_to_all | solution.py:71
  244.6 20.9 %all-to-all-done.6 = bf16[32,4,3072]{2,1,0:T(4,128)(2,1)} async-done(((bf16[32,4,3072]{2,1,0:T(4,128)(2,1)}), bf16[32,4,3072]{2,1,0:T(4,128)(2,1)}, u32[]{:S(2)}, u32[]{:S(2)}) %all-to-all-start.6) | async-done | bytes 786464 | tf_op jit(solution)/shard_map/all_to_all | solution.py:71
  265.5 1.6 reshape.442
  267.1 1.9 slice-done
  271.6 4.3 %all-to-all-start.7 = ((bf16[32,16,96]{2,1,0:T(8,128)(2,1)}), bf16[32,16,96]{2,1,0:T(8,128)(2,1)S(1)}, u32[]{:S(2)}, u32[]{:S(2)}) async-start(bf16[32,16,96]{2,1,0:T(8,128)(2,1)} %bitcast.55), calls=%async_computation.7 | async-start | bytes 262144 | tf_op jit(solution)/shard_map/all_to_all | solution.py:64
  276.0 3.7 %fusion = bf16[128,3072]{1,0:T(8,128)(2,1)} fusion(bf16[1,384,3072]{2,1,0:T(8,128)(2,1)S(1)} %copy-done, bf16[128,3072]{1,0:T(8,128)(2,1)S(1)} %reshape.442, bf16[1,3072,384]{2,1,0:T(8,128)(2,1)} %param.30), kind=kOutput, calls=%fused_computation.3 | convolution fusion | flops 604422144 | bytes 6291456 | tf_op jit(solution)/shard_map/dot_general | solution.py:236
  279.7 6.7 %all-to-all-done.7 = bf16[32,16,96]{2,1,0:T(8,128)(2,1)S(1)} async-done(((bf16[32,16,96]{2,1,0:T(8,128)(2,1)}), bf16[32,16,96]{2,1,0:T(8,128)(2,1)S(1)}, u32[]{:S(2)}, u32[]{:S(2)}) %all-to-all-start.7) | async-done | bytes 98336 | tf_op jit(solution)/shard_map/all_to_all | solution.py:64
  288.9 2.4 reshape.445
  291.3 3.9 %all-to-all-start.8 = ((bf16[32,4,3072]{2,1,0:T(4,128)(2,1)}), bf16[32,4,3072]{2,1,0:T(4,128)(2,1)S(1)}, u32[]{:S(2)}, u32[]{:S(2)}) async-start(bf16[32,4,3072]{2,1,0:T(4,128)(2,1)} %reshape.445), calls=%async_computation.8 | async-start | bytes 1572864 | tf_op jit(solution)/shard_map/all_to_all | solution.py:239
  298.0 3.0 collective-permute-start.5
  301.0 17.5 %all-to-all-done.8 = bf16[32,4,3072]{2,1,0:T(4,128)(2,1)S(1)} async-done(((bf16[32,4,3072]{2,1,0:T(4,128)(2,1)}), bf16[32,4,3072]{2,1,0:T(4,128)(2,1)S(1)}, u32[]{:S(2)}, u32[]{:S(2)}) %all-to-all-start.8) | async-done | bytes 786464 | tf_op jit(solution)/shard_map/all_to_all | solution.py:239
  318.9 3.1 collective-permute-start.4
  322.0 2.3 collective-permute-done.4
  324.7 1.7 fusion.27
  (170 shorter events, 45.0 us)
Async XLA Ops:
  7.2 268.8 %copy-start = (bf16[1,384,3072]{2,1,0:T(8,128)(2,1)S(1)}, bf16[1,384,3072]{2,1,0:T(8,128)(2,1)}, u32[]{:S(2)}) copy-start(bf16[1,384,3072]{2,1,0:T(8,128)(2,1)} %param.31) | copy-start | bytes 7077892
  7.2 20.5 %copy-start.13 = (bf16[1,4,18432]{2,1,0:T(4,128)(2,1)S(1)}, bf16[1,4,18432]{2,1,0:T(4,128)(2,1)}, u32[]{:S(2)}) copy-start(bf16[1,4,18432]{2,1,0:T(4,128)(2,1)} %param.23) | copy-start | bytes 442372
  7.2 21.2 %copy-start.7 = (bf16[1,1,4,3072]{3,2,1,0:T(4,128)(2,1)S(1)}, bf16[1,1,4,3072]{3,2,1,0:T(4,128)(2,1)}, u32[]{:S(2)}) copy-start(bf16[1,1,4,3072]{3,2,1,0:T(4,128)(2,1)} %param.18) | copy-start | bytes 73732
  7.2 21.6 %copy-start.14 = (bf16[1,4,9216]{2,1,0:T(4,128)(2,1)S(1)}, bf16[1,4,9216]{2,1,0:T(4,128)(2,1)}, u32[]{:S(2)}) copy-start(bf16[1,4,9216]{2,1,0:T(4,128)(2,1)} %param.24) | copy-start | bytes 221188
  7.2 22.2 %copy-start.1 = (bf16[1,1,16,3072]{3,2,1,0:T(8,128)(2,1)S(1)}, bf16[1,1,16,3072]{3,2,1,0:T(8,128)(2,1)}, u32[]{:S(2)}) copy-start(bf16[1,1,16,3072]{3,2,1,0:T(8,128)(2,1)} %param.19) | copy-start | bytes 294916
  8.4 33.1 %copy-start.17 = (f32[1,4,128]{2,1,0:T(4,128)S(1)}, f32[1,4,128]{2,1,0:T(4,128)}, u32[]{:S(2)}) copy-start(f32[1,4,128]{2,1,0:T(4,128)} %param.27) | copy-start | bytes 6148
  9.2 23.1 %all-to-all-start = ((bf16[32,32,128]{2,1,0:T(8,128)(2,1)}), bf16[32,32,128]{2,1,0:T(8,128)(2,1)S(1)}, u32[]{:S(2)}, u32[]{:S(2)}) async-start(bf16[32,32,128]{2,1,0:T(8,128)(2,1)} %pad.9.clone), calls=%async_computation | async-start | bytes 524288 | tf_op jit(solution)/shard_map/all_to_all | solution.py:128
  19.1 83.3 %all-gather.4.cloned.1.call-start = ((), (), s32[]{:S(2)}) async-start(), calls=%async_computation.9 | async-start | bytes 3244032 | tf_op jit(solution)/shard_map/all_gather | solution.py:134
  33.3 34.8 %all-to-all-start.1 = ((bf16[32,4,3072]{2,1,0:T(4,128)(2,1)}), bf16[32,4,3072]{2,1,0:T(4,128)(2,1)}, u32[]{:S(2)}, u32[]{:S(2)}) async-start(bf16[32,4,3072]{2,1,0:T(4,128)(2,1)} %broadcast_in_dim.48), calls=%async_computation.1 | async-start | bytes 1572864 | tf_op jit(solution)/shard_map/all_to_all | solution.py:71
  107.7 25.1 %all-to-all-start.2 = ((bf16[32,20,288]{2,1,0:T(8,128)(2,1)}), bf16[32,20,288]{2,1,0:T(8,128)(2,1)S(1)}, u32[]{:S(2)}, u32[]{:S(2)}) async-start(bf16[32,20,288]{2,1,0:T(8,128)(2,1)} %pad_maximum_fusion), calls=%async_computation.2 | async-start | bytes 1179648 | tf_op jit(solution)/shard_map/all_to_all | solution.py:64
  133.0 4.5 %copy-start.8 = (bf16[4,3072]{1,0:T(4,128)(2,1)}, bf16[4,3072]{1,0:T(4,128)(2,1)S(1)}, u32[]{:S(2)}) copy-start(bf16[4,3072]{1,0:T(4,128)(2,1)S(1)} %slice.228) | copy-start | bytes 73732
  134.7 6.8 %collective-permute-start = (bf16[4,6144]{1,0:T(4,128)(2,1)}, bf16[4,6144]{1,0:T(4,128)(2,1)}, u32[]{:S(2)}, u32[]{:S(2)}) collective-permute-start(bf16[4,6144]{1,0:T(4,128)(2,1)} %get-tuple-element.45), channel_id=1, source_target_pairs={{0,1},{1,2},{2,3},{3,0},{4,5},{5,6},{6,7},{7,4},{8,9},{9,10},{10,1... | collective-permute-start | bytes 147464 | tf_op jit(solution)/shard_map/ppermute | solution.py:169
  134.7 6.8 %collective-permute-start.1 = (bf16[4,6144]{1,0:T(4,128)(2,1)}, bf16[4,6144]{1,0:T(4,128)(2,1)}, u32[]{:S(2)}, u32[]{:S(2)}) collective-permute-start(bf16[4,6144]{1,0:T(4,128)(2,1)} %get-tuple-element.45), channel_id=1, source_target_pairs={{0,2},{1,3},{2,0},{3,1},{4,6},{5,7},{6,4},{7,5},{8,10},{9,11},{10,... | collective-permute-start | bytes 147464 | tf_op jit(solution)/shard_map/ppermute | solution.py:169
  136.1 5.3 %collective-permute-start.2 = (bf16[4,6144]{1,0:T(4,128)(2,1)}, bf16[4,6144]{1,0:T(4,128)(2,1)}, u32[]{:S(2)}, u32[]{:S(2)}) collective-permute-start(bf16[4,6144]{1,0:T(4,128)(2,1)} %get-tuple-element.45), channel_id=1, source_target_pairs={{0,3},{1,0},{2,1},{3,2},{4,7},{5,4},{6,5},{7,6},{8,11},{9,8},{10,9... | collective-permute-start | bytes 147464 | tf_op jit(solution)/shard_map/ppermute | solution.py:169
  138.3 5.8 %copy-start.18 = (pred[16]{0:T(512)(128)(4,1)S(1)}, pred[16]{0:T(512)(128)(4,1)}, u32[]{:S(2)}) copy-start(pred[16]{0:T(512)(128)(4,1)} %broadcast_in_dim.50) | copy-start | bytes 52
  141.3 15.3 %copy-start.2 = (bf16[1,1,16,6144]{3,2,1,0:T(8,128)(2,1)S(1)}, bf16[1,1,16,6144]{3,2,1,0:T(8,128)(2,1)}, u32[]{:S(2)}) copy-start(bf16[1,1,16,6144]{3,2,1,0:T(8,128)(2,1)} %param.32) | copy-start | bytes 589828
  144.0 31.0 %copy-start.10 = (bf16[32,16,128]{2,1,0:T(8,128)(2,1)S(1)}, bf16[32,16,128]{2,1,0:T(8,128)(2,1)}, u32[]{:S(2)}) copy-start(bf16[32,16,128]{2,1,0:T(8,128)(2,1)} %get-tuple-element.31) | copy-start | bytes 393220
  144.0 31.0 %copy-start.16 = (pred[1024]{0:T(1024)(128)(4,1)S(1)}, pred[1024]{0:T(1024)(128)(4,1)}, u32[]{:S(2)}) copy-start(pred[1024]{0:T(1024)(128)(4,1)} %concatenate.51) | copy-start | bytes 3076
  144.9 11.7 %collective-permute-start.3 = (bf16[16,6144]{1,0:T(8,128)(2,1)}, bf16[16,6144]{1,0:T(8,128)(2,1)}, u32[]{:S(2)}, u32[]{:S(2)}) collective-permute-start(bf16[16,6144]{1,0:T(8,128)(2,1)} %broadcast_select_fusion), channel_id=1, source_target_pairs={{0,0},{1,8},{2,16},{3,24},{4,1},{5,9},{6,17},{7,25},{8,2},{9,10},{... | collective-permute-start | bytes 589832 | tf_op jit(solution)/shard_map/ppermute | solution.py:173
  150.5 24.4 %all-to-all-start.3 = ((bf16[32,60,128]{2,1,0:T(8,128)(2,1)}), bf16[32,60,128]{2,1,0:T(8,128)(2,1)S(1)}, u32[]{:S(2)}, u32[]{:S(2)}) async-start(bf16[32,60,128]{2,1,0:T(8,128)(2,1)} %pad.10.clone), calls=%async_computation.3 | async-start | bytes 1048576 | tf_op jit(solution)/shard_map/all_to_all | solution.py:128
  156.4 110.7 %all-gather.6.cloned.1.call-start = ((), (), s32[]{:S(2)}) async-start(), calls=%async_computation.10 | async-start | bytes 4325376 | tf_op jit(solution)/shard_map/all_gather | solution.py:208
  179.3 40.3 %all-to-all-start.4 = ((bf16[32,128,128]{2,1,0:T(8,128)(2,1)}), bf16[32,128,128]{2,1,0:T(8,128)(2,1)S(1)}, u32[]{:S(2)}, u32[]{:S(2)}) async-start(bf16[32,128,128]{2,1,0:T(8,128)(2,1)} %broadcast_in_dim.94), calls=%async_computation.4 | async-start | bytes 2097152 | tf_op jit(solution)/shard_map/all_to_all | solution.py:71
  237.3 28.1 %all-to-all-start.6 = ((bf16[32,4,3072]{2,1,0:T(4,128)(2,1)}), bf16[32,4,3072]{2,1,0:T(4,128)(2,1)}, u32[]{:S(2)}, u32[]{:S(2)}) async-start(bf16[32,4,3072]{2,1,0:T(4,128)(2,1)} %broadcast_in_dim.95), calls=%async_computation.6 | async-start | bytes 1572864 | tf_op jit(solution)/shard_map/all_to_all | solution.py:71
  271.6 14.8 %all-to-all-start.7 = ((bf16[32,16,96]{2,1,0:T(8,128)(2,1)}), bf16[32,16,96]{2,1,0:T(8,128)(2,1)S(1)}, u32[]{:S(2)}, u32[]{:S(2)}) async-start(bf16[32,16,96]{2,1,0:T(8,128)(2,1)} %bitcast.55), calls=%async_computation.7 | async-start | bytes 262144 | tf_op jit(solution)/shard_map/all_to_all | solution.py:64
  279.7 17.6 %copy-start.15 = (bf16[4,6144]{1,0:T(4,128)(2,1)S(1)}, bf16[4,6144]{1,0:T(4,128)(2,1)}, u32[]{:S(2)}) copy-start(bf16[4,6144]{1,0:T(4,128)(2,1)} %param.33) | copy-start | bytes 147460
  279.7 17.6 %copy-start.11 = (f32[1,1,3072]{2,1,0:T(1,128)S(1)}, f32[1,1,3072]{2,1,0:T(1,128)}, u32[]{:S(2)}) copy-start(f32[1,1,3072]{2,1,0:T(1,128)} %get-tuple-element.46) | copy-start | bytes 36868
  279.7 39.2 %copy-start.12 = (f32[1,1,3072]{2,1,0:T(1,128)S(1)}, f32[1,1,3072]{2,1,0:T(1,128)}, u32[]{:S(2)}) copy-start(f32[1,1,3072]{2,1,0:T(1,128)} %get-tuple-element.34) | copy-start | bytes 36868
  279.7 45.0 %copy-start.19 = (f32[1,4,32]{2,1,0:T(4,128)S(1)}, f32[1,4,32]{2,1,0:T(4,128)}, u32[]{:S(2)}) copy-start(f32[1,4,32]{2,1,0:T(4,128)} %param.35) | copy-start | bytes 1540
  288.9 8.5 %copy-start.6 = (bf16[16,3072]{1,0:T(8,128)(2,1)S(1)}, bf16[16,3072]{1,0:T(8,128)(2,1)}, u32[]{:S(2)}) copy-start(bf16[16,3072]{1,0:T(8,128)(2,1)} %reshape.444) | copy-start | bytes 294916
  291.3 27.2 %all-to-all-start.8 = ((bf16[32,4,3072]{2,1,0:T(4,128)(2,1)}), bf16[32,4,3072]{2,1,0:T(4,128)(2,1)S(1)}, u32[]{:S(2)}, u32[]{:S(2)}) async-start(bf16[32,4,3072]{2,1,0:T(4,128)(2,1)} %reshape.445), calls=%async_computation.8 | async-start | bytes 1572864 | tf_op jit(solution)/shard_map/all_to_all | solution.py:239
  298.0 23.9 %collective-permute-start.5 = (bf16[16,3072]{1,0:T(8,128)(2,1)}, bf16[16,3072]{1,0:T(8,128)(2,1)S(1)}, u32[]{:S(2)}, u32[]{:S(2)}) collective-permute-start(bf16[16,3072]{1,0:T(8,128)(2,1)} %fusion.54), channel_id=1, source_target_pairs={{128,0},{0,128},{129,1},{1,129},{130,2},{2,130},{131,3},{3,131},{1... | collective-permute-start | bytes 294920 | tf_op jit(solution)/shard_map/ppermute | solution.py:20
  318.9 5.4 %collective-permute-start.4 = (bf16[4,3072]{1,0:T(4,128)(2,1)S(1)}, bf16[4,3072]{1,0:T(4,128)(2,1)S(1)}, u32[]{:S(2)}, u32[]{:S(2)}) collective-permute-start(bf16[4,3072]{1,0:T(4,128)(2,1)S(1)} %add_convert_fusion), channel_id=1, source_target_pairs={{128,0},{0,128},{129,1},{1,129},{130,2},{2,130},{131,3},{3,131},{1... | collective-permute-start | bytes 73736 | tf_op jit(solution)/shard_map/ppermute | solution.py:20
  (5 other events, 5.8 us)
Sparse Core Ops, SparseCore 0:
  32.4 69.9 all-gather.3
  178.0 75.5 all-gather.5

commit v14 on v13

--- a/solution.py
+++ b/solution.py
@@ -127,12 +127,10 @@
         pack = jnp.pad(pack, ((0, devices - heads), (0, 0), (0, 0)))
         return lax.all_to_all(pack, TOK, split_axis=0, concat_axis=0, tiled=True)
 
-    got_cache = by_head([stale[:, :width], stale[:, width:]])
-    got_cache, image_normed, text_normed = lax.optimization_barrier(
-        (got_cache, image_normed, text_normed)
-    )
     every_text = lax.all_gather(text_normed, TOK, axis=0, tiled=True)
     every_image = broadcast_rows(image_normed, devices)
+    stale_late, every_image = lax.optimization_barrier((stale, every_image))
+    got_cache = by_head([stale_late[:, :width], stale_late[:, width:]])
     image_cols = jnp.dot(every_image, image_to_heads[0], preferred_element_type=jnp.float32)
     text_cols = jnp.dot(every_text, text_to_heads[0], preferred_element_type=jnp.float32)
     proj = cols_to_rows(

time: 337 us -> 325 us (0.964)
  waiting for transfers between devices: 175 us -> 164 us
    all_gather x1, waiting for transfers between devices: 31.5 us -> 20.8 us  [shards(): every_text = lax.all_gather(text_normed, TOK, axis=0, tiled=True)]
    all_to_all x2, starting transfers between devices: 15.8 us -> 11.4 us  [by_head(): return lax.all_to_all(pack, TOK, split_axis=0, concat_axis=0, tiled=True)]
    unnamed x61 -> x57, local copies, waits for them, and re-layouts: 10.4 us -> 7.93 us
  transfers between devices with their start and end apart: 16 -> 16, of which waited for: 10 -> 9; matrix products, arithmetic and copies ran while one was open for 11% -> 13% of each run, Pallas kernels for 0% -> 0%
where the time goes in v14:
time: 325 us; the launch traced here: 322 us
  waiting for transfers between devices  164 us (50%)
  starting transfers between devices  54.8 us (17%)
  local copies, waits for them, and re-layouts  33.7 us (10%)
  between operations  24.5 us (8%)
  other arithmetic  16.8 us (5%)
  matrix products  15.5 us (5%)
  blocking collectives  13.2 us (4%)
    all_to_all x3, waiting for transfers between devices, broadcast_rows(): got = lax.all_to_all(copies, TOK, split_axis=0, concat_axis=0, tiled=True)  83.9 us
    all_to_all x2, waiting for transfers between devices, cols_to_rows(): got = lax.all_to_all(cols, TOK, split_axis=0, concat_axis=0, tiled=True)  21.8 us
    all_gather x1, waiting for transfers between devices, shards(): every_text = lax.all_gather(text_normed, TOK, axis=0, tiled=True)  20.8 us
    all_to_all x3, starting transfers between devices, broadcast_rows(): got = lax.all_to_all(copies, TOK, split_axis=0, concat_axis=0, tiled=True)  18.6 us
    all_to_all x1, waiting for transfers between devices, shards(): lax.all_to_all(partial.astype(jnp.bfloat16).reshape(devices, image_rows,...  18.3 us
    all_to_all x2, waiting for transfers between devices, by_head(): return lax.all_to_all(pack, TOK, split_axis=0, concat_axis=0, tiled=True)  16.6 us
    all_to_all x1, blocking collectives, cols_to_rows(): got = lax.all_to_all(cols, TOK, split_axis=0, concat_axis=0, tiled=True)  13.2 us
    all_to_all x2, starting transfers between devices, by_head(): return lax.all_to_all(pack, TOK, split_axis=0, concat_axis=0, tiled=True)  11.4 us
  transfers between devices with their start and end apart: 16, of which 9 were waited for; matrix products, arithmetic and copies ran while one was open for 13% of the time, Pallas kernels for 0%

profile of v14, /device:TPU:2, one launch (start us, length us, event | category | flops | bytes accessed | tf_op | source)
XLA Modules:
  0.0 322.2 jit_solution(7398584440197819726)
XLA Ops:
  18.9 1.6 fusion.53
  26.0 9.9 %all-to-all-start = ((bf16[32,4,3072]{2,1,0:T(4,128)(2,1)}), bf16[32,4,3072]{2,1,0:T(4,128)(2,1)S(1)}, u32[]{:S(2)}, u32[]{:S(2)}) async-start(bf16[32,4,3072]{2,1,0:T(4,128)(2,1)} %broadcast_in_dim.48), calls=%async_computation | async-start | bytes 1572864 | tf_op jit(solution)/shard_map/all_to_all | solution.py:71
  36.6 28.2 %all-to-all-done = bf16[32,4,3072]{2,1,0:T(4,128)(2,1)S(1)} async-done(((bf16[32,4,3072]{2,1,0:T(4,128)(2,1)}), bf16[32,4,3072]{2,1,0:T(4,128)(2,1)S(1)}, u32[]{:S(2)}, u32[]{:S(2)}) %all-to-all-start) | async-done | bytes 786464 | tf_op jit(solution)/shard_map/all_to_all | solution.py:71
  65.8 1.7 dot_general.33
  67.5 2.3 fusion.22
  70.8 3.9 %all-to-all-start.1 = ((bf16[32,32,128]{2,1,0:T(8,128)(2,1)}), bf16[32,32,128]{2,1,0:T(8,128)(2,1)S(1)}, u32[]{:S(2)}, u32[]{:S(2)}) async-start(bf16[32,32,128]{2,1,0:T(8,128)(2,1)} %pad.9.clone), calls=%async_computation.1 | async-start | bytes 524288 | tf_op jit(solution)/shard_map/all_to_all | solution.py:128
  74.7 20.8 %all-gather.4.cloned.1.call-done = bf16[512,3072]{1,0:T(8,128)(2,1)} async-done(((bf16[16,3072]{1,0:T(8,128)(2,1)}), bf16[512,3072]{1,0:T(8,128)(2,1)}) %all-gather.4.cloned.1.call-update) | async-done | bytes 3145744 | tf_op jit(solution)/shard_map/all_gather | solution.py:130
  95.5 4.2 %fusion.15 = bf16[32,16,288]{2,1,0:T(8,128)(2,1)S(1)} fusion(bf16[32,16,3072]{2,1,0:T(8,128)(2,1)} %bitcast.306, bf16[1,3072,288]{1,2,0:T(8,128)(2,1)} %param.26), kind=kOutput, calls=%fused_computation.18 | convolution fusion | flops 906117120 | bytes 5210112 | tf_op jit(solution)/shard_map/dot_general | solution.py:135
  100.7 6.0 %all-to-all-start.2 = ((bf16[32,20,288]{2,1,0:T(8,128)(2,1)}), bf16[32,20,288]{2,1,0:T(8,128)(2,1)S(1)}, u32[]{:S(2)}, u32[]{:S(2)}) async-start(bf16[32,20,288]{2,1,0:T(8,128)(2,1)} %pad_maximum_fusion), calls=%async_computation.2 | async-start | bytes 1179648 | tf_op jit(solution)/shard_map/all_to_all | solution.py:64
  111.3 15.0 %all-to-all-done.2 = bf16[32,20,288]{2,1,0:T(8,128)(2,1)S(1)} async-done(((bf16[32,20,288]{2,1,0:T(8,128)(2,1)}), bf16[32,20,288]{2,1,0:T(8,128)(2,1)S(1)}, u32[]{:S(2)}, u32[]{:S(2)}) %all-to-all-start.2) | async-done | bytes 368672 | tf_op jit(solution)/shard_map/all_to_all | solution.py:64
  127.6 1.5 collective-permute-start.1
  139.5 7.6 %all-to-all-start.3 = ((bf16[32,60,128]{2,1,0:T(8,128)(2,1)}), bf16[32,60,128]{2,1,0:T(8,128)(2,1)S(1)}, u32[]{:S(2)}, u32[]{:S(2)}) async-start(bf16[32,60,128]{2,1,0:T(8,128)(2,1)} %pad.10.clone), calls=%async_computation.3 | async-start | bytes 1048576 | tf_op jit(solution)/shard_map/all_to_all | solution.py:128
  147.3 1.6 broadcast_select_fusion.1
  148.9 16.6 %all-to-all-done.3 = bf16[32,60,128]{2,1,0:T(8,128)(2,1)S(1)} async-done(((bf16[32,60,128]{2,1,0:T(8,128)(2,1)}), bf16[32,60,128]{2,1,0:T(8,128)(2,1)S(1)}, u32[]{:S(2)}, u32[]{:S(2)}) %all-to-all-start.3) | async-done | bytes 491552 | tf_op jit(solution)/shard_map/all_to_all | solution.py:128
  170.0 4.1 %all-to-all-start.4 = ((bf16[32,128,128]{2,1,0:T(8,128)(2,1)}), bf16[32,128,128]{2,1,0:T(8,128)(2,1)S(1)}, u32[]{:S(2)}, u32[]{:S(2)}) async-start(bf16[32,128,128]{2,1,0:T(8,128)(2,1)} %broadcast_in_dim.94), calls=%async_computation.4 | async-start | bytes 2097152 | tf_op jit(solution)/shard_map/all_to_all | solution.py:71
  174.0 2.0 copy.90
  176.1 34.3 %all-to-all-done.4 = bf16[32,128,128]{2,1,0:T(8,128)(2,1)S(1)} async-done(((bf16[32,128,128]{2,1,0:T(8,128)(2,1)}), bf16[32,128,128]{2,1,0:T(8,128)(2,1)S(1)}, u32[]{:S(2)}, u32[]{:S(2)}) %all-to-all-start.4) | async-done | bytes 1048608 | tf_op jit(solution)/shard_map/all_to_all | solution.py:71
  211.9 13.2 %all_to_all.45 = bf16[32,4,96]{2,1,0:T(4,128)(2,1)S(1)} all-to-all(bf16[32,4,96]{2,1,0:T(4,128)(2,1)S(1)} %bitcast.284), channel_id=1, replica_groups=mesh['section'=2,'grp'=4,'ta'=8,'tb'=4] {'ta','tb'}, dimensions={0} | all-to-all | bytes 49152 | tf_op jit(solution)/shard_map/all_to_all | solution.py:64
  226.8 4.6 %all-to-all-start.6 = ((bf16[32,4,3072]{2,1,0:T(4,128)(2,1)}), bf16[32,4,3072]{2,1,0:T(4,128)(2,1)}, u32[]{:S(2)}, u32[]{:S(2)}) async-start(bf16[32,4,3072]{2,1,0:T(4,128)(2,1)} %broadcast_in_dim.95), calls=%async_computation.6 | async-start | bytes 1572864 | tf_op jit(solution)/shard_map/all_to_all | solution.py:71
  234.1 21.5 %all-to-all-done.6 = bf16[32,4,3072]{2,1,0:T(4,128)(2,1)} async-done(((bf16[32,4,3072]{2,1,0:T(4,128)(2,1)}), bf16[32,4,3072]{2,1,0:T(4,128)(2,1)}, u32[]{:S(2)}, u32[]{:S(2)}) %all-to-all-start.6) | async-done | bytes 786464 | tf_op jit(solution)/shard_map/all_to_all | solution.py:71
  255.6 1.6 reshape.504
  257.2 1.9 slice-done
  261.7 4.2 %all-to-all-start.7 = ((bf16[32,16,96]{2,1,0:T(8,128)(2,1)}), bf16[32,16,96]{2,1,0:T(8,128)(2,1)S(1)}, u32[]{:S(2)}, u32[]{:S(2)}) async-start(bf16[32,16,96]{2,1,0:T(8,128)(2,1)} %bitcast.55), calls=%async_computation.7 | async-start | bytes 262144 | tf_op jit(solution)/shard_map/all_to_all | solution.py:64
  266.0 3.7 %fusion = bf16[128,3072]{1,0:T(8,128)(2,1)} fusion(bf16[1,384,3072]{2,1,0:T(8,128)(2,1)S(1)} %copy-done, bf16[128,3072]{1,0:T(8,128)(2,1)S(1)} %reshape.504, bf16[1,3072,384]{2,1,0:T(8,128)(2,1)} %param.30), kind=kOutput, calls=%fused_computation.3 | convolution fusion | flops 604422144 | bytes 6291456 | tf_op jit(solution)/shard_map/dot_general | solution.py:234
  269.7 6.7 %all-to-all-done.7 = bf16[32,16,96]{2,1,0:T(8,128)(2,1)S(1)} async-done(((bf16[32,16,96]{2,1,0:T(8,128)(2,1)}), bf16[32,16,96]{2,1,0:T(8,128)(2,1)S(1)}, u32[]{:S(2)}, u32[]{:S(2)}) %all-to-all-start.7) | async-done | bytes 98336 | tf_op jit(solution)/shard_map/all_to_all | solution.py:64
  276.6 2.4 reshape.507
  279.0 3.9 %all-to-all-start.8 = ((bf16[32,4,3072]{2,1,0:T(4,128)(2,1)}), bf16[32,4,3072]{2,1,0:T(4,128)(2,1)S(1)}, u32[]{:S(2)}, u32[]{:S(2)}) async-start(bf16[32,4,3072]{2,1,0:T(4,128)(2,1)} %reshape.507), calls=%async_computation.8 | async-start | bytes 1572864 | tf_op jit(solution)/shard_map/all_to_all | solution.py:237
  284.9 3.1 collective-permute-start.5
  287.9 18.3 %all-to-all-done.8 = bf16[32,4,3072]{2,1,0:T(4,128)(2,1)S(1)} async-done(((bf16[32,4,3072]{2,1,0:T(4,128)(2,1)}), bf16[32,4,3072]{2,1,0:T(4,128)(2,1)S(1)}, u32[]{:S(2)}, u32[]{:S(2)}) %all-to-all-start.8) | async-done | bytes 786464 | tf_op jit(solution)/shard_map/all_to_all | solution.py:237
  306.6 3.1 collective-permute-start.4
  309.7 2.3 collective-permute-done.4
  312.4 1.7 fusion.27
  (168 shorter events, 44.2 us)
Async XLA Ops:
  7.2 258.8 %copy-start = (bf16[1,384,3072]{2,1,0:T(8,128)(2,1)S(1)}, bf16[1,384,3072]{2,1,0:T(8,128)(2,1)}, u32[]{:S(2)}) copy-start(bf16[1,384,3072]{2,1,0:T(8,128)(2,1)} %param.31) | copy-start | bytes 7077892
  7.2 29.4 %copy-start.15 = (f32[1,4,128]{2,1,0:T(4,128)S(1)}, f32[1,4,128]{2,1,0:T(4,128)}, u32[]{:S(2)}) copy-start(f32[1,4,128]{2,1,0:T(4,128)} %param.27) | copy-start | bytes 6148
  7.2 88.3 %all-gather.4.cloned.1.call-start = ((), (), s32[]{:S(2)}) async-start(), calls=%async_computation.9 | async-start | bytes 3244032 | tf_op jit(solution)/shard_map/all_gather | solution.py:130
  26.0 38.8 %all-to-all-start = ((bf16[32,4,3072]{2,1,0:T(4,128)(2,1)}), bf16[32,4,3072]{2,1,0:T(4,128)(2,1)S(1)}, u32[]{:S(2)}, u32[]{:S(2)}) async-start(bf16[32,4,3072]{2,1,0:T(4,128)(2,1)} %broadcast_in_dim.48), calls=%async_computation | async-start | bytes 1572864 | tf_op jit(solution)/shard_map/all_to_all | solution.py:71
  65.8 4.1 %copy-start.2 = (bf16[1,1,16,6144]{3,2,1,0:T(8,128)(2,1)S(1)}, bf16[1,1,16,6144]{3,2,1,0:T(8,128)(2,1)}, u32[]{:S(2)}) copy-start(bf16[1,1,16,6144]{3,2,1,0:T(8,128)(2,1)} %param.32) | copy-start | bytes 589828
  70.8 29.9 %all-to-all-start.1 = ((bf16[32,32,128]{2,1,0:T(8,128)(2,1)}), bf16[32,32,128]{2,1,0:T(8,128)(2,1)S(1)}, u32[]{:S(2)}, u32[]{:S(2)}) async-start(bf16[32,32,128]{2,1,0:T(8,128)(2,1)} %pad.9.clone), calls=%async_computation.1 | async-start | bytes 524288 | tf_op jit(solution)/shard_map/all_to_all | solution.py:128
  100.7 25.6 %all-to-all-start.2 = ((bf16[32,20,288]{2,1,0:T(8,128)(2,1)}), bf16[32,20,288]{2,1,0:T(8,128)(2,1)S(1)}, u32[]{:S(2)}, u32[]{:S(2)}) async-start(bf16[32,20,288]{2,1,0:T(8,128)(2,1)} %pad_maximum_fusion), calls=%async_computation.2 | async-start | bytes 1179648 | tf_op jit(solution)/shard_map/all_to_all | solution.py:64
  126.9 5.0 %copy-start.12 = (f32[3072]{0:T(1024)S(1)}, f32[3072]{0:T(1024)}, u32[]{:S(2)}) copy-start(f32[3072]{0:T(1024)} %get-tuple-element.61) | copy-start | bytes 36868
  127.6 5.3 %collective-permute-start = (bf16[4,6144]{1,0:T(4,128)(2,1)}, bf16[4,6144]{1,0:T(4,128)(2,1)}, u32[]{:S(2)}, u32[]{:S(2)}) collective-permute-start(bf16[4,6144]{1,0:T(4,128)(2,1)} %get-tuple-element.43), channel_id=1, source_target_pairs={{0,1},{1,2},{2,3},{3,0},{4,5},{5,6},{6,7},{7,4},{8,9},{9,10},{10,1... | collective-permute-start | bytes 147464 | tf_op jit(solution)/shard_map/ppermute | solution.py:167
  127.6 5.3 %collective-permute-start.1 = (bf16[4,6144]{1,0:T(4,128)(2,1)}, bf16[4,6144]{1,0:T(4,128)(2,1)}, u32[]{:S(2)}, u32[]{:S(2)}) collective-permute-start(bf16[4,6144]{1,0:T(4,128)(2,1)} %get-tuple-element.43), channel_id=1, source_target_pairs={{0,2},{1,3},{2,0},{3,1},{4,6},{5,7},{6,4},{7,5},{8,10},{9,11},{10,... | collective-permute-start | bytes 147464 | tf_op jit(solution)/shard_map/ppermute | solution.py:167
  129.1 3.9 %collective-permute-start.2 = (bf16[4,6144]{1,0:T(4,128)(2,1)}, bf16[4,6144]{1,0:T(4,128)(2,1)}, u32[]{:S(2)}, u32[]{:S(2)}) collective-permute-start(bf16[4,6144]{1,0:T(4,128)(2,1)} %get-tuple-element.43), channel_id=1, source_target_pairs={{0,3},{1,0},{2,1},{3,2},{4,7},{5,4},{6,5},{7,6},{8,11},{9,8},{10,9... | collective-permute-start | bytes 147464 | tf_op jit(solution)/shard_map/ppermute | solution.py:167
  131.2 4.2 %copy-start.16 = (pred[16]{0:T(512)(128)(4,1)S(1)}, pred[16]{0:T(512)(128)(4,1)}, u32[]{:S(2)}) copy-start(pred[16]{0:T(512)(128)(4,1)} %broadcast_in_dim.50) | copy-start | bytes 52
  135.4 30.3 %copy-start.7 = (bf16[32,16,128]{2,1,0:T(8,128)(2,1)S(1)}, bf16[32,16,128]{2,1,0:T(8,128)(2,1)}, u32[]{:S(2)}) copy-start(bf16[32,16,128]{2,1,0:T(8,128)(2,1)} %get-tuple-element.29) | copy-start | bytes 393220
  135.4 30.3 %copy-start.14 = (pred[1024]{0:T(1024)(128)(4,1)S(1)}, pred[1024]{0:T(1024)(128)(4,1)}, u32[]{:S(2)}) copy-start(pred[1024]{0:T(1024)(128)(4,1)} %concatenate.51) | copy-start | bytes 3076
  135.5 11.8 %collective-permute-start.3 = (bf16[16,6144]{1,0:T(8,128)(2,1)S(1)}, bf16[16,6144]{1,0:T(8,128)(2,1)}, u32[]{:S(2)}, u32[]{:S(2)}) collective-permute-start(bf16[16,6144]{1,0:T(8,128)(2,1)S(1)} %broadcast_select_fusion), channel_id=1, source_target_pairs={{0,0},{1,8},{2,16},{3,24},{4,1},{5,9},{6,17},{7,25},{8,2},{9,10},{... | collective-permute-start | bytes 589832 | tf_op jit(solution)/shard_map/ppermute | solution.py:171
  139.5 26.0 %all-to-all-start.3 = ((bf16[32,60,128]{2,1,0:T(8,128)(2,1)}), bf16[32,60,128]{2,1,0:T(8,128)(2,1)S(1)}, u32[]{:S(2)}, u32[]{:S(2)}) async-start(bf16[32,60,128]{2,1,0:T(8,128)(2,1)} %pad.10.clone), calls=%async_computation.3 | async-start | bytes 1048576 | tf_op jit(solution)/shard_map/all_to_all | solution.py:128
  147.1 110.1 %all-gather.6.cloned.1.call-start = ((), (), s32[]{:S(2)}) async-start(), calls=%async_computation.10 | async-start | bytes 4325376 | tf_op jit(solution)/shard_map/all_gather | solution.py:206
  170.0 55.3 %copy-start.5 = (bf16[1,1,4,3072]{3,2,1,0:T(4,128)(2,1)S(1)}, bf16[1,1,4,3072]{3,2,1,0:T(4,128)(2,1)}, u32[]{:S(2)}) copy-start(bf16[1,1,4,3072]{3,2,1,0:T(4,128)(2,1)} %param.18) | copy-start | bytes 73732
  170.0 55.3 %copy-start.11 = (f32[1,1,3072]{2,1,0:T(1,128)S(1)}, f32[1,1,3072]{2,1,0:T(1,128)}, u32[]{:S(2)}) copy-start(f32[1,1,3072]{2,1,0:T(1,128)} %get-tuple-element.37) | copy-start | bytes 36868
  170.0 55.6 %copy-start.9 = (f32[1,1,3072]{2,1,0:T(1,128)S(1)}, f32[1,1,3072]{2,1,0:T(1,128)}, u32[]{:S(2)}) copy-start(f32[1,1,3072]{2,1,0:T(1,128)} %get-tuple-element.33) | copy-start | bytes 36868
  170.0 55.7 %copy-start.10 = (f32[1,1,3072]{2,1,0:T(1,128)S(1)}, f32[1,1,3072]{2,1,0:T(1,128)}, u32[]{:S(2)}) copy-start(f32[1,1,3072]{2,1,0:T(1,128)} %get-tuple-element.34) | copy-start | bytes 36868
  170.0 40.4 %all-to-all-start.4 = ((bf16[32,128,128]{2,1,0:T(8,128)(2,1)}), bf16[32,128,128]{2,1,0:T(8,128)(2,1)S(1)}, u32[]{:S(2)}, u32[]{:S(2)}) async-start(bf16[32,128,128]{2,1,0:T(8,128)(2,1)} %broadcast_in_dim.94), calls=%async_computation.4 | async-start | bytes 2097152 | tf_op jit(solution)/shard_map/all_to_all | solution.py:71
  226.8 28.7 %all-to-all-start.6 = ((bf16[32,4,3072]{2,1,0:T(4,128)(2,1)}), bf16[32,4,3072]{2,1,0:T(4,128)(2,1)}, u32[]{:S(2)}, u32[]{:S(2)}) async-start(bf16[32,4,3072]{2,1,0:T(4,128)(2,1)} %broadcast_in_dim.95), calls=%async_computation.6 | async-start | bytes 1572864 | tf_op jit(solution)/shard_map/all_to_all | solution.py:71
  257.2 1.9 slice-start
  261.7 14.7 %all-to-all-start.7 = ((bf16[32,16,96]{2,1,0:T(8,128)(2,1)}), bf16[32,16,96]{2,1,0:T(8,128)(2,1)S(1)}, u32[]{:S(2)}, u32[]{:S(2)}) async-start(bf16[32,16,96]{2,1,0:T(8,128)(2,1)} %bitcast.55), calls=%async_computation.7 | async-start | bytes 262144 | tf_op jit(solution)/shard_map/all_to_all | solution.py:64
  269.7 15.1 %copy-start.13 = (bf16[4,6144]{1,0:T(4,128)(2,1)S(1)}, bf16[4,6144]{1,0:T(4,128)(2,1)}, u32[]{:S(2)}) copy-start(bf16[4,6144]{1,0:T(4,128)(2,1)} %param.33) | copy-start | bytes 147460
  269.7 15.1 %copy-start.1 = (bf16[1,1,16,3072]{3,2,1,0:T(8,128)(2,1)S(1)}, bf16[1,1,16,3072]{3,2,1,0:T(8,128)(2,1)}, u32[]{:S(2)}) copy-start(bf16[1,1,16,3072]{3,2,1,0:T(8,128)(2,1)} %param.19) | copy-start | bytes 294916
  269.7 36.9 %copy-start.8 = (f32[1,1,3072]{2,1,0:T(1,128)S(1)}, f32[1,1,3072]{2,1,0:T(1,128)}, u32[]{:S(2)}) copy-start(f32[1,1,3072]{2,1,0:T(1,128)} %get-tuple-element.32) | copy-start | bytes 36868
  269.7 42.7 %copy-start.17 = (f32[1,4,32]{2,1,0:T(4,128)S(1)}, f32[1,4,32]{2,1,0:T(4,128)}, u32[]{:S(2)}) copy-start(f32[1,4,32]{2,1,0:T(4,128)} %param.35) | copy-start | bytes 1540
  279.0 27.2 %all-to-all-start.8 = ((bf16[32,4,3072]{2,1,0:T(4,128)(2,1)}), bf16[32,4,3072]{2,1,0:T(4,128)(2,1)S(1)}, u32[]{:S(2)}, u32[]{:S(2)}) async-start(bf16[32,4,3072]{2,1,0:T(4,128)(2,1)} %reshape.507), calls=%async_computation.8 | async-start | bytes 1572864 | tf_op jit(solution)/shard_map/all_to_all | solution.py:237
  284.9 24.8 %collective-permute-start.5 = (bf16[16,3072]{1,0:T(8,128)(2,1)S(1)}, bf16[16,3072]{1,0:T(8,128)(2,1)S(1)}, u32[]{:S(2)}, u32[]{:S(2)}) collective-permute-start(bf16[16,3072]{1,0:T(8,128)(2,1)S(1)} %fusion.54), channel_id=1, source_target_pairs={{128,0},{0,128},{129,1},{1,129},{130,2},{2,130},{131,3},{3,131},{1... | collective-permute-start | bytes 294920 | tf_op jit(solution)/shard_map/ppermute | solution.py:20
  306.6 5.4 %collective-permute-start.4 = (bf16[4,3072]{1,0:T(4,128)(2,1)S(1)}, bf16[4,3072]{1,0:T(4,128)(2,1)S(1)}, u32[]{:S(2)}, u32[]{:S(2)}) collective-permute-start(bf16[4,3072]{1,0:T(4,128)(2,1)S(1)} %add_convert_fusion), channel_id=1, source_target_pairs={{128,0},{0,128},{129,1},{1,129},{130,2},{2,130},{131,3},{3,131},{1... | collective-permute-start | bytes 73736 | tf_op jit(solution)/shard_map/ppermute | solution.py:20
  (3 other events, 3.3 us)
Sparse Core Ops, SparseCore 0:
  20.7 74.6 all-gather.3
  168.7 75.6 all-gather.5

commit v15 on v14

--- a/solution.py
+++ b/solution.py
@@ -133,17 +133,8 @@
     got_cache = by_head([stale_late[:, :width], stale_late[:, width:]])
     image_cols = jnp.dot(every_image, image_to_heads[0], preferred_element_type=jnp.float32)
     text_cols = jnp.dot(every_text, text_to_heads[0], preferred_element_type=jnp.float32)
-    proj = cols_to_rows(
-        jnp.concatenate(
-            [
-                image_cols.reshape(devices, image_rows, -1),
-                text_cols.reshape(devices, text_rows, -1),
-            ],
-            axis=1,
-        ).astype(jnp.bfloat16)
-    )
-    image_proj = proj[:image_rows]
-    text_proj = proj[image_rows:]
+    image_proj = cols_to_rows(image_cols.astype(jnp.bfloat16).reshape(devices, image_rows, -1))
+    text_proj = cols_to_rows(text_cols.astype(jnp.bfloat16).reshape(devices, text_rows, -1))
     gains = head_gain[0]
     image_query = head_norm(image_proj[:, :width].astype(jnp.float32), gains[0]).astype(
         jnp.bfloat16

time: 325 us -> 324 us (level)
  starting transfers between devices: 54.8 us -> 59.6 us
    all_gather x1, waiting for transfers between devices: 20.8 us -> 5.41 us  [shards(): every_text = lax.all_gather(text_normed, TOK, axis=0, tiled=True)]
    all_to_all x2, waiting for transfers between devices: 16.6 us -> 23.9 us  [by_head(): return lax.all_to_all(pack, TOK, split_axis=0, concat_axis=0, tiled=True)]
    all_to_all x2 -> x3, waiting for transfers between devices: 21.8 us -> 28.4 us  [cols_to_rows(): got = lax.all_to_all(cols, TOK, split_axis=0, concat_axis=0, tiled=True)]
    all_to_all x2 -> x3, starting transfers between devices: 10.3 us -> 14.3 us  [cols_to_rows(): got = lax.all_to_all(cols, TOK, split_axis=0, concat_axis=0, tiled=True)]
    all_to_all x3, waiting for transfers between devices: 83.9 us -> 80.7 us  [broadcast_rows(): got = lax.all_to_all(copies, TOK, split_axis=0, concat_axis=0, tiled=True)]
    unnamed x57 -> x51, local copies, waits for them, and re-layouts: 7.93 us -> 9.68 us
  transfers between devices with their start and end apart: 16 -> 17, of which waited for: 9 -> 13; matrix products, arithmetic and copies ran while one was open for 13% -> 12% of each run, Pallas kernels for 0% -> 0%
where the time goes in v15:
time: 324 us; the launch traced here: 322 us
  waiting for transfers between devices  161 us (50%)
  starting transfers between devices  59.6 us (18%)
  local copies, waits for them, and re-layouts  34.1 us (11%)
  between operations  24.4 us (8%)
  matrix products  14.8 us (5%)
  other arithmetic  14.7 us (5%)
  blocking collectives  12.9 us (4%)
    all_to_all x3, waiting for transfers between devices, broadcast_rows(): got = lax.all_to_all(copies, TOK, split_axis=0, concat_axis=0, tiled=True)  80.7 us
    all_to_all x3, waiting for transfers between devices, cols_to_rows(): got = lax.all_to_all(cols, TOK, split_axis=0, concat_axis=0, tiled=True)  28.4 us
    all_to_all x2, waiting for transfers between devices, by_head(): return lax.all_to_all(pack, TOK, split_axis=0, concat_axis=0, tiled=True)  23.9 us
    all_to_all x3, starting transfers between devices, broadcast_rows(): got = lax.all_to_all(copies, TOK, split_axis=0, concat_axis=0, tiled=True)  18.6 us
    all_to_all x1, waiting for transfers between devices, shards(): lax.all_to_all(partial.astype(jnp.bfloat16).reshape(devices, image_rows,...  18.4 us
    all_to_all x3, starting transfers between devices, cols_to_rows(): got = lax.all_to_all(cols, TOK, split_axis=0, concat_axis=0, tiled=True)  14.3 us
    all_to_all x1, blocking collectives, cols_to_rows(): got = lax.all_to_all(cols, TOK, split_axis=0, concat_axis=0, tiled=True)  12.9 us
    all_to_all x2, starting transfers between devices, by_head(): return lax.all_to_all(pack, TOK, split_axis=0, concat_axis=0, tiled=True)  11.3 us
  transfers between devices with their start and end apart: 17, of which 13 were waited for; matrix products, arithmetic and copies ran while one was open for 12% of the time, Pallas kernels for 0%

profile of v15, /device:TPU:2, one launch (start us, length us, event | category | flops | bytes accessed | tf_op | source)
XLA Modules:
  0.0 321.6 jit_solution(18322396627102716972)
XLA Ops:
  19.5 1.6 fusion.52
  26.6 9.9 %all-to-all-start = ((bf16[32,4,3072]{2,1,0:T(4,128)(2,1)}), bf16[32,4,3072]{2,1,0:T(4,128)(2,1)S(1)}, u32[]{:S(2)}, u32[]{:S(2)}) async-start(bf16[32,4,3072]{2,1,0:T(4,128)(2,1)} %broadcast_in_dim.48), calls=%async_computation | async-start | bytes 1572864 | tf_op jit(solution)/shard_map/all_to_all | solution.py:71
  40.4 25.0 %all-to-all-done = bf16[32,4,3072]{2,1,0:T(4,128)(2,1)S(1)} async-done(((bf16[32,4,3072]{2,1,0:T(4,128)(2,1)}), bf16[32,4,3072]{2,1,0:T(4,128)(2,1)S(1)}, u32[]{:S(2)}, u32[]{:S(2)}) %all-to-all-start) | async-done | bytes 786464 | tf_op jit(solution)/shard_map/all_to_all | solution.py:71
  66.4 2.4 fusion.22
  69.6 3.9 %all-to-all-start.2 = ((bf16[32,4,288]{2,1,0:T(4,128)(2,1)}), bf16[32,4,288]{2,1,0:T(4,128)(2,1)S(1)}, u32[]{:S(2)}, u32[]{:S(2)}) async-start(bf16[32,4,288]{2,1,0:T(4,128)(2,1)} %reshape.499), calls=%async_computation.2 | async-start | bytes 196608 | tf_op jit(solution)/shard_map/all_to_all | solution.py:64
  74.4 9.7 %all-to-all-done.2 = bf16[32,4,288]{2,1,0:T(4,128)(2,1)S(1)} async-done(((bf16[32,4,288]{2,1,0:T(4,128)(2,1)}), bf16[32,4,288]{2,1,0:T(4,128)(2,1)S(1)}, u32[]{:S(2)}, u32[]{:S(2)}) %all-to-all-start.2) | async-done | bytes 73760 | tf_op jit(solution)/shard_map/all_to_all | solution.py:64
  90.5 5.4 %all-gather.4.cloned.1.call-done = bf16[512,3072]{1,0:T(8,128)(2,1)} async-done(((bf16[16,3072]{1,0:T(8,128)(2,1)}), bf16[512,3072]{1,0:T(8,128)(2,1)}) %all-gather.4.cloned.1.call-update) | async-done | bytes 3145744 | tf_op jit(solution)/shard_map/all_gather | solution.py:130
  95.9 3.5 %fusion.15 = bf16[512,288]{0,1:T(8,128)(2,1)S(1)} fusion(bf16[512,3072]{1,0:T(8,128)(2,1)} %all-gather.4.cloned.1.call-done, bf16[1,3072,288]{1,2,0:T(8,128)(2,1)} %param.26), kind=kOutput, calls=%fused_computation.18 | convolution fusion | flops 906117120 | bytes 5210112 | tf_op jit(solution)/shard_map/dot_general | solution.py:135
  100.4 5.7 %all-to-all-start.3 = ((bf16[32,16,288]{2,1,0:T(8,128)(2,1)}), bf16[32,16,288]{2,1,0:T(8,128)(2,1)S(1)}, u32[]{:S(2)}, u32[]{:S(2)}) async-start(bf16[32,16,288]{2,1,0:T(8,128)(2,1)} %bitcast.17), calls=%async_computation.3 | async-start | bytes 786432 | tf_op jit(solution)/shard_map/all_to_all | solution.py:64
  106.9 3.0 collective-permute-start.3
  109.9 12.0 %all-to-all-done.3 = bf16[32,16,288]{2,1,0:T(8,128)(2,1)S(1)} async-done(((bf16[32,16,288]{2,1,0:T(8,128)(2,1)}), bf16[32,16,288]{2,1,0:T(8,128)(2,1)S(1)}, u32[]{:S(2)}, u32[]{:S(2)}) %all-to-all-start.3) | async-done | bytes 294944 | tf_op jit(solution)/shard_map/all_to_all | solution.py:64
  121.9 7.4 %all-to-all-start.1 = ((bf16[32,32,128]{2,1,0:T(8,128)(2,1)}), bf16[32,32,128]{2,1,0:T(8,128)(2,1)S(1)}, u32[]{:S(2)}, u32[]{:S(2)}) async-start(bf16[32,32,128]{2,1,0:T(8,128)(2,1)} %pad.9.clone), calls=%async_computation.1 | async-start | bytes 524288 | tf_op jit(solution)/shard_map/all_to_all | solution.py:128
  136.0 6.4 %all-to-all-done.1 = bf16[32,32,128]{2,1,0:T(8,128)(2,1)S(1)} async-done(((bf16[32,32,128]{2,1,0:T(8,128)(2,1)}), bf16[32,32,128]{2,1,0:T(8,128)(2,1)S(1)}, u32[]{:S(2)}, u32[]{:S(2)}) %all-to-all-start.1) | async-done | bytes 262176 | tf_op jit(solution)/shard_map/all_to_all | solution.py:128
  142.4 3.9 %all-to-all-start.4 = ((bf16[32,60,128]{2,1,0:T(8,128)(2,1)}), bf16[32,60,128]{2,1,0:T(8,128)(2,1)S(1)}, u32[]{:S(2)}, u32[]{:S(2)}) async-start(bf16[32,60,128]{2,1,0:T(8,128)(2,1)} %pad.10.clone), calls=%async_computation.4 | async-start | bytes 1048576 | tf_op jit(solution)/shard_map/all_to_all | solution.py:128
  147.3 17.5 %all-to-all-done.4 = bf16[32,60,128]{2,1,0:T(8,128)(2,1)S(1)} async-done(((bf16[32,60,128]{2,1,0:T(8,128)(2,1)}), bf16[32,60,128]{2,1,0:T(8,128)(2,1)S(1)}, u32[]{:S(2)}, u32[]{:S(2)}) %all-to-all-start.4) | async-done | bytes 491552 | tf_op jit(solution)/shard_map/all_to_all | solution.py:128
  169.2 4.1 %all-to-all-start.5 = ((bf16[32,128,128]{2,1,0:T(8,128)(2,1)}), bf16[32,128,128]{2,1,0:T(8,128)(2,1)S(1)}, u32[]{:S(2)}, u32[]{:S(2)}) async-start(bf16[32,128,128]{2,1,0:T(8,128)(2,1)} %broadcast_in_dim.94), calls=%async_computation.5 | async-start | bytes 2097152 | tf_op jit(solution)/shard_map/all_to_all | solution.py:71
  173.3 2.0 copy.89
  175.3 34.5 %all-to-all-done.5 = bf16[32,128,128]{2,1,0:T(8,128)(2,1)S(1)} async-done(((bf16[32,128,128]{2,1,0:T(8,128)(2,1)}), bf16[32,128,128]{2,1,0:T(8,128)(2,1)S(1)}, u32[]{:S(2)}, u32[]{:S(2)}) %all-to-all-start.5) | async-done | bytes 1048608 | tf_op jit(solution)/shard_map/all_to_all | solution.py:71
  211.4 12.9 %all_to_all.50 = bf16[32,4,96]{2,1,0:T(4,128)(2,1)S(1)} all-to-all(bf16[32,4,96]{2,1,0:T(4,128)(2,1)S(1)} %bitcast.284), channel_id=1, replica_groups=mesh['section'=2,'grp'=4,'ta'=8,'tb'=4] {'ta','tb'}, dimensions={0} | all-to-all | bytes 49152 | tf_op jit(solution)/shard_map/all_to_all | solution.py:64
  226.0 4.6 %all-to-all-start.7 = ((bf16[32,4,3072]{2,1,0:T(4,128)(2,1)}), bf16[32,4,3072]{2,1,0:T(4,128)(2,1)}, u32[]{:S(2)}, u32[]{:S(2)}) async-start(bf16[32,4,3072]{2,1,0:T(4,128)(2,1)} %broadcast_in_dim.95), calls=%async_computation.7 | async-start | bytes 1572864 | tf_op jit(solution)/shard_map/all_to_all | solution.py:71
  233.3 21.2 %all-to-all-done.7 = bf16[32,4,3072]{2,1,0:T(4,128)(2,1)} async-done(((bf16[32,4,3072]{2,1,0:T(4,128)(2,1)}), bf16[32,4,3072]{2,1,0:T(4,128)(2,1)}, u32[]{:S(2)}, u32[]{:S(2)}) %all-to-all-start.7) | async-done | bytes 786464 | tf_op jit(solution)/shard_map/all_to_all | solution.py:71
  256.1 1.9 slice-done
  260.6 4.7 %all-to-all-start.8 = ((bf16[32,16,96]{2,1,0:T(8,128)(2,1)}), bf16[32,16,96]{2,1,0:T(8,128)(2,1)S(1)}, u32[]{:S(2)}, u32[]{:S(2)}) async-start(bf16[32,16,96]{2,1,0:T(8,128)(2,1)} %bitcast.54), calls=%async_computation.8 | async-start | bytes 262144 | tf_op jit(solution)/shard_map/all_to_all | solution.py:64
  265.3 3.7 %fusion = bf16[128,3072]{1,0:T(8,128)(2,1)} fusion(bf16[1,384,3072]{2,1,0:T(8,128)(2,1)S(1)} %copy-done, bf16[128,3072]{1,0:T(8,128)(2,1)S(1)} %reshape.513, bf16[1,3072,384]{2,1,0:T(8,128)(2,1)} %param.30), kind=kOutput, calls=%fused_computation.3 | convolution fusion | flops 604422144 | bytes 6291456 | tf_op jit(solution)/shard_map/dot_general | solution.py:225
  269.1 6.7 %all-to-all-done.8 = bf16[32,16,96]{2,1,0:T(8,128)(2,1)S(1)} async-done(((bf16[32,16,96]{2,1,0:T(8,128)(2,1)}), bf16[32,16,96]{2,1,0:T(8,128)(2,1)S(1)}, u32[]{:S(2)}, u32[]{:S(2)}) %all-to-all-start.8) | async-done | bytes 98336 | tf_op jit(solution)/shard_map/all_to_all | solution.py:64
  276.0 2.4 reshape.516
  278.4 3.9 %all-to-all-start.9 = ((bf16[32,4,3072]{2,1,0:T(4,128)(2,1)}), bf16[32,4,3072]{2,1,0:T(4,128)(2,1)S(1)}, u32[]{:S(2)}, u32[]{:S(2)}) async-start(bf16[32,4,3072]{2,1,0:T(4,128)(2,1)} %reshape.516), calls=%async_computation.9 | async-start | bytes 1572864 | tf_op jit(solution)/shard_map/all_to_all | solution.py:228
  284.2 3.0 collective-permute-start.5
  287.2 18.4 %all-to-all-done.9 = bf16[32,4,3072]{2,1,0:T(4,128)(2,1)S(1)} async-done(((bf16[32,4,3072]{2,1,0:T(4,128)(2,1)}), bf16[32,4,3072]{2,1,0:T(4,128)(2,1)S(1)}, u32[]{:S(2)}, u32[]{:S(2)}) %all-to-all-start.9) | async-done | bytes 786464 | tf_op jit(solution)/shard_map/all_to_all | solution.py:228
  306.0 3.0 collective-permute-start.4
  309.0 2.4 collective-permute-done.4
  311.7 1.7 fusion.27
  (162 shorter events, 48.8 us)
Async XLA Ops:
  7.2 258.2 %copy-start = (bf16[1,384,3072]{2,1,0:T(8,128)(2,1)S(1)}, bf16[1,384,3072]{2,1,0:T(8,128)(2,1)}, u32[]{:S(2)}) copy-start(bf16[1,384,3072]{2,1,0:T(8,128)(2,1)} %param.31) | copy-start | bytes 7077892
  7.2 32.0 %copy-start.13 = (f32[1,4,128]{2,1,0:T(4,128)S(1)}, f32[1,4,128]{2,1,0:T(4,128)}, u32[]{:S(2)}) copy-start(f32[1,4,128]{2,1,0:T(4,128)} %param.27) | copy-start | bytes 6148
  7.2 88.7 %all-gather.4.cloned.1.call-start = ((), (), s32[]{:S(2)}) async-start(), calls=%async_computation.10 | async-start | bytes 3244032 | tf_op jit(solution)/shard_map/all_gather | solution.py:130
  26.6 38.8 %all-to-all-start = ((bf16[32,4,3072]{2,1,0:T(4,128)(2,1)}), bf16[32,4,3072]{2,1,0:T(4,128)(2,1)S(1)}, u32[]{:S(2)}, u32[]{:S(2)}) async-start(bf16[32,4,3072]{2,1,0:T(4,128)(2,1)} %broadcast_in_dim.48), calls=%async_computation | async-start | bytes 1572864 | tf_op jit(solution)/shard_map/all_to_all | solution.py:71
  36.4 37.1 %copy-start.2 = (bf16[1,1,16,6144]{3,2,1,0:T(8,128)(2,1)S(1)}, bf16[1,1,16,6144]{3,2,1,0:T(8,128)(2,1)}, u32[]{:S(2)}) copy-start(bf16[1,1,16,6144]{3,2,1,0:T(8,128)(2,1)} %param.32) | copy-start | bytes 589828
  69.6 14.5 %all-to-all-start.2 = ((bf16[32,4,288]{2,1,0:T(4,128)(2,1)}), bf16[32,4,288]{2,1,0:T(4,128)(2,1)S(1)}, u32[]{:S(2)}, u32[]{:S(2)}) async-start(bf16[32,4,288]{2,1,0:T(4,128)(2,1)} %reshape.499), calls=%async_computation.2 | async-start | bytes 196608 | tf_op jit(solution)/shard_map/all_to_all | solution.py:64
  84.7 3.6 %collective-permute-start = (bf16[4,6144]{1,0:T(4,128)(2,1)S(1)}, bf16[4,6144]{1,0:T(4,128)(2,1)S(1)}, u32[]{:S(2)}, u32[]{:S(2)}) collective-permute-start(bf16[4,6144]{1,0:T(4,128)(2,1)S(1)} %get-tuple-element.43), channel_id=1, source_target_pairs={{0,1},{1,2},{2,3},{3,0},{4,5},{5,6},{6,7},{7,4},{8,9},{9,10},{10,1... | collective-permute-start | bytes 147464 | tf_op jit(solution)/shard_map/ppermute | solution.py:158
  84.8 4.7 %collective-permute-start.1 = (bf16[4,6144]{1,0:T(4,128)(2,1)S(1)}, bf16[4,6144]{1,0:T(4,128)(2,1)S(1)}, u32[]{:S(2)}, u32[]{:S(2)}) collective-permute-start(bf16[4,6144]{1,0:T(4,128)(2,1)S(1)} %get-tuple-element.43), channel_id=1, source_target_pairs={{0,2},{1,3},{2,0},{3,1},{4,6},{5,7},{6,4},{7,5},{8,10},{9,11},{10,... | collective-permute-start | bytes 147464 | tf_op jit(solution)/shard_map/ppermute | solution.py:158
  85.7 3.9 %collective-permute-start.2 = (bf16[4,6144]{1,0:T(4,128)(2,1)S(1)}, bf16[4,6144]{1,0:T(4,128)(2,1)S(1)}, u32[]{:S(2)}, u32[]{:S(2)}) collective-permute-start(bf16[4,6144]{1,0:T(4,128)(2,1)S(1)} %get-tuple-element.43), channel_id=1, source_target_pairs={{0,3},{1,0},{2,1},{3,2},{4,7},{5,4},{6,5},{7,6},{8,11},{9,8},{10,9... | collective-permute-start | bytes 147464 | tf_op jit(solution)/shard_map/ppermute | solution.py:158
  100.4 21.5 %all-to-all-start.3 = ((bf16[32,16,288]{2,1,0:T(8,128)(2,1)}), bf16[32,16,288]{2,1,0:T(8,128)(2,1)S(1)}, u32[]{:S(2)}, u32[]{:S(2)}) async-start(bf16[32,16,288]{2,1,0:T(8,128)(2,1)} %bitcast.17), calls=%async_computation.3 | async-start | bytes 786432 | tf_op jit(solution)/shard_map/all_to_all | solution.py:64
  106.9 39.7 %collective-permute-start.3 = (bf16[16,6144]{1,0:T(8,128)(2,1)}, bf16[16,6144]{1,0:T(8,128)(2,1)}, u32[]{:S(2)}, u32[]{:S(2)}) collective-permute-start(bf16[16,6144]{1,0:T(8,128)(2,1)} %broadcast_select_fusion), channel_id=1, source_target_pairs={{0,0},{1,8},{2,16},{3,24},{4,1},{5,9},{6,17},{7,25},{8,2},{9,10},{... | collective-permute-start | bytes 589832 | tf_op jit(solution)/shard_map/ppermute | solution.py:162
  121.9 20.6 %all-to-all-start.1 = ((bf16[32,32,128]{2,1,0:T(8,128)(2,1)}), bf16[32,32,128]{2,1,0:T(8,128)(2,1)S(1)}, u32[]{:S(2)}, u32[]{:S(2)}) async-start(bf16[32,32,128]{2,1,0:T(8,128)(2,1)} %pad.9.clone), calls=%async_computation.1 | async-start | bytes 524288 | tf_op jit(solution)/shard_map/all_to_all | solution.py:128
  130.5 16.1 %copy-start.3 = (bf16[1,1,16,6144]{3,2,1,0:T(8,128)(2,1)S(1)}, bf16[1,1,16,6144]{3,2,1,0:T(8,128)(2,1)}, u32[]{:S(2)}) copy-start(bf16[1,1,16,6144]{3,2,1,0:T(8,128)(2,1)} %param.32) | copy-start | bytes 589828
  133.4 31.6 %copy-start.12 = (pred[1024]{0:T(1024)(128)(4,1)S(1)}, pred[1024]{0:T(1024)(128)(4,1)}, u32[]{:S(2)}) copy-start(pred[1024]{0:T(1024)(128)(4,1)} %concatenate.46) | copy-start | bytes 3076
  142.4 22.4 %all-to-all-start.4 = ((bf16[32,60,128]{2,1,0:T(8,128)(2,1)}), bf16[32,60,128]{2,1,0:T(8,128)(2,1)S(1)}, u32[]{:S(2)}, u32[]{:S(2)}) async-start(bf16[32,60,128]{2,1,0:T(8,128)(2,1)} %pad.10.clone), calls=%async_computation.4 | async-start | bytes 1048576 | tf_op jit(solution)/shard_map/all_to_all | solution.py:128
  146.3 109.7 %all-gather.6.cloned.1.call-start = ((), (), s32[]{:S(2)}) async-start(), calls=%async_computation.11 | async-start | bytes 4325376 | tf_op jit(solution)/shard_map/all_gather | solution.py:197
  169.2 55.2 %copy-start.5 = (bf16[1,1,4,3072]{3,2,1,0:T(4,128)(2,1)S(1)}, bf16[1,1,4,3072]{3,2,1,0:T(4,128)(2,1)}, u32[]{:S(2)}) copy-start(bf16[1,1,4,3072]{3,2,1,0:T(4,128)(2,1)} %param.18) | copy-start | bytes 73732
  169.2 55.2 %copy-start.10 = (f32[1,1,3072]{2,1,0:T(1,128)S(1)}, f32[1,1,3072]{2,1,0:T(1,128)}, u32[]{:S(2)}) copy-start(f32[1,1,3072]{2,1,0:T(1,128)} %get-tuple-element.37) | copy-start | bytes 36868
  169.2 55.6 %copy-start.8 = (f32[1,1,3072]{2,1,0:T(1,128)S(1)}, f32[1,1,3072]{2,1,0:T(1,128)}, u32[]{:S(2)}) copy-start(f32[1,1,3072]{2,1,0:T(1,128)} %get-tuple-element.33) | copy-start | bytes 36868
  169.2 55.6 %copy-start.9 = (f32[1,1,3072]{2,1,0:T(1,128)S(1)}, f32[1,1,3072]{2,1,0:T(1,128)}, u32[]{:S(2)}) copy-start(f32[1,1,3072]{2,1,0:T(1,128)} %get-tuple-element.34) | copy-start | bytes 36868
  169.2 40.6 %all-to-all-start.5 = ((bf16[32,128,128]{2,1,0:T(8,128)(2,1)}), bf16[32,128,128]{2,1,0:T(8,128)(2,1)S(1)}, u32[]{:S(2)}, u32[]{:S(2)}) async-start(bf16[32,128,128]{2,1,0:T(8,128)(2,1)} %broadcast_in_dim.94), calls=%async_computation.5 | async-start | bytes 2097152 | tf_op jit(solution)/shard_map/all_to_all | solution.py:71
  226.0 28.4 %all-to-all-start.7 = ((bf16[32,4,3072]{2,1,0:T(4,128)(2,1)}), bf16[32,4,3072]{2,1,0:T(4,128)(2,1)}, u32[]{:S(2)}, u32[]{:S(2)}) async-start(bf16[32,4,3072]{2,1,0:T(4,128)(2,1)} %broadcast_in_dim.95), calls=%async_computation.7 | async-start | bytes 1572864 | tf_op jit(solution)/shard_map/all_to_all | solution.py:71
  256.0 1.9 slice-start
  260.6 15.2 %all-to-all-start.8 = ((bf16[32,16,96]{2,1,0:T(8,128)(2,1)}), bf16[32,16,96]{2,1,0:T(8,128)(2,1)S(1)}, u32[]{:S(2)}, u32[]{:S(2)}) async-start(bf16[32,16,96]{2,1,0:T(8,128)(2,1)} %bitcast.54), calls=%async_computation.8 | async-start | bytes 262144 | tf_op jit(solution)/shard_map/all_to_all | solution.py:64
  269.1 15.1 %copy-start.11 = (bf16[4,6144]{1,0:T(4,128)(2,1)S(1)}, bf16[4,6144]{1,0:T(4,128)(2,1)}, u32[]{:S(2)}) copy-start(bf16[4,6144]{1,0:T(4,128)(2,1)} %param.33) | copy-start | bytes 147460
  269.1 15.1 %copy-start.1 = (bf16[1,1,16,3072]{3,2,1,0:T(8,128)(2,1)S(1)}, bf16[1,1,16,3072]{3,2,1,0:T(8,128)(2,1)}, u32[]{:S(2)}) copy-start(bf16[1,1,16,3072]{3,2,1,0:T(8,128)(2,1)} %param.19) | copy-start | bytes 294916
  269.1 15.1 %copy-start.6 = (f32[1,1,3072]{2,1,0:T(1,128)S(1)}, f32[1,1,3072]{2,1,0:T(1,128)}, u32[]{:S(2)}) copy-start(f32[1,1,3072]{2,1,0:T(1,128)} %get-tuple-element.44) | copy-start | bytes 36868
  269.1 36.9 %copy-start.7 = (f32[1,1,3072]{2,1,0:T(1,128)S(1)}, f32[1,1,3072]{2,1,0:T(1,128)}, u32[]{:S(2)}) copy-start(f32[1,1,3072]{2,1,0:T(1,128)} %get-tuple-element.32) | copy-start | bytes 36868
  269.1 42.7 %copy-start.14 = (f32[1,4,32]{2,1,0:T(4,128)S(1)}, f32[1,4,32]{2,1,0:T(4,128)}, u32[]{:S(2)}) copy-start(f32[1,4,32]{2,1,0:T(4,128)} %param.35) | copy-start | bytes 1540
  278.4 27.2 %all-to-all-start.9 = ((bf16[32,4,3072]{2,1,0:T(4,128)(2,1)}), bf16[32,4,3072]{2,1,0:T(4,128)(2,1)S(1)}, u32[]{:S(2)}, u32[]{:S(2)}) async-start(bf16[32,4,3072]{2,1,0:T(4,128)(2,1)} %reshape.516), calls=%async_computation.9 | async-start | bytes 1572864 | tf_op jit(solution)/shard_map/all_to_all | solution.py:228
  284.2 24.7 %collective-permute-start.5 = (bf16[16,3072]{1,0:T(8,128)(2,1)S(1)}, bf16[16,3072]{1,0:T(8,128)(2,1)S(1)}, u32[]{:S(2)}, u32[]{:S(2)}) collective-permute-start(bf16[16,3072]{1,0:T(8,128)(2,1)S(1)} %fusion.53), channel_id=1, source_target_pairs={{128,0},{0,128},{129,1},{1,129},{130,2},{2,130},{131,3},{3,131},{1... | collective-permute-start | bytes 294920 | tf_op jit(solution)/shard_map/ppermute | solution.py:20
  306.0 5.4 %collective-permute-start.4 = (bf16[4,3072]{1,0:T(4,128)(2,1)S(1)}, bf16[4,3072]{1,0:T(4,128)(2,1)S(1)}, u32[]{:S(2)}, u32[]{:S(2)}) collective-permute-start(bf16[4,3072]{1,0:T(4,128)(2,1)S(1)} %add_convert_fusion), channel_id=1, source_target_pairs={{128,0},{0,128},{129,1},{1,129},{130,2},{2,130},{131,3},{3,131},{1... | collective-permute-start | bytes 73736 | tf_op jit(solution)/shard_map/ppermute | solution.py:20
  (1 other events, 1.3 us)
Sparse Core Ops, SparseCore 0:
  21.3 74.5 all-gather.3
  168.0 75.3 all-gather.5

commit v16 on v15

--- a/solution.py
+++ b/solution.py
@@ -132,6 +132,7 @@
     stale_late, every_image = lax.optimization_barrier((stale, every_image))
     got_cache = by_head([stale_late[:, :width], stale_late[:, width:]])
     image_cols = jnp.dot(every_image, image_to_heads[0], preferred_element_type=jnp.float32)
+    got_cache, every_text = lax.optimization_barrier((got_cache, every_text))
     text_cols = jnp.dot(every_text, text_to_heads[0], preferred_element_type=jnp.float32)
     image_proj = cols_to_rows(image_cols.astype(jnp.bfloat16).reshape(devices, image_rows, -1))
     text_proj = cols_to_rows(text_cols.astype(jnp.bfloat16).reshape(devices, text_rows, -1))

time: 324 us -> 318 us (0.981)
  waiting for transfers between devices: 161 us -> 155 us
    all_gather x1, waiting for transfers between devices: 5.41 us -> 0.01 us  [shards(): every_text = lax.all_gather(text_normed, TOK, axis=0, tiled=True)]
    all_to_all x2, waiting for transfers between devices: 23.9 us -> 19.1 us  [by_head(): return lax.all_to_all(pack, TOK, split_axis=0, concat_axis=0, tiled=True)]
    ppermute x3, waiting for transfers between devices: 1.89 us -> 5.96 us  [shards(): quad.append(lax.ppermute(fresh_image, TOK, turn))]
    unnamed x51 -> x57, local copies, waits for them, and re-layouts: 9.68 us -> 9.72 us
  transfers between devices with their start and end apart: 17 -> 17, of which waited for: 13 -> 12; matrix products, arithmetic and copies ran while one was open for 12% -> 12% of each run, Pallas kernels for 0% -> 0%
where the time goes in v16:
time: 318 us; the launch traced here: 316 us
  waiting for transfers between devices  155 us (49%)
  starting transfers between devices  58.5 us (18%)
  local copies, waits for them, and re-layouts  34.8 us (11%)
  between operations  24.6 us (8%)
  other arithmetic  15.3 us (5%)
  matrix products  14.9 us (5%)
  blocking collectives  12.9 us (4%)
    all_to_all x3, waiting for transfers between devices, broadcast_rows(): got = lax.all_to_all(copies, TOK, split_axis=0, concat_axis=0, tiled=True)  79.9 us
    all_to_all x3, waiting for transfers between devices, cols_to_rows(): got = lax.all_to_all(cols, TOK, split_axis=0, concat_axis=0, tiled=True)  28.5 us
    all_to_all x2, waiting for transfers between devices, by_head(): return lax.all_to_all(pack, TOK, split_axis=0, concat_axis=0, tiled=True)  19.1 us
    all_to_all x1, waiting for transfers between devices, shards(): lax.all_to_all(partial.astype(jnp.bfloat16).reshape(devices, image_rows,...  18.7 us
    all_to_all x3, starting transfers between devices, broadcast_rows(): got = lax.all_to_all(copies, TOK, split_axis=0, concat_axis=0, tiled=True)  18.6 us
    all_to_all x3, starting transfers between devices, cols_to_rows(): got = lax.all_to_all(cols, TOK, split_axis=0, concat_axis=0, tiled=True)  13.5 us
    all_to_all x1, blocking collectives, cols_to_rows(): got = lax.all_to_all(cols, TOK, split_axis=0, concat_axis=0, tiled=True)  12.9 us
    all_to_all x2, starting transfers between devices, by_head(): return lax.all_to_all(pack, TOK, split_axis=0, concat_axis=0, tiled=True)  11.2 us
  transfers between devices with their start and end apart: 17, of which 12 were waited for; matrix products, arithmetic and copies ran while one was open for 12% of the time, Pallas kernels for 0%

profile of v16, /device:TPU:2, one launch (start us, length us, event | category | flops | bytes accessed | tf_op | source)
XLA Modules:
  0.0 316.2 jit_solution(10084457309268771715)
XLA Ops:
  19.6 1.6 fusion.52
  26.6 9.9 %all-to-all-start = ((bf16[32,4,3072]{2,1,0:T(4,128)(2,1)}), bf16[32,4,3072]{2,1,0:T(4,128)(2,1)S(1)}, u32[]{:S(2)}, u32[]{:S(2)}) async-start(bf16[32,4,3072]{2,1,0:T(4,128)(2,1)} %broadcast_in_dim.48), calls=%async_computation | async-start | bytes 1572864 | tf_op jit(solution)/shard_map/all_to_all | solution.py:71
  41.6 23.9 %all-to-all-done = bf16[32,4,3072]{2,1,0:T(4,128)(2,1)S(1)} async-done(((bf16[32,4,3072]{2,1,0:T(4,128)(2,1)}), bf16[32,4,3072]{2,1,0:T(4,128)(2,1)S(1)}, u32[]{:S(2)}, u32[]{:S(2)}) %all-to-all-start) | async-done | bytes 786464 | tf_op jit(solution)/shard_map/all_to_all | solution.py:71
  66.5 2.4 fusion.22
  69.7 3.9 %all-to-all-start.2 = ((bf16[32,4,288]{2,1,0:T(4,128)(2,1)}), bf16[32,4,288]{2,1,0:T(4,128)(2,1)S(1)}, u32[]{:S(2)}, u32[]{:S(2)}) async-start(bf16[32,4,288]{2,1,0:T(4,128)(2,1)} %reshape.499), calls=%async_computation.2 | async-start | bytes 196608 | tf_op jit(solution)/shard_map/all_to_all | solution.py:64
  74.4 9.8 %all-to-all-done.2 = bf16[32,4,288]{2,1,0:T(4,128)(2,1)S(1)} async-done(((bf16[32,4,288]{2,1,0:T(4,128)(2,1)}), bf16[32,4,288]{2,1,0:T(4,128)(2,1)S(1)}, u32[]{:S(2)}, u32[]{:S(2)}) %all-to-all-start.2) | async-done | bytes 73760 | tf_op jit(solution)/shard_map/all_to_all | solution.py:64
  84.2 3.9 %all-to-all-start.1 = ((bf16[32,32,128]{2,1,0:T(8,128)(2,1)}), bf16[32,32,128]{2,1,0:T(8,128)(2,1)S(1)}, u32[]{:S(2)}, u32[]{:S(2)}) async-start(bf16[32,32,128]{2,1,0:T(8,128)(2,1)} %pad.9.clone), calls=%async_computation.1 | async-start | bytes 524288 | tf_op jit(solution)/shard_map/all_to_all | solution.py:128
  89.0 1.7 collective-permute-start.1
  92.6 4.9 %collective-permute-done = bf16[4,6144]{1,0:T(4,128)(2,1)S(1)} collective-permute-done((bf16[4,6144]{1,0:T(4,128)(2,1)S(1)}, bf16[4,6144]{1,0:T(4,128)(2,1)S(1)}, u32[]{:S(2)}, u32[]{:S(2)}) %collective-permute-start) | collective-permute-done | bytes 49184 | tf_op jit(solution)/shard_map/ppermute | solution.py:159
  101.3 3.5 %fusion.15 = bf16[512,288]{0,1:T(8,128)(2,1)S(1)} fusion(bf16[512,3072]{1,0:T(8,128)(2,1)} %all-gather.4.cloned.1.call-done, bf16[1,3072,288]{1,2,0:T(8,128)(2,1)} %param.26), kind=kOutput, calls=%fused_computation.18 | convolution fusion | flops 906117120 | bytes 5210112 | tf_op jit(solution)/shard_map/dot_general | solution.py:136
  105.7 5.4 %all-to-all-start.3 = ((bf16[32,16,288]{2,1,0:T(8,128)(2,1)}), bf16[32,16,288]{2,1,0:T(8,128)(2,1)S(1)}, u32[]{:S(2)}, u32[]{:S(2)}) async-start(bf16[32,16,288]{2,1,0:T(8,128)(2,1)} %bitcast.17), calls=%async_computation.3 | async-start | bytes 786432 | tf_op jit(solution)/shard_map/all_to_all | solution.py:64
  111.9 3.0 collective-permute-start.3
  114.9 12.0 %all-to-all-done.3 = bf16[32,16,288]{2,1,0:T(8,128)(2,1)S(1)} async-done(((bf16[32,16,288]{2,1,0:T(8,128)(2,1)}), bf16[32,16,288]{2,1,0:T(8,128)(2,1)S(1)}, u32[]{:S(2)}, u32[]{:S(2)}) %all-to-all-start.3) | async-done | bytes 294944 | tf_op jit(solution)/shard_map/all_to_all | solution.py:64
  133.6 7.4 %all-to-all-start.4 = ((bf16[32,60,128]{2,1,0:T(8,128)(2,1)}), bf16[32,60,128]{2,1,0:T(8,128)(2,1)S(1)}, u32[]{:S(2)}, u32[]{:S(2)}) async-start(bf16[32,60,128]{2,1,0:T(8,128)(2,1)} %pad.10.clone), calls=%async_computation.4 | async-start | bytes 1048576 | tf_op jit(solution)/shard_map/all_to_all | solution.py:128
  142.0 17.5 %all-to-all-done.4 = bf16[32,60,128]{2,1,0:T(8,128)(2,1)S(1)} async-done(((bf16[32,60,128]{2,1,0:T(8,128)(2,1)}), bf16[32,60,128]{2,1,0:T(8,128)(2,1)S(1)}, u32[]{:S(2)}, u32[]{:S(2)}) %all-to-all-start.4) | async-done | bytes 491552 | tf_op jit(solution)/shard_map/all_to_all | solution.py:128
  163.9 4.1 %all-to-all-start.5 = ((bf16[32,128,128]{2,1,0:T(8,128)(2,1)}), bf16[32,128,128]{2,1,0:T(8,128)(2,1)S(1)}, u32[]{:S(2)}, u32[]{:S(2)}) async-start(bf16[32,128,128]{2,1,0:T(8,128)(2,1)} %broadcast_in_dim.94), calls=%async_computation.5 | async-start | bytes 2097152 | tf_op jit(solution)/shard_map/all_to_all | solution.py:71
  168.0 2.0 copy.89
  170.0 34.5 %all-to-all-done.5 = bf16[32,128,128]{2,1,0:T(8,128)(2,1)S(1)} async-done(((bf16[32,128,128]{2,1,0:T(8,128)(2,1)}), bf16[32,128,128]{2,1,0:T(8,128)(2,1)S(1)}, u32[]{:S(2)}, u32[]{:S(2)}) %all-to-all-start.5) | async-done | bytes 1048608 | tf_op jit(solution)/shard_map/all_to_all | solution.py:71
  206.0 12.9 %all_to_all.50 = bf16[32,4,96]{2,1,0:T(4,128)(2,1)S(1)} all-to-all(bf16[32,4,96]{2,1,0:T(4,128)(2,1)S(1)} %bitcast.284), channel_id=1, replica_groups=mesh['section'=2,'grp'=4,'ta'=8,'tb'=4] {'ta','tb'}, dimensions={0} | all-to-all | bytes 49152 | tf_op jit(solution)/shard_map/all_to_all | solution.py:64
  220.7 4.6 %all-to-all-start.7 = ((bf16[32,4,3072]{2,1,0:T(4,128)(2,1)}), bf16[32,4,3072]{2,1,0:T(4,128)(2,1)}, u32[]{:S(2)}, u32[]{:S(2)}) async-start(bf16[32,4,3072]{2,1,0:T(4,128)(2,1)} %broadcast_in_dim.95), calls=%async_computation.7 | async-start | bytes 1572864 | tf_op jit(solution)/shard_map/all_to_all | solution.py:71
  228.0 21.5 %all-to-all-done.7 = bf16[32,4,3072]{2,1,0:T(4,128)(2,1)} async-done(((bf16[32,4,3072]{2,1,0:T(4,128)(2,1)}), bf16[32,4,3072]{2,1,0:T(4,128)(2,1)}, u32[]{:S(2)}, u32[]{:S(2)}) %all-to-all-start.7) | async-done | bytes 786464 | tf_op jit(solution)/shard_map/all_to_all | solution.py:71
  251.1 1.9 slice-done
  255.6 4.3 %all-to-all-start.8 = ((bf16[32,16,96]{2,1,0:T(8,128)(2,1)}), bf16[32,16,96]{2,1,0:T(8,128)(2,1)S(1)}, u32[]{:S(2)}, u32[]{:S(2)}) async-start(bf16[32,16,96]{2,1,0:T(8,128)(2,1)} %bitcast.54), calls=%async_computation.8 | async-start | bytes 262144 | tf_op jit(solution)/shard_map/all_to_all | solution.py:64
  260.0 3.8 %fusion = bf16[128,3072]{1,0:T(8,128)(2,1)} fusion(bf16[1,384,3072]{2,1,0:T(8,128)(2,1)S(1)} %copy-done, bf16[128,3072]{1,0:T(8,128)(2,1)S(1)} %reshape.513, bf16[1,3072,384]{2,1,0:T(8,128)(2,1)} %param.30), kind=kOutput, calls=%fused_computation.3 | convolution fusion | flops 604422144 | bytes 6291456 | tf_op jit(solution)/shard_map/dot_general | solution.py:226
  263.7 6.7 %all-to-all-done.8 = bf16[32,16,96]{2,1,0:T(8,128)(2,1)S(1)} async-done(((bf16[32,16,96]{2,1,0:T(8,128)(2,1)}), bf16[32,16,96]{2,1,0:T(8,128)(2,1)S(1)}, u32[]{:S(2)}, u32[]{:S(2)}) %all-to-all-start.8) | async-done | bytes 98336 | tf_op jit(solution)/shard_map/all_to_all | solution.py:64
  270.6 2.4 reshape.516
  273.0 3.9 %all-to-all-start.9 = ((bf16[32,4,3072]{2,1,0:T(4,128)(2,1)}), bf16[32,4,3072]{2,1,0:T(4,128)(2,1)S(1)}, u32[]{:S(2)}, u32[]{:S(2)}) async-start(bf16[32,4,3072]{2,1,0:T(4,128)(2,1)} %reshape.516), calls=%async_computation.9 | async-start | bytes 1572864 | tf_op jit(solution)/shard_map/all_to_all | solution.py:229
  279.1 2.4 collective-permute-start.5
  281.5 18.7 %all-to-all-done.9 = bf16[32,4,3072]{2,1,0:T(4,128)(2,1)S(1)} async-done(((bf16[32,4,3072]{2,1,0:T(4,128)(2,1)}), bf16[32,4,3072]{2,1,0:T(4,128)(2,1)S(1)}, u32[]{:S(2)}, u32[]{:S(2)}) %all-to-all-start.9) | async-done | bytes 786464 | tf_op jit(solution)/shard_map/all_to_all | solution.py:229
  300.6 2.4 collective-permute-start.4
  303.0 3.0 collective-permute-done.4
  306.4 1.7 fusion.27
  (168 shorter events, 50.2 us)
Async XLA Ops:
  7.2 252.8 %copy-start = (bf16[1,384,3072]{2,1,0:T(8,128)(2,1)S(1)}, bf16[1,384,3072]{2,1,0:T(8,128)(2,1)}, u32[]{:S(2)}) copy-start(bf16[1,384,3072]{2,1,0:T(8,128)(2,1)} %param.31) | copy-start | bytes 7077892
  7.2 33.2 %copy-start.15 = (f32[1,4,128]{2,1,0:T(4,128)S(1)}, f32[1,4,128]{2,1,0:T(4,128)}, u32[]{:S(2)}) copy-start(f32[1,4,128]{2,1,0:T(4,128)} %param.27) | copy-start | bytes 6148
  7.2 94.1 %all-gather.4.cloned.1.call-start = ((), (), s32[]{:S(2)}) async-start(), calls=%async_computation.10 | async-start | bytes 3244032 | tf_op jit(solution)/shard_map/all_gather | solution.py:130
  26.6 38.8 %all-to-all-start = ((bf16[32,4,3072]{2,1,0:T(4,128)(2,1)}), bf16[32,4,3072]{2,1,0:T(4,128)(2,1)S(1)}, u32[]{:S(2)}, u32[]{:S(2)}) async-start(bf16[32,4,3072]{2,1,0:T(4,128)(2,1)} %broadcast_in_dim.48), calls=%async_computation | async-start | bytes 1572864 | tf_op jit(solution)/shard_map/all_to_all | solution.py:71
  36.5 37.1 %copy-start.2 = (bf16[1,1,16,6144]{3,2,1,0:T(8,128)(2,1)S(1)}, bf16[1,1,16,6144]{3,2,1,0:T(8,128)(2,1)}, u32[]{:S(2)}) copy-start(bf16[1,1,16,6144]{3,2,1,0:T(8,128)(2,1)} %param.32) | copy-start | bytes 589828
  66.5 22.1 %copy-start.11 = (f32[3072]{0:T(1024)S(1)}, f32[3072]{0:T(1024)}, u32[]{:S(2)}) copy-start(f32[3072]{0:T(1024)} %get-tuple-element.66) | copy-start | bytes 36868
  66.5 22.1 %copy-start.12 = (f32[3072]{0:T(1024)S(1)}, f32[3072]{0:T(1024)}, u32[]{:S(2)}) copy-start(f32[3072]{0:T(1024)} %get-tuple-element.68) | copy-start | bytes 36868
  69.7 14.5 %all-to-all-start.2 = ((bf16[32,4,288]{2,1,0:T(4,128)(2,1)}), bf16[32,4,288]{2,1,0:T(4,128)(2,1)S(1)}, u32[]{:S(2)}, u32[]{:S(2)}) async-start(bf16[32,4,288]{2,1,0:T(4,128)(2,1)} %reshape.499), calls=%async_computation.2 | async-start | bytes 196608 | tf_op jit(solution)/shard_map/all_to_all | solution.py:64
  84.2 17.0 %all-to-all-start.1 = ((bf16[32,32,128]{2,1,0:T(8,128)(2,1)}), bf16[32,32,128]{2,1,0:T(8,128)(2,1)S(1)}, u32[]{:S(2)}, u32[]{:S(2)}) async-start(bf16[32,32,128]{2,1,0:T(8,128)(2,1)} %pad.9.clone), calls=%async_computation.1 | async-start | bytes 524288 | tf_op jit(solution)/shard_map/all_to_all | solution.py:128
  88.8 8.8 %collective-permute-start = (bf16[4,6144]{1,0:T(4,128)(2,1)S(1)}, bf16[4,6144]{1,0:T(4,128)(2,1)S(1)}, u32[]{:S(2)}, u32[]{:S(2)}) collective-permute-start(bf16[4,6144]{1,0:T(4,128)(2,1)S(1)} %get-tuple-element.47), channel_id=1, source_target_pairs={{0,1},{1,2},{2,3},{3,0},{4,5},{5,6},{6,7},{7,4},{8,9},{9,10},{10,1... | collective-permute-start | bytes 147464 | tf_op jit(solution)/shard_map/ppermute | solution.py:159
  89.0 9.6 %collective-permute-start.1 = (bf16[4,6144]{1,0:T(4,128)(2,1)S(1)}, bf16[4,6144]{1,0:T(4,128)(2,1)S(1)}, u32[]{:S(2)}, u32[]{:S(2)}) collective-permute-start(bf16[4,6144]{1,0:T(4,128)(2,1)S(1)} %get-tuple-element.47), channel_id=1, source_target_pairs={{0,2},{1,3},{2,0},{3,1},{4,6},{5,7},{6,4},{7,5},{8,10},{9,11},{10,... | collective-permute-start | bytes 147464 | tf_op jit(solution)/shard_map/ppermute | solution.py:159
  90.7 7.9 %collective-permute-start.2 = (bf16[4,6144]{1,0:T(4,128)(2,1)S(1)}, bf16[4,6144]{1,0:T(4,128)(2,1)S(1)}, u32[]{:S(2)}, u32[]{:S(2)}) collective-permute-start(bf16[4,6144]{1,0:T(4,128)(2,1)S(1)} %get-tuple-element.47), channel_id=1, source_target_pairs={{0,3},{1,0},{2,1},{3,2},{4,7},{5,4},{6,5},{7,6},{8,11},{9,8},{10,9... | collective-permute-start | bytes 147464 | tf_op jit(solution)/shard_map/ppermute | solution.py:159
  105.7 21.1 %all-to-all-start.3 = ((bf16[32,16,288]{2,1,0:T(8,128)(2,1)}), bf16[32,16,288]{2,1,0:T(8,128)(2,1)S(1)}, u32[]{:S(2)}, u32[]{:S(2)}) async-start(bf16[32,16,288]{2,1,0:T(8,128)(2,1)} %bitcast.17), calls=%async_computation.3 | async-start | bytes 786432 | tf_op jit(solution)/shard_map/all_to_all | solution.py:64
  111.9 29.4 %collective-permute-start.3 = (bf16[16,6144]{1,0:T(8,128)(2,1)}, bf16[16,6144]{1,0:T(8,128)(2,1)}, u32[]{:S(2)}, u32[]{:S(2)}) collective-permute-start(bf16[16,6144]{1,0:T(8,128)(2,1)} %broadcast_select_fusion), channel_id=1, source_target_pairs={{0,0},{1,8},{2,16},{3,24},{4,1},{5,9},{6,17},{7,25},{8,2},{9,10},{... | collective-permute-start | bytes 589832 | tf_op jit(solution)/shard_map/ppermute | solution.py:163
  131.0 28.6 %copy-start.14 = (pred[1024]{0:T(1024)(128)(4,1)S(1)}, pred[1024]{0:T(1024)(128)(4,1)}, u32[]{:S(2)}) copy-start(pred[1024]{0:T(1024)(128)(4,1)} %concatenate.46) | copy-start | bytes 3076
  133.6 25.8 %all-to-all-start.4 = ((bf16[32,60,128]{2,1,0:T(8,128)(2,1)}), bf16[32,60,128]{2,1,0:T(8,128)(2,1)S(1)}, u32[]{:S(2)}, u32[]{:S(2)}) async-start(bf16[32,60,128]{2,1,0:T(8,128)(2,1)} %pad.10.clone), calls=%async_computation.4 | async-start | bytes 1048576 | tf_op jit(solution)/shard_map/all_to_all | solution.py:128
  141.0 110.1 %all-gather.6.cloned.1.call-start = ((), (), s32[]{:S(2)}) async-start(), calls=%async_computation.11 | async-start | bytes 4325376 | tf_op jit(solution)/shard_map/all_gather | solution.py:198
  163.9 55.3 %copy-start.5 = (bf16[1,1,4,3072]{3,2,1,0:T(4,128)(2,1)S(1)}, bf16[1,1,4,3072]{3,2,1,0:T(4,128)(2,1)}, u32[]{:S(2)}) copy-start(bf16[1,1,4,3072]{3,2,1,0:T(4,128)(2,1)} %param.18) | copy-start | bytes 73732
  163.9 55.3 %copy-start.10 = (f32[1,1,3072]{2,1,0:T(1,128)S(1)}, f32[1,1,3072]{2,1,0:T(1,128)}, u32[]{:S(2)}) copy-start(f32[1,1,3072]{2,1,0:T(1,128)} %get-tuple-element.41) | copy-start | bytes 36868
  163.9 55.6 %copy-start.8 = (f32[1,1,3072]{2,1,0:T(1,128)S(1)}, f32[1,1,3072]{2,1,0:T(1,128)}, u32[]{:S(2)}) copy-start(f32[1,1,3072]{2,1,0:T(1,128)} %get-tuple-element.37) | copy-start | bytes 36868
  163.9 55.6 %copy-start.9 = (f32[1,1,3072]{2,1,0:T(1,128)S(1)}, f32[1,1,3072]{2,1,0:T(1,128)}, u32[]{:S(2)}) copy-start(f32[1,1,3072]{2,1,0:T(1,128)} %get-tuple-element.38) | copy-start | bytes 36868
  163.9 40.6 %all-to-all-start.5 = ((bf16[32,128,128]{2,1,0:T(8,128)(2,1)}), bf16[32,128,128]{2,1,0:T(8,128)(2,1)S(1)}, u32[]{:S(2)}, u32[]{:S(2)}) async-start(bf16[32,128,128]{2,1,0:T(8,128)(2,1)} %broadcast_in_dim.94), calls=%async_computation.5 | async-start | bytes 2097152 | tf_op jit(solution)/shard_map/all_to_all | solution.py:71
  220.7 28.8 %all-to-all-start.7 = ((bf16[32,4,3072]{2,1,0:T(4,128)(2,1)}), bf16[32,4,3072]{2,1,0:T(4,128)(2,1)}, u32[]{:S(2)}, u32[]{:S(2)}) async-start(bf16[32,4,3072]{2,1,0:T(4,128)(2,1)} %broadcast_in_dim.95), calls=%async_computation.7 | async-start | bytes 1572864 | tf_op jit(solution)/shard_map/all_to_all | solution.py:71
  255.6 14.8 %all-to-all-start.8 = ((bf16[32,16,96]{2,1,0:T(8,128)(2,1)}), bf16[32,16,96]{2,1,0:T(8,128)(2,1)S(1)}, u32[]{:S(2)}, u32[]{:S(2)}) async-start(bf16[32,16,96]{2,1,0:T(8,128)(2,1)} %bitcast.54), calls=%async_computation.8 | async-start | bytes 262144 | tf_op jit(solution)/shard_map/all_to_all | solution.py:64
  263.7 15.3 %copy-start.13 = (bf16[4,6144]{1,0:T(4,128)(2,1)S(1)}, bf16[4,6144]{1,0:T(4,128)(2,1)}, u32[]{:S(2)}) copy-start(bf16[4,6144]{1,0:T(4,128)(2,1)} %param.33) | copy-start | bytes 147460
  263.7 15.3 %copy-start.1 = (bf16[1,1,16,3072]{3,2,1,0:T(8,128)(2,1)S(1)}, bf16[1,1,16,3072]{3,2,1,0:T(8,128)(2,1)}, u32[]{:S(2)}) copy-start(bf16[1,1,16,3072]{3,2,1,0:T(8,128)(2,1)} %param.19) | copy-start | bytes 294916
  263.7 15.3 %copy-start.6 = (f32[1,1,3072]{2,1,0:T(1,128)S(1)}, f32[1,1,3072]{2,1,0:T(1,128)}, u32[]{:S(2)}) copy-start(f32[1,1,3072]{2,1,0:T(1,128)} %get-tuple-element.48) | copy-start | bytes 36868
  263.7 36.8 %copy-start.7 = (f32[1,1,3072]{2,1,0:T(1,128)S(1)}, f32[1,1,3072]{2,1,0:T(1,128)}, u32[]{:S(2)}) copy-start(f32[1,1,3072]{2,1,0:T(1,128)} %get-tuple-element.36) | copy-start | bytes 36868
  263.7 42.6 %copy-start.17 = (f32[1,4,32]{2,1,0:T(4,128)S(1)}, f32[1,4,32]{2,1,0:T(4,128)}, u32[]{:S(2)}) copy-start(f32[1,4,32]{2,1,0:T(4,128)} %param.35) | copy-start | bytes 1540
  273.0 27.2 %all-to-all-start.9 = ((bf16[32,4,3072]{2,1,0:T(4,128)(2,1)}), bf16[32,4,3072]{2,1,0:T(4,128)(2,1)S(1)}, u32[]{:S(2)}, u32[]{:S(2)}) async-start(bf16[32,4,3072]{2,1,0:T(4,128)(2,1)} %reshape.516), calls=%async_computation.9 | async-start | bytes 1572864 | tf_op jit(solution)/shard_map/all_to_all | solution.py:229
  279.1 23.9 %collective-permute-start.5 = (bf16[16,3072]{1,0:T(8,128)(2,1)S(1)}, bf16[16,3072]{1,0:T(8,128)(2,1)S(1)}, u32[]{:S(2)}, u32[]{:S(2)}) collective-permute-start(bf16[16,3072]{1,0:T(8,128)(2,1)S(1)} %fusion.53), channel_id=1, source_target_pairs={{128,0},{0,128},{129,1},{1,129},{130,2},{2,130},{131,3},{3,131},{1... | collective-permute-start | bytes 294920 | tf_op jit(solution)/shard_map/ppermute | solution.py:20
  300.6 5.4 %collective-permute-start.4 = (bf16[4,3072]{1,0:T(4,128)(2,1)S(1)}, bf16[4,3072]{1,0:T(4,128)(2,1)S(1)}, u32[]{:S(2)}, u32[]{:S(2)}) collective-permute-start(bf16[4,3072]{1,0:T(4,128)(2,1)S(1)} %add_convert_fusion), channel_id=1, source_target_pairs={{128,0},{0,128},{129,1},{1,129},{130,2},{2,130},{131,3},{3,131},{1... | collective-permute-start | bytes 73736 | tf_op jit(solution)/shard_map/ppermute | solution.py:20
  (4 other events, 27.8 us)
Sparse Core Ops, SparseCore 0:
  21.3 76.2 all-gather.3
  162.6 75.3 all-gather.5

commit v17 on v16

--- a/solution.py
+++ b/solution.py
@@ -133,9 +133,7 @@
     got_cache = by_head([stale_late[:, :width], stale_late[:, width:]])
     image_cols = jnp.dot(every_image, image_to_heads[0], preferred_element_type=jnp.float32)
     got_cache, every_text = lax.optimization_barrier((got_cache, every_text))
-    text_cols = jnp.dot(every_text, text_to_heads[0], preferred_element_type=jnp.float32)
     image_proj = cols_to_rows(image_cols.astype(jnp.bfloat16).reshape(devices, image_rows, -1))
-    text_proj = cols_to_rows(text_cols.astype(jnp.bfloat16).reshape(devices, text_rows, -1))
     gains = head_gain[0]
     image_query = head_norm(image_proj[:, :width].astype(jnp.float32), gains[0]).astype(
         jnp.bfloat16
@@ -143,11 +141,15 @@
     image_key = head_norm(image_proj[:, width : 2 * width].astype(jnp.float32), gains[1]).astype(
         jnp.bfloat16
     )
+    image_value = image_proj[:, 2 * width :]
+    got_image = by_head([image_query, image_key, image_value])
+    got_image, every_text = lax.optimization_barrier((got_image, every_text))
+    text_cols = jnp.dot(every_text, text_to_heads[0], preferred_element_type=jnp.float32)
+    text_proj = cols_to_rows(text_cols.astype(jnp.bfloat16).reshape(devices, text_rows, -1))
     text_query = head_norm(text_proj[:, :width].astype(jnp.float32), gains[2]).astype(jnp.bfloat16)
     text_key = head_norm(text_proj[:, width : 2 * width].astype(jnp.float32), gains[3]).astype(
         jnp.bfloat16
     )
-    image_value = image_proj[:, 2 * width :]
     text_value = text_proj[:, 2 * width :]
     fresh_image = jnp.concatenate([image_key, image_value], axis=1)
     group = lax.axis_size("tb")
@@ -164,21 +166,17 @@
     patch_len = image_rows * devices
     per_patch = patch_len // cache_rows
     current = jnp.where(position // per_patch == patch, moved, stale)
-    row_q = jnp.concatenate([image_query, text_query], axis=0)
-    row_k = jnp.concatenate([image_key, text_key], axis=0)
-    row_v = jnp.concatenate([image_value, text_value], axis=0)
-    got = by_head([row_q, row_k, row_v])
+    got = by_head([text_query, text_key, text_value])
     got, current = lax.optimization_barrier((got, current))
-    rows = image_rows + text_rows
 
     def part(first, count, source=got):
         return source[:, first : first + count].reshape(-1, HDIM)
 
-    queries = jnp.concatenate([part(0, image_rows), part(image_rows, text_rows)], axis=0)
-    fresh_k = part(rows, image_rows)
-    text_k = part(rows + image_rows, text_rows)
-    fresh_v = part(2 * rows, image_rows)
-    text_v = part(2 * rows + image_rows, text_rows)
+    queries = jnp.concatenate([part(0, image_rows, got_image), part(0, text_rows)], axis=0)
+    fresh_k = part(image_rows, image_rows, got_image)
+    text_k = part(text_rows, text_rows)
+    fresh_v = part(2 * image_rows, image_rows, got_image)
+    text_v = part(2 * text_rows, text_rows)
     cache_k = part(0, cache_rows, got_cache)
     cache_v = part(cache_rows, cache_rows, got_cache)
     begin = patch * patch_len

time: 318 us -> 326 us (1.025)
  waiting for transfers between devices: 155 us -> 165 us
  local copies, waits for them, and re-layouts: 34.8 us -> 31.4 us
    all_to_all x2 -> x3, waiting for transfers between devices: 19.1 us -> 31.9 us  [by_head(): return lax.all_to_all(pack, TOK, split_axis=0, concat_axis=0, tiled=True)]
    ppermute x3, waiting for transfers between devices: 5.96 us -> 0.01 us  [shards(): quad.append(lax.ppermute(fresh_image, TOK, turn))]
    all_to_all x2 -> x3, starting transfers between devices: 11.2 us -> 14.9 us  [by_head(): return lax.all_to_all(pack, TOK, split_axis=0, concat_axis=0, tiled=True)]
    unnamed x57 -> x48, local copies, waits for them, and re-layouts: 9.72 us -> 7.14 us
  transfers between devices with their start and end apart: 17 -> 18, of which waited for: 12 -> 11; matrix products, arithmetic and copies ran while one was open for 12% -> 11% of each run, Pallas kernels for 0% -> 0%
where the time goes in v17:
time: 326 us; the launch traced here: 324 us
  waiting for transfers between devices  165 us (51%)
  starting transfers between devices  59.6 us (18%)
  local copies, waits for them, and re-layouts  31.4 us (10%)
  between operations  24.7 us (8%)
  other arithmetic  15.7 us (5%)
  matrix products  14.8 us (5%)
  blocking collectives  13.4 us (4%)
    all_to_all x3, waiting for transfers between devices, broadcast_rows(): got = lax.all_to_all(copies, TOK, split_axis=0, concat_axis=0, tiled=True)  80.7 us
    all_to_all x3, waiting for transfers between devices, by_head(): return lax.all_to_all(pack, TOK, split_axis=0, concat_axis=0, tiled=True)  31.9 us
    all_to_all x3, waiting for transfers between devices, cols_to_rows(): got = lax.all_to_all(cols, TOK, split_axis=0, concat_axis=0, tiled=True)  28.6 us
    all_to_all x1, waiting for transfers between devices, shards(): lax.all_to_all(partial.astype(jnp.bfloat16).reshape(devices, image_rows,...  19.5 us
    all_to_all x3, starting transfers between devices, broadcast_rows(): got = lax.all_to_all(copies, TOK, split_axis=0, concat_axis=0, tiled=True)  18.6 us
    all_to_all x3, starting transfers between devices, by_head(): return lax.all_to_all(pack, TOK, split_axis=0, concat_axis=0, tiled=True)  14.9 us
    all_to_all x1, blocking collectives, cols_to_rows(): got = lax.all_to_all(cols, TOK, split_axis=0, concat_axis=0, tiled=True)  13.4 us
    all_to_all x3, starting transfers between devices, cols_to_rows(): got = lax.all_to_all(cols, TOK, split_axis=0, concat_axis=0, tiled=True)  12.4 us
  transfers between devices with their start and end apart: 18, of which 11 were waited for; matrix products, arithmetic and copies ran while one was open for 11% of the time, Pallas kernels for 0%

profile of v17, /device:TPU:2, one launch (start us, length us, event | category | flops | bytes accessed | tf_op | source)
XLA Modules:
  0.0 324.1 jit_solution(9002145937279823124)
XLA Ops:
  19.0 1.6 fusion.52
  26.0 9.9 %all-to-all-start = ((bf16[32,4,3072]{2,1,0:T(4,128)(2,1)}), bf16[32,4,3072]{2,1,0:T(4,128)(2,1)S(1)}, u32[]{:S(2)}, u32[]{:S(2)}) async-start(bf16[32,4,3072]{2,1,0:T(4,128)(2,1)} %broadcast_in_dim.48), calls=%async_computation | async-start | bytes 1572864 | tf_op jit(solution)/shard_map/all_to_all | solution.py:71
  39.9 25.0 %all-to-all-done = bf16[32,4,3072]{2,1,0:T(4,128)(2,1)S(1)} async-done(((bf16[32,4,3072]{2,1,0:T(4,128)(2,1)}), bf16[32,4,3072]{2,1,0:T(4,128)(2,1)S(1)}, u32[]{:S(2)}, u32[]{:S(2)}) %all-to-all-start) | async-done | bytes 786464 | tf_op jit(solution)/shard_map/all_to_all | solution.py:71
  66.0 2.3 fusion.22
  69.1 3.9 %all-to-all-start.2 = ((bf16[32,4,288]{2,1,0:T(4,128)(2,1)}), bf16[32,4,288]{2,1,0:T(4,128)(2,1)S(1)}, u32[]{:S(2)}, u32[]{:S(2)}) async-start(bf16[32,4,288]{2,1,0:T(4,128)(2,1)} %reshape.508), calls=%async_computation.2 | async-start | bytes 196608 | tf_op jit(solution)/shard_map/all_to_all | solution.py:64
  73.9 9.8 %all-to-all-done.2 = bf16[32,4,288]{2,1,0:T(4,128)(2,1)S(1)} async-done(((bf16[32,4,288]{2,1,0:T(4,128)(2,1)}), bf16[32,4,288]{2,1,0:T(4,128)(2,1)S(1)}, u32[]{:S(2)}, u32[]{:S(2)}) %all-to-all-start.2) | async-done | bytes 73760 | tf_op jit(solution)/shard_map/all_to_all | solution.py:64
  83.7 3.9 %all-to-all-start.1 = ((bf16[32,32,128]{2,1,0:T(8,128)(2,1)}), bf16[32,32,128]{2,1,0:T(8,128)(2,1)S(1)}, u32[]{:S(2)}, u32[]{:S(2)}) async-start(bf16[32,32,128]{2,1,0:T(8,128)(2,1)} %pad.13.clone), calls=%async_computation.1 | async-start | bytes 524288 | tf_op jit(solution)/shard_map/all_to_all | solution.py:128
  88.4 1.7 collective-permute-start.1
  92.1 8.6 %all-to-all-done.1 = bf16[32,32,128]{2,1,0:T(8,128)(2,1)S(1)} async-done(((bf16[32,32,128]{2,1,0:T(8,128)(2,1)}), bf16[32,32,128]{2,1,0:T(8,128)(2,1)S(1)}, u32[]{:S(2)}, u32[]{:S(2)}) %all-to-all-start.1) | async-done | bytes 262176 | tf_op jit(solution)/shard_map/all_to_all | solution.py:128
  100.7 3.9 %all-to-all-start.3 = ((bf16[32,12,128]{2,1,0:T(8,128)(2,1)}), bf16[32,12,128]{2,1,0:T(8,128)(2,1)S(1)}, u32[]{:S(2)}, u32[]{:S(2)}) async-start(bf16[32,12,128]{2,1,0:T(8,128)(2,1)} %pad.14), calls=%async_computation.3 | async-start | bytes 262144 | tf_op jit(solution)/shard_map/all_to_all | solution.py:128
  105.6 9.4 %all-to-all-done.3 = bf16[32,12,128]{2,1,0:T(8,128)(2,1)S(1)} async-done(((bf16[32,12,128]{2,1,0:T(8,128)(2,1)}), bf16[32,12,128]{2,1,0:T(8,128)(2,1)S(1)}, u32[]{:S(2)}, u32[]{:S(2)}) %all-to-all-start.3) | async-done | bytes 98336 | tf_op jit(solution)/shard_map/all_to_all | solution.py:128
  115.1 3.5 %fusion.15 = bf16[512,288]{0,1:T(8,128)(2,1)S(1)} fusion(bf16[512,3072]{1,0:T(8,128)(2,1)} %all-gather.4.cloned.1.call-done, bf16[1,3072,288]{1,2,0:T(8,128)(2,1)} %param.26), kind=kOutput, calls=%fused_computation.18 | convolution fusion | flops 906117120 | bytes 5210112 | tf_op jit(solution)/shard_map/dot_general | solution.py:147
  119.5 3.9 %all-to-all-start.4 = ((bf16[32,16,288]{2,1,0:T(8,128)(2,1)}), bf16[32,16,288]{2,1,0:T(8,128)(2,1)S(1)}, u32[]{:S(2)}, u32[]{:S(2)}) async-start(bf16[32,16,288]{2,1,0:T(8,128)(2,1)} %bitcast.24), calls=%async_computation.4 | async-start | bytes 786432 | tf_op jit(solution)/shard_map/all_to_all | solution.py:64
  124.2 3.0 collective-permute-start.3
  127.2 12.0 %all-to-all-done.4 = bf16[32,16,288]{2,1,0:T(8,128)(2,1)S(1)} async-done(((bf16[32,16,288]{2,1,0:T(8,128)(2,1)}), bf16[32,16,288]{2,1,0:T(8,128)(2,1)S(1)}, u32[]{:S(2)}, u32[]{:S(2)}) %all-to-all-start.4) | async-done | bytes 294944 | tf_op jit(solution)/shard_map/all_to_all | solution.py:64
  143.9 7.2 %all-to-all-start.5 = ((bf16[32,48,128]{2,1,0:T(8,128)(2,1)}), bf16[32,48,128]{2,1,0:T(8,128)(2,1)S(1)}, u32[]{:S(2)}, u32[]{:S(2)}) async-start(bf16[32,48,128]{2,1,0:T(8,128)(2,1)} %pad.15.clone), calls=%async_computation.5 | async-start | bytes 786432 | tf_op jit(solution)/shard_map/all_to_all | solution.py:128
  153.1 13.9 %all-to-all-done.5 = bf16[32,48,128]{2,1,0:T(8,128)(2,1)S(1)} async-done(((bf16[32,48,128]{2,1,0:T(8,128)(2,1)}), bf16[32,48,128]{2,1,0:T(8,128)(2,1)S(1)}, u32[]{:S(2)}, u32[]{:S(2)}) %all-to-all-start.5) | async-done | bytes 393248 | tf_op jit(solution)/shard_map/all_to_all | solution.py:128
  171.3 4.1 %all-to-all-start.6 = ((bf16[32,128,128]{2,1,0:T(8,128)(2,1)}), bf16[32,128,128]{2,1,0:T(8,128)(2,1)S(1)}, u32[]{:S(2)}, u32[]{:S(2)}) async-start(bf16[32,128,128]{2,1,0:T(8,128)(2,1)} %broadcast_in_dim.94), calls=%async_computation.6 | async-start | bytes 2097152 | tf_op jit(solution)/shard_map/all_to_all | solution.py:71
  175.3 2.0 copy.92
  177.3 34.6 %all-to-all-done.6 = bf16[32,128,128]{2,1,0:T(8,128)(2,1)S(1)} async-done(((bf16[32,128,128]{2,1,0:T(8,128)(2,1)}), bf16[32,128,128]{2,1,0:T(8,128)(2,1)S(1)}, u32[]{:S(2)}, u32[]{:S(2)}) %all-to-all-start.6) | async-done | bytes 1048608 | tf_op jit(solution)/shard_map/all_to_all | solution.py:71
  213.5 13.4 %all_to_all.55 = bf16[32,4,96]{2,1,0:T(4,128)(2,1)S(1)} all-to-all(bf16[32,4,96]{2,1,0:T(4,128)(2,1)S(1)} %bitcast.283), channel_id=1, replica_groups=mesh['section'=2,'grp'=4,'ta'=8,'tb'=4] {'ta','tb'}, dimensions={0} | all-to-all | bytes 49152 | tf_op jit(solution)/shard_map/all_to_all | solution.py:64
  228.6 4.6 %all-to-all-start.8 = ((bf16[32,4,3072]{2,1,0:T(4,128)(2,1)}), bf16[32,4,3072]{2,1,0:T(4,128)(2,1)}, u32[]{:S(2)}, u32[]{:S(2)}) async-start(bf16[32,4,3072]{2,1,0:T(4,128)(2,1)} %broadcast_in_dim.95), calls=%async_computation.8 | async-start | bytes 1572864 | tf_op jit(solution)/shard_map/all_to_all | solution.py:71
  235.9 21.0 %all-to-all-done.8 = bf16[32,4,3072]{2,1,0:T(4,128)(2,1)} async-done(((bf16[32,4,3072]{2,1,0:T(4,128)(2,1)}), bf16[32,4,3072]{2,1,0:T(4,128)(2,1)}, u32[]{:S(2)}, u32[]{:S(2)}) %all-to-all-start.8) | async-done | bytes 786464 | tf_op jit(solution)/shard_map/all_to_all | solution.py:71
  258.5 1.9 slice-done
  263.1 4.7 %all-to-all-start.9 = ((bf16[32,16,96]{2,1,0:T(8,128)(2,1)}), bf16[32,16,96]{2,1,0:T(8,128)(2,1)S(1)}, u32[]{:S(2)}, u32[]{:S(2)}) async-start(bf16[32,16,96]{2,1,0:T(8,128)(2,1)} %bitcast.58), calls=%async_computation.9 | async-start | bytes 262144 | tf_op jit(solution)/shard_map/all_to_all | solution.py:64
  267.8 3.7 %fusion = bf16[128,3072]{1,0:T(8,128)(2,1)} fusion(bf16[1,384,3072]{2,1,0:T(8,128)(2,1)S(1)} %copy-done, bf16[128,3072]{1,0:T(8,128)(2,1)S(1)} %reshape.527, bf16[1,3072,384]{2,1,0:T(8,128)(2,1)} %param.30), kind=kOutput, calls=%fused_computation.3 | convolution fusion | flops 604422144 | bytes 6291456 | tf_op jit(solution)/shard_map/dot_general | solution.py:224
  271.5 6.7 %all-to-all-done.9 = bf16[32,16,96]{2,1,0:T(8,128)(2,1)S(1)} async-done(((bf16[32,16,96]{2,1,0:T(8,128)(2,1)}), bf16[32,16,96]{2,1,0:T(8,128)(2,1)S(1)}, u32[]{:S(2)}, u32[]{:S(2)}) %all-to-all-start.9) | async-done | bytes 98336 | tf_op jit(solution)/shard_map/all_to_all | solution.py:64
  278.4 2.4 reshape.530
  280.9 3.9 %all-to-all-start.10 = ((bf16[32,4,3072]{2,1,0:T(4,128)(2,1)}), bf16[32,4,3072]{2,1,0:T(4,128)(2,1)S(1)}, u32[]{:S(2)}, u32[]{:S(2)}) async-start(bf16[32,4,3072]{2,1,0:T(4,128)(2,1)} %reshape.530), calls=%async_computation.10 | async-start | bytes 1572864 | tf_op jit(solution)/shard_map/all_to_all | solution.py:227
  288.6 19.5 %all-to-all-done.10 = bf16[32,4,3072]{2,1,0:T(4,128)(2,1)S(1)} async-done(((bf16[32,4,3072]{2,1,0:T(4,128)(2,1)}), bf16[32,4,3072]{2,1,0:T(4,128)(2,1)S(1)}, u32[]{:S(2)}, u32[]{:S(2)}) %all-to-all-start.10) | async-done | bytes 786464 | tf_op jit(solution)/shard_map/all_to_all | solution.py:227
  310.1 3.8 %collective-permute-done.4 = bf16[4,3072]{1,0:T(4,128)(2,1)S(1)} collective-permute-done((bf16[4,3072]{1,0:T(4,128)(2,1)S(1)}, bf16[4,3072]{1,0:T(4,128)(2,1)S(1)}, u32[]{:S(2)}, u32[]{:S(2)}) %collective-permute-start.4) | collective-permute-done | bytes 24608 | tf_op jit(solution)/shard_map/ppermute | solution.py:20
  314.2 1.7 fusion.27
  (161 shorter events, 47.8 us)
Async XLA Ops:
  7.2 260.6 %copy-start = (bf16[1,384,3072]{2,1,0:T(8,128)(2,1)S(1)}, bf16[1,384,3072]{2,1,0:T(8,128)(2,1)}, u32[]{:S(2)}) copy-start(bf16[1,384,3072]{2,1,0:T(8,128)(2,1)} %param.31) | copy-start | bytes 7077892
  7.2 32.0 %copy-start.12 = (f32[1,4,128]{2,1,0:T(4,128)S(1)}, f32[1,4,128]{2,1,0:T(4,128)}, u32[]{:S(2)}) copy-start(f32[1,4,128]{2,1,0:T(4,128)} %param.27) | copy-start | bytes 6148
  7.2 98.4 %all-gather.4.cloned.1.call-start = ((), (), s32[]{:S(2)}) async-start(), calls=%async_computation.11 | async-start | bytes 3244032 | tf_op jit(solution)/shard_map/all_gather | solution.py:130
  26.0 38.8 %all-to-all-start = ((bf16[32,4,3072]{2,1,0:T(4,128)(2,1)}), bf16[32,4,3072]{2,1,0:T(4,128)(2,1)S(1)}, u32[]{:S(2)}, u32[]{:S(2)}) async-start(bf16[32,4,3072]{2,1,0:T(4,128)(2,1)} %broadcast_in_dim.48), calls=%async_computation | async-start | bytes 1572864 | tf_op jit(solution)/shard_map/all_to_all | solution.py:71
  35.9 37.1 %copy-start.2 = (bf16[1,1,16,6144]{3,2,1,0:T(8,128)(2,1)S(1)}, bf16[1,1,16,6144]{3,2,1,0:T(8,128)(2,1)}, u32[]{:S(2)}) copy-start(bf16[1,1,16,6144]{3,2,1,0:T(8,128)(2,1)} %param.32) | copy-start | bytes 589828
  69.1 14.5 %all-to-all-start.2 = ((bf16[32,4,288]{2,1,0:T(4,128)(2,1)}), bf16[32,4,288]{2,1,0:T(4,128)(2,1)S(1)}, u32[]{:S(2)}, u32[]{:S(2)}) async-start(bf16[32,4,288]{2,1,0:T(4,128)(2,1)} %reshape.508), calls=%async_computation.2 | async-start | bytes 196608 | tf_op jit(solution)/shard_map/all_to_all | solution.py:64
  83.7 17.1 %all-to-all-start.1 = ((bf16[32,32,128]{2,1,0:T(8,128)(2,1)}), bf16[32,32,128]{2,1,0:T(8,128)(2,1)S(1)}, u32[]{:S(2)}, u32[]{:S(2)}) async-start(bf16[32,32,128]{2,1,0:T(8,128)(2,1)} %pad.13.clone), calls=%async_computation.1 | async-start | bytes 524288 | tf_op jit(solution)/shard_map/all_to_all | solution.py:128
  88.2 16.4 %collective-permute-start = (bf16[4,6144]{1,0:T(4,128)(2,1)S(1)}, bf16[4,6144]{1,0:T(4,128)(2,1)S(1)}, u32[]{:S(2)}, u32[]{:S(2)}) collective-permute-start(bf16[4,6144]{1,0:T(4,128)(2,1)S(1)} %get-tuple-element.53), channel_id=1, source_target_pairs={{0,1},{1,2},{2,3},{3,0},{4,5},{5,6},{6,7},{7,4},{8,9},{9,10},{10,1... | collective-permute-start | bytes 147464 | tf_op jit(solution)/shard_map/ppermute | solution.py:161
  88.4 16.2 %collective-permute-start.1 = (bf16[4,6144]{1,0:T(4,128)(2,1)S(1)}, bf16[4,6144]{1,0:T(4,128)(2,1)S(1)}, u32[]{:S(2)}, u32[]{:S(2)}) collective-permute-start(bf16[4,6144]{1,0:T(4,128)(2,1)S(1)} %get-tuple-element.53), channel_id=1, source_target_pairs={{0,2},{1,3},{2,0},{3,1},{4,6},{5,7},{6,4},{7,5},{8,10},{9,11},{10,... | collective-permute-start | bytes 147464 | tf_op jit(solution)/shard_map/ppermute | solution.py:161
  90.1 14.5 %collective-permute-start.2 = (bf16[4,6144]{1,0:T(4,128)(2,1)S(1)}, bf16[4,6144]{1,0:T(4,128)(2,1)S(1)}, u32[]{:S(2)}, u32[]{:S(2)}) collective-permute-start(bf16[4,6144]{1,0:T(4,128)(2,1)S(1)} %get-tuple-element.53), channel_id=1, source_target_pairs={{0,3},{1,0},{2,1},{3,2},{4,7},{5,4},{6,5},{7,6},{8,11},{9,8},{10,9... | collective-permute-start | bytes 147464 | tf_op jit(solution)/shard_map/ppermute | solution.py:161
  100.7 14.3 %all-to-all-start.3 = ((bf16[32,12,128]{2,1,0:T(8,128)(2,1)}), bf16[32,12,128]{2,1,0:T(8,128)(2,1)S(1)}, u32[]{:S(2)}, u32[]{:S(2)}) async-start(bf16[32,12,128]{2,1,0:T(8,128)(2,1)} %pad.14), calls=%async_computation.3 | async-start | bytes 262144 | tf_op jit(solution)/shard_map/all_to_all | solution.py:128
  105.6 17.8 %copy-start.13 = (pred[16]{0:T(512)(128)(4,1)S(1)}, pred[16]{0:T(512)(128)(4,1)}, u32[]{:S(2)}) copy-start(pred[16]{0:T(512)(128)(4,1)} %broadcast_in_dim.50) | copy-start | bytes 52
  119.5 19.7 %all-to-all-start.4 = ((bf16[32,16,288]{2,1,0:T(8,128)(2,1)}), bf16[32,16,288]{2,1,0:T(8,128)(2,1)S(1)}, u32[]{:S(2)}, u32[]{:S(2)}) async-start(bf16[32,16,288]{2,1,0:T(8,128)(2,1)} %bitcast.24), calls=%async_computation.4 | async-start | bytes 786432 | tf_op jit(solution)/shard_map/all_to_all | solution.py:64
  124.2 27.1 %collective-permute-start.3 = (bf16[16,6144]{1,0:T(8,128)(2,1)}, bf16[16,6144]{1,0:T(8,128)(2,1)}, u32[]{:S(2)}, u32[]{:S(2)}) collective-permute-start(bf16[16,6144]{1,0:T(8,128)(2,1)} %broadcast_select_fusion), channel_id=1, source_target_pairs={{0,0},{1,8},{2,16},{3,24},{4,1},{5,9},{6,17},{7,25},{8,2},{9,10},{... | collective-permute-start | bytes 589832 | tf_op jit(solution)/shard_map/ppermute | solution.py:165
  140.7 10.7 %copy-start.3 = (bf16[1,1,16,6144]{3,2,1,0:T(8,128)(2,1)S(1)}, bf16[1,1,16,6144]{3,2,1,0:T(8,128)(2,1)}, u32[]{:S(2)}) copy-start(bf16[1,1,16,6144]{3,2,1,0:T(8,128)(2,1)} %param.32) | copy-start | bytes 589828
  143.0 24.1 %copy-start.11 = (pred[1024]{0:T(1024)(128)(4,1)S(1)}, pred[1024]{0:T(1024)(128)(4,1)}, u32[]{:S(2)}) copy-start(pred[1024]{0:T(1024)(128)(4,1)} %concatenate.29) | copy-start | bytes 3076
  143.9 23.1 %all-to-all-start.5 = ((bf16[32,48,128]{2,1,0:T(8,128)(2,1)}), bf16[32,48,128]{2,1,0:T(8,128)(2,1)S(1)}, u32[]{:S(2)}, u32[]{:S(2)}) async-start(bf16[32,48,128]{2,1,0:T(8,128)(2,1)} %pad.15.clone), calls=%async_computation.5 | async-start | bytes 786432 | tf_op jit(solution)/shard_map/all_to_all | solution.py:128
  151.1 107.4 %all-gather.6.cloned.1.call-start = ((), (), s32[]{:S(2)}) async-start(), calls=%async_computation.12 | async-start | bytes 4325376 | tf_op jit(solution)/shard_map/all_gather | solution.py:196
  171.3 55.8 %copy-start.5 = (bf16[1,1,4,3072]{3,2,1,0:T(4,128)(2,1)S(1)}, bf16[1,1,4,3072]{3,2,1,0:T(4,128)(2,1)}, u32[]{:S(2)}) copy-start(bf16[1,1,4,3072]{3,2,1,0:T(4,128)(2,1)} %param.18) | copy-start | bytes 73732
  171.3 55.8 %copy-start.9 = (f32[1,1,3072]{2,1,0:T(1,128)S(1)}, f32[1,1,3072]{2,1,0:T(1,128)}, u32[]{:S(2)}) copy-start(f32[1,1,3072]{2,1,0:T(1,128)} %get-tuple-element.45) | copy-start | bytes 36868
  171.3 56.1 %copy-start.7 = (f32[1,1,3072]{2,1,0:T(1,128)S(1)}, f32[1,1,3072]{2,1,0:T(1,128)}, u32[]{:S(2)}) copy-start(f32[1,1,3072]{2,1,0:T(1,128)} %get-tuple-element.41) | copy-start | bytes 36868
  171.3 56.1 %copy-start.8 = (f32[1,1,3072]{2,1,0:T(1,128)S(1)}, f32[1,1,3072]{2,1,0:T(1,128)}, u32[]{:S(2)}) copy-start(f32[1,1,3072]{2,1,0:T(1,128)} %get-tuple-element.42) | copy-start | bytes 36868
  171.3 40.7 %all-to-all-start.6 = ((bf16[32,128,128]{2,1,0:T(8,128)(2,1)}), bf16[32,128,128]{2,1,0:T(8,128)(2,1)S(1)}, u32[]{:S(2)}, u32[]{:S(2)}) async-start(bf16[32,128,128]{2,1,0:T(8,128)(2,1)} %broadcast_in_dim.94), calls=%async_computation.6 | async-start | bytes 2097152 | tf_op jit(solution)/shard_map/all_to_all | solution.py:71
  228.6 28.3 %all-to-all-start.8 = ((bf16[32,4,3072]{2,1,0:T(4,128)(2,1)}), bf16[32,4,3072]{2,1,0:T(4,128)(2,1)}, u32[]{:S(2)}, u32[]{:S(2)}) async-start(bf16[32,4,3072]{2,1,0:T(4,128)(2,1)} %broadcast_in_dim.95), calls=%async_computation.8 | async-start | bytes 1572864 | tf_op jit(solution)/shard_map/all_to_all | solution.py:71
  263.1 15.1 %all-to-all-start.9 = ((bf16[32,16,96]{2,1,0:T(8,128)(2,1)}), bf16[32,16,96]{2,1,0:T(8,128)(2,1)S(1)}, u32[]{:S(2)}, u32[]{:S(2)}) async-start(bf16[32,16,96]{2,1,0:T(8,128)(2,1)} %bitcast.58), calls=%async_computation.9 | async-start | bytes 262144 | tf_op jit(solution)/shard_map/all_to_all | solution.py:64
  271.5 15.4 %copy-start.10 = (bf16[4,6144]{1,0:T(4,128)(2,1)S(1)}, bf16[4,6144]{1,0:T(4,128)(2,1)}, u32[]{:S(2)}) copy-start(bf16[4,6144]{1,0:T(4,128)(2,1)} %param.33) | copy-start | bytes 147460
  271.5 15.4 %copy-start.1 = (bf16[1,1,16,3072]{3,2,1,0:T(8,128)(2,1)S(1)}, bf16[1,1,16,3072]{3,2,1,0:T(8,128)(2,1)}, u32[]{:S(2)}) copy-start(bf16[1,1,16,3072]{3,2,1,0:T(8,128)(2,1)} %param.19) | copy-start | bytes 294916
  271.5 36.9 %copy-start.6 = (f32[1,1,3072]{2,1,0:T(1,128)S(1)}, f32[1,1,3072]{2,1,0:T(1,128)}, u32[]{:S(2)}) copy-start(f32[1,1,3072]{2,1,0:T(1,128)} %get-tuple-element.40) | copy-start | bytes 36868
  271.5 42.7 %copy-start.14 = (f32[1,4,32]{2,1,0:T(4,128)S(1)}, f32[1,4,32]{2,1,0:T(4,128)}, u32[]{:S(2)}) copy-start(f32[1,4,32]{2,1,0:T(4,128)} %param.35) | copy-start | bytes 1540
  280.9 27.2 %all-to-all-start.10 = ((bf16[32,4,3072]{2,1,0:T(4,128)(2,1)}), bf16[32,4,3072]{2,1,0:T(4,128)(2,1)S(1)}, u32[]{:S(2)}, u32[]{:S(2)}) async-start(bf16[32,4,3072]{2,1,0:T(4,128)(2,1)} %reshape.530), calls=%async_computation.10 | async-start | bytes 1572864 | tf_op jit(solution)/shard_map/all_to_all | solution.py:227
  286.9 23.1 %collective-permute-start.5 = (bf16[16,3072]{1,0:T(8,128)(2,1)S(1)}, bf16[16,3072]{1,0:T(8,128)(2,1)S(1)}, u32[]{:S(2)}, u32[]{:S(2)}) collective-permute-start(bf16[16,3072]{1,0:T(8,128)(2,1)S(1)} %fusion.53), channel_id=1, source_target_pairs={{128,0},{0,128},{129,1},{1,129},{130,2},{2,130},{131,3},{3,131},{1... | collective-permute-start | bytes 294920 | tf_op jit(solution)/shard_map/ppermute | solution.py:20
  308.4 5.4 %collective-permute-start.4 = (bf16[4,3072]{1,0:T(4,128)(2,1)S(1)}, bf16[4,3072]{1,0:T(4,128)(2,1)S(1)}, u32[]{:S(2)}, u32[]{:S(2)}) collective-permute-start(bf16[4,3072]{1,0:T(4,128)(2,1)S(1)} %add_convert_fusion), channel_id=1, source_target_pairs={{128,0},{0,128},{129,1},{1,129},{130,2},{2,130},{131,3},{3,131},{1... | collective-permute-start | bytes 73736 | tf_op jit(solution)/shard_map/ppermute | solution.py:20
  (2 other events, 3.2 us)
Sparse Core Ops, SparseCore 0:
  20.8 75.6 all-gather.3
  170.0 75.1 all-gather.5
